TPU v7x, 512 devices: a whole 4x4x16 slice. The times are simulated.
512 devices in a mesh: grp: 16 (over z_hi, x, core), dev: 32 (over y, z_lo).
Axes of the slice: x: 4, y: 4, z: 16 (z_hi: 2, z_lo: 8; z = z_hi * 8 + z_lo), core: 2. Of those that a mesh axis runs over, the one named last changes fastest.
Arguments:
- samples: bfloat16 [16384, 1024], P(('grp', 'dev')), may hold values from -0.1875 to 0.1875
- set_labels: int32 [16384], P(('grp', 'dev')), may hold values 0 or 1
- sign_words: int32 [16384, 25], P(('grp', 'dev')), may hold values from 0 to 2097151
- corpus: bfloat16 [16384, 1024], P(('grp', 'dev')), may hold values from -0.1875 to 0.1875
- scale_grid: float32 [16], replicated, may hold values from 0.25 to 4
- scale_pick: int32 [4], replicated, may hold values from 0 to 15
Outputs:
- quad_forms: float32 [4, 512], replicated
- test_scores: float32 [4], replicated
- proof: float32 [4, 16384], P(None, ('grp', 'dev'))
Inputs may be any that keep to these rules, and one draw needn't show every extreme that they name: `sign_words`: every word is below 2 ** 21; each of its 21 bits is a sign, 1 for +1 and 0 for -1. `scale_pick`: indices into the grid, from 0 to 15.
All inputs are finite; a program needn't handle non-finite values. No bound on the sum of `set_labels` on one device may be relied on, other than what follows from the above.
Results may differ from a plain program's by a relative error of at most 0.0099.
Values may be sent and summed in bfloat16 or wider, within the bound.
No kernel may reach another device: no remote copies, remote signals or barrier semaphores. Data moves between devices by JAX's collectives and lax.ppermute only.
A program may use at most 64 MiB of HBM per device.

v0:
```python
import jax
import jax.numpy as jnp
from jax import lax
from jax.sharding import PartitionSpec as P

NB = 4
BOOT = 511


word_bits = 21


def make_vectors(set_labels, sign_words):
    weights = (1 - 2 * set_labels).astype(jnp.float32)
    shifts = jnp.arange(word_bits, dtype=jnp.int32)
    bit_flags = jnp.right_shift(sign_words[:, :, None], shifts[None, None, :]) & 1
    bit_flags = bit_flags.reshape(sign_words.shape[0], -1)[:, :BOOT]
    sign_values = (2 * bit_flags - 1).astype(jnp.float32)
    vectors = jnp.concatenate([weights[:, None], sign_values * weights[:, None]], axis=1)
    return vectors.astype(jnp.bfloat16)


def band_scales(scale_grid, scale_pick):
    onehot = (
        scale_pick[:, None] == jnp.arange(scale_grid.shape[0], dtype=jnp.int32)[None, :]
    ).astype(jnp.float32)
    chosen = jnp.sum(onehot * scale_grid[None, :], axis=1)
    return 0.5 / chosen


def squares(matrix):
    wide = matrix.astype(jnp.float32)
    return jnp.sum(wide * wide, axis=1)


def distances(left, left_sq, right, right_sq):
    cross = lax.dot_general(
        left, right, (((1,), (1,)), ((), ())), preferred_element_type=jnp.float32
    )
    return left_sq[:, None] + right_sq[None, :] - 2.0 * cross


def test_terms(block_rows, block_vec, col_rows, col_sq, col_vec, scales):
    dist = distances(block_rows, squares(block_rows), col_rows, col_sq)
    block_wide = block_vec.astype(jnp.float32)
    results = []
    for kernel_id in range(NB):
        kern = jnp.exp(-dist * scales[kernel_id]).astype(jnp.bfloat16)
        product = jnp.dot(kern, col_vec, preferred_element_type=jnp.float32)
        results.append(jnp.sum(block_wide * product, axis=0))
    return jnp.stack(results)


def proof_terms(corp_rows, corp_sq, sample_rows, sample_sq, sample_weights, scales):
    dist = distances(corp_rows, corp_sq, sample_rows, sample_sq)
    results = []
    for kernel_id in range(NB):
        kern = jnp.exp(-dist * scales[kernel_id]).astype(jnp.bfloat16)
        results.append(jnp.dot(kern, sample_weights, preferred_element_type=jnp.float32))
    return jnp.stack(results)


def per_device(samples, set_labels, sign_words, corpus, scale_grid, scale_pick):
    scales = band_scales(scale_grid, scale_pick)
    col_rows, col_labels, col_words = (
        lax.all_gather(samples, "grp", axis=0, tiled=True),
        lax.all_gather(set_labels, "grp", axis=0, tiled=True),
        lax.all_gather(sign_words, "grp", axis=0, tiled=True),
    )
    col_vec = make_vectors(col_labels, col_words)
    col_sq = squares(col_rows)
    total = col_rows.shape[0] * lax.axis_size("dev")
    inv_root = jnp.float32(1.0) / jnp.sqrt(jnp.float32(total))
    block_rows = lax.all_gather(samples, "dev", axis=0, tiled=True)
    block_labels = lax.all_gather(set_labels, "dev", axis=0, tiled=True)
    block_words = lax.all_gather(sign_words, "dev", axis=0, tiled=True)
    block_vec = make_vectors(block_labels, block_words)
    forms_part = test_terms(block_rows, block_vec, col_rows, col_sq, col_vec, scales)
    group_corpus = lax.all_gather(corpus, "dev", axis=0, tiled=True)
    proof_part = proof_terms(
        group_corpus, squares(group_corpus), col_rows, col_sq, col_vec[:, 0], scales
    )
    proof = lax.psum_scatter(proof_part, "dev", scatter_dimension=1, tiled=True) * inv_root
    quad_forms = lax.psum(forms_part, ("grp", "dev")) / total
    bootstrap = quad_forms[:, 1:]
    centre = jnp.mean(bootstrap, axis=1)
    spread = jnp.mean(jnp.square(bootstrap - centre[:, None]), axis=1)
    test_scores = (quad_forms[:, 0] - centre) / jnp.sqrt(spread + 1e-06)
    return (quad_forms, test_scores, proof)


def solution(mesh):
    in_specs = (
        P(("grp", "dev"), None),
        P(("grp", "dev")),
        P(("grp", "dev"), None),
        P(("grp", "dev"), None),
        P(),
        P(),
    )
    out_specs = (P(), P(), P(None, ("grp", "dev")))
    return jax.shard_map(
        per_device, mesh=mesh, in_specs=in_specs, out_specs=out_specs, check_vma=False
    )
```

profile of v0, /device:TPU:6, one launch (start us, length us, event | category | flops | bytes accessed | tf_op | source)
XLA Modules:
  0.0 904.4 jit_solution(65554573227792653)
XLA Ops:
  9.4 1.3 dynamic-slice.1
  10.7 1.3 dynamic-slice
  14.1 22.7 %all-reduce.1 = s32[512]{0:T(512)S(1)} all-reduce(s32[512]{0:T(512)S(1)} %dynamic-update-slice.1), channel_id=1, replica_groups=mesh['grp'=16,'dev'=32] {'grp'}, use_global_device_ids=true, to_apply=%add.1 | all-reduce | flops 512 | bytes 4096
  37.7 19.0 %all-reduce = s32[1024]{0:T(1024)S(1)} all-reduce(s32[1024]{0:T(1024)S(1)} %dynamic-update-slice), channel_id=1, replica_groups=mesh['grp'=16,'dev'=32] {'dev'}, use_global_device_ids=true, to_apply=%add | all-reduce | flops 1024 | bytes 8192
  57.4 35.1 %all_gather.26 = s32[512,25]{1,0:T(8,128)S(1)} all-gather(s32[32,25]{1,0:T(8,128)} %param.8), channel_id=1, replica_groups=mesh['grp'=16,'dev'=32] {'grp'}, dimensions={0}, use_global_device_ids=true | all-gather | bytes 54400 | tf_op jit(solution)/shard_map/all_gather | solution.py:68
  92.6 128.3 %all_gather.22 = s32[1024,25]{1,0:T(8,128)S(1)} all-gather(s32[32,25]{1,0:T(8,128)} %param.8), channel_id=1, replica_groups=mesh['grp'=16,'dev'=32] {'dev'}, dimensions={0}, use_global_device_ids=true | all-gather | bytes 105600 | tf_op jit(solution)/shard_map/all_gather | solution.py:76
  222.0 1.2 shift_right_arithmetic.40
  223.2 1.6 shift_right_arithmetic.41
  226.4 1.1 fusion.19
  227.5 3.1 fusion.9
  230.6 1.6 multiply_reduce_fusion.2
  232.2 83.6 %all-gather.8.cloned.1.call-done = bf16[1024,1024]{1,0:T(8,128)(2,1)} async-done(((bf16[32,1024]{1,0:T(8,128)(2,1)}), bf16[1024,1024]{1,0:T(8,128)(2,1)}) %all-gather.8.cloned.1.call-update) | async-done | bytes 2097168 | tf_op jit(solution)/shard_map/all_gather | solution.py:79
  315.8 2.2 multiply_reduce_fusion
  318.0 1.3 subtract_negate_fusion
  321.4 222.6 %all-gather.4.cloned.1.call-done = bf16[1024,1024]{1,0:T(8,128)(2,1)} async-done(((bf16[32,1024]{1,0:T(8,128)(2,1)}), bf16[1024,1024]{1,0:T(8,128)(2,1)}) %all-gather.4.cloned.1.call-update) | async-done | bytes 2097168 | tf_op jit(solution)/shard_map/all_gather | solution.py:74
  543.9 2.2 multiply_reduce_fusion.1
  546.2 1.3 subtract_negate_fusion.1
  547.5 1.6 fusion.3
  549.1 1.6 fusion.2
  551.7 1.5 fusion.1
  553.2 1.0 fusion.10
  554.2 1.6 fusion
  555.9 101.5 %psum.7 = f32[4,512]{1,0:T(4,128)S(1)} all-reduce(f32[4,512]{1,0:T(4,128)S(1)} %pad_maximum_fusion.3), channel_id=1, replica_groups=mesh['grp'=16,'dev'=32] {'grp','dev'}, use_global_device_ids=true, to_apply=%region_7.0 | all-reduce | flops 2048 | bytes 16384 | tf_op jit(solution)/shard_map/psum | solution.py:84
  659.5 237.0 %reduce-scatter.4.cloned.1.call-done = f32[32,4]{1,0:T(8,128)} async-done(((f32[1024,4]{1,0:T(8,128)}), f32[32,4]{1,0:T(8,128)}) %reduce-scatter.4.cloned.1.call-update) | async-done | bytes 528
  (55 shorter events, 13.9 us)
Async XLA Ops:
  7.2 223.4 %all-gather.6.cloned.1.call-start = ((), (), s32[]{:S(2)}) async-start(), calls=%async_computation.2 | async-start | bytes 1114112 | tf_op jit(solution)/shard_map/all_gather | solution.py:66
  7.9 307.9 %all-gather.8.cloned.1.call-start = ((), (), s32[]{:S(2)}) async-start(), calls=%async_computation.3 | async-start | bytes 2162688 | tf_op jit(solution)/shard_map/all_gather | solution.py:79
  8.6 535.3 %all-gather.4.cloned.1.call-start = ((), (), s32[]{:S(2)}) async-start(), calls=%async_computation.1 | async-start | bytes 2162688 | tf_op jit(solution)/shard_map/all_gather | solution.py:74
  9.4 887.1 %reduce-scatter.4.cloned.1.call-start = ((), (), s32[]{:S(2)}) async-start(), calls=%async_computation.4 | async-start | bytes 540672
  230.6 87.4 %copy-start.2 = (bf16[512,1024]{1,0:T(8,128)(2,1)S(1)}, bf16[512,1024]{1,0:T(8,128)(2,1)}, u32[]{:S(2)}) copy-start(bf16[512,1024]{1,0:T(8,128)(2,1)} %all-gather.6.cloned.1.call-done) | copy-start | bytes 3145732
  315.8 2.2 copy-start.1
  543.9 2.2 copy-start
  546.2 1.3 copy-start.3
  546.2 1.3 copy-start.4
  546.2 1.3 copy-start.6
  657.4 240.5 %copy-start.5 = (f32[4,512]{1,0:T(4,128)}, f32[4,512]{1,0:T(4,128)S(1)}, u32[]{:S(2)}) copy-start(f32[4,512]{1,0:T(4,128)S(1)} %broadcast_multiply_fusion) | copy-start | bytes 24580
Sparse Core Ops, SparseCore 0:
  11.3 83.4 all-gather.5
  96.9 218.8 all-gather.7
  317.8 226.0 all-gather.3
  658.9 237.5 reduce-scatter.3
where the time goes:
time: 905 us; the launch traced here: 904 us
  waiting for transfers between devices  545 us (60%)
  blocking collectives  307 us (34%)
  between operations  15.2 us (2%)
  matrix products  13 us (1%)
  other arithmetic  12.7 us (1%)
  local copies, waits for them, and re-layouts  11.6 us (1%)
    unnamed x5, waiting for transfers between devices  239 us
    all_gather x1, waiting for transfers between devices, per_device(): block_rows = lax.all_gather(samples, 'dev', axis=0, tiled=True)  223 us
    all_gather x1, blocking collectives, per_device(): block_words = lax.all_gather(sign_words, 'dev', axis=0, tiled=True)  128 us
    psum x1, blocking collectives, per_device(): quad_forms = lax.psum(forms_part, ('grp', 'dev')) / total  102 us
    all_gather x1, waiting for transfers between devices, per_device(): group_corpus = lax.all_gather(corpus, 'dev', axis=0, tiled=True)  83.6 us
    unnamed x2, blocking collectives  41.7 us
    all_gather x1, blocking collectives, per_device(): lax.all_gather(sign_words, 'grp', axis=0, tiled=True)  35.1 us
  transfers between devices with their start and end apart: 4, of which 3 were waited for; matrix products, arithmetic and copies ran while one was open for 3% of the time, Pallas kernels for 0%

commit v1 on v0

v1 whole, which is shorter than its diff:
```python
import numpy as np
import jax
import jax.numpy as jnp
from jax import lax
from jax.sharding import PartitionSpec as P

NB = 4
BOOT = 511
D = 1024
META = 128
CHUNK = 7


word_bits = 21


def make_vectors(set_labels, sign_words):
    weights = (1 - 2 * set_labels).astype(jnp.float32)
    shifts = jnp.arange(word_bits, dtype=jnp.int32)
    bit_flags = jnp.right_shift(sign_words[:, :, None], shifts[None, None, :]) & 1
    bit_flags = bit_flags.reshape(sign_words.shape[0], -1)[:, :BOOT]
    sign_values = (2 * bit_flags - 1).astype(jnp.float32)
    vectors = jnp.concatenate([weights[:, None], sign_values * weights[:, None]], axis=1)
    return vectors.astype(jnp.bfloat16)


def band_scales(scale_grid, scale_pick):
    onehot = (
        scale_pick[:, None] == jnp.arange(scale_grid.shape[0], dtype=jnp.int32)[None, :]
    ).astype(jnp.float32)
    chosen = jnp.sum(onehot * scale_grid[None, :], axis=1)
    return 0.5 / chosen


def squares(matrix):
    wide = matrix.astype(jnp.float32)
    return jnp.sum(wide * wide, axis=1)


def distances(left, left_sq, right, right_sq):
    cross = lax.dot_general(
        left, right, (((1,), (1,)), ((), ())), preferred_element_type=jnp.float32
    )
    return left_sq[:, None] + right_sq[None, :] - 2.0 * cross


def pack_meta(set_labels, sign_words):
    words = sign_words.shape[1]
    chunks = [(sign_words >> (CHUNK * c)) & ((1 << CHUNK) - 1) for c in range(3)]
    meta = jnp.concatenate([set_labels[:, None]] + chunks, axis=1)
    pad = META - meta.shape[1]
    meta = jnp.pad(meta, ((0, 0), (0, pad)))
    return meta.astype(jnp.bfloat16), words


def unpack(buf, words):
    rows = buf[:, :D]
    meta = buf[:, D:D + 1 + 3 * words].astype(jnp.float32).astype(jnp.int32)
    labels = meta[:, 0]
    c = [meta[:, 1 + k * words:1 + (k + 1) * words] for k in range(3)]
    sign_words = c[0] + (c[1] << CHUNK) + (c[2] << (2 * CHUNK))
    return rows, make_vectors(labels, sign_words)


def xor_gather(x, axis, n, bits):
    idx = lax.axis_index(axis)
    buf = x[None]
    for b in bits:
        k = 1 << b
        other = lax.ppermute(buf, axis, [(i, i ^ k) for i in range(n)])
        lo = (idx & k) == 0
        buf = jnp.where(lo, jnp.concatenate([buf, other]), jnp.concatenate([other, buf]))
    order = [sum(((t >> j) & 1) << b for j, b in enumerate(bits)) for t in range(n)]
    return buf, order


def per_device(samples, set_labels, sign_words, corpus, scale_grid, scale_pick):
    scales = band_scales(scale_grid, scale_pick)
    n_grp = lax.axis_size("grp")
    n_dev = lax.axis_size("dev")
    rows_here = samples.shape[0]
    total = rows_here * n_grp * n_dev
    inv_root = jnp.float32(1.0) / jnp.sqrt(jnp.float32(total))

    meta, words = pack_meta(set_labels, sign_words)
    own = jnp.concatenate([samples, meta], axis=1)
    own_wide = jnp.concatenate([own, corpus], axis=1)

    grp_bits = [b for b in range(1, n_grp.bit_length() - 1)] + [0]
    dev_bits = list(range(n_dev.bit_length() - 1))
    col_buf, col_order = xor_gather(own_wide, "grp", n_grp, grp_bits)
    blk_buf, _ = xor_gather(own, "dev", n_dev, dev_bits)

    col_buf = col_buf.reshape(n_grp * rows_here, -1)
    blk_buf = blk_buf.reshape(n_dev * rows_here, -1)
    col_rows, col_vec = unpack(col_buf[:, :D + META], words)
    col_corpus = col_buf[:, D + META:]
    block_rows, block_vec = unpack(blk_buf, words)

    col_sq = squares(col_rows)
    block_sq = squares(block_rows)

    dist = distances(block_rows, block_sq, col_rows, col_sq)
    block_wide = block_vec.astype(jnp.float32)
    forms = []
    for kernel_id in range(NB):
        kern = jnp.exp(-dist * scales[kernel_id]).astype(jnp.bfloat16)
        product = jnp.dot(kern, col_vec, preferred_element_type=jnp.float32)
        forms.append(jnp.sum(block_wide * product, axis=0))
    forms_part = jnp.stack(forms)

    cdist = distances(col_corpus, squares(col_corpus), block_rows, block_sq)
    weights = block_vec[:, 0]
    proofs = []
    for kernel_id in range(NB):
        kern = jnp.exp(-cdist * scales[kernel_id]).astype(jnp.bfloat16)
        proofs.append(jnp.dot(kern, weights, preferred_element_type=jnp.float32))
    proof_part = jnp.stack(proofs).reshape(NB, n_grp, rows_here)
    inverse = np.argsort(np.array(col_order))
    proof_part = jnp.take(proof_part, jnp.asarray(inverse, jnp.int32), axis=1)
    proof_part = jnp.transpose(proof_part, (1, 0, 2))
    got = lax.all_to_all(proof_part, "grp", 0, 0, tiled=True)
    proof = jnp.sum(got, axis=0) * inv_root

    quad_forms = lax.psum(forms_part, ("grp", "dev")) / total
    bootstrap = quad_forms[:, 1:]
    centre = jnp.mean(bootstrap, axis=1)
    spread = jnp.mean(jnp.square(bootstrap - centre[:, None]), axis=1)
    test_scores = (quad_forms[:, 0] - centre) / jnp.sqrt(spread + 1e-06)
    return (quad_forms, test_scores, proof)


def solution(mesh):
    in_specs = (
        P(("grp", "dev"), None),
        P(("grp", "dev")),
        P(("grp", "dev"), None),
        P(("grp", "dev"), None),
        P(),
        P(),
    )
    out_specs = (P(), P(), P(None, ("grp", "dev")))
    return jax.shard_map(
        per_device, mesh=mesh, in_specs=in_specs, out_specs=out_specs, check_vma=False
    )
```

time: 905 us -> 326 us (0.36)
  waiting for transfers between devices: 545 us -> 127 us
  blocking collectives: 307 us -> 99.9 us
  starting transfers between devices: 0.15 us -> 51.1 us
  between operations: 15.2 us -> 1.06 us
    all_gather x3 -> x0, waiting for transfers between devices: 306 us -> none  [the longest x1 223 us: per_device(): block_rows = lax.all_gather(samples, 'dev', axis=0, tiled=True)]
    unnamed x5 -> x0, waiting for transfers between devices: 239 us -> none
    all_gather x2 -> x0, blocking collectives: 163 us -> none  [the longest x1 128 us: per_device(): block_words = lax.all_gather(sign_words, 'dev', axis=0, tiled=True)]
    ppermute x0 -> x9, waiting for transfers between devices: none -> 115 us  [xor_gather(): other = lax.ppermute(buf, axis, [(i, i ^ k) for i in range(n)])]
    ppermute x0 -> x9, starting transfers between devices: none -> 43.1 us  [xor_gather(): other = lax.ppermute(buf, axis, [(i, i ^ k) for i in range(n)])]
    unnamed x2 -> x0, blocking collectives: 41.7 us -> none
    all_to_all x0 -> x1, waiting for transfers between devices: none -> 12.1 us  [per_device(): got = lax.all_to_all(proof_part, 'grp', 0, 0, tiled=True)]
  transfers between devices with their start and end apart: 4 -> 10, of which waited for: 3 -> 7; matrix products, arithmetic and copies ran while one was open for 3% -> 3% of each run, Pallas kernels for 0% -> 0%
where the time goes in v1:
time: 326 us; the launch traced here: 323 us
  waiting for transfers between devices  127 us (39%)
  blocking collectives  99.9 us (31%)
  starting transfers between devices  51.1 us (16%)
  other arithmetic  18.2 us (6%)
  matrix products  18.1 us (6%)
  local copies, waits for them, and re-layouts  7.41 us (2%)
    ppermute x9, waiting for transfers between devices, xor_gather(): other = lax.ppermute(buf, axis, [(i, i ^ k) for i in range(n)])  115 us
    psum x1, blocking collectives, per_device(): quad_forms = lax.psum(forms_part, ('grp', 'dev')) / total  99.9 us
    ppermute x9, starting transfers between devices, xor_gather(): other = lax.ppermute(buf, axis, [(i, i ^ k) for i in range(n)])  43.1 us
    all_to_all x1, waiting for transfers between devices, per_device(): got = lax.all_to_all(proof_part, 'grp', 0, 0, tiled=True)  12.1 us
    dot_general x2, matrix products, distances(): lax.dot_general(left, right, (((1,), (1,)), ((), ())), preferred_element_...  8.5 us
    all_to_all x1, starting transfers between devices, per_device(): got = lax.all_to_all(proof_part, 'grp', 0, 0, tiled=True)  8.01 us
  transfers between devices with their start and end apart: 10, of which 7 were waited for; matrix products, arithmetic and copies ran while one was open for 3% of the time, Pallas kernels for 0%

profile of v1, /device:TPU:6, one launch (start us, length us, event | category | flops | bytes accessed | tf_op | source)
XLA Modules:
  0.0 322.7 jit_solution(3288057333134248958)
XLA Ops:
  3.1 2.7 collective-permute-start.5
  5.9 4.6 %collective-permute-done.5 = bf16[1,32,2176]{2,1,0:T(8,128)(2,1)S(1)} collective-permute-done((bf16[1,32,2176]{2,1,0:T(8,128)(2,1)S(1)}, bf16[1,32,2176]{2,1,0:T(8,128)(2,1)S(1)}, u32[]{:S(2)}, u32[]{:S(2)}) %collective-permute-start.5) | collective-permute-done | bytes 139296 | tf_op jit(solution)/shard_map/ppermute | solution.py:70
  10.4 6.8 %collective-permute-start.6 = (bf16[2,32,2176]{2,1,0:T(8,128)(2,1)S(1)}, bf16[2,32,2176]{2,1,0:T(8,128)(2,1)S(1)}, u32[]{:S(2)}, u32[]{:S(2)}) collective-permute-start(bf16[2,32,2176]{2,1,0:T(8,128)(2,1)S(1)} %maximum_select_fusion.7), channel_id=1, source_target_pairs={{0,128},{32,160},{64,192},{96,224},{128,0},{160,32},{192,64},{224,... | collective-permute-start | bytes 835592 | tf_op jit(solution)/shard_map/ppermute | solution.py:70
  18.1 1.9 collective-permute-start
  20.1 1.7 collective-permute-done.6
  21.9 15.3 %collective-permute-start.7 = (bf16[4,32,2176]{2,1,0:T(8,128)(2,1)S(1)}, bf16[4,32,2176]{2,1,0:T(8,128)(2,1)S(1)}, u32[]{:S(2)}, u32[]{:S(2)}) collective-permute-start(bf16[4,32,2176]{2,1,0:T(8,128)(2,1)S(1)} %maximum_select_fusion.5), channel_id=1, source_target_pairs={{0,256},{32,288},{64,320},{96,352},{128,384},{160,416},{192,448},{... | collective-permute-start | bytes 1671176 | tf_op jit(solution)/shard_map/ppermute | solution.py:70
  37.3 3.5 %collective-permute-start.1 = (bf16[2,32,1152]{2,1,0:T(8,128)(2,1)S(1)}, bf16[2,32,1152]{2,1,0:T(8,128)(2,1)S(1)}, u32[]{:S(2)}, u32[]{:S(2)}) collective-permute-start(bf16[2,32,1152]{2,1,0:T(8,128)(2,1)S(1)} %maximum_select_fusion.8), channel_id=1, source_target_pairs={{0,2},{1,3},{2,0},{3,1},{4,6},{5,7},{6,4},{7,5},{8,10},{9,11},{10,... | collective-permute-start | bytes 442376 | tf_op jit(solution)/shard_map/ppermute | solution.py:70
  40.8 50.2 %collective-permute-done.1 = bf16[2,32,1152]{2,1,0:T(8,128)(2,1)S(1)} collective-permute-done((bf16[2,32,1152]{2,1,0:T(8,128)(2,1)S(1)}, bf16[2,32,1152]{2,1,0:T(8,128)(2,1)S(1)}, u32[]{:S(2)}, u32[]{:S(2)}) %collective-permute-start.1) | collective-permute-done | bytes 147488 | tf_op jit(solution)/shard_map/ppermute | solution.py:70
  91.1 2.3 collective-permute-start.2
  93.6 1.9 collective-permute-start.8
  95.5 26.9 %collective-permute-done.2 = bf16[4,32,1152]{2,1,0:T(8,128)(2,1)S(1)} collective-permute-done((bf16[4,32,1152]{2,1,0:T(8,128)(2,1)S(1)}, bf16[4,32,1152]{2,1,0:T(8,128)(2,1)S(1)}, u32[]{:S(2)}, u32[]{:S(2)}) %collective-permute-start.2) | collective-permute-done | bytes 294944 | tf_op jit(solution)/shard_map/ppermute | solution.py:70
  122.6 3.5 %collective-permute-start.3 = (bf16[8,32,1152]{2,1,0:T(8,128)(2,1)S(1)}, bf16[8,32,1152]{2,1,0:T(8,128)(2,1)S(1)}, u32[]{:S(2)}, u32[]{:S(2)}) collective-permute-start(bf16[8,32,1152]{2,1,0:T(8,128)(2,1)S(1)} %maximum_select_fusion.4), channel_id=1, source_target_pairs={{0,8},{1,9},{2,10},{3,11},{4,12},{5,13},{6,14},{7,15},{8,0},{9,1},... | collective-permute-start | bytes 1769480 | tf_op jit(solution)/shard_map/ppermute | solution.py:70
  127.1 12.6 %collective-permute-done.3 = bf16[8,32,1152]{2,1,0:T(8,128)(2,1)S(1)} collective-permute-done((bf16[8,32,1152]{2,1,0:T(8,128)(2,1)S(1)}, bf16[8,32,1152]{2,1,0:T(8,128)(2,1)S(1)}, u32[]{:S(2)}, u32[]{:S(2)}) %collective-permute-start.3) | collective-permute-done | bytes 589856 | tf_op jit(solution)/shard_map/ppermute | solution.py:70
  140.9 5.1 %collective-permute-start.4 = (bf16[16,32,1152]{2,1,0:T(8,128)(2,1)}, bf16[16,32,1152]{2,1,0:T(8,128)(2,1)}, u32[]{:S(2)}, u32[]{:S(2)}) collective-permute-start(bf16[16,32,1152]{2,1,0:T(8,128)(2,1)} %maximum_select_fusion.2), channel_id=1, source_target_pairs={{0,16},{1,17},{2,18},{3,19},{4,20},{5,21},{6,22},{7,23},{8,24},{9,... | collective-permute-start | bytes 3538952 | tf_op jit(solution)/shard_map/ppermute | solution.py:70
  146.1 2.0 maximum_select_fusion.1
  152.9 18.7 %collective-permute-done.4 = bf16[16,32,1152]{2,1,0:T(8,128)(2,1)} collective-permute-done((bf16[16,32,1152]{2,1,0:T(8,128)(2,1)}, bf16[16,32,1152]{2,1,0:T(8,128)(2,1)}, u32[]{:S(2)}, u32[]{:S(2)}) %collective-permute-start.4) | collective-permute-done | bytes 1179680 | tf_op jit(solution)/shard_map/ppermute | solution.py:70
  171.7 2.6 maximum_select_fusion
  176.3 1.7 shift_right_arithmetic.65
  178.0 2.2 fusion.9
  180.3 2.5 subtract_negate_fusion.1
  189.3 99.9 %psum.7 = f32[4,512]{1,0:T(4,128)S(1)} all-reduce(f32[4,512]{1,0:T(4,128)S(1)} %pad_maximum_fusion.3), channel_id=1, replica_groups=mesh['grp'=16,'dev'=32] {'grp','dev'}, use_global_device_ids=true, to_apply=%region_7.8 | all-reduce | flops 2048 | bytes 16384 | tf_op jit(solution)/shard_map/psum | solution.py:125
  289.5 6.0 %exponential_convert_fusion.3 = (bf16[512,1024]{1,0:T(8,128)(2,1)S(1)}, bf16[512,1024]{1,0:T(8,128)(2,1)S(1)}, bf16[512,1024]{1,0:T(8,128)(2,1)S(1)}, bf16[512,1024]{1,0:T(8,128)(2,1)S(1)}) fusion(f32[]{:T(128)} %bitcast.6, f32[]{:T(128)} %bitcast.13, f32[]{:T(128)} %bitcast.11, f32[]{:T(128)} %bitcast.9, bf16[1024,1152]{1,0:T(8,128)(2,1)S(1)} %bitcast.50, ...), kind=kOutput, calls=%fused_computation.22 | convolution fusion | flops 1080033280 | bytes 7348224 | tf_op jit(solution)/shard_map/dot_general | solution.py:41
  300.0 8.0 %all-to-all-start = ((f32[16,1,128]{2,1,0:T(1,128)}), f32[16,1,128]{2,1,0:T(1,128)S(1)}, u32[]{:S(2)}, u32[]{:S(2)}) async-start(f32[16,1,128]{2,1,0:T(1,128)} %reshape.96), calls=%async_computation | async-start | bytes 16384 | tf_op jit(solution)/shard_map/all_to_all | solution.py:122
  308.7 12.1 %all-to-all-done = f32[16,1,128]{2,1,0:T(1,128)S(1)} async-done(((f32[16,1,128]{2,1,0:T(1,128)}), f32[16,1,128]{2,1,0:T(1,128)S(1)}, u32[]{:S(2)}, u32[]{:S(2)}) %all-to-all-start) | async-done | bytes 8224 | tf_op jit(solution)/shard_map/all_to_all | solution.py:122
  (78 shorter events, 26.7 us)
Async XLA Ops:
  3.1 7.3 %collective-permute-start.5 = (bf16[1,32,2176]{2,1,0:T(8,128)(2,1)S(1)}, bf16[1,32,2176]{2,1,0:T(8,128)(2,1)S(1)}, u32[]{:S(2)}, u32[]{:S(2)}) collective-permute-start(bf16[1,32,2176]{2,1,0:T(8,128)(2,1)S(1)} %maximum_bitcast_fusion), channel_id=1, source_target_pairs={{0,64},{32,96},{64,0},{96,32},{128,192},{160,224},{192,128},{224,1... | collective-permute-start | bytes 417800 | tf_op jit(solution)/shard_map/ppermute | solution.py:70
  10.4 11.3 %collective-permute-start.6 = (bf16[2,32,2176]{2,1,0:T(8,128)(2,1)S(1)}, bf16[2,32,2176]{2,1,0:T(8,128)(2,1)S(1)}, u32[]{:S(2)}, u32[]{:S(2)}) collective-permute-start(bf16[2,32,2176]{2,1,0:T(8,128)(2,1)S(1)} %maximum_select_fusion.7), channel_id=1, source_target_pairs={{0,128},{32,160},{64,192},{96,224},{128,0},{160,32},{192,64},{224,... | collective-permute-start | bytes 835592 | tf_op jit(solution)/shard_map/ppermute | solution.py:70
  18.1 19.1 %collective-permute-start = (bf16[1,32,1152]{2,1,0:T(8,128)(2,1)S(1)}, bf16[1,32,1152]{2,1,0:T(8,128)(2,1)S(1)}, u32[]{:S(2)}, u32[]{:S(2)}) collective-permute-start(bf16[1,32,1152]{2,1,0:T(8,128)(2,1)S(1)} %maximum_bitcast_fusion.1), channel_id=1, source_target_pairs={{0,1},{1,0},{2,3},{3,2},{4,5},{5,4},{6,7},{7,6},{8,9},{9,8},{10,11... | collective-permute-start | bytes 221192 | tf_op jit(solution)/shard_map/ppermute | solution.py:70
  21.9 71.5 %collective-permute-start.7 = (bf16[4,32,2176]{2,1,0:T(8,128)(2,1)S(1)}, bf16[4,32,2176]{2,1,0:T(8,128)(2,1)S(1)}, u32[]{:S(2)}, u32[]{:S(2)}) collective-permute-start(bf16[4,32,2176]{2,1,0:T(8,128)(2,1)S(1)} %maximum_select_fusion.5), channel_id=1, source_target_pairs={{0,256},{32,288},{64,320},{96,352},{128,384},{160,416},{192,448},{... | collective-permute-start | bytes 1671176 | tf_op jit(solution)/shard_map/ppermute | solution.py:70
  37.3 88.9 %copy-start.5 = (s32[16]{0:T(128)S(1)}, s32[16]{0:T(128)}, u32[]{:S(2)}) copy-start(s32[16]{0:T(128)} %constant.97) | copy-start | bytes 196
  37.3 88.9 %copy-start.6 = (f32[16]{0:T(128)S(1)}, f32[16]{0:T(128)}, u32[]{:S(2)}) copy-start(f32[16]{0:T(128)} %param.11) | copy-start | bytes 196
  37.3 88.9 %copy-start.7 = (s32[4]{0:T(128)S(1)}, s32[4]{0:T(128)}, u32[]{:S(2)}) copy-start(s32[4]{0:T(128)} %param.12) | copy-start | bytes 52
  37.3 53.7 %collective-permute-start.1 = (bf16[2,32,1152]{2,1,0:T(8,128)(2,1)S(1)}, bf16[2,32,1152]{2,1,0:T(8,128)(2,1)S(1)}, u32[]{:S(2)}, u32[]{:S(2)}) collective-permute-start(bf16[2,32,1152]{2,1,0:T(8,128)(2,1)S(1)} %maximum_select_fusion.8), channel_id=1, source_target_pairs={{0,2},{1,3},{2,0},{3,1},{4,6},{5,7},{6,4},{7,5},{8,10},{9,11},{10,... | collective-permute-start | bytes 442376 | tf_op jit(solution)/shard_map/ppermute | solution.py:70
  91.1 31.4 %collective-permute-start.2 = (bf16[4,32,1152]{2,1,0:T(8,128)(2,1)S(1)}, bf16[4,32,1152]{2,1,0:T(8,128)(2,1)S(1)}, u32[]{:S(2)}, u32[]{:S(2)}) collective-permute-start(bf16[4,32,1152]{2,1,0:T(8,128)(2,1)S(1)} %maximum_select_fusion.6), channel_id=1, source_target_pairs={{0,4},{1,5},{2,6},{3,7},{4,0},{5,1},{6,2},{7,3},{8,12},{9,13},{10,... | collective-permute-start | bytes 884744 | tf_op jit(solution)/shard_map/ppermute | solution.py:70
  93.6 52.4 %collective-permute-start.8 = (bf16[8,32,2176]{2,1,0:T(8,128)(2,1)S(1)}, bf16[8,32,2176]{2,1,0:T(8,128)(2,1)}, u32[]{:S(2)}, u32[]{:S(2)}) collective-permute-start(bf16[8,32,2176]{2,1,0:T(8,128)(2,1)S(1)} %maximum_select_fusion.3), channel_id=1, source_target_pairs={{0,32},{32,0},{64,96},{96,64},{128,160},{160,128},{192,224},{224,1... | collective-permute-start | bytes 3342344 | tf_op jit(solution)/shard_map/ppermute | solution.py:70
  122.6 17.1 %collective-permute-start.3 = (bf16[8,32,1152]{2,1,0:T(8,128)(2,1)S(1)}, bf16[8,32,1152]{2,1,0:T(8,128)(2,1)S(1)}, u32[]{:S(2)}, u32[]{:S(2)}) collective-permute-start(bf16[8,32,1152]{2,1,0:T(8,128)(2,1)S(1)} %maximum_select_fusion.4), channel_id=1, source_target_pairs={{0,8},{1,9},{2,10},{3,11},{4,12},{5,13},{6,14},{7,15},{8,0},{9,1},... | collective-permute-start | bytes 1769480 | tf_op jit(solution)/shard_map/ppermute | solution.py:70
  140.9 30.7 %collective-permute-start.4 = (bf16[16,32,1152]{2,1,0:T(8,128)(2,1)}, bf16[16,32,1152]{2,1,0:T(8,128)(2,1)}, u32[]{:S(2)}, u32[]{:S(2)}) collective-permute-start(bf16[16,32,1152]{2,1,0:T(8,128)(2,1)} %maximum_select_fusion.2), channel_id=1, source_target_pairs={{0,16},{1,17},{2,18},{3,19},{4,20},{5,21},{6,22},{7,23},{8,24},{9,... | collective-permute-start | bytes 3538952 | tf_op jit(solution)/shard_map/ppermute | solution.py:70
  148.0 4.1 %copy-start.2 = (bf16[16,32,2176]{2,1,0:T(8,128)(2,1)}, bf16[16,32,2176]{2,1,0:T(8,128)(2,1)S(1)}, u32[]{:S(2)}) copy-start(bf16[16,32,2176]{2,1,0:T(8,128)(2,1)S(1)} %maximum_select_fusion.1) | copy-start | bytes 6684676
  151.3 1.3 copy-start.3
  174.3 1.4 copy-start
  178.0 2.3 copy-start.1
  289.2 18.8 %copy-start.4 = (f32[4,512]{1,0:T(4,128)}, f32[4,512]{1,0:T(4,128)S(1)}, u32[]{:S(2)}) copy-start(f32[4,512]{1,0:T(4,128)S(1)} %broadcast_multiply_fusion) | copy-start | bytes 24580
  300.0 20.8 %all-to-all-start = ((f32[16,1,128]{2,1,0:T(1,128)}), f32[16,1,128]{2,1,0:T(1,128)S(1)}, u32[]{:S(2)}, u32[]{:S(2)}) async-start(f32[16,1,128]{2,1,0:T(1,128)} %reshape.96), calls=%async_computation | async-start | bytes 16384 | tf_op jit(solution)/shard_map/all_to_all | solution.py:122

commit v2 on v1

--- a/solution.py
+++ b/solution.py
@@ -74,6 +74,28 @@
     return buf, order
 
 
+GRP_ORDER = (3, 1, 2, 0)
+DEV_ORDER = (2, 4, 1, 0, 3)
+SUM_ORDER = (("grp", 0), ("dev", 0), ("dev", 1), ("dev", 2), ("grp", 1), ("grp", 2), ("dev", 3), ("dev", 4), ("grp", 3))
+
+
+def axis_order(n, preferred):
+    nbits = n.bit_length() - 1
+    bits = [b for b in preferred if b < nbits]
+    return bits + [b for b in range(nbits) if b not in bits]
+
+
+def xor_sum(x, n_grp, n_dev):
+    sizes = {"grp": n_grp, "dev": n_dev}
+    steps = [(a, b) for a, b in SUM_ORDER if (1 << b) < sizes[a]]
+    for a in sizes:
+        steps += [(a, b) for b in range(sizes[a].bit_length() - 1) if (a, b) not in steps]
+    for a, b in steps:
+        k = 1 << b
+        x = x + lax.ppermute(x, a, [(i, i ^ k) for i in range(sizes[a])])
+    return x
+
+
 def per_device(samples, set_labels, sign_words, corpus, scale_grid, scale_pick):
     scales = band_scales(scale_grid, scale_pick)
     n_grp = lax.axis_size("grp")
@@ -86,8 +108,8 @@
     own = jnp.concatenate([samples, meta], axis=1)
     own_wide = jnp.concatenate([own, corpus], axis=1)
 
-    grp_bits = [b for b in range(1, n_grp.bit_length() - 1)] + [0]
-    dev_bits = list(range(n_dev.bit_length() - 1))
+    grp_bits = axis_order(n_grp, GRP_ORDER)
+    dev_bits = axis_order(n_dev, DEV_ORDER)
     col_buf, col_order = xor_gather(own_wide, "grp", n_grp, grp_bits)
     blk_buf, _ = xor_gather(own, "dev", n_dev, dev_bits)
 
@@ -122,7 +144,7 @@
     got = lax.all_to_all(proof_part, "grp", 0, 0, tiled=True)
     proof = jnp.sum(got, axis=0) * inv_root
 
-    quad_forms = lax.psum(forms_part, ("grp", "dev")) / total
+    quad_forms = xor_sum(forms_part, n_grp, n_dev) / total
     bootstrap = quad_forms[:, 1:]
     centre = jnp.mean(bootstrap, axis=1)
     spread = jnp.mean(jnp.square(bootstrap - centre[:, None]), axis=1)

time: 326 us -> 216 us (0.66)
  blocking collectives: 99.9 us -> 0 us
  waiting for transfers between devices: 127 us -> 65 us
  starting transfers between devices: 51.1 us -> 105 us
    psum x1 -> x0, blocking collectives: 99.9 us -> none  [per_device(): quad_forms = lax.psum(forms_part, ('grp', 'dev')) / total]
    ppermute x9, waiting for transfers between devices: 115 us -> 47.6 us  [xor_gather(): other = lax.ppermute(buf, axis, [(i, i ^ k) for i in range(n)])]
    ppermute x0 -> x9, starting transfers between devices: none -> 38.8 us  [xor_sum(): x = x + lax.ppermute(x, a, [(i, i ^ k) for i in range(sizes[a])])]
    ppermute x0 -> x9, waiting for transfers between devices: none -> 17.4 us  [xor_sum(): x = x + lax.ppermute(x, a, [(i, i ^ k) for i in range(sizes[a])])]
    all_to_all x1, waiting for transfers between devices: 12.1 us -> 0.01 us  [per_device(): got = lax.all_to_all(proof_part, 'grp', 0, 0, tiled=True)]
    ppermute x9, starting transfers between devices: 43.1 us -> 52.9 us  [xor_gather(): other = lax.ppermute(buf, axis, [(i, i ^ k) for i in range(n)])]
    all_to_all x1, starting transfers between devices: 8.01 us -> 13.2 us  [per_device(): got = lax.all_to_all(proof_part, 'grp', 0, 0, tiled=True)]
  transfers between devices with their start and end apart: 10 -> 19, of which waited for: 7 -> 13; matrix products, arithmetic and copies ran while one was open for 3% -> 8% of each run, Pallas kernels for 0% -> 0%
where the time goes in v2:
time: 216 us; the launch traced here: 215 us
  starting transfers between devices  105 us (49%)
  waiting for transfers between devices  65 us (30%)
  other arithmetic  18.3 us (8%)
  matrix products  18 us (8%)
  local copies, waits for them, and re-layouts  7.36 us (3%)
    ppermute x9, starting transfers between devices, xor_gather(): other = lax.ppermute(buf, axis, [(i, i ^ k) for i in range(n)])  52.9 us
    ppermute x9, waiting for transfers between devices, xor_gather(): other = lax.ppermute(buf, axis, [(i, i ^ k) for i in range(n)])  47.6 us
    ppermute x9, starting transfers between devices, xor_sum(): x = x + lax.ppermute(x, a, [(i, i ^ k) for i in range(sizes[a])])  38.8 us
    ppermute x9, waiting for transfers between devices, xor_sum(): x = x + lax.ppermute(x, a, [(i, i ^ k) for i in range(sizes[a])])  17.4 us
    all_to_all x1, starting transfers between devices, per_device(): got = lax.all_to_all(proof_part, 'grp', 0, 0, tiled=True)  13.2 us
    dot_general x2, matrix products, distances(): lax.dot_general(left, right, (((1,), (1,)), ((), ())), preferred_element_...  8.48 us
    dot_general x4, matrix products, per_device(): product = jnp.dot(kern, col_vec, preferred_element_type=jnp.float32)  6.38 us
    select_n x9, other arithmetic, xor_gather(): jnp.where(lo, jnp.concatenate([buf, other]), jnp.concatenate([other, buf]))  6.31 us
  transfers between devices with their start and end apart: 19, of which 13 were waited for; matrix products, arithmetic and copies ran while one was open for 8% of the time, Pallas kernels for 0%

profile of v2, /device:TPU:6, one launch (start us, length us, event | category | flops | bytes accessed | tf_op | source)
XLA Modules:
  0.0 214.7 jit_solution(1740036054202822329)
XLA Ops:
  3.1 15.7 %collective-permute-start.5 = (bf16[1,32,2176]{2,1,0:T(8,128)(2,1)S(1)}, bf16[1,32,2176]{2,1,0:T(8,128)(2,1)S(1)}, u32[]{:S(2)}, u32[]{:S(2)}) collective-permute-start(bf16[1,32,2176]{2,1,0:T(8,128)(2,1)S(1)} %maximum_bitcast_fusion), channel_id=1, source_target_pairs={{0,256},{32,288},{64,320},{96,352},{128,384},{160,416},{192,448},{... | collective-permute-start | bytes 417800 | tf_op jit(solution)/shard_map/ppermute | solution.py:70
  18.8 3.9 %collective-permute-done.5 = bf16[1,32,2176]{2,1,0:T(8,128)(2,1)S(1)} collective-permute-done((bf16[1,32,2176]{2,1,0:T(8,128)(2,1)S(1)}, bf16[1,32,2176]{2,1,0:T(8,128)(2,1)S(1)}, u32[]{:S(2)}, u32[]{:S(2)}) %collective-permute-start.5) | collective-permute-done | bytes 139296 | tf_op jit(solution)/shard_map/ppermute | solution.py:70
  22.8 2.7 %collective-permute-start.6 = (bf16[2,32,2176]{2,1,0:T(8,128)(2,1)S(1)}, bf16[2,32,2176]{2,1,0:T(8,128)(2,1)S(1)}, u32[]{:S(2)}, u32[]{:S(2)}) collective-permute-start(bf16[2,32,2176]{2,1,0:T(8,128)(2,1)S(1)} %maximum_select_fusion.7), channel_id=1, source_target_pairs={{0,64},{32,96},{64,0},{96,32},{128,192},{160,224},{192,128},{224,1... | collective-permute-start | bytes 835592 | tf_op jit(solution)/shard_map/ppermute | solution.py:70
  26.4 12.7 %collective-permute-start = (bf16[1,32,1152]{2,1,0:T(8,128)(2,1)S(1)}, bf16[1,32,1152]{2,1,0:T(8,128)(2,1)S(1)}, u32[]{:S(2)}, u32[]{:S(2)}) collective-permute-start(bf16[1,32,1152]{2,1,0:T(8,128)(2,1)S(1)} %maximum_bitcast_fusion.1), channel_id=1, source_target_pairs={{0,4},{1,5},{2,6},{3,7},{4,0},{5,1},{6,2},{7,3},{8,12},{9,13},{10,... | collective-permute-start | bytes 221192 | tf_op jit(solution)/shard_map/ppermute | solution.py:70
  39.3 3.0 %collective-permute-start.7 = (bf16[4,32,2176]{2,1,0:T(8,128)(2,1)S(1)}, bf16[4,32,2176]{2,1,0:T(8,128)(2,1)S(1)}, u32[]{:S(2)}, u32[]{:S(2)}) collective-permute-start(bf16[4,32,2176]{2,1,0:T(8,128)(2,1)S(1)} %maximum_select_fusion.5), channel_id=1, source_target_pairs={{0,128},{32,160},{64,192},{96,224},{128,0},{160,32},{192,64},{224,... | collective-permute-start | bytes 1671176 | tf_op jit(solution)/shard_map/ppermute | solution.py:70
  42.3 5.3 %collective-permute-start.1 = (bf16[2,32,1152]{2,1,0:T(8,128)(2,1)S(1)}, bf16[2,32,1152]{2,1,0:T(8,128)(2,1)S(1)}, u32[]{:S(2)}, u32[]{:S(2)}) collective-permute-start(bf16[2,32,1152]{2,1,0:T(8,128)(2,1)S(1)} %maximum_select_fusion.8), channel_id=1, source_target_pairs={{0,16},{1,17},{2,18},{3,19},{4,20},{5,21},{6,22},{7,23},{8,24},{9,... | collective-permute-start | bytes 442376 | tf_op jit(solution)/shard_map/ppermute | solution.py:70
  47.6 3.4 %collective-permute-done.1 = bf16[2,32,1152]{2,1,0:T(8,128)(2,1)S(1)} collective-permute-done((bf16[2,32,1152]{2,1,0:T(8,128)(2,1)S(1)}, bf16[2,32,1152]{2,1,0:T(8,128)(2,1)S(1)}, u32[]{:S(2)}, u32[]{:S(2)}) %collective-permute-start.1) | collective-permute-done | bytes 147488 | tf_op jit(solution)/shard_map/ppermute | solution.py:70
  51.1 6.1 %collective-permute-start.2 = (bf16[4,32,1152]{2,1,0:T(8,128)(2,1)S(1)}, bf16[4,32,1152]{2,1,0:T(8,128)(2,1)S(1)}, u32[]{:S(2)}, u32[]{:S(2)}) collective-permute-start(bf16[4,32,1152]{2,1,0:T(8,128)(2,1)S(1)} %maximum_select_fusion.6), channel_id=1, source_target_pairs={{0,2},{1,3},{2,0},{3,1},{4,6},{5,7},{6,4},{7,5},{8,10},{9,11},{10,... | collective-permute-start | bytes 884744 | tf_op jit(solution)/shard_map/ppermute | solution.py:70
  59.3 9.6 %collective-permute-done.2 = bf16[4,32,1152]{2,1,0:T(8,128)(2,1)S(1)} collective-permute-done((bf16[4,32,1152]{2,1,0:T(8,128)(2,1)S(1)}, bf16[4,32,1152]{2,1,0:T(8,128)(2,1)S(1)}, u32[]{:S(2)}, u32[]{:S(2)}) %collective-permute-start.2) | collective-permute-done | bytes 294944 | tf_op jit(solution)/shard_map/ppermute | solution.py:70
  71.9 13.1 %collective-permute-done.3 = bf16[8,32,1152]{2,1,0:T(8,128)(2,1)S(1)} collective-permute-done((bf16[8,32,1152]{2,1,0:T(8,128)(2,1)S(1)}, bf16[8,32,1152]{2,1,0:T(8,128)(2,1)S(1)}, u32[]{:S(2)}, u32[]{:S(2)}) %collective-permute-start.3) | collective-permute-done | bytes 589856 | tf_op jit(solution)/shard_map/ppermute | solution.py:70
  86.2 3.5 %collective-permute-start.4 = (bf16[16,32,1152]{2,1,0:T(8,128)(2,1)}, bf16[16,32,1152]{2,1,0:T(8,128)(2,1)}, u32[]{:S(2)}, u32[]{:S(2)}) collective-permute-start(bf16[16,32,1152]{2,1,0:T(8,128)(2,1)} %maximum_select_fusion.2), channel_id=1, source_target_pairs={{0,8},{1,9},{2,10},{3,11},{4,12},{5,13},{6,14},{7,15},{8,0},{9,1},... | collective-permute-start | bytes 3538952 | tf_op jit(solution)/shard_map/ppermute | solution.py:70
  96.6 17.7 %collective-permute-done.4 = bf16[16,32,1152]{2,1,0:T(8,128)(2,1)} collective-permute-done((bf16[16,32,1152]{2,1,0:T(8,128)(2,1)}, bf16[16,32,1152]{2,1,0:T(8,128)(2,1)}, u32[]{:S(2)}, u32[]{:S(2)}) %collective-permute-start.4) | collective-permute-done | bytes 1179680 | tf_op jit(solution)/shard_map/ppermute | solution.py:70
  114.2 2.6 %maximum_select_fusion = bf16[32,32,1152]{2,1,0:T(8,128)(2,1)S(1)} fusion(bf16[16,32,1152]{2,1,0:T(8,128)(2,1)} %collective-permute-done.4, bf16[16,32,1152]{2,1,0:T(8,128)(2,1)} %maximum_select_fusion.2, pred[]{:T(512)S(6)} %eq.40), kind=kLoop, calls=%fused_computation.6 | loop fusion | flops 3538944 | bytes 4718593 | tf_op jit(solution)/shard_map/jit(_where)/select_n | solution.py:72
  131.7 6.0 %exponential_convert_fusion.3 = (bf16[512,1024]{1,0:T(8,128)(2,1)S(1)}, bf16[512,1024]{1,0:T(8,128)(2,1)S(1)}, bf16[512,1024]{1,0:T(8,128)(2,1)S(1)}, bf16[512,1024]{1,0:T(8,128)(2,1)S(1)}) fusion(f32[]{:T(128)} %bitcast.6, f32[]{:T(128)} %bitcast.13, f32[]{:T(128)} %bitcast.11, f32[]{:T(128)} %bitcast.9, bf16[1024,1152]{1,0:T(8,128)(2,1)S(1)} %bitcast.50, ...), kind=kOutput, calls=%fused_computation.22 | convolution fusion | flops 1080033280 | bytes 7348224 | tf_op jit(solution)/shard_map/dot_general | solution.py:41
  149.1 3.7 %collective-permute-done.11 = f32[4,512]{1,0:T(4,128)S(1)} collective-permute-done((f32[4,512]{1,0:T(4,128)S(1)}, f32[4,512]{1,0:T(4,128)S(1)}, u32[]{:S(2)}, u32[]{:S(2)}) %collective-permute-start.11) | collective-permute-done | bytes 8224 | tf_op jit(solution)/shard_map/ppermute | solution.py:95
  152.8 5.6 %collective-permute-start.12 = (f32[4,512]{1,0:T(4,128)S(1)}, f32[4,512]{1,0:T(4,128)S(1)}, u32[]{:S(2)}, u32[]{:S(2)}) collective-permute-start(f32[4,512]{1,0:T(4,128)S(1)} %add.85), channel_id=1, source_target_pairs={{0,4},{1,5},{2,6},{3,7},{4,0},{5,1},{6,2},{7,3},{8,12},{9,13},{10,... | collective-permute-start | bytes 24584 | tf_op jit(solution)/shard_map/ppermute | solution.py:95
  159.2 3.1 %collective-permute-done.12 = f32[4,512]{1,0:T(4,128)S(1)} collective-permute-done((f32[4,512]{1,0:T(4,128)S(1)}, f32[4,512]{1,0:T(4,128)S(1)}, u32[]{:S(2)}, u32[]{:S(2)}) %collective-permute-start.12) | collective-permute-done | bytes 8224 | tf_op jit(solution)/shard_map/ppermute | solution.py:95
  162.3 2.9 %collective-permute-start.13 = (f32[4,512]{1,0:T(4,128)S(1)}, f32[4,512]{1,0:T(4,128)S(1)}, u32[]{:S(2)}, u32[]{:S(2)}) collective-permute-start(f32[4,512]{1,0:T(4,128)S(1)} %add.86), channel_id=1, source_target_pairs={{0,64},{32,96},{64,0},{96,32},{128,192},{160,224},{192,128},{224,1... | collective-permute-start | bytes 24584 | tf_op jit(solution)/shard_map/ppermute | solution.py:95
  166.6 13.2 %all-to-all-start = ((f32[16,1,128]{2,1,0:T(1,128)}), f32[16,1,128]{2,1,0:T(1,128)S(1)}, u32[]{:S(2)}, u32[]{:S(2)}) async-start(f32[16,1,128]{2,1,0:T(1,128)} %reshape.96), calls=%async_computation | async-start | bytes 16384 | tf_op jit(solution)/shard_map/all_to_all | solution.py:144
  179.8 3.4 %collective-permute-start.14 = (f32[4,512]{1,0:T(4,128)S(1)}, f32[4,512]{1,0:T(4,128)S(1)}, u32[]{:S(2)}, u32[]{:S(2)}) collective-permute-start(f32[4,512]{1,0:T(4,128)S(1)} %add.87), channel_id=1, source_target_pairs={{0,128},{32,160},{64,192},{96,224},{128,0},{160,32},{192,64},{224,... | collective-permute-start | bytes 24584 | tf_op jit(solution)/shard_map/ppermute | solution.py:95
  183.2 3.7 %collective-permute-done.14 = f32[4,512]{1,0:T(4,128)S(1)} collective-permute-done((f32[4,512]{1,0:T(4,128)S(1)}, f32[4,512]{1,0:T(4,128)S(1)}, u32[]{:S(2)}, u32[]{:S(2)}) %collective-permute-start.14) | collective-permute-done | bytes 8224 | tf_op jit(solution)/shard_map/ppermute | solution.py:95
  186.8 3.5 %collective-permute-start.15 = (f32[4,512]{1,0:T(4,128)S(1)}, f32[4,512]{1,0:T(4,128)S(1)}, u32[]{:S(2)}, u32[]{:S(2)}) collective-permute-start(f32[4,512]{1,0:T(4,128)S(1)} %add.88), channel_id=1, source_target_pairs={{0,8},{1,9},{2,10},{3,11},{4,12},{5,13},{6,14},{7,15},{8,0},{9,1},... | collective-permute-start | bytes 24584 | tf_op jit(solution)/shard_map/ppermute | solution.py:95
  192.4 5.1 %collective-permute-start.16 = (f32[4,512]{1,0:T(4,128)S(1)}, f32[4,512]{1,0:T(4,128)S(1)}, u32[]{:S(2)}, u32[]{:S(2)}) collective-permute-start(f32[4,512]{1,0:T(4,128)S(1)} %add.89), channel_id=1, source_target_pairs={{0,16},{1,17},{2,18},{3,19},{4,20},{5,21},{6,22},{7,23},{8,24},{9,... | collective-permute-start | bytes 24584 | tf_op jit(solution)/shard_map/ppermute | solution.py:95
  199.4 12.1 %collective-permute-start.17 = (f32[4,512]{1,0:T(4,128)S(1)}, f32[4,512]{1,0:T(4,128)S(1)}, u32[]{:S(2)}, u32[]{:S(2)}) collective-permute-start(f32[4,512]{1,0:T(4,128)S(1)} %add.90), channel_id=1, source_target_pairs={{0,256},{32,288},{64,320},{96,352},{128,384},{160,416},{192,448},{... | collective-permute-start | bytes 24584 | tf_op jit(solution)/shard_map/ppermute | solution.py:95
  (103 shorter events, 52.1 us)
Async XLA Ops:
  3.1 19.7 %collective-permute-start.5 = (bf16[1,32,2176]{2,1,0:T(8,128)(2,1)S(1)}, bf16[1,32,2176]{2,1,0:T(8,128)(2,1)S(1)}, u32[]{:S(2)}, u32[]{:S(2)}) collective-permute-start(bf16[1,32,2176]{2,1,0:T(8,128)(2,1)S(1)} %maximum_bitcast_fusion), channel_id=1, source_target_pairs={{0,256},{32,288},{64,320},{96,352},{128,384},{160,416},{192,448},{... | collective-permute-start | bytes 417800 | tf_op jit(solution)/shard_map/ppermute | solution.py:70
  22.8 16.3 %collective-permute-start.6 = (bf16[2,32,2176]{2,1,0:T(8,128)(2,1)S(1)}, bf16[2,32,2176]{2,1,0:T(8,128)(2,1)S(1)}, u32[]{:S(2)}, u32[]{:S(2)}) collective-permute-start(bf16[2,32,2176]{2,1,0:T(8,128)(2,1)S(1)} %maximum_select_fusion.7), channel_id=1, source_target_pairs={{0,64},{32,96},{64,0},{96,32},{128,192},{160,224},{192,128},{224,1... | collective-permute-start | bytes 835592 | tf_op jit(solution)/shard_map/ppermute | solution.py:70
  26.4 15.8 %collective-permute-start = (bf16[1,32,1152]{2,1,0:T(8,128)(2,1)S(1)}, bf16[1,32,1152]{2,1,0:T(8,128)(2,1)S(1)}, u32[]{:S(2)}, u32[]{:S(2)}) collective-permute-start(bf16[1,32,1152]{2,1,0:T(8,128)(2,1)S(1)} %maximum_bitcast_fusion.1), channel_id=1, source_target_pairs={{0,4},{1,5},{2,6},{3,7},{4,0},{5,1},{6,2},{7,3},{8,12},{9,13},{10,... | collective-permute-start | bytes 221192 | tf_op jit(solution)/shard_map/ppermute | solution.py:70
  39.3 17.9 %collective-permute-start.7 = (bf16[4,32,2176]{2,1,0:T(8,128)(2,1)S(1)}, bf16[4,32,2176]{2,1,0:T(8,128)(2,1)S(1)}, u32[]{:S(2)}, u32[]{:S(2)}) collective-permute-start(bf16[4,32,2176]{2,1,0:T(8,128)(2,1)S(1)} %maximum_select_fusion.5), channel_id=1, source_target_pairs={{0,128},{32,160},{64,192},{96,224},{128,0},{160,32},{192,64},{224,... | collective-permute-start | bytes 1671176 | tf_op jit(solution)/shard_map/ppermute | solution.py:70
  42.3 28.8 %copy-start.5 = (s32[16]{0:T(128)S(1)}, s32[16]{0:T(128)}, u32[]{:S(2)}) copy-start(s32[16]{0:T(128)} %constant.97) | copy-start | bytes 196
  42.3 28.8 %copy-start.6 = (f32[16]{0:T(128)S(1)}, f32[16]{0:T(128)}, u32[]{:S(2)}) copy-start(f32[16]{0:T(128)} %param.11) | copy-start | bytes 196
  42.3 28.8 %copy-start.7 = (s32[4]{0:T(128)S(1)}, s32[4]{0:T(128)}, u32[]{:S(2)}) copy-start(s32[4]{0:T(128)} %param.12) | copy-start | bytes 52
  42.3 8.7 %collective-permute-start.1 = (bf16[2,32,1152]{2,1,0:T(8,128)(2,1)S(1)}, bf16[2,32,1152]{2,1,0:T(8,128)(2,1)S(1)}, u32[]{:S(2)}, u32[]{:S(2)}) collective-permute-start(bf16[2,32,1152]{2,1,0:T(8,128)(2,1)S(1)} %maximum_select_fusion.8), channel_id=1, source_target_pairs={{0,16},{1,17},{2,18},{3,19},{4,20},{5,21},{6,22},{7,23},{8,24},{9,... | collective-permute-start | bytes 442376 | tf_op jit(solution)/shard_map/ppermute | solution.py:70
  51.1 17.8 %collective-permute-start.2 = (bf16[4,32,1152]{2,1,0:T(8,128)(2,1)S(1)}, bf16[4,32,1152]{2,1,0:T(8,128)(2,1)S(1)}, u32[]{:S(2)}, u32[]{:S(2)}) collective-permute-start(bf16[4,32,1152]{2,1,0:T(8,128)(2,1)S(1)} %maximum_select_fusion.6), channel_id=1, source_target_pairs={{0,2},{1,3},{2,0},{3,1},{4,6},{5,7},{6,4},{7,5},{8,10},{9,11},{10,... | collective-permute-start | bytes 884744 | tf_op jit(solution)/shard_map/ppermute | solution.py:70
  57.4 32.3 %collective-permute-start.8 = (bf16[8,32,2176]{2,1,0:T(8,128)(2,1)S(1)}, bf16[8,32,2176]{2,1,0:T(8,128)(2,1)}, u32[]{:S(2)}, u32[]{:S(2)}) collective-permute-start(bf16[8,32,2176]{2,1,0:T(8,128)(2,1)S(1)} %maximum_select_fusion.3), channel_id=1, source_target_pairs={{0,32},{32,0},{64,96},{96,64},{128,160},{160,128},{192,224},{224,1... | collective-permute-start | bytes 3342344 | tf_op jit(solution)/shard_map/ppermute | solution.py:70
  69.0 16.0 %collective-permute-start.3 = (bf16[8,32,1152]{2,1,0:T(8,128)(2,1)S(1)}, bf16[8,32,1152]{2,1,0:T(8,128)(2,1)S(1)}, u32[]{:S(2)}, u32[]{:S(2)}) collective-permute-start(bf16[8,32,1152]{2,1,0:T(8,128)(2,1)S(1)} %maximum_select_fusion.4), channel_id=1, source_target_pairs={{0,1},{1,0},{2,3},{3,2},{4,5},{5,4},{6,7},{7,6},{8,9},{9,8},{10,11... | collective-permute-start | bytes 1769480 | tf_op jit(solution)/shard_map/ppermute | solution.py:70
  86.2 28.1 %collective-permute-start.4 = (bf16[16,32,1152]{2,1,0:T(8,128)(2,1)}, bf16[16,32,1152]{2,1,0:T(8,128)(2,1)}, u32[]{:S(2)}, u32[]{:S(2)}) collective-permute-start(bf16[16,32,1152]{2,1,0:T(8,128)(2,1)} %maximum_select_fusion.2), channel_id=1, source_target_pairs={{0,8},{1,9},{2,10},{3,11},{4,12},{5,13},{6,14},{7,15},{8,0},{9,1},... | collective-permute-start | bytes 3538952 | tf_op jit(solution)/shard_map/ppermute | solution.py:70
  91.6 4.1 %copy-start.2 = (bf16[16,32,2176]{2,1,0:T(8,128)(2,1)}, bf16[16,32,2176]{2,1,0:T(8,128)(2,1)S(1)}, u32[]{:S(2)}) copy-start(bf16[16,32,2176]{2,1,0:T(8,128)(2,1)S(1)} %maximum_select_fusion.1) | copy-start | bytes 6684676
  120.5 2.3 %copy-start.1 = (bf16[32,32,1152]{2,1,0:T(8,128)(2,1)S(1)}, bf16[32,32,1152]{2,1,0:T(8,128)(2,1)}, u32[]{:S(2)}) copy-start(bf16[32,32,1152]{2,1,0:T(8,128)(2,1)} %copy-done) | copy-start | bytes 7077892
  137.7 3.1 %collective-permute-start.9 = (f32[4,512]{1,0:T(4,128)S(1)}, f32[4,512]{1,0:T(4,128)S(1)}, u32[]{:S(2)}, u32[]{:S(2)}) collective-permute-start(f32[4,512]{1,0:T(4,128)S(1)} %pad_maximum_fusion.3), channel_id=1, source_target_pairs={{0,32},{32,0},{64,96},{96,64},{128,160},{160,128},{192,224},{224,1... | collective-permute-start | bytes 24584 | tf_op jit(solution)/shard_map/ppermute | solution.py:95
  140.8 5.5 %collective-permute-start.10 = (f32[4,512]{1,0:T(4,128)S(1)}, f32[4,512]{1,0:T(4,128)S(1)}, u32[]{:S(2)}, u32[]{:S(2)}) collective-permute-start(f32[4,512]{1,0:T(4,128)S(1)} %fusion.51), channel_id=1, source_target_pairs={{0,1},{1,0},{2,3},{3,2},{4,5},{5,4},{6,7},{7,6},{8,9},{9,8},{10,11... | collective-permute-start | bytes 24584 | tf_op jit(solution)/shard_map/ppermute | solution.py:95
  146.4 6.5 %collective-permute-start.11 = (f32[4,512]{1,0:T(4,128)S(1)}, f32[4,512]{1,0:T(4,128)S(1)}, u32[]{:S(2)}, u32[]{:S(2)}) collective-permute-start(f32[4,512]{1,0:T(4,128)S(1)} %fusion.61), channel_id=1, source_target_pairs={{0,2},{1,3},{2,0},{3,1},{4,6},{5,7},{6,4},{7,5},{8,10},{9,11},{10,... | collective-permute-start | bytes 24584 | tf_op jit(solution)/shard_map/ppermute | solution.py:95
  152.8 9.5 %collective-permute-start.12 = (f32[4,512]{1,0:T(4,128)S(1)}, f32[4,512]{1,0:T(4,128)S(1)}, u32[]{:S(2)}, u32[]{:S(2)}) collective-permute-start(f32[4,512]{1,0:T(4,128)S(1)} %add.85), channel_id=1, source_target_pairs={{0,4},{1,5},{2,6},{3,7},{4,0},{5,1},{6,2},{7,3},{8,12},{9,13},{10,... | collective-permute-start | bytes 24584 | tf_op jit(solution)/shard_map/ppermute | solution.py:95
  162.3 17.5 %collective-permute-start.13 = (f32[4,512]{1,0:T(4,128)S(1)}, f32[4,512]{1,0:T(4,128)S(1)}, u32[]{:S(2)}, u32[]{:S(2)}) collective-permute-start(f32[4,512]{1,0:T(4,128)S(1)} %add.86), channel_id=1, source_target_pairs={{0,64},{32,96},{64,0},{96,32},{128,192},{160,224},{192,128},{224,1... | collective-permute-start | bytes 24584 | tf_op jit(solution)/shard_map/ppermute | solution.py:95
  166.6 30.9 %all-to-all-start = ((f32[16,1,128]{2,1,0:T(1,128)}), f32[16,1,128]{2,1,0:T(1,128)S(1)}, u32[]{:S(2)}, u32[]{:S(2)}) async-start(f32[16,1,128]{2,1,0:T(1,128)} %reshape.96), calls=%async_computation | async-start | bytes 16384 | tf_op jit(solution)/shard_map/all_to_all | solution.py:144
  179.8 7.0 %collective-permute-start.14 = (f32[4,512]{1,0:T(4,128)S(1)}, f32[4,512]{1,0:T(4,128)S(1)}, u32[]{:S(2)}, u32[]{:S(2)}) collective-permute-start(f32[4,512]{1,0:T(4,128)S(1)} %add.87), channel_id=1, source_target_pairs={{0,128},{32,160},{64,192},{96,224},{128,0},{160,32},{192,64},{224,... | collective-permute-start | bytes 24584 | tf_op jit(solution)/shard_map/ppermute | solution.py:95
  186.8 5.5 %collective-permute-start.15 = (f32[4,512]{1,0:T(4,128)S(1)}, f32[4,512]{1,0:T(4,128)S(1)}, u32[]{:S(2)}, u32[]{:S(2)}) collective-permute-start(f32[4,512]{1,0:T(4,128)S(1)} %add.88), channel_id=1, source_target_pairs={{0,8},{1,9},{2,10},{3,11},{4,12},{5,13},{6,14},{7,15},{8,0},{9,1},... | collective-permute-start | bytes 24584 | tf_op jit(solution)/shard_map/ppermute | solution.py:95
  192.4 7.0 %collective-permute-start.16 = (f32[4,512]{1,0:T(4,128)S(1)}, f32[4,512]{1,0:T(4,128)S(1)}, u32[]{:S(2)}, u32[]{:S(2)}) collective-permute-start(f32[4,512]{1,0:T(4,128)S(1)} %add.89), channel_id=1, source_target_pairs={{0,16},{1,17},{2,18},{3,19},{4,20},{5,21},{6,22},{7,23},{8,24},{9,... | collective-permute-start | bytes 24584 | tf_op jit(solution)/shard_map/ppermute | solution.py:95
  199.4 14.2 %collective-permute-start.17 = (f32[4,512]{1,0:T(4,128)S(1)}, f32[4,512]{1,0:T(4,128)S(1)}, u32[]{:S(2)}, u32[]{:S(2)}) collective-permute-start(f32[4,512]{1,0:T(4,128)S(1)} %add.90), channel_id=1, source_target_pairs={{0,256},{32,288},{64,320},{96,352},{128,384},{160,416},{192,448},{... | collective-permute-start | bytes 24584 | tf_op jit(solution)/shard_map/ppermute | solution.py:95
  (3 other events, 3.8 us)

commit v3 on v2

--- a/solution.py
+++ b/solution.py
@@ -75,7 +75,7 @@
 
 
 GRP_ORDER = (3, 1, 2, 0)
-DEV_ORDER = (2, 4, 1, 0, 3)
+DEV_ORDERS = ((2, 4, 1, 0, 3), (4, 2, 3, 1, 0))
 SUM_ORDER = (("grp", 0), ("dev", 0), ("dev", 1), ("dev", 2), ("grp", 1), ("grp", 2), ("dev", 3), ("dev", 4), ("grp", 3))
 
 
@@ -109,9 +109,11 @@
     own_wide = jnp.concatenate([own, corpus], axis=1)
 
     grp_bits = axis_order(n_grp, GRP_ORDER)
-    dev_bits = axis_order(n_dev, DEV_ORDER)
+    halves = [own[: rows_here // 2], own[rows_here // 2:]]
     col_buf, col_order = xor_gather(own_wide, "grp", n_grp, grp_bits)
-    blk_buf, _ = xor_gather(own, "dev", n_dev, dev_bits)
+    blk_buf = jnp.concatenate(
+        [xor_gather(h, "dev", n_dev, axis_order(n_dev, o))[0] for h, o in zip(halves, DEV_ORDERS)], axis=1
+    )
 
     col_buf = col_buf.reshape(n_grp * rows_here, -1)
     blk_buf = blk_buf.reshape(n_dev * rows_here, -1)

time: 216 us -> 198 us (0.917)
  waiting for transfers between devices: 65 us -> 46.7 us
  local copies, waits for them, and re-layouts: 7.36 us -> 10.3 us
    ppermute x9 -> x14, waiting for transfers between devices: 47.6 us -> 27.4 us  [xor_gather(): other = lax.ppermute(buf, axis, [(i, i ^ k) for i in range(n)])]
    all_to_all x1, starting transfers between devices: 13.2 us -> 6.65 us  [per_device(): got = lax.all_to_all(proof_part, 'grp', 0, 0, tiled=True)]
    ppermute x9 -> x14, starting transfers between devices: 52.9 us -> 59 us  [xor_gather(): other = lax.ppermute(buf, axis, [(i, i ^ k) for i in range(n)])]
    select_n x9 -> x14, other arithmetic: 6.31 us -> 4.78 us  [xor_gather(): jnp.where(lo, jnp.concatenate([buf, other]), jnp.concatenate([other, buf]))]
  transfers between devices with their start and end apart: 19 -> 24, of which waited for: 13 -> 16; matrix products, arithmetic and copies ran while one was open for 8% -> 9% of each run, Pallas kernels for 0% -> 0%
where the time goes in v3:
time: 198 us; the launch traced here: 197 us
  starting transfers between devices  103 us (52%)
  waiting for transfers between devices  46.7 us (24%)
  matrix products  18.2 us (9%)
  other arithmetic  17.4 us (9%)
  local copies, waits for them, and re-layouts  10.3 us (5%)
    ppermute x14, starting transfers between devices, xor_gather(): other = lax.ppermute(buf, axis, [(i, i ^ k) for i in range(n)])  59 us
    ppermute x9, starting transfers between devices, xor_sum(): x = x + lax.ppermute(x, a, [(i, i ^ k) for i in range(sizes[a])])  37.3 us
    ppermute x14, waiting for transfers between devices, xor_gather(): other = lax.ppermute(buf, axis, [(i, i ^ k) for i in range(n)])  27.4 us
    ppermute x9, waiting for transfers between devices, xor_sum(): x = x + lax.ppermute(x, a, [(i, i ^ k) for i in range(sizes[a])])  19.3 us
    dot_general x2, matrix products, distances(): lax.dot_general(left, right, (((1,), (1,)), ((), ())), preferred_element_...  8.65 us
    all_to_all x1, starting transfers between devices, per_device(): got = lax.all_to_all(proof_part, 'grp', 0, 0, tiled=True)  6.65 us
    dot_general x4, matrix products, per_device(): product = jnp.dot(kern, col_vec, preferred_element_type=jnp.float32)  6.48 us
    shift_right_arithmetic x6, local copies, waits for them, and re-layouts, make_vectors(): jnp.right_shift(sign_words[:, :, None], shifts[None, None, :]) & 1  4.85 us
  transfers between devices with their start and end apart: 24, of which 16 were waited for; matrix products, arithmetic and copies ran while one was open for 9% of the time, Pallas kernels for 0%

profile of v3, /device:TPU:6, one launch (start us, length us, event | category | flops | bytes accessed | tf_op | source)
XLA Modules:
  0.0 196.8 jit_solution(895085077633747021)
XLA Ops:
  3.1 15.7 %collective-permute-start.10 = (bf16[1,32,2176]{2,1,0:T(8,128)(2,1)S(1)}, bf16[1,32,2176]{2,1,0:T(8,128)(2,1)S(1)}, u32[]{:S(2)}, u32[]{:S(2)}) collective-permute-start(bf16[1,32,2176]{2,1,0:T(8,128)(2,1)S(1)} %maximum_bitcast_fusion), channel_id=1, source_target_pairs={{0,256},{32,288},{64,320},{96,352},{128,384},{160,416},{192,448},{... | collective-permute-start | bytes 417800 | tf_op jit(solution)/shard_map/ppermute | solution.py:70
  19.6 4.3 %collective-permute-start = (bf16[1,16,1152]{2,1,0:T(8,128)(2,1)S(1)}, bf16[1,16,1152]{2,1,0:T(8,128)(2,1)S(1)}, u32[]{:S(2)}, u32[]{:S(2)}) collective-permute-start(bf16[1,16,1152]{2,1,0:T(8,128)(2,1)S(1)} %get-tuple-element.13), channel_id=1, source_target_pairs={{0,4},{1,5},{2,6},{3,7},{4,0},{5,1},{6,2},{7,3},{8,12},{9,13},{10,... | collective-permute-start | bytes 110600 | tf_op jit(solution)/shard_map/ppermute | solution.py:70
  23.9 5.1 %collective-permute-start.5 = (bf16[1,16,1152]{2,1,0:T(8,128)(2,1)S(1)}, bf16[1,16,1152]{2,1,0:T(8,128)(2,1)S(1)}, u32[]{:S(2)}, u32[]{:S(2)}) collective-permute-start(bf16[1,16,1152]{2,1,0:T(8,128)(2,1)S(1)} %get-tuple-element.14), channel_id=1, source_target_pairs={{0,16},{1,17},{2,18},{3,19},{4,20},{5,21},{6,22},{7,23},{8,24},{9,... | collective-permute-start | bytes 110600 | tf_op jit(solution)/shard_map/ppermute | solution.py:70
  30.6 4.6 %collective-permute-done = bf16[1,16,1152]{2,1,0:T(8,128)(2,1)S(1)} collective-permute-done((bf16[1,16,1152]{2,1,0:T(8,128)(2,1)S(1)}, bf16[1,16,1152]{2,1,0:T(8,128)(2,1)S(1)}, u32[]{:S(2)}, u32[]{:S(2)}) %collective-permute-start) | collective-permute-done | bytes 36896 | tf_op jit(solution)/shard_map/ppermute | solution.py:70
  35.1 5.1 %collective-permute-start.1 = (bf16[2,16,1152]{2,1,0:T(8,128)(2,1)S(1)}, bf16[2,16,1152]{2,1,0:T(8,128)(2,1)S(1)}, u32[]{:S(2)}, u32[]{:S(2)}) collective-permute-start(bf16[2,16,1152]{2,1,0:T(8,128)(2,1)S(1)} %maximum_select_fusion.12), channel_id=1, source_target_pairs={{0,16},{1,17},{2,18},{3,19},{4,20},{5,21},{6,22},{7,23},{8,24},{9,... | collective-permute-start | bytes 221192 | tf_op jit(solution)/shard_map/ppermute | solution.py:70
  40.3 3.1 %collective-permute-start.6 = (bf16[2,16,1152]{2,1,0:T(8,128)(2,1)S(1)}, bf16[2,16,1152]{2,1,0:T(8,128)(2,1)S(1)}, u32[]{:S(2)}, u32[]{:S(2)}) collective-permute-start(bf16[2,16,1152]{2,1,0:T(8,128)(2,1)S(1)} %maximum_select_fusion.13), channel_id=1, source_target_pairs={{0,4},{1,5},{2,6},{3,7},{4,0},{5,1},{6,2},{7,3},{8,12},{9,13},{10,... | collective-permute-start | bytes 221192 | tf_op jit(solution)/shard_map/ppermute | solution.py:70
  43.4 5.9 %collective-permute-start.2 = (bf16[4,16,1152]{2,1,0:T(8,128)(2,1)S(1)}, bf16[4,16,1152]{2,1,0:T(8,128)(2,1)S(1)}, u32[]{:S(2)}, u32[]{:S(2)}) collective-permute-start(bf16[4,16,1152]{2,1,0:T(8,128)(2,1)S(1)} %maximum_select_fusion.10), channel_id=1, source_target_pairs={{0,2},{1,3},{2,0},{3,1},{4,6},{5,7},{6,4},{7,5},{8,10},{9,11},{10,... | collective-permute-start | bytes 442376 | tf_op jit(solution)/shard_map/ppermute | solution.py:70
  49.4 4.1 %collective-permute-done.6 = bf16[2,16,1152]{2,1,0:T(8,128)(2,1)S(1)} collective-permute-done((bf16[2,16,1152]{2,1,0:T(8,128)(2,1)S(1)}, bf16[2,16,1152]{2,1,0:T(8,128)(2,1)S(1)}, u32[]{:S(2)}, u32[]{:S(2)}) %collective-permute-start.6) | collective-permute-done | bytes 73760 | tf_op jit(solution)/shard_map/ppermute | solution.py:70
  66.2 3.3 %collective-permute-start.12 = (bf16[4,32,2176]{2,1,0:T(8,128)(2,1)S(1)}, bf16[4,32,2176]{2,1,0:T(8,128)(2,1)S(1)}, u32[]{:S(2)}, u32[]{:S(2)}) collective-permute-start(bf16[4,32,2176]{2,1,0:T(8,128)(2,1)S(1)} %maximum_select_fusion.6), channel_id=1, source_target_pairs={{0,128},{32,160},{64,192},{96,224},{128,0},{160,32},{192,64},{224,... | collective-permute-start | bytes 1671176 | tf_op jit(solution)/shard_map/ppermute | solution.py:70
  70.5 3.0 %collective-permute-start.4 = (bf16[16,16,1152]{2,1,0:T(8,128)(2,1)S(1)}, bf16[16,16,1152]{2,1,0:T(8,128)(2,1)S(1)}, u32[]{:S(2)}, u32[]{:S(2)}) collective-permute-start(bf16[16,16,1152]{2,1,0:T(8,128)(2,1)S(1)} %maximum_select_fusion.4), channel_id=1, source_target_pairs={{0,8},{1,9},{2,10},{3,11},{4,12},{5,13},{6,14},{7,15},{8,0},{9,1},... | collective-permute-start | bytes 1769480 | tf_op jit(solution)/shard_map/ppermute | solution.py:70
  73.6 4.7 %collective-permute-done.8 = bf16[8,16,1152]{2,1,0:T(8,128)(2,1)S(1)} collective-permute-done((bf16[8,16,1152]{2,1,0:T(8,128)(2,1)S(1)}, bf16[8,16,1152]{2,1,0:T(8,128)(2,1)S(1)}, u32[]{:S(2)}, u32[]{:S(2)}) %collective-permute-start.8) | collective-permute-done | bytes 294944 | tf_op jit(solution)/shard_map/ppermute | solution.py:70
  86.3 7.8 %collective-permute-done.9 = bf16[16,16,1152]{2,1,0:T(8,128)(2,1)S(1)} collective-permute-done((bf16[16,16,1152]{2,1,0:T(8,128)(2,1)S(1)}, bf16[16,16,1152]{2,1,0:T(8,128)(2,1)S(1)}, u32[]{:S(2)}, u32[]{:S(2)}) %collective-permute-start.9) | collective-permute-done | bytes 589856 | tf_op jit(solution)/shard_map/ppermute | solution.py:70
  100.2 3.1 %fusion.9 = bf16[1024,511]{0,1:T(8,128)(2,1)} fusion(s32[1024,525]{0,1:T(8,128)} %shift_right_arithmetic.65, s32[511]{0:T(512)S(1)} %slice.113, f32[1024]{0:T(1024)S(1)} %bitcast.61), kind=kLoop, calls=%fused_computation.18 | loop fusion | flops 3662848 | bytes 3145724 | tf_op jit(solution)/shard_map/convert.3
  119.9 6.1 %exponential_convert_fusion.3 = (bf16[512,1024]{1,0:T(8,128)(2,1)S(1)}, bf16[512,1024]{1,0:T(8,128)(2,1)S(1)}, bf16[512,1024]{1,0:T(8,128)(2,1)S(1)}, bf16[512,1024]{1,0:T(8,128)(2,1)S(1)}) fusion(f32[]{:T(128)} %bitcast.7, f32[]{:T(128)} %bitcast.14, f32[]{:T(128)} %bitcast.12, f32[]{:T(128)} %bitcast.10, bf16[1024,1152]{1,0:T(8,128)(2,1)S(1)} %bitcast.52, ...), kind=kOutput, calls=%fused_computation.22 | convolution fusion | flops 1080033280 | bytes 7348224 | tf_op jit(solution)/shard_map/dot_general | solution.py:41
  137.4 3.7 %collective-permute-done.16 = f32[4,512]{1,0:T(4,128)S(1)} collective-permute-done((f32[4,512]{1,0:T(4,128)S(1)}, f32[4,512]{1,0:T(4,128)S(1)}, u32[]{:S(2)}, u32[]{:S(2)}) %collective-permute-start.16) | collective-permute-done | bytes 8224 | tf_op jit(solution)/shard_map/ppermute | solution.py:95
  141.1 5.4 %collective-permute-start.17 = (f32[4,512]{1,0:T(4,128)S(1)}, f32[4,512]{1,0:T(4,128)S(1)}, u32[]{:S(2)}, u32[]{:S(2)}) collective-permute-start(f32[4,512]{1,0:T(4,128)S(1)} %add.85), channel_id=1, source_target_pairs={{0,4},{1,5},{2,6},{3,7},{4,0},{5,1},{6,2},{7,3},{8,12},{9,13},{10,... | collective-permute-start | bytes 24584 | tf_op jit(solution)/shard_map/ppermute | solution.py:95
  147.2 3.3 %collective-permute-done.17 = f32[4,512]{1,0:T(4,128)S(1)} collective-permute-done((f32[4,512]{1,0:T(4,128)S(1)}, f32[4,512]{1,0:T(4,128)S(1)}, u32[]{:S(2)}, u32[]{:S(2)}) %collective-permute-start.17) | collective-permute-done | bytes 8224 | tf_op jit(solution)/shard_map/ppermute | solution.py:95
  150.5 3.3 %collective-permute-start.18 = (f32[4,512]{1,0:T(4,128)S(1)}, f32[4,512]{1,0:T(4,128)S(1)}, u32[]{:S(2)}, u32[]{:S(2)}) collective-permute-start(f32[4,512]{1,0:T(4,128)S(1)} %add.86), channel_id=1, source_target_pairs={{0,64},{32,96},{64,0},{96,32},{128,192},{160,224},{192,128},{224,1... | collective-permute-start | bytes 24584 | tf_op jit(solution)/shard_map/ppermute | solution.py:95
  155.2 6.6 %all-to-all-start = ((f32[16,1,128]{2,1,0:T(1,128)}), f32[16,1,128]{2,1,0:T(1,128)S(1)}, u32[]{:S(2)}, u32[]{:S(2)}) async-start(f32[16,1,128]{2,1,0:T(1,128)} %reshape.95), calls=%async_computation | async-start | bytes 16384 | tf_op jit(solution)/shard_map/all_to_all | solution.py:146
  161.9 3.4 %collective-permute-start.19 = (f32[4,512]{1,0:T(4,128)S(1)}, f32[4,512]{1,0:T(4,128)S(1)}, u32[]{:S(2)}, u32[]{:S(2)}) collective-permute-start(f32[4,512]{1,0:T(4,128)S(1)} %add.87), channel_id=1, source_target_pairs={{0,128},{32,160},{64,192},{96,224},{128,0},{160,32},{192,64},{224,... | collective-permute-start | bytes 24584 | tf_op jit(solution)/shard_map/ppermute | solution.py:95
  165.2 3.7 %collective-permute-done.19 = f32[4,512]{1,0:T(4,128)S(1)} collective-permute-done((f32[4,512]{1,0:T(4,128)S(1)}, f32[4,512]{1,0:T(4,128)S(1)}, u32[]{:S(2)}, u32[]{:S(2)}) %collective-permute-start.19) | collective-permute-done | bytes 8224 | tf_op jit(solution)/shard_map/ppermute | solution.py:95
  168.9 3.3 %collective-permute-start.20 = (f32[4,512]{1,0:T(4,128)S(1)}, f32[4,512]{1,0:T(4,128)S(1)}, u32[]{:S(2)}, u32[]{:S(2)}) collective-permute-start(f32[4,512]{1,0:T(4,128)S(1)} %add.88), channel_id=1, source_target_pairs={{0,8},{1,9},{2,10},{3,11},{4,12},{5,13},{6,14},{7,15},{8,0},{9,1},... | collective-permute-start | bytes 24584 | tf_op jit(solution)/shard_map/ppermute | solution.py:95
  174.4 3.8 %collective-permute-start.21 = (f32[4,512]{1,0:T(4,128)S(1)}, f32[4,512]{1,0:T(4,128)S(1)}, u32[]{:S(2)}, u32[]{:S(2)}) collective-permute-start(f32[4,512]{1,0:T(4,128)S(1)} %add.89), channel_id=1, source_target_pairs={{0,16},{1,17},{2,18},{3,19},{4,20},{5,21},{6,22},{7,23},{8,24},{9,... | collective-permute-start | bytes 24584 | tf_op jit(solution)/shard_map/ppermute | solution.py:95
  181.5 12.1 %collective-permute-start.22 = (f32[4,512]{1,0:T(4,128)S(1)}, f32[4,512]{1,0:T(4,128)S(1)}, u32[]{:S(2)}, u32[]{:S(2)}) collective-permute-start(f32[4,512]{1,0:T(4,128)S(1)} %add.90), channel_id=1, source_target_pairs={{0,256},{32,288},{64,320},{96,352},{128,384},{160,416},{192,448},{... | collective-permute-start | bytes 24584 | tf_op jit(solution)/shard_map/ppermute | solution.py:95
  (115 shorter events, 71.4 us)
Async XLA Ops:
  3.1 52.9 %collective-permute-start.10 = (bf16[1,32,2176]{2,1,0:T(8,128)(2,1)S(1)}, bf16[1,32,2176]{2,1,0:T(8,128)(2,1)S(1)}, u32[]{:S(2)}, u32[]{:S(2)}) collective-permute-start(bf16[1,32,2176]{2,1,0:T(8,128)(2,1)S(1)} %maximum_bitcast_fusion), channel_id=1, source_target_pairs={{0,256},{32,288},{64,320},{96,352},{128,384},{160,416},{192,448},{... | collective-permute-start | bytes 417800 | tf_op jit(solution)/shard_map/ppermute | solution.py:70
  19.6 15.5 %collective-permute-start = (bf16[1,16,1152]{2,1,0:T(8,128)(2,1)S(1)}, bf16[1,16,1152]{2,1,0:T(8,128)(2,1)S(1)}, u32[]{:S(2)}, u32[]{:S(2)}) collective-permute-start(bf16[1,16,1152]{2,1,0:T(8,128)(2,1)S(1)} %get-tuple-element.13), channel_id=1, source_target_pairs={{0,4},{1,5},{2,6},{3,7},{4,0},{5,1},{6,2},{7,3},{8,12},{9,13},{10,... | collective-permute-start | bytes 110600 | tf_op jit(solution)/shard_map/ppermute | solution.py:70
  23.9 16.3 %collective-permute-start.5 = (bf16[1,16,1152]{2,1,0:T(8,128)(2,1)S(1)}, bf16[1,16,1152]{2,1,0:T(8,128)(2,1)S(1)}, u32[]{:S(2)}, u32[]{:S(2)}) collective-permute-start(bf16[1,16,1152]{2,1,0:T(8,128)(2,1)S(1)} %get-tuple-element.14), channel_id=1, source_target_pairs={{0,16},{1,17},{2,18},{3,19},{4,20},{5,21},{6,22},{7,23},{8,24},{9,... | collective-permute-start | bytes 110600 | tf_op jit(solution)/shard_map/ppermute | solution.py:70
  35.1 8.3 %collective-permute-start.1 = (bf16[2,16,1152]{2,1,0:T(8,128)(2,1)S(1)}, bf16[2,16,1152]{2,1,0:T(8,128)(2,1)S(1)}, u32[]{:S(2)}, u32[]{:S(2)}) collective-permute-start(bf16[2,16,1152]{2,1,0:T(8,128)(2,1)S(1)} %maximum_select_fusion.12), channel_id=1, source_target_pairs={{0,16},{1,17},{2,18},{3,19},{4,20},{5,21},{6,22},{7,23},{8,24},{9,... | collective-permute-start | bytes 221192 | tf_op jit(solution)/shard_map/ppermute | solution.py:70
  40.3 13.1 %collective-permute-start.6 = (bf16[2,16,1152]{2,1,0:T(8,128)(2,1)S(1)}, bf16[2,16,1152]{2,1,0:T(8,128)(2,1)S(1)}, u32[]{:S(2)}, u32[]{:S(2)}) collective-permute-start(bf16[2,16,1152]{2,1,0:T(8,128)(2,1)S(1)} %maximum_select_fusion.13), channel_id=1, source_target_pairs={{0,4},{1,5},{2,6},{3,7},{4,0},{5,1},{6,2},{7,3},{8,12},{9,13},{10,... | collective-permute-start | bytes 221192 | tf_op jit(solution)/shard_map/ppermute | solution.py:70
  43.4 15.4 %collective-permute-start.2 = (bf16[4,16,1152]{2,1,0:T(8,128)(2,1)S(1)}, bf16[4,16,1152]{2,1,0:T(8,128)(2,1)S(1)}, u32[]{:S(2)}, u32[]{:S(2)}) collective-permute-start(bf16[4,16,1152]{2,1,0:T(8,128)(2,1)S(1)} %maximum_select_fusion.10), channel_id=1, source_target_pairs={{0,2},{1,3},{2,0},{3,1},{4,6},{5,7},{6,4},{7,5},{8,10},{9,11},{10,... | collective-permute-start | bytes 442376 | tf_op jit(solution)/shard_map/ppermute | solution.py:70
  53.4 7.5 %collective-permute-start.7 = (bf16[4,16,1152]{2,1,0:T(8,128)(2,1)S(1)}, bf16[4,16,1152]{2,1,0:T(8,128)(2,1)S(1)}, u32[]{:S(2)}, u32[]{:S(2)}) collective-permute-start(bf16[4,16,1152]{2,1,0:T(8,128)(2,1)S(1)} %maximum_select_fusion.11), channel_id=1, source_target_pairs={{0,8},{1,9},{2,10},{3,11},{4,12},{5,13},{6,14},{7,15},{8,0},{9,1},... | collective-permute-start | bytes 442376 | tf_op jit(solution)/shard_map/ppermute | solution.py:70
  56.1 10.0 %collective-permute-start.11 = (bf16[2,32,2176]{2,1,0:T(8,128)(2,1)S(1)}, bf16[2,32,2176]{2,1,0:T(8,128)(2,1)S(1)}, u32[]{:S(2)}, u32[]{:S(2)}) collective-permute-start(bf16[2,32,2176]{2,1,0:T(8,128)(2,1)S(1)} %maximum_select_fusion.9), channel_id=1, source_target_pairs={{0,64},{32,96},{64,0},{96,32},{128,192},{160,224},{192,128},{224,1... | collective-permute-start | bytes 835592 | tf_op jit(solution)/shard_map/ppermute | solution.py:70
  58.9 11.5 %collective-permute-start.3 = (bf16[8,16,1152]{2,1,0:T(8,128)(2,1)S(1)}, bf16[8,16,1152]{2,1,0:T(8,128)(2,1)S(1)}, u32[]{:S(2)}, u32[]{:S(2)}) collective-permute-start(bf16[8,16,1152]{2,1,0:T(8,128)(2,1)S(1)} %maximum_select_fusion.7), channel_id=1, source_target_pairs={{0,1},{1,0},{2,3},{3,2},{4,5},{5,4},{6,7},{7,6},{8,9},{9,8},{10,11... | collective-permute-start | bytes 884744 | tf_op jit(solution)/shard_map/ppermute | solution.py:70
  60.9 17.3 %collective-permute-start.8 = (bf16[8,16,1152]{2,1,0:T(8,128)(2,1)S(1)}, bf16[8,16,1152]{2,1,0:T(8,128)(2,1)S(1)}, u32[]{:S(2)}, u32[]{:S(2)}) collective-permute-start(bf16[8,16,1152]{2,1,0:T(8,128)(2,1)S(1)} %maximum_select_fusion.8), channel_id=1, source_target_pairs={{0,2},{1,3},{2,0},{3,1},{4,6},{5,7},{6,4},{7,5},{8,10},{9,11},{10,... | collective-permute-start | bytes 884744 | tf_op jit(solution)/shard_map/ppermute | solution.py:70
  66.2 16.6 %collective-permute-start.12 = (bf16[4,32,2176]{2,1,0:T(8,128)(2,1)S(1)}, bf16[4,32,2176]{2,1,0:T(8,128)(2,1)S(1)}, u32[]{:S(2)}, u32[]{:S(2)}) collective-permute-start(bf16[4,32,2176]{2,1,0:T(8,128)(2,1)S(1)} %maximum_select_fusion.6), channel_id=1, source_target_pairs={{0,128},{32,160},{64,192},{96,224},{128,0},{160,32},{192,64},{224,... | collective-permute-start | bytes 1671176 | tf_op jit(solution)/shard_map/ppermute | solution.py:70
  70.5 15.6 %collective-permute-start.4 = (bf16[16,16,1152]{2,1,0:T(8,128)(2,1)S(1)}, bf16[16,16,1152]{2,1,0:T(8,128)(2,1)S(1)}, u32[]{:S(2)}, u32[]{:S(2)}) collective-permute-start(bf16[16,16,1152]{2,1,0:T(8,128)(2,1)S(1)} %maximum_select_fusion.4), channel_id=1, source_target_pairs={{0,8},{1,9},{2,10},{3,11},{4,12},{5,13},{6,14},{7,15},{8,0},{9,1},... | collective-permute-start | bytes 1769480 | tf_op jit(solution)/shard_map/ppermute | solution.py:70
  78.3 15.8 %collective-permute-start.9 = (bf16[16,16,1152]{2,1,0:T(8,128)(2,1)S(1)}, bf16[16,16,1152]{2,1,0:T(8,128)(2,1)S(1)}, u32[]{:S(2)}, u32[]{:S(2)}) collective-permute-start(bf16[16,16,1152]{2,1,0:T(8,128)(2,1)S(1)} %maximum_select_fusion.5), channel_id=1, source_target_pairs={{0,1},{1,0},{2,3},{3,2},{4,5},{5,4},{6,7},{7,6},{8,9},{9,8},{10,11... | collective-permute-start | bytes 1769480 | tf_op jit(solution)/shard_map/ppermute | solution.py:70
  84.0 19.3 %collective-permute-start.13 = (bf16[8,32,2176]{2,1,0:T(8,128)(2,1)}, bf16[8,32,2176]{2,1,0:T(8,128)(2,1)}, u32[]{:S(2)}, u32[]{:S(2)}) collective-permute-start(bf16[8,32,2176]{2,1,0:T(8,128)(2,1)} %maximum_select_fusion.3), channel_id=1, source_target_pairs={{0,32},{32,0},{64,96},{96,64},{128,160},{160,128},{192,224},{224,1... | collective-permute-start | bytes 3342344 | tf_op jit(solution)/shard_map/ppermute | solution.py:70
  126.0 3.1 %collective-permute-start.14 = (f32[4,512]{1,0:T(4,128)S(1)}, f32[4,512]{1,0:T(4,128)S(1)}, u32[]{:S(2)}, u32[]{:S(2)}) collective-permute-start(f32[4,512]{1,0:T(4,128)S(1)} %pad_maximum_fusion.5), channel_id=1, source_target_pairs={{0,32},{32,0},{64,96},{96,64},{128,160},{160,128},{192,224},{224,1... | collective-permute-start | bytes 24584 | tf_op jit(solution)/shard_map/ppermute | solution.py:95
  129.1 5.5 %collective-permute-start.15 = (f32[4,512]{1,0:T(4,128)S(1)}, f32[4,512]{1,0:T(4,128)S(1)}, u32[]{:S(2)}, u32[]{:S(2)}) collective-permute-start(f32[4,512]{1,0:T(4,128)S(1)} %fusion.54), channel_id=1, source_target_pairs={{0,1},{1,0},{2,3},{3,2},{4,5},{5,4},{6,7},{7,6},{8,9},{9,8},{10,11... | collective-permute-start | bytes 24584 | tf_op jit(solution)/shard_map/ppermute | solution.py:95
  134.6 6.4 %collective-permute-start.16 = (f32[4,512]{1,0:T(4,128)S(1)}, f32[4,512]{1,0:T(4,128)S(1)}, u32[]{:S(2)}, u32[]{:S(2)}) collective-permute-start(f32[4,512]{1,0:T(4,128)S(1)} %fusion.64), channel_id=1, source_target_pairs={{0,2},{1,3},{2,0},{3,1},{4,6},{5,7},{6,4},{7,5},{8,10},{9,11},{10,... | collective-permute-start | bytes 24584 | tf_op jit(solution)/shard_map/ppermute | solution.py:95
  141.1 9.4 %collective-permute-start.17 = (f32[4,512]{1,0:T(4,128)S(1)}, f32[4,512]{1,0:T(4,128)S(1)}, u32[]{:S(2)}, u32[]{:S(2)}) collective-permute-start(f32[4,512]{1,0:T(4,128)S(1)} %add.85), channel_id=1, source_target_pairs={{0,4},{1,5},{2,6},{3,7},{4,0},{5,1},{6,2},{7,3},{8,12},{9,13},{10,... | collective-permute-start | bytes 24584 | tf_op jit(solution)/shard_map/ppermute | solution.py:95
  150.5 11.3 %collective-permute-start.18 = (f32[4,512]{1,0:T(4,128)S(1)}, f32[4,512]{1,0:T(4,128)S(1)}, u32[]{:S(2)}, u32[]{:S(2)}) collective-permute-start(f32[4,512]{1,0:T(4,128)S(1)} %add.86), channel_id=1, source_target_pairs={{0,64},{32,96},{64,0},{96,32},{128,192},{160,224},{192,128},{224,1... | collective-permute-start | bytes 24584 | tf_op jit(solution)/shard_map/ppermute | solution.py:95
  155.2 23.0 %all-to-all-start = ((f32[16,1,128]{2,1,0:T(1,128)}), f32[16,1,128]{2,1,0:T(1,128)S(1)}, u32[]{:S(2)}, u32[]{:S(2)}) async-start(f32[16,1,128]{2,1,0:T(1,128)} %reshape.95), calls=%async_computation | async-start | bytes 16384 | tf_op jit(solution)/shard_map/all_to_all | solution.py:146
  161.9 7.0 %collective-permute-start.19 = (f32[4,512]{1,0:T(4,128)S(1)}, f32[4,512]{1,0:T(4,128)S(1)}, u32[]{:S(2)}, u32[]{:S(2)}) collective-permute-start(f32[4,512]{1,0:T(4,128)S(1)} %add.87), channel_id=1, source_target_pairs={{0,128},{32,160},{64,192},{96,224},{128,0},{160,32},{192,64},{224,... | collective-permute-start | bytes 24584 | tf_op jit(solution)/shard_map/ppermute | solution.py:95
  168.9 5.5 %collective-permute-start.20 = (f32[4,512]{1,0:T(4,128)S(1)}, f32[4,512]{1,0:T(4,128)S(1)}, u32[]{:S(2)}, u32[]{:S(2)}) collective-permute-start(f32[4,512]{1,0:T(4,128)S(1)} %add.88), channel_id=1, source_target_pairs={{0,8},{1,9},{2,10},{3,11},{4,12},{5,13},{6,14},{7,15},{8,0},{9,1},... | collective-permute-start | bytes 24584 | tf_op jit(solution)/shard_map/ppermute | solution.py:95
  174.4 7.0 %collective-permute-start.21 = (f32[4,512]{1,0:T(4,128)S(1)}, f32[4,512]{1,0:T(4,128)S(1)}, u32[]{:S(2)}, u32[]{:S(2)}) collective-permute-start(f32[4,512]{1,0:T(4,128)S(1)} %add.89), channel_id=1, source_target_pairs={{0,16},{1,17},{2,18},{3,19},{4,20},{5,21},{6,22},{7,23},{8,24},{9,... | collective-permute-start | bytes 24584 | tf_op jit(solution)/shard_map/ppermute | solution.py:95
  181.5 14.2 %collective-permute-start.22 = (f32[4,512]{1,0:T(4,128)S(1)}, f32[4,512]{1,0:T(4,128)S(1)}, u32[]{:S(2)}, u32[]{:S(2)}) collective-permute-start(f32[4,512]{1,0:T(4,128)S(1)} %add.90), channel_id=1, source_target_pairs={{0,256},{32,288},{64,320},{96,352},{128,384},{160,416},{192,448},{... | collective-permute-start | bytes 24584 | tf_op jit(solution)/shard_map/ppermute | solution.py:95
  (6 other events, 75.7 us)

commit v4 on v3

--- a/solution.py
+++ b/solution.py
@@ -63,13 +63,10 @@
 
 
 def xor_gather(x, axis, n, bits):
-    idx = lax.axis_index(axis)
     buf = x[None]
     for b in bits:
-        k = 1 << b
-        other = lax.ppermute(buf, axis, [(i, i ^ k) for i in range(n)])
-        lo = (idx & k) == 0
-        buf = jnp.where(lo, jnp.concatenate([buf, other]), jnp.concatenate([other, buf]))
+        other = lax.ppermute(buf, axis, [(i, i ^ (1 << b)) for i in range(n)])
+        buf = jnp.concatenate([buf, other])
     order = [sum(((t >> j) & 1) << b for j, b in enumerate(bits)) for t in range(n)]
     return buf, order
 
@@ -140,8 +137,9 @@
         kern = jnp.exp(-cdist * scales[kernel_id]).astype(jnp.bfloat16)
         proofs.append(jnp.dot(kern, weights, preferred_element_type=jnp.float32))
     proof_part = jnp.stack(proofs).reshape(NB, n_grp, rows_here)
-    inverse = np.argsort(np.array(col_order))
-    proof_part = jnp.take(proof_part, jnp.asarray(inverse, jnp.int32), axis=1)
+    inverse = jnp.asarray(np.argsort(np.array(col_order)), jnp.int32)
+    place = inverse[jnp.arange(n_grp, dtype=jnp.int32) ^ lax.axis_index("grp")]
+    proof_part = jnp.take(proof_part, place, axis=1)
     proof_part = jnp.transpose(proof_part, (1, 0, 2))
     got = lax.all_to_all(proof_part, "grp", 0, 0, tiled=True)
     proof = jnp.sum(got, axis=0) * inv_root

time: 198 us -> 200 us (1.010)
  local copies, waits for them, and re-layouts: 10.3 us -> 17.4 us
  starting transfers between devices: 103 us -> 101 us
    select_n x14 -> x3, other arithmetic: 4.78 us -> 0.1 us  [the longest x2 0.09 us: per_device(): proof_part = jnp.take(proof_part, place, axis=1)]
    ppermute x14, waiting for transfers between devices: 27.4 us -> 23.1 us  [xor_gather(): other = lax.ppermute(buf, axis, [(i, i ^ 1 << b) for i in range(n)])]
    unnamed x16 -> x34, local copies, waits for them, and re-layouts: 3.46 us -> 7.55 us
    all_to_all x1, starting transfers between devices: 6.65 us -> 10.6 us  [per_device(): got = lax.all_to_all(proof_part, 'grp', 0, 0, tiled=True)]
    ppermute x9, starting transfers between devices: 37.3 us -> 34 us  [xor_sum(): x = x + lax.ppermute(x, a, [(i, i ^ k) for i in range(sizes[a])])]
    ppermute x9, waiting for transfers between devices: 19.3 us -> 22.5 us  [xor_sum(): x = x + lax.ppermute(x, a, [(i, i ^ k) for i in range(sizes[a])])]
    ppermute x14, starting transfers between devices: 59 us -> 56.1 us  [xor_gather(): other = lax.ppermute(buf, axis, [(i, i ^ 1 << b) for i in range(n)])]
    unnamed x0 -> x2, other arithmetic: none -> 2.28 us
  transfers between devices with their start and end apart: 24 -> 24, of which waited for: 16 -> 14; matrix products, arithmetic and copies ran while one was open for 9% -> 12% of each run, Pallas kernels for 0% -> 0%
where the time goes in v4:
time: 200 us; the launch traced here: 199 us
  starting transfers between devices  101 us (50%)
  waiting for transfers between devices  45.7 us (23%)
  matrix products  18.2 us (9%)
  local copies, waits for them, and re-layouts  17.4 us (9%)
  other arithmetic  15.8 us (8%)
    ppermute x14, starting transfers between devices, xor_gather(): other = lax.ppermute(buf, axis, [(i, i ^ 1 << b) for i in range(n)])  56.1 us
    ppermute x9, starting transfers between devices, xor_sum(): x = x + lax.ppermute(x, a, [(i, i ^ k) for i in range(sizes[a])])  34 us
    ppermute x14, waiting for transfers between devices, xor_gather(): other = lax.ppermute(buf, axis, [(i, i ^ 1 << b) for i in range(n)])  23.1 us
    ppermute x9, waiting for transfers between devices, xor_sum(): x = x + lax.ppermute(x, a, [(i, i ^ k) for i in range(sizes[a])])  22.5 us
    all_to_all x1, starting transfers between devices, per_device(): got = lax.all_to_all(proof_part, 'grp', 0, 0, tiled=True)  10.6 us
    dot_general x2, matrix products, distances(): lax.dot_general(left, right, (((1,), (1,)), ((), ())), preferred_element_...  8.61 us
    unnamed x34, local copies, waits for them, and re-layouts  7.55 us
    dot_general x4, matrix products, per_device(): product = jnp.dot(kern, col_vec, preferred_element_type=jnp.float32)  6.44 us
  transfers between devices with their start and end apart: 24, of which 14 were waited for; matrix products, arithmetic and copies ran while one was open for 12% of the time, Pallas kernels for 0%

profile of v4, /device:TPU:6, one launch (start us, length us, event | category | flops | bytes accessed | tf_op | source)
XLA Modules:
  0.0 199.0 jit_solution(12283298957388817800)
XLA Ops:
  3.6 9.1 %collective-permute-start = (bf16[1,16,1152]{2,1,0:T(8,128)(2,1)S(1)}, bf16[1,16,1152]{2,1,0:T(8,128)(2,1)S(1)}, u32[]{:S(2)}, u32[]{:S(2)}) collective-permute-start(bf16[1,16,1152]{2,1,0:T(8,128)(2,1)S(1)} %get-tuple-element.10), channel_id=1, source_target_pairs={{0,4},{1,5},{2,6},{3,7},{4,0},{5,1},{6,2},{7,3},{8,12},{9,13},{10,... | collective-permute-start | bytes 110600 | tf_op jit(solution)/shard_map/ppermute | solution.py:68
  12.7 5.1 %collective-permute-start.5 = (bf16[1,16,1152]{2,1,0:T(8,128)(2,1)S(1)}, bf16[1,16,1152]{2,1,0:T(8,128)(2,1)S(1)}, u32[]{:S(2)}, u32[]{:S(2)}) collective-permute-start(bf16[1,16,1152]{2,1,0:T(8,128)(2,1)S(1)} %get-tuple-element.28), channel_id=1, source_target_pairs={{0,16},{1,17},{2,18},{3,19},{4,20},{5,21},{6,22},{7,23},{8,24},{9,... | collective-permute-start | bytes 110600 | tf_op jit(solution)/shard_map/ppermute | solution.py:68
  18.7 10.9 %collective-permute-start.10 = (bf16[1,32,2176]{2,1,0:T(8,128)(2,1)S(1)}, bf16[1,32,2176]{2,1,0:T(8,128)(2,1)S(1)}, u32[]{:S(2)}, u32[]{:S(2)}) collective-permute-start(bf16[1,32,2176]{2,1,0:T(8,128)(2,1)S(1)} %maximum_bitcast_fusion), channel_id=1, source_target_pairs={{0,256},{32,288},{64,320},{96,352},{128,384},{160,416},{192,448},{... | collective-permute-start | bytes 417800 | tf_op jit(solution)/shard_map/ppermute | solution.py:68
  36.4 5.5 %collective-permute-start.6 = (bf16[2,16,1152]{2,1,0:T(8,128)(2,1)S(1)}, bf16[2,16,1152]{2,1,0:T(8,128)(2,1)S(1)}, u32[]{:S(2)}, u32[]{:S(2)}) collective-permute-start(bf16[2,16,1152]{2,1,0:T(8,128)(2,1)S(1)} %pad_maximum_fusion.11), channel_id=1, source_target_pairs={{0,4},{1,5},{2,6},{3,7},{4,0},{5,1},{6,2},{7,3},{8,12},{9,13},{10,... | collective-permute-start | bytes 221192 | tf_op jit(solution)/shard_map/ppermute | solution.py:68
  43.2 3.4 %collective-permute-start.2 = (bf16[4,16,1152]{2,1,0:T(8,128)(2,1)S(1)}, bf16[4,16,1152]{2,1,0:T(8,128)(2,1)S(1)}, u32[]{:S(2)}, u32[]{:S(2)}) collective-permute-start(bf16[4,16,1152]{2,1,0:T(8,128)(2,1)S(1)} %pad_maximum_fusion.8), channel_id=1, source_target_pairs={{0,2},{1,3},{2,0},{3,1},{4,6},{5,7},{6,4},{7,5},{8,10},{9,11},{10,... | collective-permute-start | bytes 442376 | tf_op jit(solution)/shard_map/ppermute | solution.py:68
  46.6 4.6 %collective-permute-done.6 = bf16[2,16,1152]{2,1,0:T(8,128)(2,1)S(1)} collective-permute-done((bf16[2,16,1152]{2,1,0:T(8,128)(2,1)S(1)}, bf16[2,16,1152]{2,1,0:T(8,128)(2,1)S(1)}, u32[]{:S(2)}, u32[]{:S(2)}) %collective-permute-start.6) | collective-permute-done | bytes 73760 | tf_op jit(solution)/shard_map/ppermute | solution.py:68
  55.2 2.9 %collective-permute-start.11 = (bf16[2,32,2176]{2,1,0:T(8,128)(2,1)S(1)}, bf16[2,32,2176]{2,1,0:T(8,128)(2,1)S(1)}, u32[]{:S(2)}, u32[]{:S(2)}) collective-permute-start(bf16[2,32,2176]{2,1,0:T(8,128)(2,1)S(1)} %pad_maximum_fusion.7), channel_id=1, source_target_pairs={{0,64},{32,96},{64,0},{96,32},{128,192},{160,224},{192,128},{224,1... | collective-permute-start | bytes 835592 | tf_op jit(solution)/shard_map/ppermute | solution.py:68
  65.4 3.3 %collective-permute-start.12 = (bf16[4,32,2176]{2,1,0:T(8,128)(2,1)S(1)}, bf16[4,32,2176]{2,1,0:T(8,128)(2,1)S(1)}, u32[]{:S(2)}, u32[]{:S(2)}) collective-permute-start(bf16[4,32,2176]{2,1,0:T(8,128)(2,1)S(1)} %pad_maximum_fusion.3), channel_id=1, source_target_pairs={{0,128},{32,160},{64,192},{96,224},{128,0},{160,32},{192,64},{224,... | collective-permute-start | bytes 1671176 | tf_op jit(solution)/shard_map/ppermute | solution.py:68
  69.5 3.3 %collective-permute-start.4 = (bf16[16,16,1152]{2,1,0:T(8,128)(2,1)S(1)}, bf16[16,16,1152]{2,1,0:T(8,128)(2,1)S(1)}, u32[]{:S(2)}, u32[]{:S(2)}) collective-permute-start(bf16[16,16,1152]{2,1,0:T(8,128)(2,1)S(1)} %get-tuple-element.17), channel_id=1, source_target_pairs={{0,8},{1,9},{2,10},{3,11},{4,12},{5,13},{6,14},{7,15},{8,0},{9,1},... | collective-permute-start | bytes 1769480 | tf_op jit(solution)/shard_map/ppermute | solution.py:68
  72.9 4.6 %collective-permute-done.8 = bf16[8,16,1152]{2,1,0:T(8,128)(2,1)S(1)} collective-permute-done((bf16[8,16,1152]{2,1,0:T(8,128)(2,1)S(1)}, bf16[8,16,1152]{2,1,0:T(8,128)(2,1)S(1)}, u32[]{:S(2)}, u32[]{:S(2)}) %collective-permute-start.8) | collective-permute-done | bytes 294944 | tf_op jit(solution)/shard_map/ppermute | solution.py:68
  79.5 2.6 %collective-permute-done.12 = bf16[4,32,2176]{2,1,0:T(8,128)(2,1)S(1)} collective-permute-done((bf16[4,32,2176]{2,1,0:T(8,128)(2,1)S(1)}, bf16[4,32,2176]{2,1,0:T(8,128)(2,1)S(1)}, u32[]{:S(2)}, u32[]{:S(2)}) %collective-permute-start.12) | collective-permute-done | bytes 557088 | tf_op jit(solution)/shard_map/ppermute | solution.py:68
  85.6 8.0 %collective-permute-done.9 = bf16[16,16,1152]{2,1,0:T(8,128)(2,1)S(1)} collective-permute-done((bf16[16,16,1152]{2,1,0:T(8,128)(2,1)S(1)}, bf16[16,16,1152]{2,1,0:T(8,128)(2,1)S(1)}, u32[]{:S(2)}, u32[]{:S(2)}) %collective-permute-start.9) | collective-permute-done | bytes 589856 | tf_op jit(solution)/shard_map/ppermute | solution.py:68
  99.7 3.2 %fusion.9 = bf16[1024,511]{0,1:T(8,128)(2,1)} fusion(s32[1024,525]{0,1:T(8,128)} %shift_right_arithmetic.65, s32[511]{0:T(512)S(1)} %slice.115, f32[1024]{0:T(1024)S(1)} %bitcast.71), kind=kLoop, calls=%fused_computation.18 | loop fusion | flops 3662848 | bytes 3145724 | tf_op jit(solution)/shard_map/convert.3
  118.2 6.0 %exponential_convert_fusion.3 = (bf16[512,1024]{1,0:T(8,128)(2,1)S(1)}, bf16[512,1024]{1,0:T(8,128)(2,1)S(1)}, bf16[512,1024]{1,0:T(8,128)(2,1)S(1)}, bf16[512,1024]{1,0:T(8,128)(2,1)S(1)}) fusion(f32[]{:T(128)} %bitcast.7, f32[]{:T(128)} %bitcast.14, f32[]{:T(128)} %bitcast.12, f32[]{:T(128)} %bitcast.10, bf16[1024,1152]{1,0:T(8,128)(2,1)S(1)} %bitcast.62, ...), kind=kOutput, calls=%fused_computation.22 | convolution fusion | flops 1080033280 | bytes 7348224 | tf_op jit(solution)/shard_map/dot_general | solution.py:41
  136.4 3.7 %collective-permute-done.16 = f32[4,512]{1,0:T(4,128)S(1)} collective-permute-done((f32[4,512]{1,0:T(4,128)S(1)}, f32[4,512]{1,0:T(4,128)S(1)}, u32[]{:S(2)}, u32[]{:S(2)}) %collective-permute-start.16) | collective-permute-done | bytes 8224 | tf_op jit(solution)/shard_map/ppermute | solution.py:92
  140.2 3.5 %collective-permute-start.17 = (f32[4,512]{1,0:T(4,128)S(1)}, f32[4,512]{1,0:T(4,128)S(1)}, u32[]{:S(2)}, u32[]{:S(2)}) collective-permute-start(f32[4,512]{1,0:T(4,128)S(1)} %add.106), channel_id=1, source_target_pairs={{0,4},{1,5},{2,6},{3,7},{4,0},{5,1},{6,2},{7,3},{8,12},{9,13},{10,... | collective-permute-start | bytes 24584 | tf_op jit(solution)/shard_map/ppermute | solution.py:92
  144.3 5.3 %collective-permute-done.17 = f32[4,512]{1,0:T(4,128)S(1)} collective-permute-done((f32[4,512]{1,0:T(4,128)S(1)}, f32[4,512]{1,0:T(4,128)S(1)}, u32[]{:S(2)}, u32[]{:S(2)}) %collective-permute-start.17) | collective-permute-done | bytes 8224 | tf_op jit(solution)/shard_map/ppermute | solution.py:92
  149.6 3.1 %collective-permute-start.18 = (f32[4,512]{1,0:T(4,128)S(1)}, f32[4,512]{1,0:T(4,128)S(1)}, u32[]{:S(2)}, u32[]{:S(2)}) collective-permute-start(f32[4,512]{1,0:T(4,128)S(1)} %add.107), channel_id=1, source_target_pairs={{0,64},{32,96},{64,0},{96,32},{128,192},{160,224},{192,128},{224,1... | collective-permute-start | bytes 24584 | tf_op jit(solution)/shard_map/ppermute | solution.py:92
  153.5 10.6 %all-to-all-start = ((f32[16,1,128]{2,1,0:T(1,128)}), f32[16,1,128]{2,1,0:T(1,128)S(1)}, u32[]{:S(2)}, u32[]{:S(2)}) async-start(f32[16,1,128]{2,1,0:T(1,128)} %reshape.131), calls=%async_computation | async-start | bytes 16384 | tf_op jit(solution)/shard_map/all_to_all | solution.py:144
  164.1 3.4 %collective-permute-start.19 = (f32[4,512]{1,0:T(4,128)S(1)}, f32[4,512]{1,0:T(4,128)S(1)}, u32[]{:S(2)}, u32[]{:S(2)}) collective-permute-start(f32[4,512]{1,0:T(4,128)S(1)} %add.108), channel_id=1, source_target_pairs={{0,128},{32,160},{64,192},{96,224},{128,0},{160,32},{192,64},{224,... | collective-permute-start | bytes 24584 | tf_op jit(solution)/shard_map/ppermute | solution.py:92
  167.5 3.7 %collective-permute-done.19 = f32[4,512]{1,0:T(4,128)S(1)} collective-permute-done((f32[4,512]{1,0:T(4,128)S(1)}, f32[4,512]{1,0:T(4,128)S(1)}, u32[]{:S(2)}, u32[]{:S(2)}) %collective-permute-start.19) | collective-permute-done | bytes 8224 | tf_op jit(solution)/shard_map/ppermute | solution.py:92
  173.3 3.3 %collective-permute-done.20 = f32[4,512]{1,0:T(4,128)S(1)} collective-permute-done((f32[4,512]{1,0:T(4,128)S(1)}, f32[4,512]{1,0:T(4,128)S(1)}, u32[]{:S(2)}, u32[]{:S(2)}) %collective-permute-start.20) | collective-permute-done | bytes 8224 | tf_op jit(solution)/shard_map/ppermute | solution.py:92
  176.7 3.7 %collective-permute-start.21 = (f32[4,512]{1,0:T(4,128)S(1)}, f32[4,512]{1,0:T(4,128)S(1)}, u32[]{:S(2)}, u32[]{:S(2)}) collective-permute-start(f32[4,512]{1,0:T(4,128)S(1)} %add.110), channel_id=1, source_target_pairs={{0,16},{1,17},{2,18},{3,19},{4,20},{5,21},{6,22},{7,23},{8,24},{9,... | collective-permute-start | bytes 24584 | tf_op jit(solution)/shard_map/ppermute | solution.py:92
  183.7 12.1 %collective-permute-start.22 = (f32[4,512]{1,0:T(4,128)S(1)}, f32[4,512]{1,0:T(4,128)S(1)}, u32[]{:S(2)}, u32[]{:S(2)}) collective-permute-start(f32[4,512]{1,0:T(4,128)S(1)} %add.111), channel_id=1, source_target_pairs={{0,256},{32,288},{64,320},{96,352},{128,384},{160,416},{192,448},{... | collective-permute-start | bytes 24584 | tf_op jit(solution)/shard_map/ppermute | solution.py:92
  (140 shorter events, 72.8 us)
Async XLA Ops:
  3.6 30.5 %collective-permute-start = (bf16[1,16,1152]{2,1,0:T(8,128)(2,1)S(1)}, bf16[1,16,1152]{2,1,0:T(8,128)(2,1)S(1)}, u32[]{:S(2)}, u32[]{:S(2)}) collective-permute-start(bf16[1,16,1152]{2,1,0:T(8,128)(2,1)S(1)} %get-tuple-element.10), channel_id=1, source_target_pairs={{0,4},{1,5},{2,6},{3,7},{4,0},{5,1},{6,2},{7,3},{8,12},{9,13},{10,... | collective-permute-start | bytes 110600 | tf_op jit(solution)/shard_map/ppermute | solution.py:68
  12.7 23.7 %collective-permute-start.5 = (bf16[1,16,1152]{2,1,0:T(8,128)(2,1)S(1)}, bf16[1,16,1152]{2,1,0:T(8,128)(2,1)S(1)}, u32[]{:S(2)}, u32[]{:S(2)}) collective-permute-start(bf16[1,16,1152]{2,1,0:T(8,128)(2,1)S(1)} %get-tuple-element.28), channel_id=1, source_target_pairs={{0,16},{1,17},{2,18},{3,19},{4,20},{5,21},{6,22},{7,23},{8,24},{9,... | collective-permute-start | bytes 110600 | tf_op jit(solution)/shard_map/ppermute | solution.py:68
  18.7 36.4 %collective-permute-start.10 = (bf16[1,32,2176]{2,1,0:T(8,128)(2,1)S(1)}, bf16[1,32,2176]{2,1,0:T(8,128)(2,1)S(1)}, u32[]{:S(2)}, u32[]{:S(2)}) collective-permute-start(bf16[1,32,2176]{2,1,0:T(8,128)(2,1)S(1)} %maximum_bitcast_fusion), channel_id=1, source_target_pairs={{0,256},{32,288},{64,320},{96,352},{128,384},{160,416},{192,448},{... | collective-permute-start | bytes 417800 | tf_op jit(solution)/shard_map/ppermute | solution.py:68
  34.1 9.0 %collective-permute-start.1 = (bf16[2,16,1152]{2,1,0:T(8,128)(2,1)S(1)}, bf16[2,16,1152]{2,1,0:T(8,128)(2,1)S(1)}, u32[]{:S(2)}, u32[]{:S(2)}) collective-permute-start(bf16[2,16,1152]{2,1,0:T(8,128)(2,1)S(1)} %pad_maximum_fusion.10), channel_id=1, source_target_pairs={{0,16},{1,17},{2,18},{3,19},{4,20},{5,21},{6,22},{7,23},{8,24},{9,... | collective-permute-start | bytes 221192 | tf_op jit(solution)/shard_map/ppermute | solution.py:68
  36.4 14.8 %collective-permute-start.6 = (bf16[2,16,1152]{2,1,0:T(8,128)(2,1)S(1)}, bf16[2,16,1152]{2,1,0:T(8,128)(2,1)S(1)}, u32[]{:S(2)}, u32[]{:S(2)}) collective-permute-start(bf16[2,16,1152]{2,1,0:T(8,128)(2,1)S(1)} %pad_maximum_fusion.11), channel_id=1, source_target_pairs={{0,4},{1,5},{2,6},{3,7},{4,0},{5,1},{6,2},{7,3},{8,12},{9,13},{10,... | collective-permute-start | bytes 221192 | tf_op jit(solution)/shard_map/ppermute | solution.py:68
  43.2 14.9 %collective-permute-start.2 = (bf16[4,16,1152]{2,1,0:T(8,128)(2,1)S(1)}, bf16[4,16,1152]{2,1,0:T(8,128)(2,1)S(1)}, u32[]{:S(2)}, u32[]{:S(2)}) collective-permute-start(bf16[4,16,1152]{2,1,0:T(8,128)(2,1)S(1)} %pad_maximum_fusion.8), channel_id=1, source_target_pairs={{0,2},{1,3},{2,0},{3,1},{4,6},{5,7},{6,4},{7,5},{8,10},{9,11},{10,... | collective-permute-start | bytes 442376 | tf_op jit(solution)/shard_map/ppermute | solution.py:68
  51.2 8.8 %collective-permute-start.7 = (bf16[4,16,1152]{2,1,0:T(8,128)(2,1)S(1)}, bf16[4,16,1152]{2,1,0:T(8,128)(2,1)S(1)}, u32[]{:S(2)}, u32[]{:S(2)}) collective-permute-start(bf16[4,16,1152]{2,1,0:T(8,128)(2,1)S(1)} %pad_maximum_fusion.9), channel_id=1, source_target_pairs={{0,8},{1,9},{2,10},{3,11},{4,12},{5,13},{6,14},{7,15},{8,0},{9,1},... | collective-permute-start | bytes 442376 | tf_op jit(solution)/shard_map/ppermute | solution.py:68
  55.2 10.2 %collective-permute-start.11 = (bf16[2,32,2176]{2,1,0:T(8,128)(2,1)S(1)}, bf16[2,32,2176]{2,1,0:T(8,128)(2,1)S(1)}, u32[]{:S(2)}, u32[]{:S(2)}) collective-permute-start(bf16[2,32,2176]{2,1,0:T(8,128)(2,1)S(1)} %pad_maximum_fusion.7), channel_id=1, source_target_pairs={{0,64},{32,96},{64,0},{96,32},{128,192},{160,224},{192,128},{224,1... | collective-permute-start | bytes 835592 | tf_op jit(solution)/shard_map/ppermute | solution.py:68
  58.1 11.3 %collective-permute-start.3 = (bf16[8,16,1152]{2,1,0:T(8,128)(2,1)S(1)}, bf16[8,16,1152]{2,1,0:T(8,128)(2,1)S(1)}, u32[]{:S(2)}, u32[]{:S(2)}) collective-permute-start(bf16[8,16,1152]{2,1,0:T(8,128)(2,1)S(1)} %pad_maximum_fusion.5), channel_id=1, source_target_pairs={{0,1},{1,0},{2,3},{3,2},{4,5},{5,4},{6,7},{7,6},{8,9},{9,8},{10,11... | collective-permute-start | bytes 884744 | tf_op jit(solution)/shard_map/ppermute | solution.py:68
  60.1 17.4 %collective-permute-start.8 = (bf16[8,16,1152]{2,1,0:T(8,128)(2,1)S(1)}, bf16[8,16,1152]{2,1,0:T(8,128)(2,1)S(1)}, u32[]{:S(2)}, u32[]{:S(2)}) collective-permute-start(bf16[8,16,1152]{2,1,0:T(8,128)(2,1)S(1)} %pad_maximum_fusion.6), channel_id=1, source_target_pairs={{0,2},{1,3},{2,0},{3,1},{4,6},{5,7},{6,4},{7,5},{8,10},{9,11},{10,... | collective-permute-start | bytes 884744 | tf_op jit(solution)/shard_map/ppermute | solution.py:68
  65.4 16.7 %collective-permute-start.12 = (bf16[4,32,2176]{2,1,0:T(8,128)(2,1)S(1)}, bf16[4,32,2176]{2,1,0:T(8,128)(2,1)S(1)}, u32[]{:S(2)}, u32[]{:S(2)}) collective-permute-start(bf16[4,32,2176]{2,1,0:T(8,128)(2,1)S(1)} %pad_maximum_fusion.3), channel_id=1, source_target_pairs={{0,128},{32,160},{64,192},{96,224},{128,0},{160,32},{192,64},{224,... | collective-permute-start | bytes 1671176 | tf_op jit(solution)/shard_map/ppermute | solution.py:68
  69.5 15.9 %collective-permute-start.4 = (bf16[16,16,1152]{2,1,0:T(8,128)(2,1)S(1)}, bf16[16,16,1152]{2,1,0:T(8,128)(2,1)S(1)}, u32[]{:S(2)}, u32[]{:S(2)}) collective-permute-start(bf16[16,16,1152]{2,1,0:T(8,128)(2,1)S(1)} %get-tuple-element.17), channel_id=1, source_target_pairs={{0,8},{1,9},{2,10},{3,11},{4,12},{5,13},{6,14},{7,15},{8,0},{9,1},... | collective-permute-start | bytes 1769480 | tf_op jit(solution)/shard_map/ppermute | solution.py:68
  77.6 16.0 %collective-permute-start.9 = (bf16[16,16,1152]{2,1,0:T(8,128)(2,1)S(1)}, bf16[16,16,1152]{2,1,0:T(8,128)(2,1)S(1)}, u32[]{:S(2)}, u32[]{:S(2)}) collective-permute-start(bf16[16,16,1152]{2,1,0:T(8,128)(2,1)S(1)} %get-tuple-element.19), channel_id=1, source_target_pairs={{0,1},{1,0},{2,3},{3,2},{4,5},{5,4},{6,7},{7,6},{8,9},{9,8},{10,11... | collective-permute-start | bytes 1769480 | tf_op jit(solution)/shard_map/ppermute | solution.py:68
  83.3 19.6 %collective-permute-start.13 = (bf16[8,32,2176]{2,1,0:T(8,128)(2,1)}, bf16[8,32,2176]{2,1,0:T(8,128)(2,1)}, u32[]{:S(2)}, u32[]{:S(2)}) collective-permute-start(bf16[8,32,2176]{2,1,0:T(8,128)(2,1)} %pad_maximum_fusion.1), channel_id=1, source_target_pairs={{0,32},{32,0},{64,96},{96,64},{128,160},{160,128},{192,224},{224,1... | collective-permute-start | bytes 3342344 | tf_op jit(solution)/shard_map/ppermute | solution.py:68
  125.1 3.1 %collective-permute-start.14 = (f32[4,512]{1,0:T(4,128)S(1)}, f32[4,512]{1,0:T(4,128)S(1)}, u32[]{:S(2)}, u32[]{:S(2)}) collective-permute-start(f32[4,512]{1,0:T(4,128)S(1)} %pad_maximum_fusion.14), channel_id=1, source_target_pairs={{0,32},{32,0},{64,96},{96,64},{128,160},{160,128},{192,224},{224,1... | collective-permute-start | bytes 24584 | tf_op jit(solution)/shard_map/ppermute | solution.py:92
  128.1 5.5 %collective-permute-start.15 = (f32[4,512]{1,0:T(4,128)S(1)}, f32[4,512]{1,0:T(4,128)S(1)}, u32[]{:S(2)}, u32[]{:S(2)}) collective-permute-start(f32[4,512]{1,0:T(4,128)S(1)} %fusion.56), channel_id=1, source_target_pairs={{0,1},{1,0},{2,3},{3,2},{4,5},{5,4},{6,7},{7,6},{8,9},{9,8},{10,11... | collective-permute-start | bytes 24584 | tf_op jit(solution)/shard_map/ppermute | solution.py:92
  133.7 6.4 %collective-permute-start.16 = (f32[4,512]{1,0:T(4,128)S(1)}, f32[4,512]{1,0:T(4,128)S(1)}, u32[]{:S(2)}, u32[]{:S(2)}) collective-permute-start(f32[4,512]{1,0:T(4,128)S(1)} %fusion.68), channel_id=1, source_target_pairs={{0,2},{1,3},{2,0},{3,1},{4,6},{5,7},{6,4},{7,5},{8,10},{9,11},{10,... | collective-permute-start | bytes 24584 | tf_op jit(solution)/shard_map/ppermute | solution.py:92
  140.2 9.4 %collective-permute-start.17 = (f32[4,512]{1,0:T(4,128)S(1)}, f32[4,512]{1,0:T(4,128)S(1)}, u32[]{:S(2)}, u32[]{:S(2)}) collective-permute-start(f32[4,512]{1,0:T(4,128)S(1)} %add.106), channel_id=1, source_target_pairs={{0,4},{1,5},{2,6},{3,7},{4,0},{5,1},{6,2},{7,3},{8,12},{9,13},{10,... | collective-permute-start | bytes 24584 | tf_op jit(solution)/shard_map/ppermute | solution.py:92
  149.6 14.5 %collective-permute-start.18 = (f32[4,512]{1,0:T(4,128)S(1)}, f32[4,512]{1,0:T(4,128)S(1)}, u32[]{:S(2)}, u32[]{:S(2)}) collective-permute-start(f32[4,512]{1,0:T(4,128)S(1)} %add.107), channel_id=1, source_target_pairs={{0,64},{32,96},{64,0},{96,32},{128,192},{160,224},{192,128},{224,1... | collective-permute-start | bytes 24584 | tf_op jit(solution)/shard_map/ppermute | solution.py:92
  153.5 26.9 %all-to-all-start = ((f32[16,1,128]{2,1,0:T(1,128)}), f32[16,1,128]{2,1,0:T(1,128)S(1)}, u32[]{:S(2)}, u32[]{:S(2)}) async-start(f32[16,1,128]{2,1,0:T(1,128)} %reshape.131), calls=%async_computation | async-start | bytes 16384 | tf_op jit(solution)/shard_map/all_to_all | solution.py:144
  164.1 7.0 %collective-permute-start.19 = (f32[4,512]{1,0:T(4,128)S(1)}, f32[4,512]{1,0:T(4,128)S(1)}, u32[]{:S(2)}, u32[]{:S(2)}) collective-permute-start(f32[4,512]{1,0:T(4,128)S(1)} %add.108), channel_id=1, source_target_pairs={{0,128},{32,160},{64,192},{96,224},{128,0},{160,32},{192,64},{224,... | collective-permute-start | bytes 24584 | tf_op jit(solution)/shard_map/ppermute | solution.py:92
  171.1 5.5 %collective-permute-start.20 = (f32[4,512]{1,0:T(4,128)S(1)}, f32[4,512]{1,0:T(4,128)S(1)}, u32[]{:S(2)}, u32[]{:S(2)}) collective-permute-start(f32[4,512]{1,0:T(4,128)S(1)} %add.109), channel_id=1, source_target_pairs={{0,8},{1,9},{2,10},{3,11},{4,12},{5,13},{6,14},{7,15},{8,0},{9,1},... | collective-permute-start | bytes 24584 | tf_op jit(solution)/shard_map/ppermute | solution.py:92
  176.7 7.0 %collective-permute-start.21 = (f32[4,512]{1,0:T(4,128)S(1)}, f32[4,512]{1,0:T(4,128)S(1)}, u32[]{:S(2)}, u32[]{:S(2)}) collective-permute-start(f32[4,512]{1,0:T(4,128)S(1)} %add.110), channel_id=1, source_target_pairs={{0,16},{1,17},{2,18},{3,19},{4,20},{5,21},{6,22},{7,23},{8,24},{9,... | collective-permute-start | bytes 24584 | tf_op jit(solution)/shard_map/ppermute | solution.py:92
  183.7 14.2 %collective-permute-start.22 = (f32[4,512]{1,0:T(4,128)S(1)}, f32[4,512]{1,0:T(4,128)S(1)}, u32[]{:S(2)}, u32[]{:S(2)}) collective-permute-start(f32[4,512]{1,0:T(4,128)S(1)} %add.111), channel_id=1, source_target_pairs={{0,256},{32,288},{64,320},{96,352},{128,384},{160,416},{192,448},{... | collective-permute-start | bytes 24584 | tf_op jit(solution)/shard_map/ppermute | solution.py:92
  (10 other events, 43.7 us)

commit v5 on v4

--- a/solution.py
+++ b/solution.py
@@ -108,35 +108,37 @@
     grp_bits = axis_order(n_grp, GRP_ORDER)
     halves = [own[: rows_here // 2], own[rows_here // 2:]]
     col_buf, col_order = xor_gather(own_wide, "grp", n_grp, grp_bits)
-    blk_buf = jnp.concatenate(
-        [xor_gather(h, "dev", n_dev, axis_order(n_dev, o))[0] for h, o in zip(halves, DEV_ORDERS)], axis=1
-    )
+    blk_bufs = [xor_gather(h, "dev", n_dev, axis_order(n_dev, o))[0] for h, o in zip(halves, DEV_ORDERS)]
 
     col_buf = col_buf.reshape(n_grp * rows_here, -1)
-    blk_buf = blk_buf.reshape(n_dev * rows_here, -1)
     col_rows, col_vec = unpack(col_buf[:, :D + META], words)
     col_corpus = col_buf[:, D + META:]
-    block_rows, block_vec = unpack(blk_buf, words)
+    col_sq = squares(col_rows)
+    corpus_sq = squares(col_corpus)
 
-    col_sq = squares(col_rows)
-    block_sq = squares(block_rows)
+    forms_part = 0.0
+    proof_sum = 0.0
+    for blk_buf in blk_bufs:
+        blk_buf = blk_buf.reshape(-1, blk_buf.shape[-1])
+        block_rows, block_vec = unpack(blk_buf, words)
+        block_sq = squares(block_rows)
+        dist = distances(block_rows, block_sq, col_rows, col_sq)
+        block_wide = block_vec.astype(jnp.float32)
+        forms = []
+        for kernel_id in range(NB):
+            kern = jnp.exp(-dist * scales[kernel_id]).astype(jnp.bfloat16)
+            product = jnp.dot(kern, col_vec, preferred_element_type=jnp.float32)
+            forms.append(jnp.sum(block_wide * product, axis=0))
+        forms_part = forms_part + jnp.stack(forms)
 
-    dist = distances(block_rows, block_sq, col_rows, col_sq)
-    block_wide = block_vec.astype(jnp.float32)
-    forms = []
-    for kernel_id in range(NB):
-        kern = jnp.exp(-dist * scales[kernel_id]).astype(jnp.bfloat16)
-        product = jnp.dot(kern, col_vec, preferred_element_type=jnp.float32)
-        forms.append(jnp.sum(block_wide * product, axis=0))
-    forms_part = jnp.stack(forms)
-
-    cdist = distances(col_corpus, squares(col_corpus), block_rows, block_sq)
-    weights = block_vec[:, 0]
-    proofs = []
-    for kernel_id in range(NB):
-        kern = jnp.exp(-cdist * scales[kernel_id]).astype(jnp.bfloat16)
-        proofs.append(jnp.dot(kern, weights, preferred_element_type=jnp.float32))
-    proof_part = jnp.stack(proofs).reshape(NB, n_grp, rows_here)
+        cdist = distances(col_corpus, corpus_sq, block_rows, block_sq)
+        weights = block_vec[:, 0]
+        proofs = []
+        for kernel_id in range(NB):
+            kern = jnp.exp(-cdist * scales[kernel_id]).astype(jnp.bfloat16)
+            proofs.append(jnp.dot(kern, weights, preferred_element_type=jnp.float32))
+        proof_sum = proof_sum + jnp.stack(proofs)
+    proof_part = proof_sum.reshape(NB, n_grp, rows_here)
     inverse = jnp.asarray(np.argsort(np.array(col_order)), jnp.int32)
     place = inverse[jnp.arange(n_grp, dtype=jnp.int32) ^ lax.axis_index("grp")]
     proof_part = jnp.take(proof_part, place, axis=1)

time: 200 us -> 214 us (1.070)
  waiting for transfers between devices: 45.7 us -> 31.4 us
  starting transfers between devices: 101 us -> 113 us
  matrix products: 18.2 us -> 24.7 us
  other arithmetic: 15.8 us -> 22.3 us
  local copies, waits for them, and re-layouts: 17.4 us -> 19.6 us
    ppermute x9, starting transfers between devices: 34 us -> 43.3 us  [xor_sum(): x = x + lax.ppermute(x, a, [(i, i ^ k) for i in range(sizes[a])])]
    ppermute x9, waiting for transfers between devices: 22.5 us -> 14.7 us  [xor_sum(): x = x + lax.ppermute(x, a, [(i, i ^ k) for i in range(sizes[a])])]
    ppermute x14, waiting for transfers between devices: 23.1 us -> 16.7 us  [xor_gather(): other = lax.ppermute(buf, axis, [(i, i ^ 1 << b) for i in range(n)])]
    dot_general x4 -> x8, matrix products: 6.44 us -> 10.2 us  [per_device(): product = jnp.dot(kern, col_vec, preferred_element_type=jnp.float32)]
    reduce_sum x2 -> x3, other arithmetic: 2.55 us -> 6.19 us  [squares(): return jnp.sum(wide * wide, axis=1)]
    concatenate x5, local copies, waits for them, and re-layouts: 1.65 us -> 5.19 us  [xor_gather(): buf = jnp.concatenate([buf, other])]
    shift_right_arithmetic x6 -> x8, local copies, waits for them, and re-layouts: 4.91 us -> 1.95 us  [make_vectors(): jnp.right_shift(sign_words[:, :, None], shifts[None, None, :]) & 1]
    another operation x6 -> x3, other arithmetic: 4.33 us -> 1.49 us
  transfers between devices with their start and end apart: 24 -> 24, of which waited for: 14 -> 15; matrix products, arithmetic and copies ran while one was open for 12% -> 14% of each run, Pallas kernels for 0% -> 0%
where the time goes in v5:
time: 214 us; the launch traced here: 213 us
  starting transfers between devices  113 us (53%)
  waiting for transfers between devices  31.4 us (15%)
  matrix products  24.7 us (12%)
  other arithmetic  22.3 us (10%)
  local copies, waits for them, and re-layouts  19.6 us (9%)
    ppermute x14, starting transfers between devices, xor_gather(): other = lax.ppermute(buf, axis, [(i, i ^ 1 << b) for i in range(n)])  58.2 us
    ppermute x9, starting transfers between devices, xor_sum(): x = x + lax.ppermute(x, a, [(i, i ^ k) for i in range(sizes[a])])  43.3 us
    ppermute x14, waiting for transfers between devices, xor_gather(): other = lax.ppermute(buf, axis, [(i, i ^ 1 << b) for i in range(n)])  16.7 us
    ppermute x9, waiting for transfers between devices, xor_sum(): x = x + lax.ppermute(x, a, [(i, i ^ k) for i in range(sizes[a])])  14.7 us
    all_to_all x1, starting transfers between devices, per_device(): got = lax.all_to_all(proof_part, 'grp', 0, 0, tiled=True)  12 us
    dot_general x4, matrix products, distances(): lax.dot_general(left, right, (((1,), (1,)), ((), ())), preferred_element_...  10.9 us
    dot_general x8, matrix products, per_device(): product = jnp.dot(kern, col_vec, preferred_element_type=jnp.float32)  10.2 us
    unnamed x59, local copies, waits for them, and re-layouts  8.71 us
  transfers between devices with their start and end apart: 24, of which 15 were waited for; matrix products, arithmetic and copies ran while one was open for 14% of the time, Pallas kernels for 0%

profile of v5, /device:TPU:6, one launch (start us, length us, event | category | flops | bytes accessed | tf_op | source)
XLA Modules:
  0.0 212.6 jit_solution(171993004211856755)
XLA Ops:
  3.7 5.1 %collective-permute-start.9 = (bf16[1,16,1152]{2,1,0:T(8,128)(2,1)S(1)}, bf16[1,16,1152]{2,1,0:T(8,128)(2,1)S(1)}, u32[]{:S(2)}, u32[]{:S(2)}) collective-permute-start(bf16[1,16,1152]{2,1,0:T(8,128)(2,1)S(1)} %get-tuple-element.8), channel_id=1, source_target_pairs={{0,16},{1,17},{2,18},{3,19},{4,20},{5,21},{6,22},{7,23},{8,24},{9,... | collective-permute-start | bytes 110600 | tf_op jit(solution)/shard_map/ppermute | solution.py:68
  9.7 15.7 %collective-permute-start.5 = (bf16[1,32,2176]{2,1,0:T(8,128)(2,1)S(1)}, bf16[1,32,2176]{2,1,0:T(8,128)(2,1)S(1)}, u32[]{:S(2)}, u32[]{:S(2)}) collective-permute-start(bf16[1,32,2176]{2,1,0:T(8,128)(2,1)S(1)} %maximum_bitcast_fusion), channel_id=1, source_target_pairs={{0,256},{32,288},{64,320},{96,352},{128,384},{160,416},{192,448},{... | collective-permute-start | bytes 417800 | tf_op jit(solution)/shard_map/ppermute | solution.py:68
  25.4 4.3 %collective-permute-start = (bf16[1,16,1152]{2,1,0:T(8,128)(2,1)S(1)}, bf16[1,16,1152]{2,1,0:T(8,128)(2,1)S(1)}, u32[]{:S(2)}, u32[]{:S(2)}) collective-permute-start(bf16[1,16,1152]{2,1,0:T(8,128)(2,1)S(1)} %get-tuple-element.34), channel_id=1, source_target_pairs={{0,4},{1,5},{2,6},{3,7},{4,0},{5,1},{6,2},{7,3},{8,12},{9,13},{10,... | collective-permute-start | bytes 110600 | tf_op jit(solution)/shard_map/ppermute | solution.py:68
  34.1 5.5 %collective-permute-start.10 = (bf16[2,16,1152]{2,1,0:T(8,128)(2,1)S(1)}, bf16[2,16,1152]{2,1,0:T(8,128)(2,1)S(1)}, u32[]{:S(2)}, u32[]{:S(2)}) collective-permute-start(bf16[2,16,1152]{2,1,0:T(8,128)(2,1)S(1)} %pad_maximum_fusion.11), channel_id=1, source_target_pairs={{0,4},{1,5},{2,6},{3,7},{4,0},{5,1},{6,2},{7,3},{8,12},{9,13},{10,... | collective-permute-start | bytes 221192 | tf_op jit(solution)/shard_map/ppermute | solution.py:68
  44.9 2.9 %collective-permute-done.10 = bf16[2,16,1152]{2,1,0:T(8,128)(2,1)S(1)} collective-permute-done((bf16[2,16,1152]{2,1,0:T(8,128)(2,1)S(1)}, bf16[2,16,1152]{2,1,0:T(8,128)(2,1)S(1)}, u32[]{:S(2)}, u32[]{:S(2)}) %collective-permute-start.10) | collective-permute-done | bytes 73760 | tf_op jit(solution)/shard_map/ppermute | solution.py:68
  53.8 2.7 %collective-permute-start.6 = (bf16[2,32,2176]{2,1,0:T(8,128)(2,1)S(1)}, bf16[2,32,2176]{2,1,0:T(8,128)(2,1)S(1)}, u32[]{:S(2)}, u32[]{:S(2)}) collective-permute-start(bf16[2,32,2176]{2,1,0:T(8,128)(2,1)S(1)} %pad_maximum_fusion.7), channel_id=1, source_target_pairs={{0,64},{32,96},{64,0},{96,32},{128,192},{160,224},{192,128},{224,1... | collective-permute-start | bytes 835592 | tf_op jit(solution)/shard_map/ppermute | solution.py:68
  56.6 4.8 %collective-permute-start.12 = (bf16[8,16,1152]{2,1,0:T(8,128)(2,1)S(1)}, bf16[8,16,1152]{2,1,0:T(8,128)(2,1)S(1)}, u32[]{:S(2)}, u32[]{:S(2)}) collective-permute-start(bf16[8,16,1152]{2,1,0:T(8,128)(2,1)S(1)} %pad_maximum_fusion.6), channel_id=1, source_target_pairs={{0,2},{1,3},{2,0},{3,1},{4,6},{5,7},{6,4},{7,5},{8,10},{9,11},{10,... | collective-permute-start | bytes 884744 | tf_op jit(solution)/shard_map/ppermute | solution.py:68
  61.9 3.0 %collective-permute-start.3 = (bf16[8,16,1152]{2,1,0:T(8,128)(2,1)S(1)}, bf16[8,16,1152]{2,1,0:T(8,128)(2,1)S(1)}, u32[]{:S(2)}, u32[]{:S(2)}) collective-permute-start(bf16[8,16,1152]{2,1,0:T(8,128)(2,1)S(1)} %pad_maximum_fusion.5), channel_id=1, source_target_pairs={{0,1},{1,0},{2,3},{3,2},{4,5},{5,4},{6,7},{7,6},{8,9},{9,8},{10,11... | collective-permute-start | bytes 884744 | tf_op jit(solution)/shard_map/ppermute | solution.py:68
  66.5 3.0 %collective-permute-start.7 = (bf16[4,32,2176]{2,1,0:T(8,128)(2,1)S(1)}, bf16[4,32,2176]{2,1,0:T(8,128)(2,1)S(1)}, u32[]{:S(2)}, u32[]{:S(2)}) collective-permute-start(bf16[4,32,2176]{2,1,0:T(8,128)(2,1)S(1)} %pad_maximum_fusion.1), channel_id=1, source_target_pairs={{0,128},{32,160},{64,192},{96,224},{128,0},{160,32},{192,64},{224,... | collective-permute-start | bytes 1671176 | tf_op jit(solution)/shard_map/ppermute | solution.py:68
  69.5 4.6 %collective-permute-done.12 = bf16[8,16,1152]{2,1,0:T(8,128)(2,1)S(1)} collective-permute-done((bf16[8,16,1152]{2,1,0:T(8,128)(2,1)S(1)}, bf16[8,16,1152]{2,1,0:T(8,128)(2,1)S(1)}, u32[]{:S(2)}, u32[]{:S(2)}) %collective-permute-start.12) | collective-permute-done | bytes 294944 | tf_op jit(solution)/shard_map/ppermute | solution.py:68
  77.8 3.2 %collective-permute-start.4 = (bf16[16,16,1152]{2,1,0:T(8,128)(2,1)}, bf16[16,16,1152]{2,1,0:T(8,128)(2,1)}, u32[]{:S(2)}, u32[]{:S(2)}) collective-permute-start(bf16[16,16,1152]{2,1,0:T(8,128)(2,1)} %get-tuple-element.25), channel_id=1, source_target_pairs={{0,8},{1,9},{2,10},{3,11},{4,12},{5,13},{6,14},{7,15},{8,0},{9,1},... | collective-permute-start | bytes 1769480 | tf_op jit(solution)/shard_map/ppermute | solution.py:68
  85.6 4.8 %collective-permute-done.13 = bf16[16,16,1152]{2,1,0:T(8,128)(2,1)S(1)} collective-permute-done((bf16[16,16,1152]{2,1,0:T(8,128)(2,1)}, bf16[16,16,1152]{2,1,0:T(8,128)(2,1)S(1)}, u32[]{:S(2)}, u32[]{:S(2)}) %collective-permute-start.13) | collective-permute-done | bytes 589856 | tf_op jit(solution)/shard_map/ppermute | solution.py:68
  120.9 3.9 %exponential_convert_fusion.3 = (bf16[512,512]{1,0:T(8,128)(2,1)S(1)}, bf16[512,512]{1,0:T(8,128)(2,1)S(1)}, bf16[512,512]{1,0:T(8,128)(2,1)S(1)}, bf16[512,512]{1,0:T(8,128)(2,1)S(1)}) fusion(f32[]{:T(128)} %bitcast.6, f32[]{:T(128)} %bitcast.13, f32[]{:T(128)} %bitcast.11, f32[]{:T(128)} %bitcast.9, bf16[512,1152]{1,0:T(8,128)(2,1)S(1)} %bitcast.105, ...), kind=kOutput, calls=%fused_computation.59 | convolution fusion | flops 540016640 | bytes 4198416 | tf_op jit(solution)/shard_map/dot_general | solution.py:41
  124.8 3.8 %exponential_convert_fusion.7 = (bf16[512,512]{1,0:T(8,128)(2,1)S(1)}, bf16[512,512]{1,0:T(8,128)(2,1)S(1)}, bf16[512,512]{1,0:T(8,128)(2,1)S(1)}, bf16[512,512]{1,0:T(8,128)(2,1)S(1)}) fusion(f32[]{:T(128)} %bitcast.6, f32[]{:T(128)} %bitcast.13, f32[]{:T(128)} %bitcast.11, f32[]{:T(128)} %bitcast.9, bf16[512,1152]{1,0:T(8,128)(2,1)S(1)} %bitcast.100, ...), kind=kOutput, calls=%fused_computation.63 | convolution fusion | flops 540016640 | bytes 4198416 | tf_op jit(solution)/shard_map/dot_general | solution.py:41
  139.8 2.8 %collective-permute-start.15 = (f32[4,512]{1,0:T(4,128)S(1)}, f32[4,512]{1,0:T(4,128)S(1)}, u32[]{:S(2)}, u32[]{:S(2)}) collective-permute-start(f32[4,512]{1,0:T(4,128)S(1)} %fusion.115), channel_id=1, source_target_pairs={{0,1},{1,0},{2,3},{3,2},{4,5},{5,4},{6,7},{7,6},{8,9},{9,8},{10,11... | collective-permute-start | bytes 24584 | tf_op jit(solution)/shard_map/ppermute | solution.py:92
  145.4 5.3 %collective-permute-start.16 = (f32[4,512]{1,0:T(4,128)S(1)}, f32[4,512]{1,0:T(4,128)S(1)}, u32[]{:S(2)}, u32[]{:S(2)}) collective-permute-start(f32[4,512]{1,0:T(4,128)S(1)} %fusion.116), channel_id=1, source_target_pairs={{0,2},{1,3},{2,0},{3,1},{4,6},{5,7},{6,4},{7,5},{8,10},{9,11},{10,... | collective-permute-start | bytes 24584 | tf_op jit(solution)/shard_map/ppermute | solution.py:92
  152.3 7.8 %collective-permute-start.17 = (f32[4,512]{1,0:T(4,128)S(1)}, f32[4,512]{1,0:T(4,128)S(1)}, u32[]{:S(2)}, u32[]{:S(2)}) collective-permute-start(f32[4,512]{1,0:T(4,128)S(1)} %add.147), channel_id=1, source_target_pairs={{0,4},{1,5},{2,6},{3,7},{4,0},{5,1},{6,2},{7,3},{8,12},{9,13},{10,... | collective-permute-start | bytes 24584 | tf_op jit(solution)/shard_map/ppermute | solution.py:92
  161.8 3.1 %collective-permute-start.18 = (f32[4,512]{1,0:T(4,128)S(1)}, f32[4,512]{1,0:T(4,128)S(1)}, u32[]{:S(2)}, u32[]{:S(2)}) collective-permute-start(f32[4,512]{1,0:T(4,128)S(1)} %add.148), channel_id=1, source_target_pairs={{0,64},{32,96},{64,0},{96,32},{128,192},{160,224},{192,128},{224,1... | collective-permute-start | bytes 24584 | tf_op jit(solution)/shard_map/ppermute | solution.py:92
  165.7 12.0 %all-to-all-start = ((f32[16,1,128]{2,1,0:T(1,128)}), f32[16,1,128]{2,1,0:T(1,128)S(1)}, u32[]{:S(2)}, u32[]{:S(2)}) async-start(f32[16,1,128]{2,1,0:T(1,128)} %reshape.189), calls=%async_computation | async-start | bytes 16384 | tf_op jit(solution)/shard_map/all_to_all | solution.py:146
  177.7 3.4 %collective-permute-start.19 = (f32[4,512]{1,0:T(4,128)S(1)}, f32[4,512]{1,0:T(4,128)S(1)}, u32[]{:S(2)}, u32[]{:S(2)}) collective-permute-start(f32[4,512]{1,0:T(4,128)S(1)} %add.149), channel_id=1, source_target_pairs={{0,128},{32,160},{64,192},{96,224},{128,0},{160,32},{192,64},{224,... | collective-permute-start | bytes 24584 | tf_op jit(solution)/shard_map/ppermute | solution.py:92
  181.1 3.7 %collective-permute-done.19 = f32[4,512]{1,0:T(4,128)S(1)} collective-permute-done((f32[4,512]{1,0:T(4,128)S(1)}, f32[4,512]{1,0:T(4,128)S(1)}, u32[]{:S(2)}, u32[]{:S(2)}) %collective-permute-start.19) | collective-permute-done | bytes 8224 | tf_op jit(solution)/shard_map/ppermute | solution.py:92
  184.7 3.2 %collective-permute-start.20 = (f32[4,512]{1,0:T(4,128)S(1)}, f32[4,512]{1,0:T(4,128)S(1)}, u32[]{:S(2)}, u32[]{:S(2)}) collective-permute-start(f32[4,512]{1,0:T(4,128)S(1)} %add.150), channel_id=1, source_target_pairs={{0,8},{1,9},{2,10},{3,11},{4,12},{5,13},{6,14},{7,15},{8,0},{9,1},... | collective-permute-start | bytes 24584 | tf_op jit(solution)/shard_map/ppermute | solution.py:92
  190.3 3.7 %collective-permute-start.21 = (f32[4,512]{1,0:T(4,128)S(1)}, f32[4,512]{1,0:T(4,128)S(1)}, u32[]{:S(2)}, u32[]{:S(2)}) collective-permute-start(f32[4,512]{1,0:T(4,128)S(1)} %add.151), channel_id=1, source_target_pairs={{0,16},{1,17},{2,18},{3,19},{4,20},{5,21},{6,22},{7,23},{8,24},{9,... | collective-permute-start | bytes 24584 | tf_op jit(solution)/shard_map/ppermute | solution.py:92
  197.3 12.1 %collective-permute-start.22 = (f32[4,512]{1,0:T(4,128)S(1)}, f32[4,512]{1,0:T(4,128)S(1)}, u32[]{:S(2)}, u32[]{:S(2)}) collective-permute-start(f32[4,512]{1,0:T(4,128)S(1)} %add.152), channel_id=1, source_target_pairs={{0,256},{32,288},{64,320},{96,352},{128,384},{160,416},{192,448},{... | collective-permute-start | bytes 24584 | tf_op jit(solution)/shard_map/ppermute | solution.py:92
  (181 shorter events, 86.8 us)
Async XLA Ops:
  3.7 30.4 %collective-permute-start.9 = (bf16[1,16,1152]{2,1,0:T(8,128)(2,1)S(1)}, bf16[1,16,1152]{2,1,0:T(8,128)(2,1)S(1)}, u32[]{:S(2)}, u32[]{:S(2)}) collective-permute-start(bf16[1,16,1152]{2,1,0:T(8,128)(2,1)S(1)} %get-tuple-element.8), channel_id=1, source_target_pairs={{0,16},{1,17},{2,18},{3,19},{4,20},{5,21},{6,22},{7,23},{8,24},{9,... | collective-permute-start | bytes 110600 | tf_op jit(solution)/shard_map/ppermute | solution.py:68
  9.7 44.1 %collective-permute-start.5 = (bf16[1,32,2176]{2,1,0:T(8,128)(2,1)S(1)}, bf16[1,32,2176]{2,1,0:T(8,128)(2,1)S(1)}, u32[]{:S(2)}, u32[]{:S(2)}) collective-permute-start(bf16[1,32,2176]{2,1,0:T(8,128)(2,1)S(1)} %maximum_bitcast_fusion), channel_id=1, source_target_pairs={{0,256},{32,288},{64,320},{96,352},{128,384},{160,416},{192,448},{... | collective-permute-start | bytes 417800 | tf_op jit(solution)/shard_map/ppermute | solution.py:68
  25.4 16.0 %collective-permute-start = (bf16[1,16,1152]{2,1,0:T(8,128)(2,1)S(1)}, bf16[1,16,1152]{2,1,0:T(8,128)(2,1)S(1)}, u32[]{:S(2)}, u32[]{:S(2)}) collective-permute-start(bf16[1,16,1152]{2,1,0:T(8,128)(2,1)S(1)} %get-tuple-element.34), channel_id=1, source_target_pairs={{0,4},{1,5},{2,6},{3,7},{4,0},{5,1},{6,2},{7,3},{8,12},{9,13},{10,... | collective-permute-start | bytes 110600 | tf_op jit(solution)/shard_map/ppermute | solution.py:68
  34.1 13.7 %collective-permute-start.10 = (bf16[2,16,1152]{2,1,0:T(8,128)(2,1)S(1)}, bf16[2,16,1152]{2,1,0:T(8,128)(2,1)S(1)}, u32[]{:S(2)}, u32[]{:S(2)}) collective-permute-start(bf16[2,16,1152]{2,1,0:T(8,128)(2,1)S(1)} %pad_maximum_fusion.11), channel_id=1, source_target_pairs={{0,4},{1,5},{2,6},{3,7},{4,0},{5,1},{6,2},{7,3},{8,12},{9,13},{10,... | collective-permute-start | bytes 221192 | tf_op jit(solution)/shard_map/ppermute | solution.py:68
  41.4 9.0 %collective-permute-start.1 = (bf16[2,16,1152]{2,1,0:T(8,128)(2,1)S(1)}, bf16[2,16,1152]{2,1,0:T(8,128)(2,1)S(1)}, u32[]{:S(2)}, u32[]{:S(2)}) collective-permute-start(bf16[2,16,1152]{2,1,0:T(8,128)(2,1)S(1)} %pad_maximum_fusion.10), channel_id=1, source_target_pairs={{0,16},{1,17},{2,18},{3,19},{4,20},{5,21},{6,22},{7,23},{8,24},{9,... | collective-permute-start | bytes 221192 | tf_op jit(solution)/shard_map/ppermute | solution.py:68
  47.8 8.7 %collective-permute-start.11 = (bf16[4,16,1152]{2,1,0:T(8,128)(2,1)S(1)}, bf16[4,16,1152]{2,1,0:T(8,128)(2,1)S(1)}, u32[]{:S(2)}, u32[]{:S(2)}) collective-permute-start(bf16[4,16,1152]{2,1,0:T(8,128)(2,1)S(1)} %pad_maximum_fusion.9), channel_id=1, source_target_pairs={{0,8},{1,9},{2,10},{3,11},{4,12},{5,13},{6,14},{7,15},{8,0},{9,1},... | collective-permute-start | bytes 442376 | tf_op jit(solution)/shard_map/ppermute | solution.py:68
  50.4 11.4 %collective-permute-start.2 = (bf16[4,16,1152]{2,1,0:T(8,128)(2,1)S(1)}, bf16[4,16,1152]{2,1,0:T(8,128)(2,1)S(1)}, u32[]{:S(2)}, u32[]{:S(2)}) collective-permute-start(bf16[4,16,1152]{2,1,0:T(8,128)(2,1)S(1)} %pad_maximum_fusion.8), channel_id=1, source_target_pairs={{0,2},{1,3},{2,0},{3,1},{4,6},{5,7},{6,4},{7,5},{8,10},{9,11},{10,... | collective-permute-start | bytes 442376 | tf_op jit(solution)/shard_map/ppermute | solution.py:68
  53.8 12.6 %collective-permute-start.6 = (bf16[2,32,2176]{2,1,0:T(8,128)(2,1)S(1)}, bf16[2,32,2176]{2,1,0:T(8,128)(2,1)S(1)}, u32[]{:S(2)}, u32[]{:S(2)}) collective-permute-start(bf16[2,32,2176]{2,1,0:T(8,128)(2,1)S(1)} %pad_maximum_fusion.7), channel_id=1, source_target_pairs={{0,64},{32,96},{64,0},{96,32},{128,192},{160,224},{192,128},{224,1... | collective-permute-start | bytes 835592 | tf_op jit(solution)/shard_map/ppermute | solution.py:68
  56.6 17.6 %collective-permute-start.12 = (bf16[8,16,1152]{2,1,0:T(8,128)(2,1)S(1)}, bf16[8,16,1152]{2,1,0:T(8,128)(2,1)S(1)}, u32[]{:S(2)}, u32[]{:S(2)}) collective-permute-start(bf16[8,16,1152]{2,1,0:T(8,128)(2,1)S(1)} %pad_maximum_fusion.6), channel_id=1, source_target_pairs={{0,2},{1,3},{2,0},{3,1},{4,6},{5,7},{6,4},{7,5},{8,10},{9,11},{10,... | collective-permute-start | bytes 884744 | tf_op jit(solution)/shard_map/ppermute | solution.py:68
  61.9 14.9 %collective-permute-start.3 = (bf16[8,16,1152]{2,1,0:T(8,128)(2,1)S(1)}, bf16[8,16,1152]{2,1,0:T(8,128)(2,1)S(1)}, u32[]{:S(2)}, u32[]{:S(2)}) collective-permute-start(bf16[8,16,1152]{2,1,0:T(8,128)(2,1)S(1)} %pad_maximum_fusion.5), channel_id=1, source_target_pairs={{0,1},{1,0},{2,3},{3,2},{4,5},{5,4},{6,7},{7,6},{8,9},{9,8},{10,11... | collective-permute-start | bytes 884744 | tf_op jit(solution)/shard_map/ppermute | solution.py:68
  66.5 15.8 %collective-permute-start.7 = (bf16[4,32,2176]{2,1,0:T(8,128)(2,1)S(1)}, bf16[4,32,2176]{2,1,0:T(8,128)(2,1)S(1)}, u32[]{:S(2)}, u32[]{:S(2)}) collective-permute-start(bf16[4,32,2176]{2,1,0:T(8,128)(2,1)S(1)} %pad_maximum_fusion.1), channel_id=1, source_target_pairs={{0,128},{32,160},{64,192},{96,224},{128,0},{160,32},{192,64},{224,... | collective-permute-start | bytes 1671176 | tf_op jit(solution)/shard_map/ppermute | solution.py:68
  74.9 15.4 %collective-permute-start.13 = (bf16[16,16,1152]{2,1,0:T(8,128)(2,1)}, bf16[16,16,1152]{2,1,0:T(8,128)(2,1)S(1)}, u32[]{:S(2)}, u32[]{:S(2)}) collective-permute-start(bf16[16,16,1152]{2,1,0:T(8,128)(2,1)} %get-tuple-element.23), channel_id=1, source_target_pairs={{0,1},{1,0},{2,3},{3,2},{4,5},{5,4},{6,7},{7,6},{8,9},{9,8},{10,11... | collective-permute-start | bytes 1769480 | tf_op jit(solution)/shard_map/ppermute | solution.py:68
  77.8 17.0 %collective-permute-start.4 = (bf16[16,16,1152]{2,1,0:T(8,128)(2,1)}, bf16[16,16,1152]{2,1,0:T(8,128)(2,1)}, u32[]{:S(2)}, u32[]{:S(2)}) collective-permute-start(bf16[16,16,1152]{2,1,0:T(8,128)(2,1)} %get-tuple-element.25), channel_id=1, source_target_pairs={{0,8},{1,9},{2,10},{3,11},{4,12},{5,13},{6,14},{7,15},{8,0},{9,1},... | collective-permute-start | bytes 1769480 | tf_op jit(solution)/shard_map/ppermute | solution.py:68
  83.4 22.0 %collective-permute-start.8 = (bf16[8,32,2176]{2,1,0:T(8,128)(2,1)}, bf16[8,32,2176]{2,1,0:T(8,128)(2,1)}, u32[]{:S(2)}, u32[]{:S(2)}) collective-permute-start(bf16[8,32,2176]{2,1,0:T(8,128)(2,1)} %pad_maximum_fusion), channel_id=1, source_target_pairs={{0,32},{32,0},{64,96},{96,64},{128,160},{160,128},{192,224},{224,1... | collective-permute-start | bytes 3342344 | tf_op jit(solution)/shard_map/ppermute | solution.py:68
  136.7 3.1 %collective-permute-start.14 = (f32[4,512]{1,0:T(4,128)S(1)}, f32[4,512]{1,0:T(4,128)S(1)}, u32[]{:S(2)}, u32[]{:S(2)}) collective-permute-start(f32[4,512]{1,0:T(4,128)S(1)} %maximum_add_fusion.1), channel_id=1, source_target_pairs={{0,32},{32,0},{64,96},{96,64},{128,160},{160,128},{192,224},{224,1... | collective-permute-start | bytes 24584 | tf_op jit(solution)/shard_map/ppermute | solution.py:92
  139.8 5.5 %collective-permute-start.15 = (f32[4,512]{1,0:T(4,128)S(1)}, f32[4,512]{1,0:T(4,128)S(1)}, u32[]{:S(2)}, u32[]{:S(2)}) collective-permute-start(f32[4,512]{1,0:T(4,128)S(1)} %fusion.115), channel_id=1, source_target_pairs={{0,1},{1,0},{2,3},{3,2},{4,5},{5,4},{6,7},{7,6},{8,9},{9,8},{10,11... | collective-permute-start | bytes 24584 | tf_op jit(solution)/shard_map/ppermute | solution.py:92
  145.4 6.9 %collective-permute-start.16 = (f32[4,512]{1,0:T(4,128)S(1)}, f32[4,512]{1,0:T(4,128)S(1)}, u32[]{:S(2)}, u32[]{:S(2)}) collective-permute-start(f32[4,512]{1,0:T(4,128)S(1)} %fusion.116), channel_id=1, source_target_pairs={{0,2},{1,3},{2,0},{3,1},{4,6},{5,7},{6,4},{7,5},{8,10},{9,11},{10,... | collective-permute-start | bytes 24584 | tf_op jit(solution)/shard_map/ppermute | solution.py:92
  152.3 9.4 %collective-permute-start.17 = (f32[4,512]{1,0:T(4,128)S(1)}, f32[4,512]{1,0:T(4,128)S(1)}, u32[]{:S(2)}, u32[]{:S(2)}) collective-permute-start(f32[4,512]{1,0:T(4,128)S(1)} %add.147), channel_id=1, source_target_pairs={{0,4},{1,5},{2,6},{3,7},{4,0},{5,1},{6,2},{7,3},{8,12},{9,13},{10,... | collective-permute-start | bytes 24584 | tf_op jit(solution)/shard_map/ppermute | solution.py:92
  161.8 15.9 %collective-permute-start.18 = (f32[4,512]{1,0:T(4,128)S(1)}, f32[4,512]{1,0:T(4,128)S(1)}, u32[]{:S(2)}, u32[]{:S(2)}) collective-permute-start(f32[4,512]{1,0:T(4,128)S(1)} %add.148), channel_id=1, source_target_pairs={{0,64},{32,96},{64,0},{96,32},{128,192},{160,224},{192,128},{224,1... | collective-permute-start | bytes 24584 | tf_op jit(solution)/shard_map/ppermute | solution.py:92
  165.7 28.3 %all-to-all-start = ((f32[16,1,128]{2,1,0:T(1,128)}), f32[16,1,128]{2,1,0:T(1,128)S(1)}, u32[]{:S(2)}, u32[]{:S(2)}) async-start(f32[16,1,128]{2,1,0:T(1,128)} %reshape.189), calls=%async_computation | async-start | bytes 16384 | tf_op jit(solution)/shard_map/all_to_all | solution.py:146
  177.7 7.0 %collective-permute-start.19 = (f32[4,512]{1,0:T(4,128)S(1)}, f32[4,512]{1,0:T(4,128)S(1)}, u32[]{:S(2)}, u32[]{:S(2)}) collective-permute-start(f32[4,512]{1,0:T(4,128)S(1)} %add.149), channel_id=1, source_target_pairs={{0,128},{32,160},{64,192},{96,224},{128,0},{160,32},{192,64},{224,... | collective-permute-start | bytes 24584 | tf_op jit(solution)/shard_map/ppermute | solution.py:92
  184.7 5.5 %collective-permute-start.20 = (f32[4,512]{1,0:T(4,128)S(1)}, f32[4,512]{1,0:T(4,128)S(1)}, u32[]{:S(2)}, u32[]{:S(2)}) collective-permute-start(f32[4,512]{1,0:T(4,128)S(1)} %add.150), channel_id=1, source_target_pairs={{0,8},{1,9},{2,10},{3,11},{4,12},{5,13},{6,14},{7,15},{8,0},{9,1},... | collective-permute-start | bytes 24584 | tf_op jit(solution)/shard_map/ppermute | solution.py:92
  190.3 7.0 %collective-permute-start.21 = (f32[4,512]{1,0:T(4,128)S(1)}, f32[4,512]{1,0:T(4,128)S(1)}, u32[]{:S(2)}, u32[]{:S(2)}) collective-permute-start(f32[4,512]{1,0:T(4,128)S(1)} %add.151), channel_id=1, source_target_pairs={{0,16},{1,17},{2,18},{3,19},{4,20},{5,21},{6,22},{7,23},{8,24},{9,... | collective-permute-start | bytes 24584 | tf_op jit(solution)/shard_map/ppermute | solution.py:92
  197.3 14.3 %collective-permute-start.22 = (f32[4,512]{1,0:T(4,128)S(1)}, f32[4,512]{1,0:T(4,128)S(1)}, u32[]{:S(2)}, u32[]{:S(2)}) collective-permute-start(f32[4,512]{1,0:T(4,128)S(1)} %add.152), channel_id=1, source_target_pairs={{0,256},{32,288},{64,320},{96,352},{128,384},{160,416},{192,448},{... | collective-permute-start | bytes 24584 | tf_op jit(solution)/shard_map/ppermute | solution.py:92
  (23 other events, 205.5 us)

commit v6 on v3

--- a/solution.py
+++ b/solution.py
@@ -85,15 +85,29 @@
     return bits + [b for b in range(nbits) if b not in bits]
 
 
-def xor_sum(x, n_grp, n_dev):
+def xor_sum(x, rider, n_grp, n_dev):
     sizes = {"grp": n_grp, "dev": n_dev}
     steps = [(a, b) for a, b in SUM_ORDER if (1 << b) < sizes[a]]
     for a in sizes:
         steps += [(a, b) for b in range(sizes[a].bit_length() - 1) if (a, b) not in steps]
+    grp_bits = n_grp.bit_length() - 1
+    rider = rider.reshape((rider.shape[0],) + (2,) * grp_bits + (rider.shape[-1],))
+    axis_bits = list(range(grp_bits - 1, -1, -1))
+    grp_idx = lax.axis_index("grp")
     for a, b in steps:
-        k = 1 << b
-        x = x + lax.ppermute(x, a, [(i, i ^ k) for i in range(sizes[a])])
-    return x
+        pairs = [(i, i ^ (1 << b)) for i in range(sizes[a])]
+        if a != "grp":
+            x = x + lax.ppermute(x, a, pairs)
+            continue
+        axis = 1 + axis_bits.index(b)
+        axis_bits.remove(b)
+        mine = (grp_idx >> b) & 1
+        keep = lax.dynamic_index_in_dim(rider, mine, axis, keepdims=False)
+        send = lax.dynamic_index_in_dim(rider, 1 - mine, axis, keepdims=False)
+        got = lax.ppermute(jnp.concatenate([x.ravel(), send.ravel()]), a, pairs)
+        x = x + got[: x.size].reshape(x.shape)
+        rider = keep + got[x.size:].reshape(keep.shape)
+    return x, rider
 
 
 def per_device(samples, set_labels, sign_words, corpus, scale_grid, scale_pick):
@@ -142,11 +156,9 @@
     proof_part = jnp.stack(proofs).reshape(NB, n_grp, rows_here)
     inverse = np.argsort(np.array(col_order))
     proof_part = jnp.take(proof_part, jnp.asarray(inverse, jnp.int32), axis=1)
-    proof_part = jnp.transpose(proof_part, (1, 0, 2))
-    got = lax.all_to_all(proof_part, "grp", 0, 0, tiled=True)
-    proof = jnp.sum(got, axis=0) * inv_root
-
-    quad_forms = xor_sum(forms_part, n_grp, n_dev) / total
+    quad_forms, proof = xor_sum(forms_part, proof_part, n_grp, n_dev)
+    quad_forms = quad_forms / total
+    proof = proof * inv_root
     bootstrap = quad_forms[:, 1:]
     centre = jnp.mean(bootstrap, axis=1)
     spread = jnp.mean(jnp.square(bootstrap - centre[:, None]), axis=1)

time: 198 us -> 202 us (1.020)
  waiting for transfers between devices: 46.7 us -> 74.1 us
  starting transfers between devices: 103 us -> 80.9 us
    ppermute x9, waiting for transfers between devices: 19.3 us -> 40.8 us  [the longest x5 20.7 us: xor_sum(): x = x + lax.ppermute(x, a, pairs)]
    ppermute x9, starting transfers between devices: 37.3 us -> 22.7 us  [the longest x5 12.8 us: xor_sum(): x = x + lax.ppermute(x, a, pairs)]
    all_to_all x1 -> x0, starting transfers between devices: 6.65 us -> none  [per_device(): got = lax.all_to_all(proof_part, 'grp', 0, 0, tiled=True)]
    ppermute x14, waiting for transfers between devices: 27.4 us -> 33.3 us  [xor_gather(): other = lax.ppermute(buf, axis, [(i, i ^ k) for i in range(n)])]
    another operation x5 -> x4, other arithmetic: 4.11 us -> 4.09 us
  transfers between devices with their start and end apart: 24 -> 23, of which waited for: 16 -> 17; matrix products, arithmetic and copies ran while one was open for 9% -> 6% of each run, Pallas kernels for 0% -> 0%
where the time goes in v6:
time: 202 us; the launch traced here: 201 us
  starting transfers between devices  80.9 us (40%)
  waiting for transfers between devices  74.1 us (37%)
  matrix products  18.3 us (9%)
  other arithmetic  16.7 us (8%)
  local copies, waits for them, and re-layouts  9.71 us (5%)
    ppermute x14, starting transfers between devices, xor_gather(): other = lax.ppermute(buf, axis, [(i, i ^ k) for i in range(n)])  58.2 us
    ppermute x14, waiting for transfers between devices, xor_gather(): other = lax.ppermute(buf, axis, [(i, i ^ k) for i in range(n)])  33.3 us
    ppermute x5, waiting for transfers between devices, xor_sum(): x = x + lax.ppermute(x, a, pairs)  20.7 us
    ppermute x4, waiting for transfers between devices, xor_sum(): got = lax.ppermute(jnp.concatenate([x.ravel(), send.ravel()]), a, pairs)  20.1 us
    ppermute x5, starting transfers between devices, xor_sum(): x = x + lax.ppermute(x, a, pairs)  12.8 us
    ppermute x4, starting transfers between devices, xor_sum(): got = lax.ppermute(jnp.concatenate([x.ravel(), send.ravel()]), a, pairs)  9.92 us
    dot_general x2, matrix products, distances(): lax.dot_general(left, right, (((1,), (1,)), ((), ())), preferred_element_...  8.66 us
    dot_general x4, matrix products, per_device(): product = jnp.dot(kern, col_vec, preferred_element_type=jnp.float32)  6.48 us
  transfers between devices with their start and end apart: 23, of which 17 were waited for; matrix products, arithmetic and copies ran while one was open for 6% of the time, Pallas kernels for 0%

profile of v6, /device:TPU:6, one launch (start us, length us, event | category | flops | bytes accessed | tf_op | source)
XLA Modules:
  0.0 201.0 jit_solution(11884602663553730673)
XLA Ops:
  3.0 5.1 %collective-permute-start.5 = (bf16[1,16,1152]{2,1,0:T(8,128)(2,1)S(1)}, bf16[1,16,1152]{2,1,0:T(8,128)(2,1)S(1)}, u32[]{:S(2)}, u32[]{:S(2)}) collective-permute-start(bf16[1,16,1152]{2,1,0:T(8,128)(2,1)S(1)} %get-tuple-element.14), channel_id=1, source_target_pairs={{0,16},{1,17},{2,18},{3,19},{4,20},{5,21},{6,22},{7,23},{8,24},{9,... | collective-permute-start | bytes 110600 | tf_op jit(solution)/shard_map/ppermute | solution.py:70
  8.1 9.1 %collective-permute-start = (bf16[1,16,1152]{2,1,0:T(8,128)(2,1)S(1)}, bf16[1,16,1152]{2,1,0:T(8,128)(2,1)S(1)}, u32[]{:S(2)}, u32[]{:S(2)}) collective-permute-start(bf16[1,16,1152]{2,1,0:T(8,128)(2,1)S(1)} %get-tuple-element.13), channel_id=1, source_target_pairs={{0,4},{1,5},{2,6},{3,7},{4,0},{5,1},{6,2},{7,3},{8,12},{9,13},{10,... | collective-permute-start | bytes 110600 | tf_op jit(solution)/shard_map/ppermute | solution.py:70
  18.1 10.9 %collective-permute-start.10 = (bf16[1,32,2176]{2,1,0:T(8,128)(2,1)S(1)}, bf16[1,32,2176]{2,1,0:T(8,128)(2,1)S(1)}, u32[]{:S(2)}, u32[]{:S(2)}) collective-permute-start(bf16[1,32,2176]{2,1,0:T(8,128)(2,1)S(1)} %maximum_bitcast_fusion), channel_id=1, source_target_pairs={{0,256},{32,288},{64,320},{96,352},{128,384},{160,416},{192,448},{... | collective-permute-start | bytes 417800 | tf_op jit(solution)/shard_map/ppermute | solution.py:70
  30.6 5.5 %collective-permute-start.6 = (bf16[2,16,1152]{2,1,0:T(8,128)(2,1)S(1)}, bf16[2,16,1152]{2,1,0:T(8,128)(2,1)S(1)}, u32[]{:S(2)}, u32[]{:S(2)}) collective-permute-start(bf16[2,16,1152]{2,1,0:T(8,128)(2,1)S(1)} %maximum_select_fusion.13), channel_id=1, source_target_pairs={{0,4},{1,5},{2,6},{3,7},{4,0},{5,1},{6,2},{7,3},{8,12},{9,13},{10,... | collective-permute-start | bytes 221192 | tf_op jit(solution)/shard_map/ppermute | solution.py:70
  38.3 12.4 %collective-permute-done.6 = bf16[2,16,1152]{2,1,0:T(8,128)(2,1)S(1)} collective-permute-done((bf16[2,16,1152]{2,1,0:T(8,128)(2,1)S(1)}, bf16[2,16,1152]{2,1,0:T(8,128)(2,1)S(1)}, u32[]{:S(2)}, u32[]{:S(2)}) %collective-permute-start.6) | collective-permute-done | bytes 73760 | tf_op jit(solution)/shard_map/ppermute | solution.py:70
  58.5 4.5 %collective-permute-start.8 = (bf16[8,16,1152]{2,1,0:T(8,128)(2,1)S(1)}, bf16[8,16,1152]{2,1,0:T(8,128)(2,1)S(1)}, u32[]{:S(2)}, u32[]{:S(2)}) collective-permute-start(bf16[8,16,1152]{2,1,0:T(8,128)(2,1)S(1)} %maximum_select_fusion.8), channel_id=1, source_target_pairs={{0,2},{1,3},{2,0},{3,1},{4,6},{5,7},{6,4},{7,5},{8,10},{9,11},{10,... | collective-permute-start | bytes 884744 | tf_op jit(solution)/shard_map/ppermute | solution.py:70
  63.0 6.4 %collective-permute-done.2 = bf16[4,16,1152]{2,1,0:T(8,128)(2,1)S(1)} collective-permute-done((bf16[4,16,1152]{2,1,0:T(8,128)(2,1)S(1)}, bf16[4,16,1152]{2,1,0:T(8,128)(2,1)S(1)}, u32[]{:S(2)}, u32[]{:S(2)}) %collective-permute-start.2) | collective-permute-done | bytes 147488 | tf_op jit(solution)/shard_map/ppermute | solution.py:70
  71.5 3.3 %collective-permute-start.12 = (bf16[4,32,2176]{2,1,0:T(8,128)(2,1)S(1)}, bf16[4,32,2176]{2,1,0:T(8,128)(2,1)S(1)}, u32[]{:S(2)}, u32[]{:S(2)}) collective-permute-start(bf16[4,32,2176]{2,1,0:T(8,128)(2,1)S(1)} %maximum_select_fusion.6), channel_id=1, source_target_pairs={{0,128},{32,160},{64,192},{96,224},{128,0},{160,32},{192,64},{224,... | collective-permute-start | bytes 1671176 | tf_op jit(solution)/shard_map/ppermute | solution.py:70
  75.9 3.2 %collective-permute-start.9 = (bf16[16,16,1152]{2,1,0:T(8,128)(2,1)S(1)}, bf16[16,16,1152]{2,1,0:T(8,128)(2,1)S(1)}, u32[]{:S(2)}, u32[]{:S(2)}) collective-permute-start(bf16[16,16,1152]{2,1,0:T(8,128)(2,1)S(1)} %maximum_select_fusion.5), channel_id=1, source_target_pairs={{0,1},{1,0},{2,3},{3,2},{4,5},{5,4},{6,7},{7,6},{8,9},{9,8},{10,11... | collective-permute-start | bytes 1769480 | tf_op jit(solution)/shard_map/ppermute | solution.py:70
  79.1 3.0 %collective-permute-done.3 = bf16[8,16,1152]{2,1,0:T(8,128)(2,1)S(1)} collective-permute-done((bf16[8,16,1152]{2,1,0:T(8,128)(2,1)S(1)}, bf16[8,16,1152]{2,1,0:T(8,128)(2,1)S(1)}, u32[]{:S(2)}, u32[]{:S(2)}) %collective-permute-start.3) | collective-permute-done | bytes 294944 | tf_op jit(solution)/shard_map/ppermute | solution.py:70
  82.2 3.3 %collective-permute-start.4 = (bf16[16,16,1152]{2,1,0:T(8,128)(2,1)S(1)}, bf16[16,16,1152]{2,1,0:T(8,128)(2,1)S(1)}, u32[]{:S(2)}, u32[]{:S(2)}) collective-permute-start(bf16[16,16,1152]{2,1,0:T(8,128)(2,1)S(1)} %maximum_select_fusion.4), channel_id=1, source_target_pairs={{0,8},{1,9},{2,10},{3,11},{4,12},{5,13},{6,14},{7,15},{8,0},{9,1},... | collective-permute-start | bytes 1769480 | tf_op jit(solution)/shard_map/ppermute | solution.py:70
  85.4 3.9 %collective-permute-done.12 = bf16[4,32,2176]{2,1,0:T(8,128)(2,1)S(1)} collective-permute-done((bf16[4,32,2176]{2,1,0:T(8,128)(2,1)S(1)}, bf16[4,32,2176]{2,1,0:T(8,128)(2,1)S(1)}, u32[]{:S(2)}, u32[]{:S(2)}) %collective-permute-start.12) | collective-permute-done | bytes 557088 | tf_op jit(solution)/shard_map/ppermute | solution.py:70
  94.8 4.4 %collective-permute-done.4 = bf16[16,16,1152]{2,1,0:T(8,128)(2,1)S(1)} collective-permute-done((bf16[16,16,1152]{2,1,0:T(8,128)(2,1)S(1)}, bf16[16,16,1152]{2,1,0:T(8,128)(2,1)S(1)}, u32[]{:S(2)}, u32[]{:S(2)}) %collective-permute-start.4) | collective-permute-done | bytes 589856 | tf_op jit(solution)/shard_map/ppermute | solution.py:70
  105.4 3.1 %fusion.9 = bf16[1024,511]{0,1:T(8,128)(2,1)} fusion(s32[1024,525]{0,1:T(8,128)} %shift_right_arithmetic.77, s32[511]{0:T(512)S(1)} %slice.199, f32[1024]{0:T(1024)S(1)} %bitcast.76), kind=kLoop, calls=%fused_computation.18 | loop fusion | flops 3662848 | bytes 3145724 | tf_op jit(solution)/shard_map/convert.3
  124.8 6.1 %exponential_convert_fusion.3 = (bf16[512,1024]{1,0:T(8,128)(2,1)S(1)}, bf16[512,1024]{1,0:T(8,128)(2,1)S(1)}, bf16[512,1024]{1,0:T(8,128)(2,1)S(1)}, bf16[512,1024]{1,0:T(8,128)(2,1)S(1)}) fusion(f32[]{:T(128)} %bitcast.7, f32[]{:T(128)} %bitcast.14, f32[]{:T(128)} %bitcast.12, f32[]{:T(128)} %bitcast.10, bf16[1024,1152]{1,0:T(8,128)(2,1)S(1)} %bitcast.67, ...), kind=kOutput, calls=%fused_computation.22 | convolution fusion | flops 1080033280 | bytes 7348224 | tf_op jit(solution)/shard_map/dot_general | solution.py:41
  139.9 3.6 %collective-permute-done.15 = f32[4,512]{1,0:T(4,128)S(1)} collective-permute-done((f32[4,512]{1,0:T(4,128)S(1)}, f32[4,512]{1,0:T(4,128)S(1)}, u32[]{:S(2)}, u32[]{:S(2)}) %collective-permute-start.15) | collective-permute-done | bytes 8224 | tf_op jit(solution)/shard_map/ppermute | solution.py:100
  145.6 4.4 %collective-permute-done.16 = f32[4,512]{1,0:T(4,128)S(1)} collective-permute-done((f32[4,512]{1,0:T(4,128)S(1)}, f32[4,512]{1,0:T(4,128)S(1)}, u32[]{:S(2)}, u32[]{:S(2)}) %collective-permute-start.16) | collective-permute-done | bytes 8224 | tf_op jit(solution)/shard_map/ppermute | solution.py:100
  152.0 7.4 %collective-permute-done.17 = f32[4,512]{1,0:T(4,128)S(1)} collective-permute-done((f32[4,512]{1,0:T(4,128)S(1)}, f32[4,512]{1,0:T(4,128)S(1)}, u32[]{:S(2)}, u32[]{:S(2)}) %collective-permute-start.17) | collective-permute-done | bytes 8224 | tf_op jit(solution)/shard_map/ppermute | solution.py:100
  165.3 3.3 %collective-permute-start.19 = (f32[2304]{0:T(1024)S(1)}, f32[2304]{0:T(1024)S(1)}, u32[]{:S(2)}, u32[]{:S(2)}) collective-permute-start(f32[2304]{0:T(1024)S(1)} %pad_maximum_fusion.7), channel_id=1, source_target_pairs={{0,128},{32,160},{64,192},{96,224},{128,0},{160,32},{192,64},{224,... | collective-permute-start | bytes 27656 | tf_op jit(solution)/shard_map/ppermute | solution.py:107
  168.6 3.7 %collective-permute-done.19 = f32[2304]{0:T(1024)S(1)} collective-permute-done((f32[2304]{0:T(1024)S(1)}, f32[2304]{0:T(1024)S(1)}, u32[]{:S(2)}, u32[]{:S(2)}) %collective-permute-start.19) | collective-permute-done | bytes 9248 | tf_op jit(solution)/shard_map/ppermute | solution.py:107
  172.4 3.3 %collective-permute-start.20 = (f32[4,512]{1,0:T(4,128)S(1)}, f32[4,512]{1,0:T(4,128)S(1)}, u32[]{:S(2)}, u32[]{:S(2)}) collective-permute-start(f32[4,512]{1,0:T(4,128)S(1)} %add.143), channel_id=1, source_target_pairs={{0,8},{1,9},{2,10},{3,11},{4,12},{5,13},{6,14},{7,15},{8,0},{9,1},... | collective-permute-start | bytes 24584 | tf_op jit(solution)/shard_map/ppermute | solution.py:100
  177.9 3.8 %collective-permute-start.21 = (f32[4,512]{1,0:T(4,128)S(1)}, f32[4,512]{1,0:T(4,128)S(1)}, u32[]{:S(2)}, u32[]{:S(2)}) collective-permute-start(f32[4,512]{1,0:T(4,128)S(1)} %add.144), channel_id=1, source_target_pairs={{0,16},{1,17},{2,18},{3,19},{4,20},{5,21},{6,22},{7,23},{8,24},{9,... | collective-permute-start | bytes 24584 | tf_op jit(solution)/shard_map/ppermute | solution.py:100
  181.8 3.2 %collective-permute-done.21 = f32[4,512]{1,0:T(4,128)S(1)} collective-permute-done((f32[4,512]{1,0:T(4,128)S(1)}, f32[4,512]{1,0:T(4,128)S(1)}, u32[]{:S(2)}, u32[]{:S(2)}) %collective-permute-start.21) | collective-permute-done | bytes 8224 | tf_op jit(solution)/shard_map/ppermute | solution.py:100
  186.9 12.4 %collective-permute-done.22 = f32[2176]{0:T(1024)S(1)} collective-permute-done((f32[2176]{0:T(1024)S(1)}, f32[2176]{0:T(1024)S(1)}, u32[]{:S(2)}, u32[]{:S(2)}) %collective-permute-start.22) | collective-permute-done | bytes 8736 | tf_op jit(solution)/shard_map/ppermute | solution.py:107
  (144 shorter events, 70.6 us)
Async XLA Ops:
  2.2 72.6 %copy-start.5 = (s32[16]{0:T(128)S(1)}, s32[16]{0:T(128)}, u32[]{:S(2)}) copy-start(s32[16]{0:T(128)} %constant.128) | copy-start | bytes 196
  3.0 27.6 %collective-permute-start.5 = (bf16[1,16,1152]{2,1,0:T(8,128)(2,1)S(1)}, bf16[1,16,1152]{2,1,0:T(8,128)(2,1)S(1)}, u32[]{:S(2)}, u32[]{:S(2)}) collective-permute-start(bf16[1,16,1152]{2,1,0:T(8,128)(2,1)S(1)} %get-tuple-element.14), channel_id=1, source_target_pairs={{0,16},{1,17},{2,18},{3,19},{4,20},{5,21},{6,22},{7,23},{8,24},{9,... | collective-permute-start | bytes 110600 | tf_op jit(solution)/shard_map/ppermute | solution.py:70
  8.1 27.9 %collective-permute-start = (bf16[1,16,1152]{2,1,0:T(8,128)(2,1)S(1)}, bf16[1,16,1152]{2,1,0:T(8,128)(2,1)S(1)}, u32[]{:S(2)}, u32[]{:S(2)}) collective-permute-start(bf16[1,16,1152]{2,1,0:T(8,128)(2,1)S(1)} %get-tuple-element.13), channel_id=1, source_target_pairs={{0,4},{1,5},{2,6},{3,7},{4,0},{5,1},{6,2},{7,3},{8,12},{9,13},{10,... | collective-permute-start | bytes 110600 | tf_op jit(solution)/shard_map/ppermute | solution.py:70
  18.1 37.2 %collective-permute-start.10 = (bf16[1,32,2176]{2,1,0:T(8,128)(2,1)S(1)}, bf16[1,32,2176]{2,1,0:T(8,128)(2,1)S(1)}, u32[]{:S(2)}, u32[]{:S(2)}) collective-permute-start(bf16[1,32,2176]{2,1,0:T(8,128)(2,1)S(1)} %maximum_bitcast_fusion), channel_id=1, source_target_pairs={{0,256},{32,288},{64,320},{96,352},{128,384},{160,416},{192,448},{... | collective-permute-start | bytes 417800 | tf_op jit(solution)/shard_map/ppermute | solution.py:70
  30.6 20.2 %collective-permute-start.6 = (bf16[2,16,1152]{2,1,0:T(8,128)(2,1)S(1)}, bf16[2,16,1152]{2,1,0:T(8,128)(2,1)S(1)}, u32[]{:S(2)}, u32[]{:S(2)}) collective-permute-start(bf16[2,16,1152]{2,1,0:T(8,128)(2,1)S(1)} %maximum_select_fusion.13), channel_id=1, source_target_pairs={{0,4},{1,5},{2,6},{3,7},{4,0},{5,1},{6,2},{7,3},{8,12},{9,13},{10,... | collective-permute-start | bytes 221192 | tf_op jit(solution)/shard_map/ppermute | solution.py:70
  36.1 17.3 %collective-permute-start.1 = (bf16[2,16,1152]{2,1,0:T(8,128)(2,1)S(1)}, bf16[2,16,1152]{2,1,0:T(8,128)(2,1)S(1)}, u32[]{:S(2)}, u32[]{:S(2)}) collective-permute-start(bf16[2,16,1152]{2,1,0:T(8,128)(2,1)S(1)} %maximum_select_fusion.12), channel_id=1, source_target_pairs={{0,16},{1,17},{2,18},{3,19},{4,20},{5,21},{6,22},{7,23},{8,24},{9,... | collective-permute-start | bytes 221192 | tf_op jit(solution)/shard_map/ppermute | solution.py:70
  50.8 7.7 %collective-permute-start.7 = (bf16[4,16,1152]{2,1,0:T(8,128)(2,1)S(1)}, bf16[4,16,1152]{2,1,0:T(8,128)(2,1)S(1)}, u32[]{:S(2)}, u32[]{:S(2)}) collective-permute-start(bf16[4,16,1152]{2,1,0:T(8,128)(2,1)S(1)} %maximum_select_fusion.11), channel_id=1, source_target_pairs={{0,8},{1,9},{2,10},{3,11},{4,12},{5,13},{6,14},{7,15},{8,0},{9,1},... | collective-permute-start | bytes 442376 | tf_op jit(solution)/shard_map/ppermute | solution.py:70
  53.4 16.0 %collective-permute-start.2 = (bf16[4,16,1152]{2,1,0:T(8,128)(2,1)S(1)}, bf16[4,16,1152]{2,1,0:T(8,128)(2,1)S(1)}, u32[]{:S(2)}, u32[]{:S(2)}) collective-permute-start(bf16[4,16,1152]{2,1,0:T(8,128)(2,1)S(1)} %maximum_select_fusion.10), channel_id=1, source_target_pairs={{0,2},{1,3},{2,0},{3,1},{4,6},{5,7},{6,4},{7,5},{8,10},{9,11},{10,... | collective-permute-start | bytes 442376 | tf_op jit(solution)/shard_map/ppermute | solution.py:70
  55.4 16.0 %collective-permute-start.11 = (bf16[2,32,2176]{2,1,0:T(8,128)(2,1)S(1)}, bf16[2,32,2176]{2,1,0:T(8,128)(2,1)S(1)}, u32[]{:S(2)}, u32[]{:S(2)}) collective-permute-start(bf16[2,32,2176]{2,1,0:T(8,128)(2,1)S(1)} %maximum_select_fusion.9), channel_id=1, source_target_pairs={{0,64},{32,96},{64,0},{96,32},{128,192},{160,224},{192,128},{224,1... | collective-permute-start | bytes 835592 | tf_op jit(solution)/shard_map/ppermute | solution.py:70
  58.5 17.3 %collective-permute-start.8 = (bf16[8,16,1152]{2,1,0:T(8,128)(2,1)S(1)}, bf16[8,16,1152]{2,1,0:T(8,128)(2,1)S(1)}, u32[]{:S(2)}, u32[]{:S(2)}) collective-permute-start(bf16[8,16,1152]{2,1,0:T(8,128)(2,1)S(1)} %maximum_select_fusion.8), channel_id=1, source_target_pairs={{0,2},{1,3},{2,0},{3,1},{4,6},{5,7},{6,4},{7,5},{8,10},{9,11},{10,... | collective-permute-start | bytes 884744 | tf_op jit(solution)/shard_map/ppermute | solution.py:70
  69.5 12.6 %collective-permute-start.3 = (bf16[8,16,1152]{2,1,0:T(8,128)(2,1)S(1)}, bf16[8,16,1152]{2,1,0:T(8,128)(2,1)S(1)}, u32[]{:S(2)}, u32[]{:S(2)}) collective-permute-start(bf16[8,16,1152]{2,1,0:T(8,128)(2,1)S(1)} %maximum_select_fusion.7), channel_id=1, source_target_pairs={{0,1},{1,0},{2,3},{3,2},{4,5},{5,4},{6,7},{7,6},{8,9},{9,8},{10,11... | collective-permute-start | bytes 884744 | tf_op jit(solution)/shard_map/ppermute | solution.py:70
  71.5 17.9 %collective-permute-start.12 = (bf16[4,32,2176]{2,1,0:T(8,128)(2,1)S(1)}, bf16[4,32,2176]{2,1,0:T(8,128)(2,1)S(1)}, u32[]{:S(2)}, u32[]{:S(2)}) collective-permute-start(bf16[4,32,2176]{2,1,0:T(8,128)(2,1)S(1)} %maximum_select_fusion.6), channel_id=1, source_target_pairs={{0,128},{32,160},{64,192},{96,224},{128,0},{160,32},{192,64},{224,... | collective-permute-start | bytes 1671176 | tf_op jit(solution)/shard_map/ppermute | solution.py:70
  75.9 18.8 %collective-permute-start.9 = (bf16[16,16,1152]{2,1,0:T(8,128)(2,1)S(1)}, bf16[16,16,1152]{2,1,0:T(8,128)(2,1)S(1)}, u32[]{:S(2)}, u32[]{:S(2)}) collective-permute-start(bf16[16,16,1152]{2,1,0:T(8,128)(2,1)S(1)} %maximum_select_fusion.5), channel_id=1, source_target_pairs={{0,1},{1,0},{2,3},{3,2},{4,5},{5,4},{6,7},{7,6},{8,9},{9,8},{10,11... | collective-permute-start | bytes 1769480 | tf_op jit(solution)/shard_map/ppermute | solution.py:70
  82.2 17.1 %collective-permute-start.4 = (bf16[16,16,1152]{2,1,0:T(8,128)(2,1)S(1)}, bf16[16,16,1152]{2,1,0:T(8,128)(2,1)S(1)}, u32[]{:S(2)}, u32[]{:S(2)}) collective-permute-start(bf16[16,16,1152]{2,1,0:T(8,128)(2,1)S(1)} %maximum_select_fusion.4), channel_id=1, source_target_pairs={{0,8},{1,9},{2,10},{3,11},{4,12},{5,13},{6,14},{7,15},{8,0},{9,1},... | collective-permute-start | bytes 1769480 | tf_op jit(solution)/shard_map/ppermute | solution.py:70
  90.6 17.9 %collective-permute-start.13 = (bf16[8,32,2176]{2,1,0:T(8,128)(2,1)}, bf16[8,32,2176]{2,1,0:T(8,128)(2,1)}, u32[]{:S(2)}, u32[]{:S(2)}) collective-permute-start(bf16[8,32,2176]{2,1,0:T(8,128)(2,1)} %maximum_select_fusion.3), channel_id=1, source_target_pairs={{0,32},{32,0},{64,96},{96,64},{128,160},{160,128},{192,224},{224,1... | collective-permute-start | bytes 3342344 | tf_op jit(solution)/shard_map/ppermute | solution.py:70
  134.8 3.1 %collective-permute-start.14 = (f32[3072]{0:T(1024)S(1)}, f32[3072]{0:T(1024)S(1)}, u32[]{:S(2)}, u32[]{:S(2)}) collective-permute-start(f32[3072]{0:T(1024)S(1)} %pad_maximum_fusion.5), channel_id=1, source_target_pairs={{0,32},{32,0},{64,96},{96,64},{128,160},{160,128},{192,224},{224,1... | collective-permute-start | bytes 36872 | tf_op jit(solution)/shard_map/ppermute | solution.py:107
  137.9 5.5 %collective-permute-start.15 = (f32[4,512]{1,0:T(4,128)S(1)}, f32[4,512]{1,0:T(4,128)S(1)}, u32[]{:S(2)}, u32[]{:S(2)}) collective-permute-start(f32[4,512]{1,0:T(4,128)S(1)} %fusion.50), channel_id=1, source_target_pairs={{0,1},{1,0},{2,3},{3,2},{4,5},{5,4},{6,7},{7,6},{8,9},{9,8},{10,11... | collective-permute-start | bytes 24584 | tf_op jit(solution)/shard_map/ppermute | solution.py:100
  143.5 6.4 %collective-permute-start.16 = (f32[4,512]{1,0:T(4,128)S(1)}, f32[4,512]{1,0:T(4,128)S(1)}, u32[]{:S(2)}, u32[]{:S(2)}) collective-permute-start(f32[4,512]{1,0:T(4,128)S(1)} %fusion.65), channel_id=1, source_target_pairs={{0,2},{1,3},{2,0},{3,1},{4,6},{5,7},{6,4},{7,5},{8,10},{9,11},{10,... | collective-permute-start | bytes 24584 | tf_op jit(solution)/shard_map/ppermute | solution.py:100
  150.0 9.5 %collective-permute-start.17 = (f32[4,512]{1,0:T(4,128)S(1)}, f32[4,512]{1,0:T(4,128)S(1)}, u32[]{:S(2)}, u32[]{:S(2)}) collective-permute-start(f32[4,512]{1,0:T(4,128)S(1)} %add.134), channel_id=1, source_target_pairs={{0,4},{1,5},{2,6},{3,7},{4,0},{5,1},{6,2},{7,3},{8,12},{9,13},{10,... | collective-permute-start | bytes 24584 | tf_op jit(solution)/shard_map/ppermute | solution.py:100
  159.4 5.6 %collective-permute-start.18 = (f32[2560]{0:T(1024)S(1)}, f32[2560]{0:T(1024)S(1)}, u32[]{:S(2)}, u32[]{:S(2)}) collective-permute-start(f32[2560]{0:T(1024)S(1)} %pad_maximum_fusion.6), channel_id=1, source_target_pairs={{0,64},{32,96},{64,0},{96,32},{128,192},{160,224},{192,128},{224,1... | collective-permute-start | bytes 30728 | tf_op jit(solution)/shard_map/ppermute | solution.py:107
  165.3 7.1 %collective-permute-start.19 = (f32[2304]{0:T(1024)S(1)}, f32[2304]{0:T(1024)S(1)}, u32[]{:S(2)}, u32[]{:S(2)}) collective-permute-start(f32[2304]{0:T(1024)S(1)} %pad_maximum_fusion.7), channel_id=1, source_target_pairs={{0,128},{32,160},{64,192},{96,224},{128,0},{160,32},{192,64},{224,... | collective-permute-start | bytes 27656 | tf_op jit(solution)/shard_map/ppermute | solution.py:107
  172.4 5.5 %collective-permute-start.20 = (f32[4,512]{1,0:T(4,128)S(1)}, f32[4,512]{1,0:T(4,128)S(1)}, u32[]{:S(2)}, u32[]{:S(2)}) collective-permute-start(f32[4,512]{1,0:T(4,128)S(1)} %add.143), channel_id=1, source_target_pairs={{0,8},{1,9},{2,10},{3,11},{4,12},{5,13},{6,14},{7,15},{8,0},{9,1},... | collective-permute-start | bytes 24584 | tf_op jit(solution)/shard_map/ppermute | solution.py:100
  177.9 7.0 %collective-permute-start.21 = (f32[4,512]{1,0:T(4,128)S(1)}, f32[4,512]{1,0:T(4,128)S(1)}, u32[]{:S(2)}, u32[]{:S(2)}) collective-permute-start(f32[4,512]{1,0:T(4,128)S(1)} %add.144), channel_id=1, source_target_pairs={{0,16},{1,17},{2,18},{3,19},{4,20},{5,21},{6,22},{7,23},{8,24},{9,... | collective-permute-start | bytes 24584 | tf_op jit(solution)/shard_map/ppermute | solution.py:100
  185.0 14.3 %collective-permute-start.22 = (f32[2176]{0:T(1024)S(1)}, f32[2176]{0:T(1024)S(1)}, u32[]{:S(2)}, u32[]{:S(2)}) collective-permute-start(f32[2176]{0:T(1024)S(1)} %pad_maximum_fusion.8), channel_id=1, source_target_pairs={{0,256},{32,288},{64,320},{96,352},{128,384},{160,416},{192,448},{... | collective-permute-start | bytes 26120 | tf_op jit(solution)/shard_map/ppermute | solution.py:107
  (5 other events, 10.2 us)

commit v7 on v6

--- a/solution.py
+++ b/solution.py
@@ -124,7 +124,8 @@
 
     grp_bits = axis_order(n_grp, GRP_ORDER)
     halves = [own[: rows_here // 2], own[rows_here // 2:]]
-    col_buf, col_order = xor_gather(own_wide, "grp", n_grp, grp_bits)
+    col_buf = lax.all_to_all(jnp.broadcast_to(own_wide[None], (n_grp,) + own_wide.shape), "grp", 0, 0, tiled=True)
+    col_order = list(range(n_grp))
     blk_buf = jnp.concatenate(
         [xor_gather(h, "dev", n_dev, axis_order(n_dev, o))[0] for h, o in zip(halves, DEV_ORDERS)], axis=1
     )

time: 202 us -> 287 us (1.42)
  waiting for transfers between devices: 74.1 us -> 155 us
  starting transfers between devices: 80.9 us -> 85.7 us
  other arithmetic: 16.7 us -> 13 us
    ppermute x14 -> x10, waiting for transfers between devices: 33.3 us -> 126 us  [xor_gather(): other = lax.ppermute(buf, axis, [(i, i ^ k) for i in range(n)])]
    ppermute x14 -> x10, starting transfers between devices: 58.2 us -> 33.7 us  [xor_gather(): other = lax.ppermute(buf, axis, [(i, i ^ k) for i in range(n)])]
    all_to_all x0 -> x1, starting transfers between devices: none -> 18.2 us  [per_device(): lax.all_to_all(jnp.broadcast_to(own_wide[None], (n_grp,) + own_wide.shape...]
    ppermute x4, waiting for transfers between devices: 20.1 us -> 11.9 us  [xor_sum(): got = lax.ppermute(jnp.concatenate([x.ravel(), send.ravel()]), a, pairs)]
    ppermute x4, starting transfers between devices: 9.92 us -> 18.1 us  [xor_sum(): got = lax.ppermute(jnp.concatenate([x.ravel(), send.ravel()]), a, pairs)]
    select_n x14 -> x10, other arithmetic: 4.77 us -> 0.79 us  [xor_gather(): jnp.where(lo, jnp.concatenate([buf, other]), jnp.concatenate([other, buf]))]
    ppermute x5, starting transfers between devices: 12.8 us -> 15.8 us  [xor_sum(): x = x + lax.ppermute(x, a, pairs)]
    ppermute x5, waiting for transfers between devices: 20.7 us -> 17.7 us  [xor_sum(): x = x + lax.ppermute(x, a, pairs)]
  transfers between devices with their start and end apart: 23 -> 20, of which waited for: 17 -> 16; matrix products, arithmetic and copies ran while one was open for 6% -> 3% of each run, Pallas kernels for 0% -> 0%
where the time goes in v7:
time: 287 us; the launch traced here: 285 us
  waiting for transfers between devices  155 us (54%)
  starting transfers between devices  85.7 us (30%)
  matrix products  18.3 us (6%)
  other arithmetic  13 us (5%)
  local copies, waits for them, and re-layouts  11.5 us (4%)
    ppermute x10, waiting for transfers between devices, xor_gather(): other = lax.ppermute(buf, axis, [(i, i ^ k) for i in range(n)])  126 us
    ppermute x10, starting transfers between devices, xor_gather(): other = lax.ppermute(buf, axis, [(i, i ^ k) for i in range(n)])  33.7 us
    all_to_all x1, starting transfers between devices, per_device(): lax.all_to_all(jnp.broadcast_to(own_wide[None], (n_grp,) + own_wide.shape...  18.2 us
    ppermute x4, starting transfers between devices, xor_sum(): got = lax.ppermute(jnp.concatenate([x.ravel(), send.ravel()]), a, pairs)  18.1 us
    ppermute x5, waiting for transfers between devices, xor_sum(): x = x + lax.ppermute(x, a, pairs)  17.7 us
    ppermute x5, starting transfers between devices, xor_sum(): x = x + lax.ppermute(x, a, pairs)  15.8 us
    ppermute x4, waiting for transfers between devices, xor_sum(): got = lax.ppermute(jnp.concatenate([x.ravel(), send.ravel()]), a, pairs)  11.9 us
    dot_general x2, matrix products, distances(): lax.dot_general(left, right, (((1,), (1,)), ((), ())), preferred_element_...  8.65 us
  transfers between devices with their start and end apart: 20, of which 16 were waited for; matrix products, arithmetic and copies ran while one was open for 3% of the time, Pallas kernels for 0%

profile of v7, /device:TPU:6, one launch (start us, length us, event | category | flops | bytes accessed | tf_op | source)
XLA Modules:
  0.0 285.0 jit_solution(6600537795745639241)
XLA Ops:
  4.7 18.2 %all-to-all-start = ((bf16[16,32,2176]{2,1,0:T(8,128)(2,1)}), bf16[16,32,2176]{2,1,0:T(8,128)(2,1)}, u32[]{:S(2)}, u32[]{:S(2)}) async-start(bf16[16,32,2176]{2,1,0:T(8,128)(2,1)} %broadcast_in_dim.23), calls=%async_computation | async-start | bytes 4456448 | tf_op jit(solution)/shard_map/all_to_all | solution.py:127
  22.9 5.1 %collective-permute-start.5 = (bf16[1,16,1152]{2,1,0:T(8,128)(2,1)S(1)}, bf16[1,16,1152]{2,1,0:T(8,128)(2,1)S(1)}, u32[]{:S(2)}, u32[]{:S(2)}) collective-permute-start(bf16[1,16,1152]{2,1,0:T(8,128)(2,1)S(1)} %get-tuple-element.14), channel_id=1, source_target_pairs={{0,16},{1,17},{2,18},{3,19},{4,20},{5,21},{6,22},{7,23},{8,24},{9,... | collective-permute-start | bytes 110600 | tf_op jit(solution)/shard_map/ppermute | solution.py:70
  28.0 4.3 %collective-permute-start = (bf16[1,16,1152]{2,1,0:T(8,128)(2,1)S(1)}, bf16[1,16,1152]{2,1,0:T(8,128)(2,1)S(1)}, u32[]{:S(2)}, u32[]{:S(2)}) collective-permute-start(bf16[1,16,1152]{2,1,0:T(8,128)(2,1)S(1)} %get-tuple-element.13), channel_id=1, source_target_pairs={{0,4},{1,5},{2,6},{3,7},{4,0},{5,1},{6,2},{7,3},{8,12},{9,13},{10,... | collective-permute-start | bytes 110600 | tf_op jit(solution)/shard_map/ppermute | solution.py:70
  32.5 5.5 %collective-permute-start.6 = (bf16[2,16,1152]{2,1,0:T(8,128)(2,1)S(1)}, bf16[2,16,1152]{2,1,0:T(8,128)(2,1)S(1)}, u32[]{:S(2)}, u32[]{:S(2)}) collective-permute-start(bf16[2,16,1152]{2,1,0:T(8,128)(2,1)S(1)} %maximum_select_fusion.9), channel_id=1, source_target_pairs={{0,4},{1,5},{2,6},{3,7},{4,0},{5,1},{6,2},{7,3},{8,12},{9,13},{10,... | collective-permute-start | bytes 221192 | tf_op jit(solution)/shard_map/ppermute | solution.py:70
  38.0 92.5 %collective-permute-done = bf16[1,16,1152]{2,1,0:T(8,128)(2,1)S(1)} collective-permute-done((bf16[1,16,1152]{2,1,0:T(8,128)(2,1)S(1)}, bf16[1,16,1152]{2,1,0:T(8,128)(2,1)S(1)}, u32[]{:S(2)}, u32[]{:S(2)}) %collective-permute-start) | collective-permute-done | bytes 36896 | tf_op jit(solution)/shard_map/ppermute | solution.py:70
  130.5 5.2 %collective-permute-start.1 = (bf16[2,16,1152]{2,1,0:T(8,128)(2,1)S(1)}, bf16[2,16,1152]{2,1,0:T(8,128)(2,1)S(1)}, u32[]{:S(2)}, u32[]{:S(2)}) collective-permute-start(bf16[2,16,1152]{2,1,0:T(8,128)(2,1)S(1)} %maximum_select_fusion.8), channel_id=1, source_target_pairs={{0,16},{1,17},{2,18},{3,19},{4,20},{5,21},{6,22},{7,23},{8,24},{9,... | collective-permute-start | bytes 221192 | tf_op jit(solution)/shard_map/ppermute | solution.py:70
  145.2 9.1 %collective-permute-done.2 = bf16[4,16,1152]{2,1,0:T(8,128)(2,1)S(1)} collective-permute-done((bf16[4,16,1152]{2,1,0:T(8,128)(2,1)S(1)}, bf16[4,16,1152]{2,1,0:T(8,128)(2,1)S(1)}, u32[]{:S(2)}, u32[]{:S(2)}) %collective-permute-start.2) | collective-permute-done | bytes 147488 | tf_op jit(solution)/shard_map/ppermute | solution.py:70
  156.3 4.3 %collective-permute-done.8 = bf16[8,16,1152]{2,1,0:T(8,128)(2,1)S(1)} collective-permute-done((bf16[8,16,1152]{2,1,0:T(8,128)(2,1)S(1)}, bf16[8,16,1152]{2,1,0:T(8,128)(2,1)S(1)}, u32[]{:S(2)}, u32[]{:S(2)}) %collective-permute-start.8) | collective-permute-done | bytes 294944 | tf_op jit(solution)/shard_map/ppermute | solution.py:70
  162.8 4.0 %collective-permute-done.3 = bf16[8,16,1152]{2,1,0:T(8,128)(2,1)S(1)} collective-permute-done((bf16[8,16,1152]{2,1,0:T(8,128)(2,1)S(1)}, bf16[8,16,1152]{2,1,0:T(8,128)(2,1)S(1)}, u32[]{:S(2)}, u32[]{:S(2)}) %collective-permute-start.3) | collective-permute-done | bytes 294944 | tf_op jit(solution)/shard_map/ppermute | solution.py:70
  167.0 3.4 %collective-permute-start.4 = (bf16[16,16,1152]{2,1,0:T(8,128)(2,1)S(1)}, bf16[16,16,1152]{2,1,0:T(8,128)(2,1)S(1)}, u32[]{:S(2)}, u32[]{:S(2)}) collective-permute-start(bf16[16,16,1152]{2,1,0:T(8,128)(2,1)S(1)} %maximum_select_fusion.2), channel_id=1, source_target_pairs={{0,8},{1,9},{2,10},{3,11},{4,12},{5,13},{6,14},{7,15},{8,0},{9,1},... | collective-permute-start | bytes 1769480 | tf_op jit(solution)/shard_map/ppermute | solution.py:70
  171.0 8.4 %collective-permute-done.9 = bf16[16,16,1152]{2,1,0:T(8,128)(2,1)S(1)} collective-permute-done((bf16[16,16,1152]{2,1,0:T(8,128)(2,1)S(1)}, bf16[16,16,1152]{2,1,0:T(8,128)(2,1)S(1)}, u32[]{:S(2)}, u32[]{:S(2)}) %collective-permute-start.9) | collective-permute-done | bytes 589856 | tf_op jit(solution)/shard_map/ppermute | solution.py:70
  179.6 4.4 %collective-permute-done.4 = bf16[16,16,1152]{2,1,0:T(8,128)(2,1)S(1)} collective-permute-done((bf16[16,16,1152]{2,1,0:T(8,128)(2,1)S(1)}, bf16[16,16,1152]{2,1,0:T(8,128)(2,1)S(1)}, u32[]{:S(2)}, u32[]{:S(2)}) %collective-permute-start.4) | collective-permute-done | bytes 589856 | tf_op jit(solution)/shard_map/ppermute | solution.py:70
  190.2 3.1 %fusion.9 = bf16[1024,511]{0,1:T(8,128)(2,1)} fusion(s32[1024,525]{0,1:T(8,128)} %shift_right_arithmetic.77, s32[511]{0:T(512)S(1)} %slice.199, f32[1024]{0:T(1024)S(1)} %bitcast.70), kind=kLoop, calls=%fused_computation.17 | loop fusion | flops 3662848 | bytes 3145724 | tf_op jit(solution)/shard_map/convert.3
  208.6 6.1 %exponential_convert_fusion.3 = (bf16[512,1024]{1,0:T(8,128)(2,1)S(1)}, bf16[512,1024]{1,0:T(8,128)(2,1)S(1)}, bf16[512,1024]{1,0:T(8,128)(2,1)S(1)}, bf16[512,1024]{1,0:T(8,128)(2,1)S(1)}) fusion(f32[]{:T(128)} %bitcast.6, f32[]{:T(128)} %bitcast.13, f32[]{:T(128)} %bitcast.11, f32[]{:T(128)} %bitcast.9, bf16[1024,1152]{1,0:T(8,128)(2,1)S(1)} %bitcast.65, ...), kind=kOutput, calls=%fused_computation.21 | convolution fusion | flops 1080033280 | bytes 7348224 | tf_op jit(solution)/shard_map/dot_general | solution.py:41
  223.9 3.6 %collective-permute-done.11 = f32[4,512]{1,0:T(4,128)S(1)} collective-permute-done((f32[4,512]{1,0:T(4,128)S(1)}, f32[4,512]{1,0:T(4,128)S(1)}, u32[]{:S(2)}, u32[]{:S(2)}) %collective-permute-start.11) | collective-permute-done | bytes 8224 | tf_op jit(solution)/shard_map/ppermute | solution.py:100
  229.5 4.4 %collective-permute-done.12 = f32[4,512]{1,0:T(4,128)S(1)} collective-permute-done((f32[4,512]{1,0:T(4,128)S(1)}, f32[4,512]{1,0:T(4,128)S(1)}, u32[]{:S(2)}, u32[]{:S(2)}) %collective-permute-start.12) | collective-permute-done | bytes 8224 | tf_op jit(solution)/shard_map/ppermute | solution.py:100
  233.9 3.9 %collective-permute-start.13 = (f32[4,512]{1,0:T(4,128)S(1)}, f32[4,512]{1,0:T(4,128)S(1)}, u32[]{:S(2)}, u32[]{:S(2)}) collective-permute-start(f32[4,512]{1,0:T(4,128)S(1)} %add.134), channel_id=1, source_target_pairs={{0,4},{1,5},{2,6},{3,7},{4,0},{5,1},{6,2},{7,3},{8,12},{9,13},{10,... | collective-permute-start | bytes 24584 | tf_op jit(solution)/shard_map/ppermute | solution.py:100
  238.0 5.4 %collective-permute-done.13 = f32[4,512]{1,0:T(4,128)S(1)} collective-permute-done((f32[4,512]{1,0:T(4,128)S(1)}, f32[4,512]{1,0:T(4,128)S(1)}, u32[]{:S(2)}, u32[]{:S(2)}) %collective-permute-start.13) | collective-permute-done | bytes 8224 | tf_op jit(solution)/shard_map/ppermute | solution.py:100
  245.9 3.1 %collective-permute-done.14 = f32[2560]{0:T(1024)S(1)} collective-permute-done((f32[2560]{0:T(1024)S(1)}, f32[2560]{0:T(1024)S(1)}, u32[]{:S(2)}, u32[]{:S(2)}) %collective-permute-start.14) | collective-permute-done | bytes 10272 | tf_op jit(solution)/shard_map/ppermute | solution.py:107
  251.9 4.4 %collective-permute-done.15 = f32[2304]{0:T(1024)S(1)} collective-permute-done((f32[2304]{0:T(1024)S(1)}, f32[2304]{0:T(1024)S(1)}, u32[]{:S(2)}, u32[]{:S(2)}) %collective-permute-start.15) | collective-permute-done | bytes 9248 | tf_op jit(solution)/shard_map/ppermute | solution.py:107
  256.4 3.4 %collective-permute-start.16 = (f32[4,512]{1,0:T(4,128)S(1)}, f32[4,512]{1,0:T(4,128)S(1)}, u32[]{:S(2)}, u32[]{:S(2)}) collective-permute-start(f32[4,512]{1,0:T(4,128)S(1)} %add.143), channel_id=1, source_target_pairs={{0,8},{1,9},{2,10},{3,11},{4,12},{5,13},{6,14},{7,15},{8,0},{9,1},... | collective-permute-start | bytes 24584 | tf_op jit(solution)/shard_map/ppermute | solution.py:100
  261.9 4.7 %collective-permute-start.17 = (f32[4,512]{1,0:T(4,128)S(1)}, f32[4,512]{1,0:T(4,128)S(1)}, u32[]{:S(2)}, u32[]{:S(2)}) collective-permute-start(f32[4,512]{1,0:T(4,128)S(1)} %add.144), channel_id=1, source_target_pairs={{0,16},{1,17},{2,18},{3,19},{4,20},{5,21},{6,22},{7,23},{8,24},{9,... | collective-permute-start | bytes 24584 | tf_op jit(solution)/shard_map/ppermute | solution.py:100
  269.0 11.0 %collective-permute-start.18 = (f32[2176]{0:T(1024)S(1)}, f32[2176]{0:T(1024)S(1)}, u32[]{:S(2)}, u32[]{:S(2)}) collective-permute-start(f32[2176]{0:T(1024)S(1)} %pad_maximum_fusion.9), channel_id=1, source_target_pairs={{0,256},{32,288},{64,320},{96,352},{128,384},{160,416},{192,448},{... | collective-permute-start | bytes 26120 | tf_op jit(solution)/shard_map/ppermute | solution.py:107
  280.0 3.3 %collective-permute-done.18 = f32[2176]{0:T(1024)S(1)} collective-permute-done((f32[2176]{0:T(1024)S(1)}, f32[2176]{0:T(1024)S(1)}, u32[]{:S(2)}, u32[]{:S(2)}) %collective-permute-start.18) | collective-permute-done | bytes 8736 | tf_op jit(solution)/shard_map/ppermute | solution.py:107
  (141 shorter events, 63.1 us)
Async XLA Ops:
  4.7 18.2 %copy-start.3 = (bf16[32,1024]{1,0:T(8,128)(2,1)S(1)}, bf16[32,1024]{1,0:T(8,128)(2,1)}, u32[]{:S(2)}) copy-start(bf16[32,1024]{1,0:T(8,128)(2,1)} %param.7) | copy-start | bytes 196612
  4.7 27.6 %copy-start.5 = (f32[16]{0:T(128)S(1)}, f32[16]{0:T(128)}, u32[]{:S(2)}) copy-start(f32[16]{0:T(128)} %param.11) | copy-start | bytes 196
  4.7 27.6 %copy-start.6 = (s32[4]{0:T(128)S(1)}, s32[4]{0:T(128)}, u32[]{:S(2)}) copy-start(s32[4]{0:T(128)} %param.12) | copy-start | bytes 52
  4.7 188.7 %all-to-all-start = ((bf16[16,32,2176]{2,1,0:T(8,128)(2,1)}), bf16[16,32,2176]{2,1,0:T(8,128)(2,1)}, u32[]{:S(2)}, u32[]{:S(2)}) async-start(bf16[16,32,2176]{2,1,0:T(8,128)(2,1)} %broadcast_in_dim.23), calls=%async_computation | async-start | bytes 4456448 | tf_op jit(solution)/shard_map/all_to_all | solution.py:127
  22.9 9.6 %collective-permute-start.5 = (bf16[1,16,1152]{2,1,0:T(8,128)(2,1)S(1)}, bf16[1,16,1152]{2,1,0:T(8,128)(2,1)S(1)}, u32[]{:S(2)}, u32[]{:S(2)}) collective-permute-start(bf16[1,16,1152]{2,1,0:T(8,128)(2,1)S(1)} %get-tuple-element.14), channel_id=1, source_target_pairs={{0,16},{1,17},{2,18},{3,19},{4,20},{5,21},{6,22},{7,23},{8,24},{9,... | collective-permute-start | bytes 110600 | tf_op jit(solution)/shard_map/ppermute | solution.py:70
  28.0 102.6 %collective-permute-start = (bf16[1,16,1152]{2,1,0:T(8,128)(2,1)S(1)}, bf16[1,16,1152]{2,1,0:T(8,128)(2,1)S(1)}, u32[]{:S(2)}, u32[]{:S(2)}) collective-permute-start(bf16[1,16,1152]{2,1,0:T(8,128)(2,1)S(1)} %get-tuple-element.13), channel_id=1, source_target_pairs={{0,4},{1,5},{2,6},{3,7},{4,0},{5,1},{6,2},{7,3},{8,12},{9,13},{10,... | collective-permute-start | bytes 110600 | tf_op jit(solution)/shard_map/ppermute | solution.py:70
  32.5 103.2 %collective-permute-start.6 = (bf16[2,16,1152]{2,1,0:T(8,128)(2,1)S(1)}, bf16[2,16,1152]{2,1,0:T(8,128)(2,1)S(1)}, u32[]{:S(2)}, u32[]{:S(2)}) collective-permute-start(bf16[2,16,1152]{2,1,0:T(8,128)(2,1)S(1)} %maximum_select_fusion.9), channel_id=1, source_target_pairs={{0,4},{1,5},{2,6},{3,7},{4,0},{5,1},{6,2},{7,3},{8,12},{9,13},{10,... | collective-permute-start | bytes 221192 | tf_op jit(solution)/shard_map/ppermute | solution.py:70
  130.5 7.8 %collective-permute-start.1 = (bf16[2,16,1152]{2,1,0:T(8,128)(2,1)S(1)}, bf16[2,16,1152]{2,1,0:T(8,128)(2,1)S(1)}, u32[]{:S(2)}, u32[]{:S(2)}) collective-permute-start(bf16[2,16,1152]{2,1,0:T(8,128)(2,1)S(1)} %maximum_select_fusion.8), channel_id=1, source_target_pairs={{0,16},{1,17},{2,18},{3,19},{4,20},{5,21},{6,22},{7,23},{8,24},{9,... | collective-permute-start | bytes 221192 | tf_op jit(solution)/shard_map/ppermute | solution.py:70
  135.8 7.3 %collective-permute-start.7 = (bf16[4,16,1152]{2,1,0:T(8,128)(2,1)S(1)}, bf16[4,16,1152]{2,1,0:T(8,128)(2,1)S(1)}, u32[]{:S(2)}, u32[]{:S(2)}) collective-permute-start(bf16[4,16,1152]{2,1,0:T(8,128)(2,1)S(1)} %maximum_select_fusion.7), channel_id=1, source_target_pairs={{0,8},{1,9},{2,10},{3,11},{4,12},{5,13},{6,14},{7,15},{8,0},{9,1},... | collective-permute-start | bytes 442376 | tf_op jit(solution)/shard_map/ppermute | solution.py:70
  138.3 16.0 %collective-permute-start.2 = (bf16[4,16,1152]{2,1,0:T(8,128)(2,1)S(1)}, bf16[4,16,1152]{2,1,0:T(8,128)(2,1)S(1)}, u32[]{:S(2)}, u32[]{:S(2)}) collective-permute-start(bf16[4,16,1152]{2,1,0:T(8,128)(2,1)S(1)} %maximum_select_fusion.6), channel_id=1, source_target_pairs={{0,2},{1,3},{2,0},{3,1},{4,6},{5,7},{6,4},{7,5},{8,10},{9,11},{10,... | collective-permute-start | bytes 442376 | tf_op jit(solution)/shard_map/ppermute | solution.py:70
  143.1 17.4 %collective-permute-start.8 = (bf16[8,16,1152]{2,1,0:T(8,128)(2,1)S(1)}, bf16[8,16,1152]{2,1,0:T(8,128)(2,1)S(1)}, u32[]{:S(2)}, u32[]{:S(2)}) collective-permute-start(bf16[8,16,1152]{2,1,0:T(8,128)(2,1)S(1)} %maximum_select_fusion.5), channel_id=1, source_target_pairs={{0,2},{1,3},{2,0},{3,1},{4,6},{5,7},{6,4},{7,5},{8,10},{9,11},{10,... | collective-permute-start | bytes 884744 | tf_op jit(solution)/shard_map/ppermute | solution.py:70
  154.4 12.5 %collective-permute-start.3 = (bf16[8,16,1152]{2,1,0:T(8,128)(2,1)S(1)}, bf16[8,16,1152]{2,1,0:T(8,128)(2,1)S(1)}, u32[]{:S(2)}, u32[]{:S(2)}) collective-permute-start(bf16[8,16,1152]{2,1,0:T(8,128)(2,1)S(1)} %maximum_select_fusion.4), channel_id=1, source_target_pairs={{0,1},{1,0},{2,3},{3,2},{4,5},{5,4},{6,7},{7,6},{8,9},{9,8},{10,11... | collective-permute-start | bytes 884744 | tf_op jit(solution)/shard_map/ppermute | solution.py:70
  160.7 18.8 %collective-permute-start.9 = (bf16[16,16,1152]{2,1,0:T(8,128)(2,1)S(1)}, bf16[16,16,1152]{2,1,0:T(8,128)(2,1)S(1)}, u32[]{:S(2)}, u32[]{:S(2)}) collective-permute-start(bf16[16,16,1152]{2,1,0:T(8,128)(2,1)S(1)} %maximum_select_fusion.3), channel_id=1, source_target_pairs={{0,1},{1,0},{2,3},{3,2},{4,5},{5,4},{6,7},{7,6},{8,9},{9,8},{10,11... | collective-permute-start | bytes 1769480 | tf_op jit(solution)/shard_map/ppermute | solution.py:70
  167.0 17.1 %collective-permute-start.4 = (bf16[16,16,1152]{2,1,0:T(8,128)(2,1)S(1)}, bf16[16,16,1152]{2,1,0:T(8,128)(2,1)S(1)}, u32[]{:S(2)}, u32[]{:S(2)}) collective-permute-start(bf16[16,16,1152]{2,1,0:T(8,128)(2,1)S(1)} %maximum_select_fusion.2), channel_id=1, source_target_pairs={{0,8},{1,9},{2,10},{3,11},{4,12},{5,13},{6,14},{7,15},{8,0},{9,1},... | collective-permute-start | bytes 1769480 | tf_op jit(solution)/shard_map/ppermute | solution.py:70
  199.2 2.9 %copy-start.2 = (bf16[1024,511]{0,1:T(8,128)(2,1)S(1)}, bf16[1024,511]{0,1:T(8,128)(2,1)}, u32[]{:S(2)}) copy-start(bf16[1024,511]{0,1:T(8,128)(2,1)} %fusion.9) | copy-start | bytes 3139588
  218.8 3.1 %collective-permute-start.10 = (f32[3072]{0:T(1024)S(1)}, f32[3072]{0:T(1024)S(1)}, u32[]{:S(2)}, u32[]{:S(2)}) collective-permute-start(f32[3072]{0:T(1024)S(1)} %pad_maximum_fusion.6), channel_id=1, source_target_pairs={{0,32},{32,0},{64,96},{96,64},{128,160},{160,128},{192,224},{224,1... | collective-permute-start | bytes 36872 | tf_op jit(solution)/shard_map/ppermute | solution.py:107
  221.9 5.5 %collective-permute-start.11 = (f32[4,512]{1,0:T(4,128)S(1)}, f32[4,512]{1,0:T(4,128)S(1)}, u32[]{:S(2)}, u32[]{:S(2)}) collective-permute-start(f32[4,512]{1,0:T(4,128)S(1)} %fusion.50), channel_id=1, source_target_pairs={{0,1},{1,0},{2,3},{3,2},{4,5},{5,4},{6,7},{7,6},{8,9},{9,8},{10,11... | collective-permute-start | bytes 24584 | tf_op jit(solution)/shard_map/ppermute | solution.py:100
  227.5 6.4 %collective-permute-start.12 = (f32[4,512]{1,0:T(4,128)S(1)}, f32[4,512]{1,0:T(4,128)S(1)}, u32[]{:S(2)}, u32[]{:S(2)}) collective-permute-start(f32[4,512]{1,0:T(4,128)S(1)} %fusion.65), channel_id=1, source_target_pairs={{0,2},{1,3},{2,0},{3,1},{4,6},{5,7},{6,4},{7,5},{8,10},{9,11},{10,... | collective-permute-start | bytes 24584 | tf_op jit(solution)/shard_map/ppermute | solution.py:100
  233.9 9.5 %collective-permute-start.13 = (f32[4,512]{1,0:T(4,128)S(1)}, f32[4,512]{1,0:T(4,128)S(1)}, u32[]{:S(2)}, u32[]{:S(2)}) collective-permute-start(f32[4,512]{1,0:T(4,128)S(1)} %add.134), channel_id=1, source_target_pairs={{0,4},{1,5},{2,6},{3,7},{4,0},{5,1},{6,2},{7,3},{8,12},{9,13},{10,... | collective-permute-start | bytes 24584 | tf_op jit(solution)/shard_map/ppermute | solution.py:100
  243.4 5.6 %collective-permute-start.14 = (f32[2560]{0:T(1024)S(1)}, f32[2560]{0:T(1024)S(1)}, u32[]{:S(2)}, u32[]{:S(2)}) collective-permute-start(f32[2560]{0:T(1024)S(1)} %pad_maximum_fusion.7), channel_id=1, source_target_pairs={{0,64},{32,96},{64,0},{96,32},{128,192},{160,224},{192,128},{224,1... | collective-permute-start | bytes 30728 | tf_op jit(solution)/shard_map/ppermute | solution.py:107
  249.3 7.1 %collective-permute-start.15 = (f32[2304]{0:T(1024)S(1)}, f32[2304]{0:T(1024)S(1)}, u32[]{:S(2)}, u32[]{:S(2)}) collective-permute-start(f32[2304]{0:T(1024)S(1)} %pad_maximum_fusion.8), channel_id=1, source_target_pairs={{0,128},{32,160},{64,192},{96,224},{128,0},{160,32},{192,64},{224,... | collective-permute-start | bytes 27656 | tf_op jit(solution)/shard_map/ppermute | solution.py:107
  256.4 5.5 %collective-permute-start.16 = (f32[4,512]{1,0:T(4,128)S(1)}, f32[4,512]{1,0:T(4,128)S(1)}, u32[]{:S(2)}, u32[]{:S(2)}) collective-permute-start(f32[4,512]{1,0:T(4,128)S(1)} %add.143), channel_id=1, source_target_pairs={{0,8},{1,9},{2,10},{3,11},{4,12},{5,13},{6,14},{7,15},{8,0},{9,1},... | collective-permute-start | bytes 24584 | tf_op jit(solution)/shard_map/ppermute | solution.py:100
  261.9 7.0 %collective-permute-start.17 = (f32[4,512]{1,0:T(4,128)S(1)}, f32[4,512]{1,0:T(4,128)S(1)}, u32[]{:S(2)}, u32[]{:S(2)}) collective-permute-start(f32[4,512]{1,0:T(4,128)S(1)} %add.144), channel_id=1, source_target_pairs={{0,16},{1,17},{2,18},{3,19},{4,20},{5,21},{6,22},{7,23},{8,24},{9,... | collective-permute-start | bytes 24584 | tf_op jit(solution)/shard_map/ppermute | solution.py:100
  269.0 14.3 %collective-permute-start.18 = (f32[2176]{0:T(1024)S(1)}, f32[2176]{0:T(1024)S(1)}, u32[]{:S(2)}, u32[]{:S(2)}) collective-permute-start(f32[2176]{0:T(1024)S(1)} %pad_maximum_fusion.9), channel_id=1, source_target_pairs={{0,256},{32,288},{64,320},{96,352},{128,384},{160,416},{192,448},{... | collective-permute-start | bytes 26120 | tf_op jit(solution)/shard_map/ppermute | solution.py:107
  (3 other events, 5.9 us)

commit v8 on v6

--- a/solution.py
+++ b/solution.py
@@ -62,9 +62,9 @@
     return rows, make_vectors(labels, sign_words)
 
 
-def xor_gather(x, axis, n, bits):
+def xor_gather(x, axis, n, bits, buf=None):
     idx = lax.axis_index(axis)
-    buf = x[None]
+    buf = x[None] if buf is None else buf
     for b in bits:
         k = 1 << b
         other = lax.ppermute(buf, axis, [(i, i ^ k) for i in range(n)])
@@ -75,7 +75,8 @@
 
 
 GRP_ORDER = (3, 1, 2, 0)
-DEV_ORDERS = ((2, 4, 1, 0, 3), (4, 2, 3, 1, 0))
+DEV_JOINT = (2, 4)
+DEV_ORDERS = ((1, 0, 3), (3, 1, 0))
 SUM_ORDER = (("grp", 0), ("dev", 0), ("dev", 1), ("dev", 2), ("grp", 1), ("grp", 2), ("dev", 3), ("dev", 4), ("grp", 3))
 
 
@@ -123,11 +124,17 @@
     own_wide = jnp.concatenate([own, corpus], axis=1)
 
     grp_bits = axis_order(n_grp, GRP_ORDER)
-    halves = [own[: rows_here // 2], own[rows_here // 2:]]
+    dev_nbits = n_dev.bit_length() - 1
+    joint = [b for b in DEV_JOINT if b < dev_nbits]
     col_buf, col_order = xor_gather(own_wide, "grp", n_grp, grp_bits)
-    blk_buf = jnp.concatenate(
-        [xor_gather(h, "dev", n_dev, axis_order(n_dev, o))[0] for h, o in zip(halves, DEV_ORDERS)], axis=1
-    )
+    blk_buf, _ = xor_gather(own, "dev", n_dev, joint)
+    half = rows_here // 2
+    parts = []
+    for h, o in zip((blk_buf[:, :half], blk_buf[:, half:]), DEV_ORDERS):
+        rest = axis_order(n_dev, [b for b in o if b not in joint])
+        rest = [b for b in rest if b not in joint]
+        parts.append(xor_gather(None, "dev", n_dev, rest, buf=h)[0])
+    blk_buf = jnp.concatenate(parts, axis=1)
 
     col_buf = col_buf.reshape(n_grp * rows_here, -1)
     blk_buf = blk_buf.reshape(n_dev * rows_here, -1)

time: 202 us -> 187 us (0.926)
  waiting for transfers between devices: 74.1 us -> 43.7 us
  starting transfers between devices: 80.9 us -> 95.3 us
    ppermute x14 -> x12, waiting for transfers between devices: 33.3 us -> 19.1 us  [xor_gather(): other = lax.ppermute(buf, axis, [(i, i ^ k) for i in range(n)])]
    ppermute x4, waiting for transfers between devices: 20.1 us -> 10.4 us  [xor_sum(): got = lax.ppermute(jnp.concatenate([x.ravel(), send.ravel()]), a, pairs)]
    ppermute x4, starting transfers between devices: 9.92 us -> 19.6 us  [xor_sum(): got = lax.ppermute(jnp.concatenate([x.ravel(), send.ravel()]), a, pairs)]
    ppermute x5, starting transfers between devices: 12.8 us -> 19.8 us  [xor_sum(): x = x + lax.ppermute(x, a, pairs)]
    ppermute x5, waiting for transfers between devices: 20.7 us -> 14.2 us  [xor_sum(): x = x + lax.ppermute(x, a, pairs)]
    ppermute x14 -> x12, starting transfers between devices: 58.2 us -> 55.9 us  [xor_gather(): other = lax.ppermute(buf, axis, [(i, i ^ k) for i in range(n)])]
    select_n x14 -> x12, other arithmetic: 4.77 us -> 4.77 us  [xor_gather(): jnp.where(lo, jnp.concatenate([buf, other]), jnp.concatenate([other, buf]))]
  transfers between devices with their start and end apart: 23 -> 21, of which waited for: 17 -> 16; matrix products, arithmetic and copies ran while one was open for 6% -> 7% of each run, Pallas kernels for 0% -> 0%
where the time goes in v8:
time: 187 us; the launch traced here: 185 us
  starting transfers between devices  95.3 us (51%)
  waiting for transfers between devices  43.7 us (23%)
  matrix products  18.3 us (10%)
  other arithmetic  16.8 us (9%)
  local copies, waits for them, and re-layouts  9.78 us (5%)
    ppermute x12, starting transfers between devices, xor_gather(): other = lax.ppermute(buf, axis, [(i, i ^ k) for i in range(n)])  55.9 us
    ppermute x5, starting transfers between devices, xor_sum(): x = x + lax.ppermute(x, a, pairs)  19.8 us
    ppermute x4, starting transfers between devices, xor_sum(): got = lax.ppermute(jnp.concatenate([x.ravel(), send.ravel()]), a, pairs)  19.6 us
    ppermute x12, waiting for transfers between devices, xor_gather(): other = lax.ppermute(buf, axis, [(i, i ^ k) for i in range(n)])  19.1 us
    ppermute x5, waiting for transfers between devices, xor_sum(): x = x + lax.ppermute(x, a, pairs)  14.2 us
    ppermute x4, waiting for transfers between devices, xor_sum(): got = lax.ppermute(jnp.concatenate([x.ravel(), send.ravel()]), a, pairs)  10.4 us
    dot_general x2, matrix products, distances(): lax.dot_general(left, right, (((1,), (1,)), ((), ())), preferred_element_...  8.65 us
    dot_general x4, matrix products, per_device(): product = jnp.dot(kern, col_vec, preferred_element_type=jnp.float32)  6.49 us
  transfers between devices with their start and end apart: 21, of which 16 were waited for; matrix products, arithmetic and copies ran while one was open for 7% of the time, Pallas kernels for 0%

profile of v8, /device:TPU:6, one launch (start us, length us, event | category | flops | bytes accessed | tf_op | source)
XLA Modules:
  0.0 185.1 jit_solution(10001720397396653670)
XLA Ops:
  3.1 9.1 %collective-permute-start = (bf16[1,32,1152]{2,1,0:T(8,128)(2,1)S(1)}, bf16[1,32,1152]{2,1,0:T(8,128)(2,1)S(1)}, u32[]{:S(2)}, u32[]{:S(2)}) collective-permute-start(bf16[1,32,1152]{2,1,0:T(8,128)(2,1)S(1)} %maximum_bitcast_fusion.1), channel_id=1, source_target_pairs={{0,4},{1,5},{2,6},{3,7},{4,0},{5,1},{6,2},{7,3},{8,12},{9,13},{10,... | collective-permute-start | bytes 221192 | tf_op jit(solution)/shard_map/ppermute | solution.py:70
  13.0 10.9 %collective-permute-start.8 = (bf16[1,32,2176]{2,1,0:T(8,128)(2,1)S(1)}, bf16[1,32,2176]{2,1,0:T(8,128)(2,1)S(1)}, u32[]{:S(2)}, u32[]{:S(2)}) collective-permute-start(bf16[1,32,2176]{2,1,0:T(8,128)(2,1)S(1)} %maximum_bitcast_fusion), channel_id=1, source_target_pairs={{0,256},{32,288},{64,320},{96,352},{128,384},{160,416},{192,448},{... | collective-permute-start | bytes 417800 | tf_op jit(solution)/shard_map/ppermute | solution.py:70
  24.9 5.1 %collective-permute-start.1 = (bf16[2,32,1152]{2,1,0:T(8,128)(2,1)S(1)}, bf16[2,32,1152]{2,1,0:T(8,128)(2,1)S(1)}, u32[]{:S(2)}, u32[]{:S(2)}) collective-permute-start(bf16[2,32,1152]{2,1,0:T(8,128)(2,1)S(1)} %maximum_select_fusion.11), channel_id=1, source_target_pairs={{0,16},{1,17},{2,18},{3,19},{4,20},{5,21},{6,22},{7,23},{8,24},{9,... | collective-permute-start | bytes 442376 | tf_op jit(solution)/shard_map/ppermute | solution.py:70
  30.7 2.7 %collective-permute-done.1 = bf16[2,32,1152]{2,1,0:T(8,128)(2,1)S(1)} collective-permute-done((bf16[2,32,1152]{2,1,0:T(8,128)(2,1)S(1)}, bf16[2,32,1152]{2,1,0:T(8,128)(2,1)S(1)}, u32[]{:S(2)}, u32[]{:S(2)}) %collective-permute-start.1) | collective-permute-done | bytes 147488 | tf_op jit(solution)/shard_map/ppermute | solution.py:70
  33.5 3.4 %collective-permute-start.2 = (bf16[4,16,1152]{2,1,0:T(8,128)(2,1)S(1)}, bf16[4,16,1152]{2,1,0:T(8,128)(2,1)S(1)}, u32[]{:S(2)}, u32[]{:S(2)}) collective-permute-start(bf16[4,16,1152]{2,1,0:T(8,128)(2,1)S(1)} %get-tuple-element.13), channel_id=1, source_target_pairs={{0,2},{1,3},{2,0},{3,1},{4,6},{5,7},{6,4},{7,5},{8,10},{9,11},{10,... | collective-permute-start | bytes 442376 | tf_op jit(solution)/shard_map/ppermute | solution.py:70
  37.0 2.7 %collective-permute-start.9 = (bf16[2,32,2176]{2,1,0:T(8,128)(2,1)S(1)}, bf16[2,32,2176]{2,1,0:T(8,128)(2,1)S(1)}, u32[]{:S(2)}, u32[]{:S(2)}) collective-permute-start(bf16[2,32,2176]{2,1,0:T(8,128)(2,1)S(1)} %maximum_select_fusion.10), channel_id=1, source_target_pairs={{0,64},{32,96},{64,0},{96,32},{128,192},{160,224},{192,128},{224,1... | collective-permute-start | bytes 835592 | tf_op jit(solution)/shard_map/ppermute | solution.py:70
  39.7 3.5 %collective-permute-start.5 = (bf16[4,16,1152]{2,1,0:T(8,128)(2,1)S(1)}, bf16[4,16,1152]{2,1,0:T(8,128)(2,1)S(1)}, u32[]{:S(2)}, u32[]{:S(2)}) collective-permute-start(bf16[4,16,1152]{2,1,0:T(8,128)(2,1)S(1)} %get-tuple-element.14), channel_id=1, source_target_pairs={{0,8},{1,9},{2,10},{3,11},{4,12},{5,13},{6,14},{7,15},{8,0},{9,1},... | collective-permute-start | bytes 442376 | tf_op jit(solution)/shard_map/ppermute | solution.py:70
  46.8 7.6 %collective-permute-start.6 = (bf16[8,16,1152]{2,1,0:T(8,128)(2,1)S(1)}, bf16[8,16,1152]{2,1,0:T(8,128)(2,1)S(1)}, u32[]{:S(2)}, u32[]{:S(2)}) collective-permute-start(bf16[8,16,1152]{2,1,0:T(8,128)(2,1)S(1)} %maximum_select_fusion.9), channel_id=1, source_target_pairs={{0,2},{1,3},{2,0},{3,1},{4,6},{5,7},{6,4},{7,5},{8,10},{9,11},{10,... | collective-permute-start | bytes 884744 | tf_op jit(solution)/shard_map/ppermute | solution.py:70
  54.5 3.0 %collective-permute-start.10 = (bf16[4,32,2176]{2,1,0:T(8,128)(2,1)S(1)}, bf16[4,32,2176]{2,1,0:T(8,128)(2,1)S(1)}, u32[]{:S(2)}, u32[]{:S(2)}) collective-permute-start(bf16[4,32,2176]{2,1,0:T(8,128)(2,1)S(1)} %maximum_select_fusion.6), channel_id=1, source_target_pairs={{0,128},{32,160},{64,192},{96,224},{128,0},{160,32},{192,64},{224,... | collective-permute-start | bytes 1671176 | tf_op jit(solution)/shard_map/ppermute | solution.py:70
  58.3 4.3 %collective-permute-start.4 = (bf16[16,16,1152]{2,1,0:T(8,128)(2,1)S(1)}, bf16[16,16,1152]{2,1,0:T(8,128)(2,1)S(1)}, u32[]{:S(2)}, u32[]{:S(2)}) collective-permute-start(bf16[16,16,1152]{2,1,0:T(8,128)(2,1)S(1)} %maximum_select_fusion.4), channel_id=1, source_target_pairs={{0,8},{1,9},{2,10},{3,11},{4,12},{5,13},{6,14},{7,15},{8,0},{9,1},... | collective-permute-start | bytes 1769480 | tf_op jit(solution)/shard_map/ppermute | solution.py:70
  62.7 4.2 %collective-permute-done.6 = bf16[8,16,1152]{2,1,0:T(8,128)(2,1)S(1)} collective-permute-done((bf16[8,16,1152]{2,1,0:T(8,128)(2,1)S(1)}, bf16[8,16,1152]{2,1,0:T(8,128)(2,1)S(1)}, u32[]{:S(2)}, u32[]{:S(2)}) %collective-permute-start.6) | collective-permute-done | bytes 294944 | tf_op jit(solution)/shard_map/ppermute | solution.py:70
  74.4 8.4 %collective-permute-done.7 = bf16[16,16,1152]{2,1,0:T(8,128)(2,1)S(1)} collective-permute-done((bf16[16,16,1152]{2,1,0:T(8,128)(2,1)S(1)}, bf16[16,16,1152]{2,1,0:T(8,128)(2,1)S(1)}, u32[]{:S(2)}, u32[]{:S(2)}) %collective-permute-start.7) | collective-permute-done | bytes 589856 | tf_op jit(solution)/shard_map/ppermute | solution.py:70
  88.9 3.1 %fusion.9 = bf16[1024,511]{0,1:T(8,128)(2,1)} fusion(s32[1024,525]{0,1:T(8,128)} %shift_right_arithmetic.77, s32[511]{0:T(512)S(1)} %slice.199, f32[1024]{0:T(1024)S(1)} %bitcast.74), kind=kLoop, calls=%fused_computation.18 | loop fusion | flops 3662848 | bytes 3145724 | tf_op jit(solution)/shard_map/convert.3
  108.4 6.1 %exponential_convert_fusion.3 = (bf16[512,1024]{1,0:T(8,128)(2,1)S(1)}, bf16[512,1024]{1,0:T(8,128)(2,1)S(1)}, bf16[512,1024]{1,0:T(8,128)(2,1)S(1)}, bf16[512,1024]{1,0:T(8,128)(2,1)S(1)}) fusion(f32[]{:T(128)} %bitcast.6, f32[]{:T(128)} %bitcast.13, f32[]{:T(128)} %bitcast.11, f32[]{:T(128)} %bitcast.9, bf16[1024,1152]{1,0:T(8,128)(2,1)S(1)} %bitcast.65, ...), kind=kOutput, calls=%fused_computation.22 | convolution fusion | flops 1080033280 | bytes 7348224 | tf_op jit(solution)/shard_map/dot_general | solution.py:41
  121.6 3.6 %collective-permute-start.13 = (f32[4,512]{1,0:T(4,128)S(1)}, f32[4,512]{1,0:T(4,128)S(1)}, u32[]{:S(2)}, u32[]{:S(2)}) collective-permute-start(f32[4,512]{1,0:T(4,128)S(1)} %fusion.47), channel_id=1, source_target_pairs={{0,1},{1,0},{2,3},{3,2},{4,5},{5,4},{6,7},{7,6},{8,9},{9,8},{10,11... | collective-permute-start | bytes 24584 | tf_op jit(solution)/shard_map/ppermute | solution.py:101
  127.1 5.3 %collective-permute-start.14 = (f32[4,512]{1,0:T(4,128)S(1)}, f32[4,512]{1,0:T(4,128)S(1)}, u32[]{:S(2)}, u32[]{:S(2)}) collective-permute-start(f32[4,512]{1,0:T(4,128)S(1)} %fusion.63), channel_id=1, source_target_pairs={{0,2},{1,3},{2,0},{3,1},{4,6},{5,7},{6,4},{7,5},{8,10},{9,11},{10,... | collective-permute-start | bytes 24584 | tf_op jit(solution)/shard_map/ppermute | solution.py:101
  134.1 2.8 %collective-permute-start.15 = (f32[4,512]{1,0:T(4,128)S(1)}, f32[4,512]{1,0:T(4,128)S(1)}, u32[]{:S(2)}, u32[]{:S(2)}) collective-permute-start(f32[4,512]{1,0:T(4,128)S(1)} %add.134), channel_id=1, source_target_pairs={{0,4},{1,5},{2,6},{3,7},{4,0},{5,1},{6,2},{7,3},{8,12},{9,13},{10,... | collective-permute-start | bytes 24584 | tf_op jit(solution)/shard_map/ppermute | solution.py:101
  137.0 6.5 %collective-permute-done.15 = f32[4,512]{1,0:T(4,128)S(1)} collective-permute-done((f32[4,512]{1,0:T(4,128)S(1)}, f32[4,512]{1,0:T(4,128)S(1)}, u32[]{:S(2)}, u32[]{:S(2)}) %collective-permute-start.15) | collective-permute-done | bytes 8224 | tf_op jit(solution)/shard_map/ppermute | solution.py:101
  143.5 3.1 %collective-permute-start.16 = (f32[2560]{0:T(1024)S(1)}, f32[2560]{0:T(1024)S(1)}, u32[]{:S(2)}, u32[]{:S(2)}) collective-permute-start(f32[2560]{0:T(1024)S(1)} %pad_maximum_fusion.5), channel_id=1, source_target_pairs={{0,64},{32,96},{64,0},{96,32},{128,192},{160,224},{192,128},{224,1... | collective-permute-start | bytes 30728 | tf_op jit(solution)/shard_map/ppermute | solution.py:108
  149.4 3.0 %collective-permute-start.17 = (f32[2304]{0:T(1024)S(1)}, f32[2304]{0:T(1024)S(1)}, u32[]{:S(2)}, u32[]{:S(2)}) collective-permute-start(f32[2304]{0:T(1024)S(1)} %pad_maximum_fusion.6), channel_id=1, source_target_pairs={{0,128},{32,160},{64,192},{96,224},{128,0},{160,32},{192,64},{224,... | collective-permute-start | bytes 27656 | tf_op jit(solution)/shard_map/ppermute | solution.py:108
  152.4 4.1 %collective-permute-done.17 = f32[2304]{0:T(1024)S(1)} collective-permute-done((f32[2304]{0:T(1024)S(1)}, f32[2304]{0:T(1024)S(1)}, u32[]{:S(2)}, u32[]{:S(2)}) %collective-permute-start.17) | collective-permute-done | bytes 9248 | tf_op jit(solution)/shard_map/ppermute | solution.py:108
  156.5 3.0 %collective-permute-start.18 = (f32[4,512]{1,0:T(4,128)S(1)}, f32[4,512]{1,0:T(4,128)S(1)}, u32[]{:S(2)}, u32[]{:S(2)}) collective-permute-start(f32[4,512]{1,0:T(4,128)S(1)} %add.143), channel_id=1, source_target_pairs={{0,8},{1,9},{2,10},{3,11},{4,12},{5,13},{6,14},{7,15},{8,0},{9,1},... | collective-permute-start | bytes 24584 | tf_op jit(solution)/shard_map/ppermute | solution.py:101
  162.0 5.0 %collective-permute-start.19 = (f32[4,512]{1,0:T(4,128)S(1)}, f32[4,512]{1,0:T(4,128)S(1)}, u32[]{:S(2)}, u32[]{:S(2)}) collective-permute-start(f32[4,512]{1,0:T(4,128)S(1)} %add.144), channel_id=1, source_target_pairs={{0,16},{1,17},{2,18},{3,19},{4,20},{5,21},{6,22},{7,23},{8,24},{9,... | collective-permute-start | bytes 24584 | tf_op jit(solution)/shard_map/ppermute | solution.py:101
  169.1 11.6 %collective-permute-start.20 = (f32[2176]{0:T(1024)S(1)}, f32[2176]{0:T(1024)S(1)}, u32[]{:S(2)}, u32[]{:S(2)}) collective-permute-start(f32[2176]{0:T(1024)S(1)} %pad_maximum_fusion.7), channel_id=1, source_target_pairs={{0,256},{32,288},{64,320},{96,352},{128,384},{160,416},{192,448},{... | collective-permute-start | bytes 26120 | tf_op jit(solution)/shard_map/ppermute | solution.py:108
  (139 shorter events, 61.7 us)
Async XLA Ops:
  3.1 21.8 %collective-permute-start = (bf16[1,32,1152]{2,1,0:T(8,128)(2,1)S(1)}, bf16[1,32,1152]{2,1,0:T(8,128)(2,1)S(1)}, u32[]{:S(2)}, u32[]{:S(2)}) collective-permute-start(bf16[1,32,1152]{2,1,0:T(8,128)(2,1)S(1)} %maximum_bitcast_fusion.1), channel_id=1, source_target_pairs={{0,4},{1,5},{2,6},{3,7},{4,0},{5,1},{6,2},{7,3},{8,12},{9,13},{10,... | collective-permute-start | bytes 221192 | tf_op jit(solution)/shard_map/ppermute | solution.py:70
  13.0 23.9 %collective-permute-start.8 = (bf16[1,32,2176]{2,1,0:T(8,128)(2,1)S(1)}, bf16[1,32,2176]{2,1,0:T(8,128)(2,1)S(1)}, u32[]{:S(2)}, u32[]{:S(2)}) collective-permute-start(bf16[1,32,2176]{2,1,0:T(8,128)(2,1)S(1)} %maximum_bitcast_fusion), channel_id=1, source_target_pairs={{0,256},{32,288},{64,320},{96,352},{128,384},{160,416},{192,448},{... | collective-permute-start | bytes 417800 | tf_op jit(solution)/shard_map/ppermute | solution.py:70
  24.9 32.7 %copy-start.5 = (s32[16]{0:T(128)S(1)}, s32[16]{0:T(128)}, u32[]{:S(2)}) copy-start(s32[16]{0:T(128)} %constant.128) | copy-start | bytes 196
  24.9 8.5 %collective-permute-start.1 = (bf16[2,32,1152]{2,1,0:T(8,128)(2,1)S(1)}, bf16[2,32,1152]{2,1,0:T(8,128)(2,1)S(1)}, u32[]{:S(2)}, u32[]{:S(2)}) collective-permute-start(bf16[2,32,1152]{2,1,0:T(8,128)(2,1)S(1)} %maximum_select_fusion.11), channel_id=1, source_target_pairs={{0,16},{1,17},{2,18},{3,19},{4,20},{5,21},{6,22},{7,23},{8,24},{9,... | collective-permute-start | bytes 442376 | tf_op jit(solution)/shard_map/ppermute | solution.py:70
  33.5 10.8 %collective-permute-start.2 = (bf16[4,16,1152]{2,1,0:T(8,128)(2,1)S(1)}, bf16[4,16,1152]{2,1,0:T(8,128)(2,1)S(1)}, u32[]{:S(2)}, u32[]{:S(2)}) collective-permute-start(bf16[4,16,1152]{2,1,0:T(8,128)(2,1)S(1)} %get-tuple-element.13), channel_id=1, source_target_pairs={{0,2},{1,3},{2,0},{3,1},{4,6},{5,7},{6,4},{7,5},{8,10},{9,11},{10,... | collective-permute-start | bytes 442376 | tf_op jit(solution)/shard_map/ppermute | solution.py:70
  37.0 17.4 %collective-permute-start.9 = (bf16[2,32,2176]{2,1,0:T(8,128)(2,1)S(1)}, bf16[2,32,2176]{2,1,0:T(8,128)(2,1)S(1)}, u32[]{:S(2)}, u32[]{:S(2)}) collective-permute-start(bf16[2,32,2176]{2,1,0:T(8,128)(2,1)S(1)} %maximum_select_fusion.10), channel_id=1, source_target_pairs={{0,64},{32,96},{64,0},{96,32},{128,192},{160,224},{192,128},{224,1... | collective-permute-start | bytes 835592 | tf_op jit(solution)/shard_map/ppermute | solution.py:70
  39.7 7.0 %collective-permute-start.5 = (bf16[4,16,1152]{2,1,0:T(8,128)(2,1)S(1)}, bf16[4,16,1152]{2,1,0:T(8,128)(2,1)S(1)}, u32[]{:S(2)}, u32[]{:S(2)}) collective-permute-start(bf16[4,16,1152]{2,1,0:T(8,128)(2,1)S(1)} %get-tuple-element.14), channel_id=1, source_target_pairs={{0,8},{1,9},{2,10},{3,11},{4,12},{5,13},{6,14},{7,15},{8,0},{9,1},... | collective-permute-start | bytes 442376 | tf_op jit(solution)/shard_map/ppermute | solution.py:70
  44.3 13.9 %collective-permute-start.3 = (bf16[8,16,1152]{2,1,0:T(8,128)(2,1)S(1)}, bf16[8,16,1152]{2,1,0:T(8,128)(2,1)S(1)}, u32[]{:S(2)}, u32[]{:S(2)}) collective-permute-start(bf16[8,16,1152]{2,1,0:T(8,128)(2,1)S(1)} %maximum_select_fusion.8), channel_id=1, source_target_pairs={{0,1},{1,0},{2,3},{3,2},{4,5},{5,4},{6,7},{7,6},{8,9},{9,8},{10,11... | collective-permute-start | bytes 884744 | tf_op jit(solution)/shard_map/ppermute | solution.py:70
  46.8 20.1 %collective-permute-start.6 = (bf16[8,16,1152]{2,1,0:T(8,128)(2,1)S(1)}, bf16[8,16,1152]{2,1,0:T(8,128)(2,1)S(1)}, u32[]{:S(2)}, u32[]{:S(2)}) collective-permute-start(bf16[8,16,1152]{2,1,0:T(8,128)(2,1)S(1)} %maximum_select_fusion.9), channel_id=1, source_target_pairs={{0,2},{1,3},{2,0},{3,1},{4,6},{5,7},{6,4},{7,5},{8,10},{9,11},{10,... | collective-permute-start | bytes 884744 | tf_op jit(solution)/shard_map/ppermute | solution.py:70
  54.5 16.6 %collective-permute-start.10 = (bf16[4,32,2176]{2,1,0:T(8,128)(2,1)S(1)}, bf16[4,32,2176]{2,1,0:T(8,128)(2,1)S(1)}, u32[]{:S(2)}, u32[]{:S(2)}) collective-permute-start(bf16[4,32,2176]{2,1,0:T(8,128)(2,1)S(1)} %maximum_select_fusion.6), channel_id=1, source_target_pairs={{0,128},{32,160},{64,192},{96,224},{128,0},{160,32},{192,64},{224,... | collective-permute-start | bytes 1671176 | tf_op jit(solution)/shard_map/ppermute | solution.py:70
  58.3 15.9 %collective-permute-start.4 = (bf16[16,16,1152]{2,1,0:T(8,128)(2,1)S(1)}, bf16[16,16,1152]{2,1,0:T(8,128)(2,1)S(1)}, u32[]{:S(2)}, u32[]{:S(2)}) collective-permute-start(bf16[16,16,1152]{2,1,0:T(8,128)(2,1)S(1)} %maximum_select_fusion.4), channel_id=1, source_target_pairs={{0,8},{1,9},{2,10},{3,11},{4,12},{5,13},{6,14},{7,15},{8,0},{9,1},... | collective-permute-start | bytes 1769480 | tf_op jit(solution)/shard_map/ppermute | solution.py:70
  67.0 15.9 %collective-permute-start.7 = (bf16[16,16,1152]{2,1,0:T(8,128)(2,1)S(1)}, bf16[16,16,1152]{2,1,0:T(8,128)(2,1)S(1)}, u32[]{:S(2)}, u32[]{:S(2)}) collective-permute-start(bf16[16,16,1152]{2,1,0:T(8,128)(2,1)S(1)} %maximum_select_fusion.5), channel_id=1, source_target_pairs={{0,1},{1,0},{2,3},{3,2},{4,5},{5,4},{6,7},{7,6},{8,9},{9,8},{10,11... | collective-permute-start | bytes 1769480 | tf_op jit(solution)/shard_map/ppermute | solution.py:70
  72.3 19.7 %collective-permute-start.11 = (bf16[8,32,2176]{2,1,0:T(8,128)(2,1)}, bf16[8,32,2176]{2,1,0:T(8,128)(2,1)}, u32[]{:S(2)}, u32[]{:S(2)}) collective-permute-start(bf16[8,32,2176]{2,1,0:T(8,128)(2,1)} %maximum_select_fusion.3), channel_id=1, source_target_pairs={{0,32},{32,0},{64,96},{96,64},{128,160},{160,128},{192,224},{224,1... | collective-permute-start | bytes 3342344 | tf_op jit(solution)/shard_map/ppermute | solution.py:70
  97.2 2.0 %copy-start.1 = (bf16[32,32,1152]{2,1,0:T(8,128)(2,1)S(1)}, bf16[32,32,1152]{2,1,0:T(8,128)(2,1)}, u32[]{:S(2)}) copy-start(bf16[32,32,1152]{2,1,0:T(8,128)(2,1)} %copy-done) | copy-start | bytes 7077892
  99.3 2.6 %copy-start.3 = (bf16[1024,511]{0,1:T(8,128)(2,1)S(1)}, bf16[1024,511]{0,1:T(8,128)(2,1)}, u32[]{:S(2)}) copy-start(bf16[1024,511]{0,1:T(8,128)(2,1)} %fusion.9) | copy-start | bytes 3139588
  118.5 3.1 %collective-permute-start.12 = (f32[3072]{0:T(1024)S(1)}, f32[3072]{0:T(1024)S(1)}, u32[]{:S(2)}, u32[]{:S(2)}) collective-permute-start(f32[3072]{0:T(1024)S(1)} %pad_maximum_fusion.4), channel_id=1, source_target_pairs={{0,32},{32,0},{64,96},{96,64},{128,160},{160,128},{192,224},{224,1... | collective-permute-start | bytes 36872 | tf_op jit(solution)/shard_map/ppermute | solution.py:108
  121.6 5.5 %collective-permute-start.13 = (f32[4,512]{1,0:T(4,128)S(1)}, f32[4,512]{1,0:T(4,128)S(1)}, u32[]{:S(2)}, u32[]{:S(2)}) collective-permute-start(f32[4,512]{1,0:T(4,128)S(1)} %fusion.47), channel_id=1, source_target_pairs={{0,1},{1,0},{2,3},{3,2},{4,5},{5,4},{6,7},{7,6},{8,9},{9,8},{10,11... | collective-permute-start | bytes 24584 | tf_op jit(solution)/shard_map/ppermute | solution.py:101
  127.1 6.9 %collective-permute-start.14 = (f32[4,512]{1,0:T(4,128)S(1)}, f32[4,512]{1,0:T(4,128)S(1)}, u32[]{:S(2)}, u32[]{:S(2)}) collective-permute-start(f32[4,512]{1,0:T(4,128)S(1)} %fusion.63), channel_id=1, source_target_pairs={{0,2},{1,3},{2,0},{3,1},{4,6},{5,7},{6,4},{7,5},{8,10},{9,11},{10,... | collective-permute-start | bytes 24584 | tf_op jit(solution)/shard_map/ppermute | solution.py:101
  134.1 9.4 %collective-permute-start.15 = (f32[4,512]{1,0:T(4,128)S(1)}, f32[4,512]{1,0:T(4,128)S(1)}, u32[]{:S(2)}, u32[]{:S(2)}) collective-permute-start(f32[4,512]{1,0:T(4,128)S(1)} %add.134), channel_id=1, source_target_pairs={{0,4},{1,5},{2,6},{3,7},{4,0},{5,1},{6,2},{7,3},{8,12},{9,13},{10,... | collective-permute-start | bytes 24584 | tf_op jit(solution)/shard_map/ppermute | solution.py:101
  143.5 5.6 %collective-permute-start.16 = (f32[2560]{0:T(1024)S(1)}, f32[2560]{0:T(1024)S(1)}, u32[]{:S(2)}, u32[]{:S(2)}) collective-permute-start(f32[2560]{0:T(1024)S(1)} %pad_maximum_fusion.5), channel_id=1, source_target_pairs={{0,64},{32,96},{64,0},{96,32},{128,192},{160,224},{192,128},{224,1... | collective-permute-start | bytes 30728 | tf_op jit(solution)/shard_map/ppermute | solution.py:108
  149.4 7.1 %collective-permute-start.17 = (f32[2304]{0:T(1024)S(1)}, f32[2304]{0:T(1024)S(1)}, u32[]{:S(2)}, u32[]{:S(2)}) collective-permute-start(f32[2304]{0:T(1024)S(1)} %pad_maximum_fusion.6), channel_id=1, source_target_pairs={{0,128},{32,160},{64,192},{96,224},{128,0},{160,32},{192,64},{224,... | collective-permute-start | bytes 27656 | tf_op jit(solution)/shard_map/ppermute | solution.py:108
  156.5 5.5 %collective-permute-start.18 = (f32[4,512]{1,0:T(4,128)S(1)}, f32[4,512]{1,0:T(4,128)S(1)}, u32[]{:S(2)}, u32[]{:S(2)}) collective-permute-start(f32[4,512]{1,0:T(4,128)S(1)} %add.143), channel_id=1, source_target_pairs={{0,8},{1,9},{2,10},{3,11},{4,12},{5,13},{6,14},{7,15},{8,0},{9,1},... | collective-permute-start | bytes 24584 | tf_op jit(solution)/shard_map/ppermute | solution.py:101
  162.0 7.0 %collective-permute-start.19 = (f32[4,512]{1,0:T(4,128)S(1)}, f32[4,512]{1,0:T(4,128)S(1)}, u32[]{:S(2)}, u32[]{:S(2)}) collective-permute-start(f32[4,512]{1,0:T(4,128)S(1)} %add.144), channel_id=1, source_target_pairs={{0,16},{1,17},{2,18},{3,19},{4,20},{5,21},{6,22},{7,23},{8,24},{9,... | collective-permute-start | bytes 24584 | tf_op jit(solution)/shard_map/ppermute | solution.py:101
  169.1 14.3 %collective-permute-start.20 = (f32[2176]{0:T(1024)S(1)}, f32[2176]{0:T(1024)S(1)}, u32[]{:S(2)}, u32[]{:S(2)}) collective-permute-start(f32[2176]{0:T(1024)S(1)} %pad_maximum_fusion.7), channel_id=1, source_target_pairs={{0,256},{32,288},{64,320},{96,352},{128,384},{160,416},{192,448},{... | collective-permute-start | bytes 26120 | tf_op jit(solution)/shard_map/ppermute | solution.py:108
  (3 other events, 4.5 us)

commit v9 on v8

--- a/solution.py
+++ b/solution.py
@@ -44,13 +44,27 @@
     return left_sq[:, None] + right_sq[None, :] - 2.0 * cross
 
 
-def pack_meta(set_labels, sign_words):
+def split3(x):
+    hi = lax.reduce_precision(x, exponent_bits=8, mantissa_bits=7)
+    rest = x - hi
+    mid = lax.reduce_precision(rest, exponent_bits=8, mantissa_bits=7)
+    lo = rest - mid
+    return jnp.stack([hi, mid, lo], axis=1).astype(jnp.bfloat16)
+
+
+def join3(parts):
+    wide = parts.astype(jnp.float32)
+    return (wide[:, 0] + wide[:, 1]) + wide[:, 2]
+
+
+def pack_meta(set_labels, sign_words, samples, corpus):
     words = sign_words.shape[1]
     chunks = [(sign_words >> (CHUNK * c)) & ((1 << CHUNK) - 1) for c in range(3)]
-    meta = jnp.concatenate([set_labels[:, None]] + chunks, axis=1)
+    meta = jnp.concatenate([set_labels[:, None]] + chunks, axis=1).astype(jnp.bfloat16)
+    meta = jnp.concatenate([meta, split3(squares(samples)), split3(squares(corpus))], axis=1)
     pad = META - meta.shape[1]
     meta = jnp.pad(meta, ((0, 0), (0, pad)))
-    return meta.astype(jnp.bfloat16), words
+    return meta, words
 
 
 def unpack(buf, words):
@@ -59,7 +73,8 @@
     labels = meta[:, 0]
     c = [meta[:, 1 + k * words:1 + (k + 1) * words] for k in range(3)]
     sign_words = c[0] + (c[1] << CHUNK) + (c[2] << (2 * CHUNK))
-    return rows, make_vectors(labels, sign_words)
+    at = D + 1 + 3 * words
+    return rows, make_vectors(labels, sign_words), join3(buf[:, at:at + 3]), join3(buf[:, at + 3:at + 6])
 
 
 def xor_gather(x, axis, n, bits, buf=None):
@@ -77,7 +92,7 @@
 GRP_ORDER = (3, 1, 2, 0)
 DEV_JOINT = (2, 4)
 DEV_ORDERS = ((1, 0, 3), (3, 1, 0))
-SUM_ORDER = (("grp", 0), ("dev", 0), ("dev", 1), ("dev", 2), ("grp", 1), ("grp", 2), ("dev", 3), ("dev", 4), ("grp", 3))
+SUM_ORDER = (("dev", 0), ("dev", 1), ("dev", 2), ("dev", 3), ("dev", 4), ("grp", 0), ("grp", 1), ("grp", 2), ("grp", 3))
 
 
 def axis_order(n, preferred):
@@ -119,7 +134,7 @@
     total = rows_here * n_grp * n_dev
     inv_root = jnp.float32(1.0) / jnp.sqrt(jnp.float32(total))
 
-    meta, words = pack_meta(set_labels, sign_words)
+    meta, words = pack_meta(set_labels, sign_words, samples, corpus)
     own = jnp.concatenate([samples, meta], axis=1)
     own_wide = jnp.concatenate([own, corpus], axis=1)
 
@@ -138,12 +153,10 @@
 
     col_buf = col_buf.reshape(n_grp * rows_here, -1)
     blk_buf = blk_buf.reshape(n_dev * rows_here, -1)
-    col_rows, col_vec = unpack(col_buf[:, :D + META], words)
+    col_rows, col_vec, col_sq, corpus_sq = unpack(col_buf[:, :D + META], words)
     col_corpus = col_buf[:, D + META:]
-    block_rows, block_vec = unpack(blk_buf, words)
-
-    col_sq = squares(col_rows)
-    block_sq = squares(block_rows)
+    block_rows, block_vec, block_sq, _ = unpack(blk_buf, words)
+
 
     dist = distances(block_rows, block_sq, col_rows, col_sq)
     block_wide = block_vec.astype(jnp.float32)
@@ -154,7 +167,7 @@
         forms.append(jnp.sum(block_wide * product, axis=0))
     forms_part = jnp.stack(forms)
 
-    cdist = distances(col_corpus, squares(col_corpus), block_rows, block_sq)
+    cdist = distances(col_corpus, corpus_sq, block_rows, block_sq)
     weights = block_vec[:, 0]
     proofs = []
     for kernel_id in range(NB):

time: 187 us -> 193 us (1.032)
  waiting for transfers between devices: 43.7 us -> 66.2 us
  starting transfers between devices: 95.3 us -> 79.8 us
    ppermute x12, waiting for transfers between devices: 19.1 us -> 35.3 us  [xor_gather(): other = lax.ppermute(buf, axis, [(i, i ^ k) for i in range(n)])]
    ppermute x4, waiting for transfers between devices: 10.4 us -> 17.9 us  [xor_sum(): got = lax.ppermute(jnp.concatenate([x.ravel(), send.ravel()]), a, pairs)]
    ppermute x4, starting transfers between devices: 19.6 us -> 12.2 us  [xor_sum(): got = lax.ppermute(jnp.concatenate([x.ravel(), send.ravel()]), a, pairs)]
    ppermute x12, starting transfers between devices: 55.9 us -> 49.8 us  [xor_gather(): other = lax.ppermute(buf, axis, [(i, i ^ k) for i in range(n)])]
    shift_right_arithmetic x6, local copies, waits for them, and re-layouts: 4.85 us -> 2.31 us  [make_vectors(): jnp.right_shift(sign_words[:, :, None], shifts[None, None, :]) & 1]
    ppermute x5, starting transfers between devices: 19.8 us -> 17.8 us  [xor_sum(): x = x + lax.ppermute(x, a, pairs)]
    another operation x4 -> x7, other arithmetic: 4.09 us -> 2.6 us
  transfers between devices with their start and end apart: 21 -> 21, of which waited for: 16 -> 18; matrix products, arithmetic and copies ran while one was open for 7% -> 7% of each run, Pallas kernels for 0% -> 0%
where the time goes in v9:
time: 193 us; the launch traced here: 192 us
  starting transfers between devices  79.8 us (41%)
  waiting for transfers between devices  66.2 us (34%)
  matrix products  18.3 us (9%)
  other arithmetic  17 us (9%)
  local copies, waits for them, and re-layouts  9.25 us (5%)
    ppermute x12, starting transfers between devices, xor_gather(): other = lax.ppermute(buf, axis, [(i, i ^ k) for i in range(n)])  49.8 us
    ppermute x12, waiting for transfers between devices, xor_gather(): other = lax.ppermute(buf, axis, [(i, i ^ k) for i in range(n)])  35.3 us
    ppermute x4, waiting for transfers between devices, xor_sum(): got = lax.ppermute(jnp.concatenate([x.ravel(), send.ravel()]), a, pairs)  17.9 us
    ppermute x5, starting transfers between devices, xor_sum(): x = x + lax.ppermute(x, a, pairs)  17.8 us
    ppermute x5, waiting for transfers between devices, xor_sum(): x = x + lax.ppermute(x, a, pairs)  13 us
    ppermute x4, starting transfers between devices, xor_sum(): got = lax.ppermute(jnp.concatenate([x.ravel(), send.ravel()]), a, pairs)  12.2 us
    dot_general x2, matrix products, distances(): lax.dot_general(left, right, (((1,), (1,)), ((), ())), preferred_element_...  8.7 us
    dot_general x4, matrix products, per_device(): product = jnp.dot(kern, col_vec, preferred_element_type=jnp.float32)  6.49 us
  transfers between devices with their start and end apart: 21, of which 18 were waited for; matrix products, arithmetic and copies ran while one was open for 7% of the time, Pallas kernels for 0%

profile of v9, /device:TPU:6, one launch (start us, length us, event | category | flops | bytes accessed | tf_op | source)
XLA Modules:
  0.0 191.8 jit_solution(3105546278893902215)
XLA Ops:
  5.7 15.7 %collective-permute-start.8 = (bf16[1,32,2176]{2,1,0:T(8,128)(2,1)S(1)}, bf16[1,32,2176]{2,1,0:T(8,128)(2,1)S(1)}, u32[]{:S(2)}, u32[]{:S(2)}) collective-permute-start(bf16[1,32,2176]{2,1,0:T(8,128)(2,1)S(1)} %maximum_bitcast_fusion), channel_id=1, source_target_pairs={{0,256},{32,288},{64,320},{96,352},{128,384},{160,416},{192,448},{... | collective-permute-start | bytes 417800 | tf_op jit(solution)/shard_map/ppermute | solution.py:85
  22.3 4.3 %collective-permute-start = (bf16[1,32,1152]{2,1,0:T(8,128)(2,1)S(1)}, bf16[1,32,1152]{2,1,0:T(8,128)(2,1)S(1)}, u32[]{:S(2)}, u32[]{:S(2)}) collective-permute-start(bf16[1,32,1152]{2,1,0:T(8,128)(2,1)S(1)} %maximum_bitcast_fusion.1), channel_id=1, source_target_pairs={{0,4},{1,5},{2,6},{3,7},{4,0},{5,1},{6,2},{7,3},{8,12},{9,13},{10,... | collective-permute-start | bytes 221192 | tf_op jit(solution)/shard_map/ppermute | solution.py:85
  27.4 13.4 %collective-permute-done = bf16[1,32,1152]{2,1,0:T(8,128)(2,1)S(1)} collective-permute-done((bf16[1,32,1152]{2,1,0:T(8,128)(2,1)S(1)}, bf16[1,32,1152]{2,1,0:T(8,128)(2,1)S(1)}, u32[]{:S(2)}, u32[]{:S(2)}) %collective-permute-start) | collective-permute-done | bytes 73760 | tf_op jit(solution)/shard_map/ppermute | solution.py:85
  40.9 5.1 %collective-permute-start.1 = (bf16[2,32,1152]{2,1,0:T(8,128)(2,1)S(1)}, bf16[2,32,1152]{2,1,0:T(8,128)(2,1)S(1)}, u32[]{:S(2)}, u32[]{:S(2)}) collective-permute-start(bf16[2,32,1152]{2,1,0:T(8,128)(2,1)S(1)} %maximum_select_fusion.11), channel_id=1, source_target_pairs={{0,16},{1,17},{2,18},{3,19},{4,20},{5,21},{6,22},{7,23},{8,24},{9,... | collective-permute-start | bytes 442376 | tf_op jit(solution)/shard_map/ppermute | solution.py:85
  46.7 3.4 %collective-permute-done.1 = bf16[2,32,1152]{2,1,0:T(8,128)(2,1)S(1)} collective-permute-done((bf16[2,32,1152]{2,1,0:T(8,128)(2,1)S(1)}, bf16[2,32,1152]{2,1,0:T(8,128)(2,1)S(1)}, u32[]{:S(2)}, u32[]{:S(2)}) %collective-permute-start.1) | collective-permute-done | bytes 147488 | tf_op jit(solution)/shard_map/ppermute | solution.py:85
  54.9 3.5 %collective-permute-start.5 = (bf16[4,16,1152]{2,1,0:T(8,128)(2,1)S(1)}, bf16[4,16,1152]{2,1,0:T(8,128)(2,1)S(1)}, u32[]{:S(2)}, u32[]{:S(2)}) collective-permute-start(bf16[4,16,1152]{2,1,0:T(8,128)(2,1)S(1)} %get-tuple-element.14), channel_id=1, source_target_pairs={{0,8},{1,9},{2,10},{3,11},{4,12},{5,13},{6,14},{7,15},{8,0},{9,1},... | collective-permute-start | bytes 442376 | tf_op jit(solution)/shard_map/ppermute | solution.py:85
  62.0 4.8 %collective-permute-start.6 = (bf16[8,16,1152]{2,1,0:T(8,128)(2,1)S(1)}, bf16[8,16,1152]{2,1,0:T(8,128)(2,1)S(1)}, u32[]{:S(2)}, u32[]{:S(2)}) collective-permute-start(bf16[8,16,1152]{2,1,0:T(8,128)(2,1)S(1)} %maximum_select_fusion.9), channel_id=1, source_target_pairs={{0,2},{1,3},{2,0},{3,1},{4,6},{5,7},{6,4},{7,5},{8,10},{9,11},{10,... | collective-permute-start | bytes 884744 | tf_op jit(solution)/shard_map/ppermute | solution.py:85
  66.9 3.0 %collective-permute-start.10 = (bf16[4,32,2176]{2,1,0:T(8,128)(2,1)S(1)}, bf16[4,32,2176]{2,1,0:T(8,128)(2,1)S(1)}, u32[]{:S(2)}, u32[]{:S(2)}) collective-permute-start(bf16[4,32,2176]{2,1,0:T(8,128)(2,1)S(1)} %maximum_select_fusion.6), channel_id=1, source_target_pairs={{0,128},{32,160},{64,192},{96,224},{128,0},{160,32},{192,64},{224,... | collective-permute-start | bytes 1671176 | tf_op jit(solution)/shard_map/ppermute | solution.py:85
  70.1 3.3 %collective-permute-done.3 = bf16[8,16,1152]{2,1,0:T(8,128)(2,1)S(1)} collective-permute-done((bf16[8,16,1152]{2,1,0:T(8,128)(2,1)S(1)}, bf16[8,16,1152]{2,1,0:T(8,128)(2,1)S(1)}, u32[]{:S(2)}, u32[]{:S(2)}) %collective-permute-start.3) | collective-permute-done | bytes 294944 | tf_op jit(solution)/shard_map/ppermute | solution.py:85
  73.5 2.8 %collective-permute-start.4 = (bf16[16,16,1152]{2,1,0:T(8,128)(2,1)S(1)}, bf16[16,16,1152]{2,1,0:T(8,128)(2,1)S(1)}, u32[]{:S(2)}, u32[]{:S(2)}) collective-permute-start(bf16[16,16,1152]{2,1,0:T(8,128)(2,1)S(1)} %maximum_select_fusion.4), channel_id=1, source_target_pairs={{0,8},{1,9},{2,10},{3,11},{4,12},{5,13},{6,14},{7,15},{8,0},{9,1},... | collective-permute-start | bytes 1769480 | tf_op jit(solution)/shard_map/ppermute | solution.py:85
  76.3 3.1 %collective-permute-done.6 = bf16[8,16,1152]{2,1,0:T(8,128)(2,1)S(1)} collective-permute-done((bf16[8,16,1152]{2,1,0:T(8,128)(2,1)S(1)}, bf16[8,16,1152]{2,1,0:T(8,128)(2,1)S(1)}, u32[]{:S(2)}, u32[]{:S(2)}) %collective-permute-start.6) | collective-permute-done | bytes 294944 | tf_op jit(solution)/shard_map/ppermute | solution.py:85
  85.6 4.0 %collective-permute-done.4 = bf16[16,16,1152]{2,1,0:T(8,128)(2,1)S(1)} collective-permute-done((bf16[16,16,1152]{2,1,0:T(8,128)(2,1)S(1)}, bf16[16,16,1152]{2,1,0:T(8,128)(2,1)S(1)}, u32[]{:S(2)}, u32[]{:S(2)}) %collective-permute-start.4) | collective-permute-done | bytes 589856 | tf_op jit(solution)/shard_map/ppermute | solution.py:85
  89.8 5.6 %collective-permute-done.7 = bf16[16,16,1152]{2,1,0:T(8,128)(2,1)S(1)} collective-permute-done((bf16[16,16,1152]{2,1,0:T(8,128)(2,1)S(1)}, bf16[16,16,1152]{2,1,0:T(8,128)(2,1)S(1)}, u32[]{:S(2)}, u32[]{:S(2)}) %collective-permute-start.7) | collective-permute-done | bytes 589856 | tf_op jit(solution)/shard_map/ppermute | solution.py:85
  118.2 6.1 %exponential_convert_fusion.3 = (bf16[512,1024]{1,0:T(8,128)(2,1)S(1)}, bf16[512,1024]{1,0:T(8,128)(2,1)S(1)}, bf16[512,1024]{1,0:T(8,128)(2,1)S(1)}, bf16[512,1024]{1,0:T(8,128)(2,1)S(1)}) fusion(f32[]{:T(128)} %bitcast.8, f32[]{:T(128)} %bitcast.15, f32[]{:T(128)} %bitcast.13, f32[]{:T(128)} %bitcast.11, bf16[1024,1152]{1,0:T(8,128)(2,1)S(1)} %bitcast.78, ...), kind=kOutput, calls=%fused_computation.21 | convolution fusion | flops 1080033280 | bytes 7348224 | tf_op jit(solution)/shard_map/dot_general | solution.py:41
  133.4 3.7 %collective-permute-done.13 = f32[4,512]{1,0:T(4,128)S(1)} collective-permute-done((f32[4,512]{1,0:T(4,128)S(1)}, f32[4,512]{1,0:T(4,128)S(1)}, u32[]{:S(2)}, u32[]{:S(2)}) %collective-permute-start.13) | collective-permute-done | bytes 8224 | tf_op jit(solution)/shard_map/ppermute | solution.py:116
  137.1 5.1 %collective-permute-start.14 = (f32[4,512]{1,0:T(4,128)S(1)}, f32[4,512]{1,0:T(4,128)S(1)}, u32[]{:S(2)}, u32[]{:S(2)}) collective-permute-start(f32[4,512]{1,0:T(4,128)S(1)} %fusion.66), channel_id=1, source_target_pairs={{0,4},{1,5},{2,6},{3,7},{4,0},{5,1},{6,2},{7,3},{8,12},{9,13},{10,... | collective-permute-start | bytes 24584 | tf_op jit(solution)/shard_map/ppermute | solution.py:116
  143.0 3.5 %collective-permute-done.14 = f32[4,512]{1,0:T(4,128)S(1)} collective-permute-done((f32[4,512]{1,0:T(4,128)S(1)}, f32[4,512]{1,0:T(4,128)S(1)}, u32[]{:S(2)}, u32[]{:S(2)}) %collective-permute-start.14) | collective-permute-done | bytes 8224 | tf_op jit(solution)/shard_map/ppermute | solution.py:116
  146.6 3.5 %collective-permute-start.15 = (f32[4,512]{1,0:T(4,128)S(1)}, f32[4,512]{1,0:T(4,128)S(1)}, u32[]{:S(2)}, u32[]{:S(2)}) collective-permute-start(f32[4,512]{1,0:T(4,128)S(1)} %add.183), channel_id=1, source_target_pairs={{0,8},{1,9},{2,10},{3,11},{4,12},{5,13},{6,14},{7,15},{8,0},{9,1},... | collective-permute-start | bytes 24584 | tf_op jit(solution)/shard_map/ppermute | solution.py:116
  152.1 5.1 %collective-permute-start.16 = (f32[4,512]{1,0:T(4,128)S(1)}, f32[4,512]{1,0:T(4,128)S(1)}, u32[]{:S(2)}, u32[]{:S(2)}) collective-permute-start(f32[4,512]{1,0:T(4,128)S(1)} %add.184), channel_id=1, source_target_pairs={{0,16},{1,17},{2,18},{3,19},{4,20},{5,21},{6,22},{7,23},{8,24},{9,... | collective-permute-start | bytes 24584 | tf_op jit(solution)/shard_map/ppermute | solution.py:116
  165.1 3.0 %collective-permute-done.18 = f32[2560]{0:T(1024)S(1)} collective-permute-done((f32[2560]{0:T(1024)S(1)}, f32[2560]{0:T(1024)S(1)}, u32[]{:S(2)}, u32[]{:S(2)}) %collective-permute-start.18) | collective-permute-done | bytes 10272 | tf_op jit(solution)/shard_map/ppermute | solution.py:123
  168.4 3.5 %collective-permute-start.19 = (f32[2304]{0:T(1024)S(1)}, f32[2304]{0:T(1024)S(1)}, u32[]{:S(2)}, u32[]{:S(2)}) collective-permute-start(f32[2304]{0:T(1024)S(1)} %pad_maximum_fusion.6), channel_id=1, source_target_pairs={{0,128},{32,160},{64,192},{96,224},{128,0},{160,32},{192,64},{224,... | collective-permute-start | bytes 27656 | tf_op jit(solution)/shard_map/ppermute | solution.py:123
  171.9 3.6 %collective-permute-done.19 = f32[2304]{0:T(1024)S(1)} collective-permute-done((f32[2304]{0:T(1024)S(1)}, f32[2304]{0:T(1024)S(1)}, u32[]{:S(2)}, u32[]{:S(2)}) %collective-permute-start.19) | collective-permute-done | bytes 9248 | tf_op jit(solution)/shard_map/ppermute | solution.py:123
  175.7 4.2 %collective-permute-start.20 = (f32[2176]{0:T(1024)S(1)}, f32[2176]{0:T(1024)S(1)}, u32[]{:S(2)}, u32[]{:S(2)}) collective-permute-start(f32[2176]{0:T(1024)S(1)} %pad_maximum_fusion.7), channel_id=1, source_target_pairs={{0,256},{32,288},{64,320},{96,352},{128,384},{160,416},{192,448},{... | collective-permute-start | bytes 26120 | tf_op jit(solution)/shard_map/ppermute | solution.py:123
  180.0 10.1 %collective-permute-done.20 = f32[2176]{0:T(1024)S(1)} collective-permute-done((f32[2176]{0:T(1024)S(1)}, f32[2176]{0:T(1024)S(1)}, u32[]{:S(2)}, u32[]{:S(2)}) %collective-permute-start.20) | collective-permute-done | bytes 8736 | tf_op jit(solution)/shard_map/ppermute | solution.py:123
  (154 shorter events, 67.0 us)
Async XLA Ops:
  5.7 46.4 %collective-permute-start.8 = (bf16[1,32,2176]{2,1,0:T(8,128)(2,1)S(1)}, bf16[1,32,2176]{2,1,0:T(8,128)(2,1)S(1)}, u32[]{:S(2)}, u32[]{:S(2)}) collective-permute-start(bf16[1,32,2176]{2,1,0:T(8,128)(2,1)S(1)} %maximum_bitcast_fusion), channel_id=1, source_target_pairs={{0,256},{32,288},{64,320},{96,352},{128,384},{160,416},{192,448},{... | collective-permute-start | bytes 417800 | tf_op jit(solution)/shard_map/ppermute | solution.py:85
  22.3 18.6 %collective-permute-start = (bf16[1,32,1152]{2,1,0:T(8,128)(2,1)S(1)}, bf16[1,32,1152]{2,1,0:T(8,128)(2,1)S(1)}, u32[]{:S(2)}, u32[]{:S(2)}) collective-permute-start(bf16[1,32,1152]{2,1,0:T(8,128)(2,1)S(1)} %maximum_bitcast_fusion.1), channel_id=1, source_target_pairs={{0,4},{1,5},{2,6},{3,7},{4,0},{5,1},{6,2},{7,3},{8,12},{9,13},{10,... | collective-permute-start | bytes 221192 | tf_op jit(solution)/shard_map/ppermute | solution.py:85
  40.9 29.1 %copy-start.6 = (s32[16]{0:T(128)S(1)}, s32[16]{0:T(128)}, u32[]{:S(2)}) copy-start(s32[16]{0:T(128)} %constant.128) | copy-start | bytes 196
  40.9 9.2 %collective-permute-start.1 = (bf16[2,32,1152]{2,1,0:T(8,128)(2,1)S(1)}, bf16[2,32,1152]{2,1,0:T(8,128)(2,1)S(1)}, u32[]{:S(2)}, u32[]{:S(2)}) collective-permute-start(bf16[2,32,1152]{2,1,0:T(8,128)(2,1)S(1)} %maximum_select_fusion.11), channel_id=1, source_target_pairs={{0,16},{1,17},{2,18},{3,19},{4,20},{5,21},{6,22},{7,23},{8,24},{9,... | collective-permute-start | bytes 442376 | tf_op jit(solution)/shard_map/ppermute | solution.py:85
  50.2 9.3 %collective-permute-start.2 = (bf16[4,16,1152]{2,1,0:T(8,128)(2,1)S(1)}, bf16[4,16,1152]{2,1,0:T(8,128)(2,1)S(1)}, u32[]{:S(2)}, u32[]{:S(2)}) collective-permute-start(bf16[4,16,1152]{2,1,0:T(8,128)(2,1)S(1)} %get-tuple-element.13), channel_id=1, source_target_pairs={{0,2},{1,3},{2,0},{3,1},{4,6},{5,7},{6,4},{7,5},{8,10},{9,11},{10,... | collective-permute-start | bytes 442376 | tf_op jit(solution)/shard_map/ppermute | solution.py:85
  52.1 14.7 %collective-permute-start.9 = (bf16[2,32,2176]{2,1,0:T(8,128)(2,1)S(1)}, bf16[2,32,2176]{2,1,0:T(8,128)(2,1)S(1)}, u32[]{:S(2)}, u32[]{:S(2)}) collective-permute-start(bf16[2,32,2176]{2,1,0:T(8,128)(2,1)S(1)} %maximum_select_fusion.10), channel_id=1, source_target_pairs={{0,64},{32,96},{64,0},{96,32},{128,192},{160,224},{192,128},{224,1... | collective-permute-start | bytes 835592 | tf_op jit(solution)/shard_map/ppermute | solution.py:85
  54.9 7.0 %collective-permute-start.5 = (bf16[4,16,1152]{2,1,0:T(8,128)(2,1)S(1)}, bf16[4,16,1152]{2,1,0:T(8,128)(2,1)S(1)}, u32[]{:S(2)}, u32[]{:S(2)}) collective-permute-start(bf16[4,16,1152]{2,1,0:T(8,128)(2,1)S(1)} %get-tuple-element.14), channel_id=1, source_target_pairs={{0,8},{1,9},{2,10},{3,11},{4,12},{5,13},{6,14},{7,15},{8,0},{9,1},... | collective-permute-start | bytes 442376 | tf_op jit(solution)/shard_map/ppermute | solution.py:85
  59.5 13.9 %collective-permute-start.3 = (bf16[8,16,1152]{2,1,0:T(8,128)(2,1)S(1)}, bf16[8,16,1152]{2,1,0:T(8,128)(2,1)S(1)}, u32[]{:S(2)}, u32[]{:S(2)}) collective-permute-start(bf16[8,16,1152]{2,1,0:T(8,128)(2,1)S(1)} %maximum_select_fusion.8), channel_id=1, source_target_pairs={{0,1},{1,0},{2,3},{3,2},{4,5},{5,4},{6,7},{7,6},{8,9},{9,8},{10,11... | collective-permute-start | bytes 884744 | tf_op jit(solution)/shard_map/ppermute | solution.py:85
  62.0 17.4 %collective-permute-start.6 = (bf16[8,16,1152]{2,1,0:T(8,128)(2,1)S(1)}, bf16[8,16,1152]{2,1,0:T(8,128)(2,1)S(1)}, u32[]{:S(2)}, u32[]{:S(2)}) collective-permute-start(bf16[8,16,1152]{2,1,0:T(8,128)(2,1)S(1)} %maximum_select_fusion.9), channel_id=1, source_target_pairs={{0,2},{1,3},{2,0},{3,1},{4,6},{5,7},{6,4},{7,5},{8,10},{9,11},{10,... | collective-permute-start | bytes 884744 | tf_op jit(solution)/shard_map/ppermute | solution.py:85
  66.9 15.4 %collective-permute-start.10 = (bf16[4,32,2176]{2,1,0:T(8,128)(2,1)S(1)}, bf16[4,32,2176]{2,1,0:T(8,128)(2,1)S(1)}, u32[]{:S(2)}, u32[]{:S(2)}) collective-permute-start(bf16[4,32,2176]{2,1,0:T(8,128)(2,1)S(1)} %maximum_select_fusion.6), channel_id=1, source_target_pairs={{0,128},{32,160},{64,192},{96,224},{128,0},{160,32},{192,64},{224,... | collective-permute-start | bytes 1671176 | tf_op jit(solution)/shard_map/ppermute | solution.py:85
  73.5 16.1 %collective-permute-start.4 = (bf16[16,16,1152]{2,1,0:T(8,128)(2,1)S(1)}, bf16[16,16,1152]{2,1,0:T(8,128)(2,1)S(1)}, u32[]{:S(2)}, u32[]{:S(2)}) collective-permute-start(bf16[16,16,1152]{2,1,0:T(8,128)(2,1)S(1)} %maximum_select_fusion.4), channel_id=1, source_target_pairs={{0,8},{1,9},{2,10},{3,11},{4,12},{5,13},{6,14},{7,15},{8,0},{9,1},... | collective-permute-start | bytes 1769480 | tf_op jit(solution)/shard_map/ppermute | solution.py:85
  79.5 15.9 %collective-permute-start.7 = (bf16[16,16,1152]{2,1,0:T(8,128)(2,1)S(1)}, bf16[16,16,1152]{2,1,0:T(8,128)(2,1)S(1)}, u32[]{:S(2)}, u32[]{:S(2)}) collective-permute-start(bf16[16,16,1152]{2,1,0:T(8,128)(2,1)S(1)} %maximum_select_fusion.5), channel_id=1, source_target_pairs={{0,1},{1,0},{2,3},{3,2},{4,5},{5,4},{6,7},{7,6},{8,9},{9,8},{10,11... | collective-permute-start | bytes 1769480 | tf_op jit(solution)/shard_map/ppermute | solution.py:85
  83.5 19.3 %collective-permute-start.11 = (bf16[8,32,2176]{2,1,0:T(8,128)(2,1)}, bf16[8,32,2176]{2,1,0:T(8,128)(2,1)}, u32[]{:S(2)}, u32[]{:S(2)}) collective-permute-start(bf16[8,32,2176]{2,1,0:T(8,128)(2,1)} %maximum_select_fusion.3), channel_id=1, source_target_pairs={{0,32},{32,0},{64,96},{96,64},{128,160},{160,128},{192,224},{224,1... | collective-permute-start | bytes 3342344 | tf_op jit(solution)/shard_map/ppermute | solution.py:85
  99.5 1.8 copy-start
  109.1 2.6 %copy-start.4 = (bf16[1024,511]{0,1:T(8,128)(2,1)S(1)}, bf16[1024,511]{0,1:T(8,128)(2,1)}, u32[]{:S(2)}) copy-start(bf16[1024,511]{0,1:T(8,128)(2,1)} %fusion.9) | copy-start | bytes 3139588
  125.1 5.5 %collective-permute-start.12 = (f32[4,512]{1,0:T(4,128)S(1)}, f32[4,512]{1,0:T(4,128)S(1)}, u32[]{:S(2)}, u32[]{:S(2)}) collective-permute-start(f32[4,512]{1,0:T(4,128)S(1)} %pad_maximum_fusion.8), channel_id=1, source_target_pairs={{0,1},{1,0},{2,3},{3,2},{4,5},{5,4},{6,7},{7,6},{8,9},{9,8},{10,11... | collective-permute-start | bytes 24584 | tf_op jit(solution)/shard_map/ppermute | solution.py:116
  130.6 6.4 %collective-permute-start.13 = (f32[4,512]{1,0:T(4,128)S(1)}, f32[4,512]{1,0:T(4,128)S(1)}, u32[]{:S(2)}, u32[]{:S(2)}) collective-permute-start(f32[4,512]{1,0:T(4,128)S(1)} %fusion.55), channel_id=1, source_target_pairs={{0,2},{1,3},{2,0},{3,1},{4,6},{5,7},{6,4},{7,5},{8,10},{9,11},{10,... | collective-permute-start | bytes 24584 | tf_op jit(solution)/shard_map/ppermute | solution.py:116
  137.1 9.5 %collective-permute-start.14 = (f32[4,512]{1,0:T(4,128)S(1)}, f32[4,512]{1,0:T(4,128)S(1)}, u32[]{:S(2)}, u32[]{:S(2)}) collective-permute-start(f32[4,512]{1,0:T(4,128)S(1)} %fusion.66), channel_id=1, source_target_pairs={{0,4},{1,5},{2,6},{3,7},{4,0},{5,1},{6,2},{7,3},{8,12},{9,13},{10,... | collective-permute-start | bytes 24584 | tf_op jit(solution)/shard_map/ppermute | solution.py:116
  146.6 5.5 %collective-permute-start.15 = (f32[4,512]{1,0:T(4,128)S(1)}, f32[4,512]{1,0:T(4,128)S(1)}, u32[]{:S(2)}, u32[]{:S(2)}) collective-permute-start(f32[4,512]{1,0:T(4,128)S(1)} %add.183), channel_id=1, source_target_pairs={{0,8},{1,9},{2,10},{3,11},{4,12},{5,13},{6,14},{7,15},{8,0},{9,1},... | collective-permute-start | bytes 24584 | tf_op jit(solution)/shard_map/ppermute | solution.py:116
  152.1 7.0 %collective-permute-start.16 = (f32[4,512]{1,0:T(4,128)S(1)}, f32[4,512]{1,0:T(4,128)S(1)}, u32[]{:S(2)}, u32[]{:S(2)}) collective-permute-start(f32[4,512]{1,0:T(4,128)S(1)} %add.184), channel_id=1, source_target_pairs={{0,16},{1,17},{2,18},{3,19},{4,20},{5,21},{6,22},{7,23},{8,24},{9,... | collective-permute-start | bytes 24584 | tf_op jit(solution)/shard_map/ppermute | solution.py:116
  159.2 3.1 %collective-permute-start.17 = (f32[3072]{0:T(1024)S(1)}, f32[3072]{0:T(1024)S(1)}, u32[]{:S(2)}, u32[]{:S(2)}) collective-permute-start(f32[3072]{0:T(1024)S(1)} %pad_maximum_fusion.4), channel_id=1, source_target_pairs={{0,32},{32,0},{64,96},{96,64},{128,160},{160,128},{192,224},{224,1... | collective-permute-start | bytes 36872 | tf_op jit(solution)/shard_map/ppermute | solution.py:123
  162.5 5.6 %collective-permute-start.18 = (f32[2560]{0:T(1024)S(1)}, f32[2560]{0:T(1024)S(1)}, u32[]{:S(2)}, u32[]{:S(2)}) collective-permute-start(f32[2560]{0:T(1024)S(1)} %pad_maximum_fusion.5), channel_id=1, source_target_pairs={{0,64},{32,96},{64,0},{96,32},{128,192},{160,224},{192,128},{224,1... | collective-permute-start | bytes 30728 | tf_op jit(solution)/shard_map/ppermute | solution.py:123
  168.4 7.1 %collective-permute-start.19 = (f32[2304]{0:T(1024)S(1)}, f32[2304]{0:T(1024)S(1)}, u32[]{:S(2)}, u32[]{:S(2)}) collective-permute-start(f32[2304]{0:T(1024)S(1)} %pad_maximum_fusion.6), channel_id=1, source_target_pairs={{0,128},{32,160},{64,192},{96,224},{128,0},{160,32},{192,64},{224,... | collective-permute-start | bytes 27656 | tf_op jit(solution)/shard_map/ppermute | solution.py:123
  175.7 14.4 %collective-permute-start.20 = (f32[2176]{0:T(1024)S(1)}, f32[2176]{0:T(1024)S(1)}, u32[]{:S(2)}, u32[]{:S(2)}) collective-permute-start(f32[2176]{0:T(1024)S(1)} %pad_maximum_fusion.7), channel_id=1, source_target_pairs={{0,256},{32,288},{64,320},{96,352},{128,384},{160,416},{192,448},{... | collective-permute-start | bytes 26120 | tf_op jit(solution)/shard_map/ppermute | solution.py:123
  (4 other events, 6.1 us)

commit v10 on v9

--- a/solution.py
+++ b/solution.py
@@ -61,10 +61,11 @@
     words = sign_words.shape[1]
     chunks = [(sign_words >> (CHUNK * c)) & ((1 << CHUNK) - 1) for c in range(3)]
     meta = jnp.concatenate([set_labels[:, None]] + chunks, axis=1).astype(jnp.bfloat16)
-    meta = jnp.concatenate([meta, split3(squares(samples)), split3(squares(corpus))], axis=1)
+    norms = jnp.concatenate([split3(squares(samples)), split3(squares(corpus))], axis=1)
     pad = META - meta.shape[1]
-    meta = jnp.pad(meta, ((0, 0), (0, pad)))
-    return meta, words
+    plain = jnp.pad(meta, ((0, 0), (0, pad)))
+    with_norms = jnp.pad(jnp.concatenate([meta, norms], axis=1), ((0, 0), (0, pad - norms.shape[1])))
+    return plain, with_norms, words
 
 
 def unpack(buf, words):
@@ -126,7 +127,7 @@
     return x, rider
 
 
-def per_device(samples, set_labels, sign_words, corpus, scale_grid, scale_pick):
+def body(samples, set_labels, sign_words, corpus, scale_grid, scale_pick):
     scales = band_scales(scale_grid, scale_pick)
     n_grp = lax.axis_size("grp")
     n_dev = lax.axis_size("dev")
@@ -134,9 +135,9 @@
     total = rows_here * n_grp * n_dev
     inv_root = jnp.float32(1.0) / jnp.sqrt(jnp.float32(total))
 
-    meta, words = pack_meta(set_labels, sign_words, samples, corpus)
+    meta, meta_norms, words = pack_meta(set_labels, sign_words, samples, corpus)
     own = jnp.concatenate([samples, meta], axis=1)
-    own_wide = jnp.concatenate([own, corpus], axis=1)
+    own_wide = jnp.concatenate([samples, meta_norms, corpus], axis=1)
 
     grp_bits = axis_order(n_grp, GRP_ORDER)
     dev_nbits = n_dev.bit_length() - 1
@@ -155,7 +156,8 @@
     blk_buf = blk_buf.reshape(n_dev * rows_here, -1)
     col_rows, col_vec, col_sq, corpus_sq = unpack(col_buf[:, :D + META], words)
     col_corpus = col_buf[:, D + META:]
-    block_rows, block_vec, block_sq, _ = unpack(blk_buf, words)
+    block_rows, block_vec, _, _ = unpack(blk_buf, words)
+    block_sq = squares(block_rows)
 
 
     dist = distances(block_rows, block_sq, col_rows, col_sq)
@@ -196,6 +198,4 @@
         P(),
     )
     out_specs = (P(), P(), P(None, ("grp", "dev")))
-    return jax.shard_map(
-        per_device, mesh=mesh, in_specs=in_specs, out_specs=out_specs, check_vma=False
-    )
+    return jax.shard_map(body, mesh=mesh, in_specs=in_specs, out_specs=out_specs, check_vma=False)

time: 193 us -> 195 us (1.010)
  other arithmetic: 17 us -> 21.1 us
  matrix products: 18.3 us -> 15.7 us
    dot_general x2, matrix products: 8.7 us -> 6.09 us  [distances(): lax.dot_general(left, right, (((1,), (1,)), ((), ())), preferred_element_...]
    shift_right_arithmetic x6, local copies, waits for them, and re-layouts: 2.31 us -> 4.85 us  [make_vectors(): jnp.right_shift(sign_words[:, :, None], shifts[None, None, :]) & 1]
    reduce_sum x2 -> x3, other arithmetic: 1.93 us -> 3.99 us  [squares(): return jnp.sum(wide * wide, axis=1)]
    another operation x8 -> x7, other arithmetic: 2.65 us -> 4.18 us
  transfers between devices with their start and end apart: 21 -> 21, of which waited for: 18 -> 18; matrix products, arithmetic and copies ran while one was open for 7% -> 8% of each run, Pallas kernels for 0% -> 0%
where the time goes in v10:
time: 195 us; the launch traced here: 194 us
  starting transfers between devices  79.7 us (41%)
  waiting for transfers between devices  66.2 us (34%)
  other arithmetic  21.1 us (11%)
  matrix products  15.7 us (8%)
  local copies, waits for them, and re-layouts  9.88 us (5%)
    ppermute x12, starting transfers between devices, xor_gather(): other = lax.ppermute(buf, axis, [(i, i ^ k) for i in range(n)])  49.8 us
    ppermute x12, waiting for transfers between devices, xor_gather(): other = lax.ppermute(buf, axis, [(i, i ^ k) for i in range(n)])  35.2 us
    ppermute x4, waiting for transfers between devices, xor_sum(): got = lax.ppermute(jnp.concatenate([x.ravel(), send.ravel()]), a, pairs)  18 us
    ppermute x5, starting transfers between devices, xor_sum(): x = x + lax.ppermute(x, a, pairs)  17.8 us
    ppermute x5, waiting for transfers between devices, xor_sum(): x = x + lax.ppermute(x, a, pairs)  13.1 us
    ppermute x4, starting transfers between devices, xor_sum(): got = lax.ppermute(jnp.concatenate([x.ravel(), send.ravel()]), a, pairs)  12.1 us
    dot_general x4, matrix products, body(): product = jnp.dot(kern, col_vec, preferred_element_type=jnp.float32)  6.48 us
    dot_general x2, matrix products, distances(): lax.dot_general(left, right, (((1,), (1,)), ((), ())), preferred_element_...  6.09 us
  transfers between devices with their start and end apart: 21, of which 18 were waited for; matrix products, arithmetic and copies ran while one was open for 8% of the time, Pallas kernels for 0%

profile of v10, /device:TPU:6, one launch (start us, length us, event | category | flops | bytes accessed | tf_op | source)
XLA Modules:
  0.0 193.8 jit_solution(13103431107675318225)
XLA Ops:
  5.3 15.7 %collective-permute-start.8 = (bf16[1,32,2176]{2,1,0:T(8,128)(2,1)S(1)}, bf16[1,32,2176]{2,1,0:T(8,128)(2,1)S(1)}, u32[]{:S(2)}, u32[]{:S(2)}) collective-permute-start(bf16[1,32,2176]{2,1,0:T(8,128)(2,1)S(1)} %fusion.30), channel_id=1, source_target_pairs={{0,256},{32,288},{64,320},{96,352},{128,384},{160,416},{192,448},{... | collective-permute-start | bytes 417800 | tf_op jit(solution)/shard_map/ppermute | solution.py:86
  21.9 4.3 %collective-permute-start = (bf16[1,32,1152]{2,1,0:T(8,128)(2,1)S(1)}, bf16[1,32,1152]{2,1,0:T(8,128)(2,1)S(1)}, u32[]{:S(2)}, u32[]{:S(2)}) collective-permute-start(bf16[1,32,1152]{2,1,0:T(8,128)(2,1)S(1)} %maximum_bitcast_fusion), channel_id=1, source_target_pairs={{0,4},{1,5},{2,6},{3,7},{4,0},{5,1},{6,2},{7,3},{8,12},{9,13},{10,... | collective-permute-start | bytes 221192 | tf_op jit(solution)/shard_map/ppermute | solution.py:86
  27.1 13.3 %collective-permute-done = bf16[1,32,1152]{2,1,0:T(8,128)(2,1)S(1)} collective-permute-done((bf16[1,32,1152]{2,1,0:T(8,128)(2,1)S(1)}, bf16[1,32,1152]{2,1,0:T(8,128)(2,1)S(1)}, u32[]{:S(2)}, u32[]{:S(2)}) %collective-permute-start) | collective-permute-done | bytes 73760 | tf_op jit(solution)/shard_map/ppermute | solution.py:86
  40.5 5.1 %collective-permute-start.1 = (bf16[2,32,1152]{2,1,0:T(8,128)(2,1)S(1)}, bf16[2,32,1152]{2,1,0:T(8,128)(2,1)S(1)}, u32[]{:S(2)}, u32[]{:S(2)}) collective-permute-start(bf16[2,32,1152]{2,1,0:T(8,128)(2,1)S(1)} %maximum_select_fusion.11), channel_id=1, source_target_pairs={{0,16},{1,17},{2,18},{3,19},{4,20},{5,21},{6,22},{7,23},{8,24},{9,... | collective-permute-start | bytes 442376 | tf_op jit(solution)/shard_map/ppermute | solution.py:86
  46.3 3.4 %collective-permute-done.1 = bf16[2,32,1152]{2,1,0:T(8,128)(2,1)S(1)} collective-permute-done((bf16[2,32,1152]{2,1,0:T(8,128)(2,1)S(1)}, bf16[2,32,1152]{2,1,0:T(8,128)(2,1)S(1)}, u32[]{:S(2)}, u32[]{:S(2)}) %collective-permute-start.1) | collective-permute-done | bytes 147488 | tf_op jit(solution)/shard_map/ppermute | solution.py:86
  54.4 3.5 %collective-permute-start.5 = (bf16[4,16,1152]{2,1,0:T(8,128)(2,1)S(1)}, bf16[4,16,1152]{2,1,0:T(8,128)(2,1)S(1)}, u32[]{:S(2)}, u32[]{:S(2)}) collective-permute-start(bf16[4,16,1152]{2,1,0:T(8,128)(2,1)S(1)} %get-tuple-element.14), channel_id=1, source_target_pairs={{0,8},{1,9},{2,10},{3,11},{4,12},{5,13},{6,14},{7,15},{8,0},{9,1},... | collective-permute-start | bytes 442376 | tf_op jit(solution)/shard_map/ppermute | solution.py:86
  61.5 4.8 %collective-permute-start.6 = (bf16[8,16,1152]{2,1,0:T(8,128)(2,1)S(1)}, bf16[8,16,1152]{2,1,0:T(8,128)(2,1)S(1)}, u32[]{:S(2)}, u32[]{:S(2)}) collective-permute-start(bf16[8,16,1152]{2,1,0:T(8,128)(2,1)S(1)} %maximum_select_fusion.9), channel_id=1, source_target_pairs={{0,2},{1,3},{2,0},{3,1},{4,6},{5,7},{6,4},{7,5},{8,10},{9,11},{10,... | collective-permute-start | bytes 884744 | tf_op jit(solution)/shard_map/ppermute | solution.py:86
  66.5 3.0 %collective-permute-start.10 = (bf16[4,32,2176]{2,1,0:T(8,128)(2,1)S(1)}, bf16[4,32,2176]{2,1,0:T(8,128)(2,1)S(1)}, u32[]{:S(2)}, u32[]{:S(2)}) collective-permute-start(bf16[4,32,2176]{2,1,0:T(8,128)(2,1)S(1)} %maximum_select_fusion.6), channel_id=1, source_target_pairs={{0,128},{32,160},{64,192},{96,224},{128,0},{160,32},{192,64},{224,... | collective-permute-start | bytes 1671176 | tf_op jit(solution)/shard_map/ppermute | solution.py:86
  69.7 3.3 %collective-permute-done.3 = bf16[8,16,1152]{2,1,0:T(8,128)(2,1)S(1)} collective-permute-done((bf16[8,16,1152]{2,1,0:T(8,128)(2,1)S(1)}, bf16[8,16,1152]{2,1,0:T(8,128)(2,1)S(1)}, u32[]{:S(2)}, u32[]{:S(2)}) %collective-permute-start.3) | collective-permute-done | bytes 294944 | tf_op jit(solution)/shard_map/ppermute | solution.py:86
  75.8 3.1 %collective-permute-done.6 = bf16[8,16,1152]{2,1,0:T(8,128)(2,1)S(1)} collective-permute-done((bf16[8,16,1152]{2,1,0:T(8,128)(2,1)S(1)}, bf16[8,16,1152]{2,1,0:T(8,128)(2,1)S(1)}, u32[]{:S(2)}, u32[]{:S(2)}) %collective-permute-start.6) | collective-permute-done | bytes 294944 | tf_op jit(solution)/shard_map/ppermute | solution.py:86
  85.2 4.0 %collective-permute-done.4 = bf16[16,16,1152]{2,1,0:T(8,128)(2,1)S(1)} collective-permute-done((bf16[16,16,1152]{2,1,0:T(8,128)(2,1)S(1)}, bf16[16,16,1152]{2,1,0:T(8,128)(2,1)S(1)}, u32[]{:S(2)}, u32[]{:S(2)}) %collective-permute-start.4) | collective-permute-done | bytes 589856 | tf_op jit(solution)/shard_map/ppermute | solution.py:86
  89.4 5.6 %collective-permute-done.7 = bf16[16,16,1152]{2,1,0:T(8,128)(2,1)S(1)} collective-permute-done((bf16[16,16,1152]{2,1,0:T(8,128)(2,1)S(1)}, bf16[16,16,1152]{2,1,0:T(8,128)(2,1)S(1)}, u32[]{:S(2)}, u32[]{:S(2)}) %collective-permute-start.7) | collective-permute-done | bytes 589856 | tf_op jit(solution)/shard_map/ppermute | solution.py:86
  101.1 3.1 %fusion.9 = bf16[1024,511]{0,1:T(8,128)(2,1)} fusion(s32[1024,525]{0,1:T(8,128)} %shift_right_arithmetic.77, s32[511]{0:T(512)S(1)} %slice.233, f32[1024]{0:T(1024)S(1)} %bitcast.75), kind=kLoop, calls=%fused_computation.18 | loop fusion | flops 3662848 | bytes 3145724 | tf_op jit(solution)/shard_map/convert.9
  121.4 4.8 %exponential_convert_fusion.3 = (bf16[512,1024]{1,0:T(8,128)(2,1)S(1)}, bf16[512,1024]{1,0:T(8,128)(2,1)S(1)}, bf16[512,1024]{1,0:T(8,128)(2,1)S(1)}, bf16[512,1024]{1,0:T(8,128)(2,1)S(1)}) fusion(f32[]{:T(128)} %bitcast.8, f32[]{:T(128)} %bitcast.15, f32[]{:T(128)} %bitcast.13, f32[]{:T(128)} %bitcast.11, bf16[1024,1152]{1,0:T(8,128)(2,1)S(1)} %bitcast.66, ...), kind=kOutput, calls=%fused_computation.22 | convolution fusion | flops 1080033280 | bytes 7346192 | tf_op jit(solution)/shard_map/dot_general | solution.py:41
  135.3 3.7 %collective-permute-done.13 = f32[4,512]{1,0:T(4,128)S(1)} collective-permute-done((f32[4,512]{1,0:T(4,128)S(1)}, f32[4,512]{1,0:T(4,128)S(1)}, u32[]{:S(2)}, u32[]{:S(2)}) %collective-permute-start.13) | collective-permute-done | bytes 8224 | tf_op jit(solution)/shard_map/ppermute | solution.py:117
  139.0 5.1 %collective-permute-start.14 = (f32[4,512]{1,0:T(4,128)S(1)}, f32[4,512]{1,0:T(4,128)S(1)}, u32[]{:S(2)}, u32[]{:S(2)}) collective-permute-start(f32[4,512]{1,0:T(4,128)S(1)} %fusion.71), channel_id=1, source_target_pairs={{0,4},{1,5},{2,6},{3,7},{4,0},{5,1},{6,2},{7,3},{8,12},{9,13},{10,... | collective-permute-start | bytes 24584 | tf_op jit(solution)/shard_map/ppermute | solution.py:117
  145.0 3.5 %collective-permute-done.14 = f32[4,512]{1,0:T(4,128)S(1)} collective-permute-done((f32[4,512]{1,0:T(4,128)S(1)}, f32[4,512]{1,0:T(4,128)S(1)}, u32[]{:S(2)}, u32[]{:S(2)}) %collective-permute-start.14) | collective-permute-done | bytes 8224 | tf_op jit(solution)/shard_map/ppermute | solution.py:117
  148.5 3.5 %collective-permute-start.15 = (f32[4,512]{1,0:T(4,128)S(1)}, f32[4,512]{1,0:T(4,128)S(1)}, u32[]{:S(2)}, u32[]{:S(2)}) collective-permute-start(f32[4,512]{1,0:T(4,128)S(1)} %add.162), channel_id=1, source_target_pairs={{0,8},{1,9},{2,10},{3,11},{4,12},{5,13},{6,14},{7,15},{8,0},{9,1},... | collective-permute-start | bytes 24584 | tf_op jit(solution)/shard_map/ppermute | solution.py:117
  154.1 5.1 %collective-permute-start.16 = (f32[4,512]{1,0:T(4,128)S(1)}, f32[4,512]{1,0:T(4,128)S(1)}, u32[]{:S(2)}, u32[]{:S(2)}) collective-permute-start(f32[4,512]{1,0:T(4,128)S(1)} %add.163), channel_id=1, source_target_pairs={{0,16},{1,17},{2,18},{3,19},{4,20},{5,21},{6,22},{7,23},{8,24},{9,... | collective-permute-start | bytes 24584 | tf_op jit(solution)/shard_map/ppermute | solution.py:117
  167.0 3.0 %collective-permute-done.18 = f32[2560]{0:T(1024)S(1)} collective-permute-done((f32[2560]{0:T(1024)S(1)}, f32[2560]{0:T(1024)S(1)}, u32[]{:S(2)}, u32[]{:S(2)}) %collective-permute-start.18) | collective-permute-done | bytes 10272 | tf_op jit(solution)/shard_map/ppermute | solution.py:124
  170.3 3.4 %collective-permute-start.19 = (f32[2304]{0:T(1024)S(1)}, f32[2304]{0:T(1024)S(1)}, u32[]{:S(2)}, u32[]{:S(2)}) collective-permute-start(f32[2304]{0:T(1024)S(1)} %pad_maximum_fusion.6), channel_id=1, source_target_pairs={{0,128},{32,160},{64,192},{96,224},{128,0},{160,32},{192,64},{224,... | collective-permute-start | bytes 27656 | tf_op jit(solution)/shard_map/ppermute | solution.py:124
  173.8 3.6 %collective-permute-done.19 = f32[2304]{0:T(1024)S(1)} collective-permute-done((f32[2304]{0:T(1024)S(1)}, f32[2304]{0:T(1024)S(1)}, u32[]{:S(2)}, u32[]{:S(2)}) %collective-permute-start.19) | collective-permute-done | bytes 9248 | tf_op jit(solution)/shard_map/ppermute | solution.py:124
  177.7 4.2 %collective-permute-start.20 = (f32[2176]{0:T(1024)S(1)}, f32[2176]{0:T(1024)S(1)}, u32[]{:S(2)}, u32[]{:S(2)}) collective-permute-start(f32[2176]{0:T(1024)S(1)} %pad_maximum_fusion.7), channel_id=1, source_target_pairs={{0,256},{32,288},{64,320},{96,352},{128,384},{160,416},{192,448},{... | collective-permute-start | bytes 26120 | tf_op jit(solution)/shard_map/ppermute | solution.py:124
  181.9 10.1 %collective-permute-done.20 = f32[2176]{0:T(1024)S(1)} collective-permute-done((f32[2176]{0:T(1024)S(1)}, f32[2176]{0:T(1024)S(1)}, u32[]{:S(2)}, u32[]{:S(2)}) %collective-permute-start.20) | collective-permute-done | bytes 8736 | tf_op jit(solution)/shard_map/ppermute | solution.py:124
  (149 shorter events, 70.0 us)
Async XLA Ops:
  5.3 46.4 %collective-permute-start.8 = (bf16[1,32,2176]{2,1,0:T(8,128)(2,1)S(1)}, bf16[1,32,2176]{2,1,0:T(8,128)(2,1)S(1)}, u32[]{:S(2)}, u32[]{:S(2)}) collective-permute-start(bf16[1,32,2176]{2,1,0:T(8,128)(2,1)S(1)} %fusion.30), channel_id=1, source_target_pairs={{0,256},{32,288},{64,320},{96,352},{128,384},{160,416},{192,448},{... | collective-permute-start | bytes 417800 | tf_op jit(solution)/shard_map/ppermute | solution.py:86
  21.9 18.5 %collective-permute-start = (bf16[1,32,1152]{2,1,0:T(8,128)(2,1)S(1)}, bf16[1,32,1152]{2,1,0:T(8,128)(2,1)S(1)}, u32[]{:S(2)}, u32[]{:S(2)}) collective-permute-start(bf16[1,32,1152]{2,1,0:T(8,128)(2,1)S(1)} %maximum_bitcast_fusion), channel_id=1, source_target_pairs={{0,4},{1,5},{2,6},{3,7},{4,0},{5,1},{6,2},{7,3},{8,12},{9,13},{10,... | collective-permute-start | bytes 221192 | tf_op jit(solution)/shard_map/ppermute | solution.py:86
  40.4 29.1 %copy-start.6 = (s32[16]{0:T(128)S(1)}, s32[16]{0:T(128)}, u32[]{:S(2)}) copy-start(s32[16]{0:T(128)} %constant.130) | copy-start | bytes 196
  40.5 9.2 %collective-permute-start.1 = (bf16[2,32,1152]{2,1,0:T(8,128)(2,1)S(1)}, bf16[2,32,1152]{2,1,0:T(8,128)(2,1)S(1)}, u32[]{:S(2)}, u32[]{:S(2)}) collective-permute-start(bf16[2,32,1152]{2,1,0:T(8,128)(2,1)S(1)} %maximum_select_fusion.11), channel_id=1, source_target_pairs={{0,16},{1,17},{2,18},{3,19},{4,20},{5,21},{6,22},{7,23},{8,24},{9,... | collective-permute-start | bytes 442376 | tf_op jit(solution)/shard_map/ppermute | solution.py:86
  49.7 9.3 %collective-permute-start.2 = (bf16[4,16,1152]{2,1,0:T(8,128)(2,1)S(1)}, bf16[4,16,1152]{2,1,0:T(8,128)(2,1)S(1)}, u32[]{:S(2)}, u32[]{:S(2)}) collective-permute-start(bf16[4,16,1152]{2,1,0:T(8,128)(2,1)S(1)} %get-tuple-element.13), channel_id=1, source_target_pairs={{0,2},{1,3},{2,0},{3,1},{4,6},{5,7},{6,4},{7,5},{8,10},{9,11},{10,... | collective-permute-start | bytes 442376 | tf_op jit(solution)/shard_map/ppermute | solution.py:86
  51.7 14.7 %collective-permute-start.9 = (bf16[2,32,2176]{2,1,0:T(8,128)(2,1)S(1)}, bf16[2,32,2176]{2,1,0:T(8,128)(2,1)S(1)}, u32[]{:S(2)}, u32[]{:S(2)}) collective-permute-start(bf16[2,32,2176]{2,1,0:T(8,128)(2,1)S(1)} %maximum_select_fusion.10), channel_id=1, source_target_pairs={{0,64},{32,96},{64,0},{96,32},{128,192},{160,224},{192,128},{224,1... | collective-permute-start | bytes 835592 | tf_op jit(solution)/shard_map/ppermute | solution.py:86
  54.4 7.0 %collective-permute-start.5 = (bf16[4,16,1152]{2,1,0:T(8,128)(2,1)S(1)}, bf16[4,16,1152]{2,1,0:T(8,128)(2,1)S(1)}, u32[]{:S(2)}, u32[]{:S(2)}) collective-permute-start(bf16[4,16,1152]{2,1,0:T(8,128)(2,1)S(1)} %get-tuple-element.14), channel_id=1, source_target_pairs={{0,8},{1,9},{2,10},{3,11},{4,12},{5,13},{6,14},{7,15},{8,0},{9,1},... | collective-permute-start | bytes 442376 | tf_op jit(solution)/shard_map/ppermute | solution.py:86
  59.1 13.9 %collective-permute-start.3 = (bf16[8,16,1152]{2,1,0:T(8,128)(2,1)S(1)}, bf16[8,16,1152]{2,1,0:T(8,128)(2,1)S(1)}, u32[]{:S(2)}, u32[]{:S(2)}) collective-permute-start(bf16[8,16,1152]{2,1,0:T(8,128)(2,1)S(1)} %maximum_select_fusion.8), channel_id=1, source_target_pairs={{0,1},{1,0},{2,3},{3,2},{4,5},{5,4},{6,7},{7,6},{8,9},{9,8},{10,11... | collective-permute-start | bytes 884744 | tf_op jit(solution)/shard_map/ppermute | solution.py:86
  61.5 17.4 %collective-permute-start.6 = (bf16[8,16,1152]{2,1,0:T(8,128)(2,1)S(1)}, bf16[8,16,1152]{2,1,0:T(8,128)(2,1)S(1)}, u32[]{:S(2)}, u32[]{:S(2)}) collective-permute-start(bf16[8,16,1152]{2,1,0:T(8,128)(2,1)S(1)} %maximum_select_fusion.9), channel_id=1, source_target_pairs={{0,2},{1,3},{2,0},{3,1},{4,6},{5,7},{6,4},{7,5},{8,10},{9,11},{10,... | collective-permute-start | bytes 884744 | tf_op jit(solution)/shard_map/ppermute | solution.py:86
  66.5 15.4 %collective-permute-start.10 = (bf16[4,32,2176]{2,1,0:T(8,128)(2,1)S(1)}, bf16[4,32,2176]{2,1,0:T(8,128)(2,1)S(1)}, u32[]{:S(2)}, u32[]{:S(2)}) collective-permute-start(bf16[4,32,2176]{2,1,0:T(8,128)(2,1)S(1)} %maximum_select_fusion.6), channel_id=1, source_target_pairs={{0,128},{32,160},{64,192},{96,224},{128,0},{160,32},{192,64},{224,... | collective-permute-start | bytes 1671176 | tf_op jit(solution)/shard_map/ppermute | solution.py:86
  73.1 16.1 %collective-permute-start.4 = (bf16[16,16,1152]{2,1,0:T(8,128)(2,1)S(1)}, bf16[16,16,1152]{2,1,0:T(8,128)(2,1)S(1)}, u32[]{:S(2)}, u32[]{:S(2)}) collective-permute-start(bf16[16,16,1152]{2,1,0:T(8,128)(2,1)S(1)} %maximum_select_fusion.4), channel_id=1, source_target_pairs={{0,8},{1,9},{2,10},{3,11},{4,12},{5,13},{6,14},{7,15},{8,0},{9,1},... | collective-permute-start | bytes 1769480 | tf_op jit(solution)/shard_map/ppermute | solution.py:86
  79.1 15.9 %collective-permute-start.7 = (bf16[16,16,1152]{2,1,0:T(8,128)(2,1)S(1)}, bf16[16,16,1152]{2,1,0:T(8,128)(2,1)S(1)}, u32[]{:S(2)}, u32[]{:S(2)}) collective-permute-start(bf16[16,16,1152]{2,1,0:T(8,128)(2,1)S(1)} %maximum_select_fusion.5), channel_id=1, source_target_pairs={{0,1},{1,0},{2,3},{3,2},{4,5},{5,4},{6,7},{7,6},{8,9},{9,8},{10,11... | collective-permute-start | bytes 1769480 | tf_op jit(solution)/shard_map/ppermute | solution.py:86
  83.1 21.1 %collective-permute-start.11 = (bf16[8,32,2176]{2,1,0:T(8,128)(2,1)}, bf16[8,32,2176]{2,1,0:T(8,128)(2,1)}, u32[]{:S(2)}, u32[]{:S(2)}) collective-permute-start(bf16[8,32,2176]{2,1,0:T(8,128)(2,1)} %maximum_select_fusion.3), channel_id=1, source_target_pairs={{0,32},{32,0},{64,96},{96,64},{128,160},{160,128},{192,224},{224,1... | collective-permute-start | bytes 3342344 | tf_op jit(solution)/shard_map/ppermute | solution.py:86
  110.0 3.5 %copy-start.1 = (bf16[32,32,1152]{2,1,0:T(8,128)(2,1)S(1)}, bf16[32,32,1152]{2,1,0:T(8,128)(2,1)}, u32[]{:S(2)}) copy-start(bf16[32,32,1152]{2,1,0:T(8,128)(2,1)} %copy-done) | copy-start | bytes 7077892
  111.6 2.0 %copy-start.3 = (bf16[16,32,2176]{2,1,0:T(8,128)(2,1)S(1)}, bf16[16,32,2176]{2,1,0:T(8,128)(2,1)}, u32[]{:S(2)}) copy-start(bf16[16,32,2176]{2,1,0:T(8,128)(2,1)} %copy-done.2) | copy-start | bytes 6684676
  127.0 5.5 %collective-permute-start.12 = (f32[4,512]{1,0:T(4,128)S(1)}, f32[4,512]{1,0:T(4,128)S(1)}, u32[]{:S(2)}, u32[]{:S(2)}) collective-permute-start(f32[4,512]{1,0:T(4,128)S(1)} %pad_maximum_fusion.8), channel_id=1, source_target_pairs={{0,1},{1,0},{2,3},{3,2},{4,5},{5,4},{6,7},{7,6},{8,9},{9,8},{10,11... | collective-permute-start | bytes 24584 | tf_op jit(solution)/shard_map/ppermute | solution.py:117
  132.6 6.4 %collective-permute-start.13 = (f32[4,512]{1,0:T(4,128)S(1)}, f32[4,512]{1,0:T(4,128)S(1)}, u32[]{:S(2)}, u32[]{:S(2)}) collective-permute-start(f32[4,512]{1,0:T(4,128)S(1)} %fusion.60), channel_id=1, source_target_pairs={{0,2},{1,3},{2,0},{3,1},{4,6},{5,7},{6,4},{7,5},{8,10},{9,11},{10,... | collective-permute-start | bytes 24584 | tf_op jit(solution)/shard_map/ppermute | solution.py:117
  139.0 9.5 %collective-permute-start.14 = (f32[4,512]{1,0:T(4,128)S(1)}, f32[4,512]{1,0:T(4,128)S(1)}, u32[]{:S(2)}, u32[]{:S(2)}) collective-permute-start(f32[4,512]{1,0:T(4,128)S(1)} %fusion.71), channel_id=1, source_target_pairs={{0,4},{1,5},{2,6},{3,7},{4,0},{5,1},{6,2},{7,3},{8,12},{9,13},{10,... | collective-permute-start | bytes 24584 | tf_op jit(solution)/shard_map/ppermute | solution.py:117
  148.5 5.6 %collective-permute-start.15 = (f32[4,512]{1,0:T(4,128)S(1)}, f32[4,512]{1,0:T(4,128)S(1)}, u32[]{:S(2)}, u32[]{:S(2)}) collective-permute-start(f32[4,512]{1,0:T(4,128)S(1)} %add.162), channel_id=1, source_target_pairs={{0,8},{1,9},{2,10},{3,11},{4,12},{5,13},{6,14},{7,15},{8,0},{9,1},... | collective-permute-start | bytes 24584 | tf_op jit(solution)/shard_map/ppermute | solution.py:117
  154.1 7.0 %collective-permute-start.16 = (f32[4,512]{1,0:T(4,128)S(1)}, f32[4,512]{1,0:T(4,128)S(1)}, u32[]{:S(2)}, u32[]{:S(2)}) collective-permute-start(f32[4,512]{1,0:T(4,128)S(1)} %add.163), channel_id=1, source_target_pairs={{0,16},{1,17},{2,18},{3,19},{4,20},{5,21},{6,22},{7,23},{8,24},{9,... | collective-permute-start | bytes 24584 | tf_op jit(solution)/shard_map/ppermute | solution.py:117
  161.1 3.1 %collective-permute-start.17 = (f32[3072]{0:T(1024)S(1)}, f32[3072]{0:T(1024)S(1)}, u32[]{:S(2)}, u32[]{:S(2)}) collective-permute-start(f32[3072]{0:T(1024)S(1)} %pad_maximum_fusion.4), channel_id=1, source_target_pairs={{0,32},{32,0},{64,96},{96,64},{128,160},{160,128},{192,224},{224,1... | collective-permute-start | bytes 36872 | tf_op jit(solution)/shard_map/ppermute | solution.py:124
  164.5 5.6 %collective-permute-start.18 = (f32[2560]{0:T(1024)S(1)}, f32[2560]{0:T(1024)S(1)}, u32[]{:S(2)}, u32[]{:S(2)}) collective-permute-start(f32[2560]{0:T(1024)S(1)} %pad_maximum_fusion.5), channel_id=1, source_target_pairs={{0,64},{32,96},{64,0},{96,32},{128,192},{160,224},{192,128},{224,1... | collective-permute-start | bytes 30728 | tf_op jit(solution)/shard_map/ppermute | solution.py:124
  170.3 7.1 %collective-permute-start.19 = (f32[2304]{0:T(1024)S(1)}, f32[2304]{0:T(1024)S(1)}, u32[]{:S(2)}, u32[]{:S(2)}) collective-permute-start(f32[2304]{0:T(1024)S(1)} %pad_maximum_fusion.6), channel_id=1, source_target_pairs={{0,128},{32,160},{64,192},{96,224},{128,0},{160,32},{192,64},{224,... | collective-permute-start | bytes 27656 | tf_op jit(solution)/shard_map/ppermute | solution.py:124
  177.7 14.4 %collective-permute-start.20 = (f32[2176]{0:T(1024)S(1)}, f32[2176]{0:T(1024)S(1)}, u32[]{:S(2)}, u32[]{:S(2)}) collective-permute-start(f32[2176]{0:T(1024)S(1)} %pad_maximum_fusion.7), channel_id=1, source_target_pairs={{0,256},{32,288},{64,320},{96,352},{128,384},{160,416},{192,448},{... | collective-permute-start | bytes 26120 | tf_op jit(solution)/shard_map/ppermute | solution.py:124
  (4 other events, 5.8 us)

commit v11 on v10

--- a/solution.py
+++ b/solution.py
@@ -135,9 +135,9 @@
     total = rows_here * n_grp * n_dev
     inv_root = jnp.float32(1.0) / jnp.sqrt(jnp.float32(total))
 
-    meta, meta_norms, words = pack_meta(set_labels, sign_words, samples, corpus)
-    own = jnp.concatenate([samples, meta], axis=1)
-    own_wide = jnp.concatenate([samples, meta_norms, corpus], axis=1)
+    _, meta_norms, words = pack_meta(set_labels, sign_words, samples, corpus)
+    own = jnp.concatenate([samples, meta_norms], axis=1)
+    own_wide = jnp.concatenate([own, corpus], axis=1)
 
     grp_bits = axis_order(n_grp, GRP_ORDER)
     dev_nbits = n_dev.bit_length() - 1
@@ -156,8 +156,7 @@
     blk_buf = blk_buf.reshape(n_dev * rows_here, -1)
     col_rows, col_vec, col_sq, corpus_sq = unpack(col_buf[:, :D + META], words)
     col_corpus = col_buf[:, D + META:]
-    block_rows, block_vec, _, _ = unpack(blk_buf, words)
-    block_sq = squares(block_rows)
+    block_rows, block_vec, block_sq, _ = unpack(blk_buf, words)
 
 
     dist = distances(block_rows, block_sq, col_rows, col_sq)

time: 195 us -> 193 us (0.990)
  other arithmetic: 21.1 us -> 17 us
  matrix products: 15.7 us -> 18.3 us
    dot_general x2, matrix products: 6.09 us -> 8.7 us  [distances(): lax.dot_general(left, right, (((1,), (1,)), ((), ())), preferred_element_...]
    shift_right_arithmetic x6, local copies, waits for them, and re-layouts: 4.85 us -> 2.31 us  [make_vectors(): jnp.right_shift(sign_words[:, :, None], shifts[None, None, :]) & 1]
    reduce_sum x3 -> x2, other arithmetic: 3.99 us -> 1.93 us  [squares(): return jnp.sum(wide * wide, axis=1)]
    another operation x5 -> x6, other arithmetic: 4.11 us -> 2.58 us
  transfers between devices with their start and end apart: 21 -> 21, of which waited for: 18 -> 18; matrix products, arithmetic and copies ran while one was open for 8% -> 7% of each run, Pallas kernels for 0% -> 0%
where the time goes in v11:
time: 193 us; the launch traced here: 192 us
  starting transfers between devices  79.8 us (41%)
  waiting for transfers between devices  66.2 us (34%)
  matrix products  18.3 us (9%)
  other arithmetic  17 us (9%)
  local copies, waits for them, and re-layouts  9.25 us (5%)
    ppermute x12, starting transfers between devices, xor_gather(): other = lax.ppermute(buf, axis, [(i, i ^ k) for i in range(n)])  49.8 us
    ppermute x12, waiting for transfers between devices, xor_gather(): other = lax.ppermute(buf, axis, [(i, i ^ k) for i in range(n)])  35.3 us
    ppermute x4, waiting for transfers between devices, xor_sum(): got = lax.ppermute(jnp.concatenate([x.ravel(), send.ravel()]), a, pairs)  17.9 us
    ppermute x5, starting transfers between devices, xor_sum(): x = x + lax.ppermute(x, a, pairs)  17.8 us
    ppermute x5, waiting for transfers between devices, xor_sum(): x = x + lax.ppermute(x, a, pairs)  13 us
    ppermute x4, starting transfers between devices, xor_sum(): got = lax.ppermute(jnp.concatenate([x.ravel(), send.ravel()]), a, pairs)  12.2 us
    dot_general x2, matrix products, distances(): lax.dot_general(left, right, (((1,), (1,)), ((), ())), preferred_element_...  8.7 us
    dot_general x4, matrix products, body(): product = jnp.dot(kern, col_vec, preferred_element_type=jnp.float32)  6.49 us
  transfers between devices with their start and end apart: 21, of which 18 were waited for; matrix products, arithmetic and copies ran while one was open for 7% of the time, Pallas kernels for 0%

profile of v11, /device:TPU:6, one launch (start us, length us, event | category | flops | bytes accessed | tf_op | source)
XLA Modules:
  0.0 191.8 jit_solution(3105546278893902215)
XLA Ops:
  5.7 15.7 %collective-permute-start.8 = (bf16[1,32,2176]{2,1,0:T(8,128)(2,1)S(1)}, bf16[1,32,2176]{2,1,0:T(8,128)(2,1)S(1)}, u32[]{:S(2)}, u32[]{:S(2)}) collective-permute-start(bf16[1,32,2176]{2,1,0:T(8,128)(2,1)S(1)} %maximum_bitcast_fusion), channel_id=1, source_target_pairs={{0,256},{32,288},{64,320},{96,352},{128,384},{160,416},{192,448},{... | collective-permute-start | bytes 417800 | tf_op jit(solution)/shard_map/ppermute | solution.py:86
  22.3 4.3 %collective-permute-start = (bf16[1,32,1152]{2,1,0:T(8,128)(2,1)S(1)}, bf16[1,32,1152]{2,1,0:T(8,128)(2,1)S(1)}, u32[]{:S(2)}, u32[]{:S(2)}) collective-permute-start(bf16[1,32,1152]{2,1,0:T(8,128)(2,1)S(1)} %maximum_bitcast_fusion.1), channel_id=1, source_target_pairs={{0,4},{1,5},{2,6},{3,7},{4,0},{5,1},{6,2},{7,3},{8,12},{9,13},{10,... | collective-permute-start | bytes 221192 | tf_op jit(solution)/shard_map/ppermute | solution.py:86
  27.4 13.4 %collective-permute-done = bf16[1,32,1152]{2,1,0:T(8,128)(2,1)S(1)} collective-permute-done((bf16[1,32,1152]{2,1,0:T(8,128)(2,1)S(1)}, bf16[1,32,1152]{2,1,0:T(8,128)(2,1)S(1)}, u32[]{:S(2)}, u32[]{:S(2)}) %collective-permute-start) | collective-permute-done | bytes 73760 | tf_op jit(solution)/shard_map/ppermute | solution.py:86
  40.9 5.1 %collective-permute-start.1 = (bf16[2,32,1152]{2,1,0:T(8,128)(2,1)S(1)}, bf16[2,32,1152]{2,1,0:T(8,128)(2,1)S(1)}, u32[]{:S(2)}, u32[]{:S(2)}) collective-permute-start(bf16[2,32,1152]{2,1,0:T(8,128)(2,1)S(1)} %maximum_select_fusion.11), channel_id=1, source_target_pairs={{0,16},{1,17},{2,18},{3,19},{4,20},{5,21},{6,22},{7,23},{8,24},{9,... | collective-permute-start | bytes 442376 | tf_op jit(solution)/shard_map/ppermute | solution.py:86
  46.7 3.4 %collective-permute-done.1 = bf16[2,32,1152]{2,1,0:T(8,128)(2,1)S(1)} collective-permute-done((bf16[2,32,1152]{2,1,0:T(8,128)(2,1)S(1)}, bf16[2,32,1152]{2,1,0:T(8,128)(2,1)S(1)}, u32[]{:S(2)}, u32[]{:S(2)}) %collective-permute-start.1) | collective-permute-done | bytes 147488 | tf_op jit(solution)/shard_map/ppermute | solution.py:86
  54.9 3.5 %collective-permute-start.5 = (bf16[4,16,1152]{2,1,0:T(8,128)(2,1)S(1)}, bf16[4,16,1152]{2,1,0:T(8,128)(2,1)S(1)}, u32[]{:S(2)}, u32[]{:S(2)}) collective-permute-start(bf16[4,16,1152]{2,1,0:T(8,128)(2,1)S(1)} %get-tuple-element.14), channel_id=1, source_target_pairs={{0,8},{1,9},{2,10},{3,11},{4,12},{5,13},{6,14},{7,15},{8,0},{9,1},... | collective-permute-start | bytes 442376 | tf_op jit(solution)/shard_map/ppermute | solution.py:86
  62.0 4.8 %collective-permute-start.6 = (bf16[8,16,1152]{2,1,0:T(8,128)(2,1)S(1)}, bf16[8,16,1152]{2,1,0:T(8,128)(2,1)S(1)}, u32[]{:S(2)}, u32[]{:S(2)}) collective-permute-start(bf16[8,16,1152]{2,1,0:T(8,128)(2,1)S(1)} %maximum_select_fusion.9), channel_id=1, source_target_pairs={{0,2},{1,3},{2,0},{3,1},{4,6},{5,7},{6,4},{7,5},{8,10},{9,11},{10,... | collective-permute-start | bytes 884744 | tf_op jit(solution)/shard_map/ppermute | solution.py:86
  66.9 3.0 %collective-permute-start.10 = (bf16[4,32,2176]{2,1,0:T(8,128)(2,1)S(1)}, bf16[4,32,2176]{2,1,0:T(8,128)(2,1)S(1)}, u32[]{:S(2)}, u32[]{:S(2)}) collective-permute-start(bf16[4,32,2176]{2,1,0:T(8,128)(2,1)S(1)} %maximum_select_fusion.6), channel_id=1, source_target_pairs={{0,128},{32,160},{64,192},{96,224},{128,0},{160,32},{192,64},{224,... | collective-permute-start | bytes 1671176 | tf_op jit(solution)/shard_map/ppermute | solution.py:86
  70.1 3.3 %collective-permute-done.3 = bf16[8,16,1152]{2,1,0:T(8,128)(2,1)S(1)} collective-permute-done((bf16[8,16,1152]{2,1,0:T(8,128)(2,1)S(1)}, bf16[8,16,1152]{2,1,0:T(8,128)(2,1)S(1)}, u32[]{:S(2)}, u32[]{:S(2)}) %collective-permute-start.3) | collective-permute-done | bytes 294944 | tf_op jit(solution)/shard_map/ppermute | solution.py:86
  73.5 2.8 %collective-permute-start.4 = (bf16[16,16,1152]{2,1,0:T(8,128)(2,1)S(1)}, bf16[16,16,1152]{2,1,0:T(8,128)(2,1)S(1)}, u32[]{:S(2)}, u32[]{:S(2)}) collective-permute-start(bf16[16,16,1152]{2,1,0:T(8,128)(2,1)S(1)} %maximum_select_fusion.4), channel_id=1, source_target_pairs={{0,8},{1,9},{2,10},{3,11},{4,12},{5,13},{6,14},{7,15},{8,0},{9,1},... | collective-permute-start | bytes 1769480 | tf_op jit(solution)/shard_map/ppermute | solution.py:86
  76.3 3.1 %collective-permute-done.6 = bf16[8,16,1152]{2,1,0:T(8,128)(2,1)S(1)} collective-permute-done((bf16[8,16,1152]{2,1,0:T(8,128)(2,1)S(1)}, bf16[8,16,1152]{2,1,0:T(8,128)(2,1)S(1)}, u32[]{:S(2)}, u32[]{:S(2)}) %collective-permute-start.6) | collective-permute-done | bytes 294944 | tf_op jit(solution)/shard_map/ppermute | solution.py:86
  85.6 4.0 %collective-permute-done.4 = bf16[16,16,1152]{2,1,0:T(8,128)(2,1)S(1)} collective-permute-done((bf16[16,16,1152]{2,1,0:T(8,128)(2,1)S(1)}, bf16[16,16,1152]{2,1,0:T(8,128)(2,1)S(1)}, u32[]{:S(2)}, u32[]{:S(2)}) %collective-permute-start.4) | collective-permute-done | bytes 589856 | tf_op jit(solution)/shard_map/ppermute | solution.py:86
  89.8 5.6 %collective-permute-done.7 = bf16[16,16,1152]{2,1,0:T(8,128)(2,1)S(1)} collective-permute-done((bf16[16,16,1152]{2,1,0:T(8,128)(2,1)S(1)}, bf16[16,16,1152]{2,1,0:T(8,128)(2,1)S(1)}, u32[]{:S(2)}, u32[]{:S(2)}) %collective-permute-start.7) | collective-permute-done | bytes 589856 | tf_op jit(solution)/shard_map/ppermute | solution.py:86
  118.2 6.1 %exponential_convert_fusion.3 = (bf16[512,1024]{1,0:T(8,128)(2,1)S(1)}, bf16[512,1024]{1,0:T(8,128)(2,1)S(1)}, bf16[512,1024]{1,0:T(8,128)(2,1)S(1)}, bf16[512,1024]{1,0:T(8,128)(2,1)S(1)}) fusion(f32[]{:T(128)} %bitcast.8, f32[]{:T(128)} %bitcast.15, f32[]{:T(128)} %bitcast.13, f32[]{:T(128)} %bitcast.11, bf16[1024,1152]{1,0:T(8,128)(2,1)S(1)} %bitcast.78, ...), kind=kOutput, calls=%fused_computation.21 | convolution fusion | flops 1080033280 | bytes 7348224 | tf_op jit(solution)/shard_map/dot_general | solution.py:41
  133.4 3.7 %collective-permute-done.13 = f32[4,512]{1,0:T(4,128)S(1)} collective-permute-done((f32[4,512]{1,0:T(4,128)S(1)}, f32[4,512]{1,0:T(4,128)S(1)}, u32[]{:S(2)}, u32[]{:S(2)}) %collective-permute-start.13) | collective-permute-done | bytes 8224 | tf_op jit(solution)/shard_map/ppermute | solution.py:117
  137.1 5.1 %collective-permute-start.14 = (f32[4,512]{1,0:T(4,128)S(1)}, f32[4,512]{1,0:T(4,128)S(1)}, u32[]{:S(2)}, u32[]{:S(2)}) collective-permute-start(f32[4,512]{1,0:T(4,128)S(1)} %fusion.66), channel_id=1, source_target_pairs={{0,4},{1,5},{2,6},{3,7},{4,0},{5,1},{6,2},{7,3},{8,12},{9,13},{10,... | collective-permute-start | bytes 24584 | tf_op jit(solution)/shard_map/ppermute | solution.py:117
  143.0 3.5 %collective-permute-done.14 = f32[4,512]{1,0:T(4,128)S(1)} collective-permute-done((f32[4,512]{1,0:T(4,128)S(1)}, f32[4,512]{1,0:T(4,128)S(1)}, u32[]{:S(2)}, u32[]{:S(2)}) %collective-permute-start.14) | collective-permute-done | bytes 8224 | tf_op jit(solution)/shard_map/ppermute | solution.py:117
  146.6 3.5 %collective-permute-start.15 = (f32[4,512]{1,0:T(4,128)S(1)}, f32[4,512]{1,0:T(4,128)S(1)}, u32[]{:S(2)}, u32[]{:S(2)}) collective-permute-start(f32[4,512]{1,0:T(4,128)S(1)} %add.183), channel_id=1, source_target_pairs={{0,8},{1,9},{2,10},{3,11},{4,12},{5,13},{6,14},{7,15},{8,0},{9,1},... | collective-permute-start | bytes 24584 | tf_op jit(solution)/shard_map/ppermute | solution.py:117
  152.1 5.1 %collective-permute-start.16 = (f32[4,512]{1,0:T(4,128)S(1)}, f32[4,512]{1,0:T(4,128)S(1)}, u32[]{:S(2)}, u32[]{:S(2)}) collective-permute-start(f32[4,512]{1,0:T(4,128)S(1)} %add.184), channel_id=1, source_target_pairs={{0,16},{1,17},{2,18},{3,19},{4,20},{5,21},{6,22},{7,23},{8,24},{9,... | collective-permute-start | bytes 24584 | tf_op jit(solution)/shard_map/ppermute | solution.py:117
  165.1 3.0 %collective-permute-done.18 = f32[2560]{0:T(1024)S(1)} collective-permute-done((f32[2560]{0:T(1024)S(1)}, f32[2560]{0:T(1024)S(1)}, u32[]{:S(2)}, u32[]{:S(2)}) %collective-permute-start.18) | collective-permute-done | bytes 10272 | tf_op jit(solution)/shard_map/ppermute | solution.py:124
  168.4 3.5 %collective-permute-start.19 = (f32[2304]{0:T(1024)S(1)}, f32[2304]{0:T(1024)S(1)}, u32[]{:S(2)}, u32[]{:S(2)}) collective-permute-start(f32[2304]{0:T(1024)S(1)} %pad_maximum_fusion.6), channel_id=1, source_target_pairs={{0,128},{32,160},{64,192},{96,224},{128,0},{160,32},{192,64},{224,... | collective-permute-start | bytes 27656 | tf_op jit(solution)/shard_map/ppermute | solution.py:124
  171.9 3.6 %collective-permute-done.19 = f32[2304]{0:T(1024)S(1)} collective-permute-done((f32[2304]{0:T(1024)S(1)}, f32[2304]{0:T(1024)S(1)}, u32[]{:S(2)}, u32[]{:S(2)}) %collective-permute-start.19) | collective-permute-done | bytes 9248 | tf_op jit(solution)/shard_map/ppermute | solution.py:124
  175.7 4.2 %collective-permute-start.20 = (f32[2176]{0:T(1024)S(1)}, f32[2176]{0:T(1024)S(1)}, u32[]{:S(2)}, u32[]{:S(2)}) collective-permute-start(f32[2176]{0:T(1024)S(1)} %pad_maximum_fusion.7), channel_id=1, source_target_pairs={{0,256},{32,288},{64,320},{96,352},{128,384},{160,416},{192,448},{... | collective-permute-start | bytes 26120 | tf_op jit(solution)/shard_map/ppermute | solution.py:124
  180.0 10.1 %collective-permute-done.20 = f32[2176]{0:T(1024)S(1)} collective-permute-done((f32[2176]{0:T(1024)S(1)}, f32[2176]{0:T(1024)S(1)}, u32[]{:S(2)}, u32[]{:S(2)}) %collective-permute-start.20) | collective-permute-done | bytes 8736 | tf_op jit(solution)/shard_map/ppermute | solution.py:124
  (154 shorter events, 67.0 us)
Async XLA Ops:
  5.7 46.4 %collective-permute-start.8 = (bf16[1,32,2176]{2,1,0:T(8,128)(2,1)S(1)}, bf16[1,32,2176]{2,1,0:T(8,128)(2,1)S(1)}, u32[]{:S(2)}, u32[]{:S(2)}) collective-permute-start(bf16[1,32,2176]{2,1,0:T(8,128)(2,1)S(1)} %maximum_bitcast_fusion), channel_id=1, source_target_pairs={{0,256},{32,288},{64,320},{96,352},{128,384},{160,416},{192,448},{... | collective-permute-start | bytes 417800 | tf_op jit(solution)/shard_map/ppermute | solution.py:86
  22.3 18.6 %collective-permute-start = (bf16[1,32,1152]{2,1,0:T(8,128)(2,1)S(1)}, bf16[1,32,1152]{2,1,0:T(8,128)(2,1)S(1)}, u32[]{:S(2)}, u32[]{:S(2)}) collective-permute-start(bf16[1,32,1152]{2,1,0:T(8,128)(2,1)S(1)} %maximum_bitcast_fusion.1), channel_id=1, source_target_pairs={{0,4},{1,5},{2,6},{3,7},{4,0},{5,1},{6,2},{7,3},{8,12},{9,13},{10,... | collective-permute-start | bytes 221192 | tf_op jit(solution)/shard_map/ppermute | solution.py:86
  40.9 29.1 %copy-start.6 = (s32[16]{0:T(128)S(1)}, s32[16]{0:T(128)}, u32[]{:S(2)}) copy-start(s32[16]{0:T(128)} %constant.128) | copy-start | bytes 196
  40.9 9.2 %collective-permute-start.1 = (bf16[2,32,1152]{2,1,0:T(8,128)(2,1)S(1)}, bf16[2,32,1152]{2,1,0:T(8,128)(2,1)S(1)}, u32[]{:S(2)}, u32[]{:S(2)}) collective-permute-start(bf16[2,32,1152]{2,1,0:T(8,128)(2,1)S(1)} %maximum_select_fusion.11), channel_id=1, source_target_pairs={{0,16},{1,17},{2,18},{3,19},{4,20},{5,21},{6,22},{7,23},{8,24},{9,... | collective-permute-start | bytes 442376 | tf_op jit(solution)/shard_map/ppermute | solution.py:86
  50.2 9.3 %collective-permute-start.2 = (bf16[4,16,1152]{2,1,0:T(8,128)(2,1)S(1)}, bf16[4,16,1152]{2,1,0:T(8,128)(2,1)S(1)}, u32[]{:S(2)}, u32[]{:S(2)}) collective-permute-start(bf16[4,16,1152]{2,1,0:T(8,128)(2,1)S(1)} %get-tuple-element.13), channel_id=1, source_target_pairs={{0,2},{1,3},{2,0},{3,1},{4,6},{5,7},{6,4},{7,5},{8,10},{9,11},{10,... | collective-permute-start | bytes 442376 | tf_op jit(solution)/shard_map/ppermute | solution.py:86
  52.1 14.7 %collective-permute-start.9 = (bf16[2,32,2176]{2,1,0:T(8,128)(2,1)S(1)}, bf16[2,32,2176]{2,1,0:T(8,128)(2,1)S(1)}, u32[]{:S(2)}, u32[]{:S(2)}) collective-permute-start(bf16[2,32,2176]{2,1,0:T(8,128)(2,1)S(1)} %maximum_select_fusion.10), channel_id=1, source_target_pairs={{0,64},{32,96},{64,0},{96,32},{128,192},{160,224},{192,128},{224,1... | collective-permute-start | bytes 835592 | tf_op jit(solution)/shard_map/ppermute | solution.py:86
  54.9 7.0 %collective-permute-start.5 = (bf16[4,16,1152]{2,1,0:T(8,128)(2,1)S(1)}, bf16[4,16,1152]{2,1,0:T(8,128)(2,1)S(1)}, u32[]{:S(2)}, u32[]{:S(2)}) collective-permute-start(bf16[4,16,1152]{2,1,0:T(8,128)(2,1)S(1)} %get-tuple-element.14), channel_id=1, source_target_pairs={{0,8},{1,9},{2,10},{3,11},{4,12},{5,13},{6,14},{7,15},{8,0},{9,1},... | collective-permute-start | bytes 442376 | tf_op jit(solution)/shard_map/ppermute | solution.py:86
  59.5 13.9 %collective-permute-start.3 = (bf16[8,16,1152]{2,1,0:T(8,128)(2,1)S(1)}, bf16[8,16,1152]{2,1,0:T(8,128)(2,1)S(1)}, u32[]{:S(2)}, u32[]{:S(2)}) collective-permute-start(bf16[8,16,1152]{2,1,0:T(8,128)(2,1)S(1)} %maximum_select_fusion.8), channel_id=1, source_target_pairs={{0,1},{1,0},{2,3},{3,2},{4,5},{5,4},{6,7},{7,6},{8,9},{9,8},{10,11... | collective-permute-start | bytes 884744 | tf_op jit(solution)/shard_map/ppermute | solution.py:86
  62.0 17.4 %collective-permute-start.6 = (bf16[8,16,1152]{2,1,0:T(8,128)(2,1)S(1)}, bf16[8,16,1152]{2,1,0:T(8,128)(2,1)S(1)}, u32[]{:S(2)}, u32[]{:S(2)}) collective-permute-start(bf16[8,16,1152]{2,1,0:T(8,128)(2,1)S(1)} %maximum_select_fusion.9), channel_id=1, source_target_pairs={{0,2},{1,3},{2,0},{3,1},{4,6},{5,7},{6,4},{7,5},{8,10},{9,11},{10,... | collective-permute-start | bytes 884744 | tf_op jit(solution)/shard_map/ppermute | solution.py:86
  66.9 15.4 %collective-permute-start.10 = (bf16[4,32,2176]{2,1,0:T(8,128)(2,1)S(1)}, bf16[4,32,2176]{2,1,0:T(8,128)(2,1)S(1)}, u32[]{:S(2)}, u32[]{:S(2)}) collective-permute-start(bf16[4,32,2176]{2,1,0:T(8,128)(2,1)S(1)} %maximum_select_fusion.6), channel_id=1, source_target_pairs={{0,128},{32,160},{64,192},{96,224},{128,0},{160,32},{192,64},{224,... | collective-permute-start | bytes 1671176 | tf_op jit(solution)/shard_map/ppermute | solution.py:86
  73.5 16.1 %collective-permute-start.4 = (bf16[16,16,1152]{2,1,0:T(8,128)(2,1)S(1)}, bf16[16,16,1152]{2,1,0:T(8,128)(2,1)S(1)}, u32[]{:S(2)}, u32[]{:S(2)}) collective-permute-start(bf16[16,16,1152]{2,1,0:T(8,128)(2,1)S(1)} %maximum_select_fusion.4), channel_id=1, source_target_pairs={{0,8},{1,9},{2,10},{3,11},{4,12},{5,13},{6,14},{7,15},{8,0},{9,1},... | collective-permute-start | bytes 1769480 | tf_op jit(solution)/shard_map/ppermute | solution.py:86
  79.5 15.9 %collective-permute-start.7 = (bf16[16,16,1152]{2,1,0:T(8,128)(2,1)S(1)}, bf16[16,16,1152]{2,1,0:T(8,128)(2,1)S(1)}, u32[]{:S(2)}, u32[]{:S(2)}) collective-permute-start(bf16[16,16,1152]{2,1,0:T(8,128)(2,1)S(1)} %maximum_select_fusion.5), channel_id=1, source_target_pairs={{0,1},{1,0},{2,3},{3,2},{4,5},{5,4},{6,7},{7,6},{8,9},{9,8},{10,11... | collective-permute-start | bytes 1769480 | tf_op jit(solution)/shard_map/ppermute | solution.py:86
  83.5 19.3 %collective-permute-start.11 = (bf16[8,32,2176]{2,1,0:T(8,128)(2,1)}, bf16[8,32,2176]{2,1,0:T(8,128)(2,1)}, u32[]{:S(2)}, u32[]{:S(2)}) collective-permute-start(bf16[8,32,2176]{2,1,0:T(8,128)(2,1)} %maximum_select_fusion.3), channel_id=1, source_target_pairs={{0,32},{32,0},{64,96},{96,64},{128,160},{160,128},{192,224},{224,1... | collective-permute-start | bytes 3342344 | tf_op jit(solution)/shard_map/ppermute | solution.py:86
  99.5 1.8 copy-start
  109.1 2.6 %copy-start.4 = (bf16[1024,511]{0,1:T(8,128)(2,1)S(1)}, bf16[1024,511]{0,1:T(8,128)(2,1)}, u32[]{:S(2)}) copy-start(bf16[1024,511]{0,1:T(8,128)(2,1)} %fusion.9) | copy-start | bytes 3139588
  125.1 5.5 %collective-permute-start.12 = (f32[4,512]{1,0:T(4,128)S(1)}, f32[4,512]{1,0:T(4,128)S(1)}, u32[]{:S(2)}, u32[]{:S(2)}) collective-permute-start(f32[4,512]{1,0:T(4,128)S(1)} %pad_maximum_fusion.8), channel_id=1, source_target_pairs={{0,1},{1,0},{2,3},{3,2},{4,5},{5,4},{6,7},{7,6},{8,9},{9,8},{10,11... | collective-permute-start | bytes 24584 | tf_op jit(solution)/shard_map/ppermute | solution.py:117
  130.6 6.4 %collective-permute-start.13 = (f32[4,512]{1,0:T(4,128)S(1)}, f32[4,512]{1,0:T(4,128)S(1)}, u32[]{:S(2)}, u32[]{:S(2)}) collective-permute-start(f32[4,512]{1,0:T(4,128)S(1)} %fusion.55), channel_id=1, source_target_pairs={{0,2},{1,3},{2,0},{3,1},{4,6},{5,7},{6,4},{7,5},{8,10},{9,11},{10,... | collective-permute-start | bytes 24584 | tf_op jit(solution)/shard_map/ppermute | solution.py:117
  137.1 9.5 %collective-permute-start.14 = (f32[4,512]{1,0:T(4,128)S(1)}, f32[4,512]{1,0:T(4,128)S(1)}, u32[]{:S(2)}, u32[]{:S(2)}) collective-permute-start(f32[4,512]{1,0:T(4,128)S(1)} %fusion.66), channel_id=1, source_target_pairs={{0,4},{1,5},{2,6},{3,7},{4,0},{5,1},{6,2},{7,3},{8,12},{9,13},{10,... | collective-permute-start | bytes 24584 | tf_op jit(solution)/shard_map/ppermute | solution.py:117
  146.6 5.5 %collective-permute-start.15 = (f32[4,512]{1,0:T(4,128)S(1)}, f32[4,512]{1,0:T(4,128)S(1)}, u32[]{:S(2)}, u32[]{:S(2)}) collective-permute-start(f32[4,512]{1,0:T(4,128)S(1)} %add.183), channel_id=1, source_target_pairs={{0,8},{1,9},{2,10},{3,11},{4,12},{5,13},{6,14},{7,15},{8,0},{9,1},... | collective-permute-start | bytes 24584 | tf_op jit(solution)/shard_map/ppermute | solution.py:117
  152.1 7.0 %collective-permute-start.16 = (f32[4,512]{1,0:T(4,128)S(1)}, f32[4,512]{1,0:T(4,128)S(1)}, u32[]{:S(2)}, u32[]{:S(2)}) collective-permute-start(f32[4,512]{1,0:T(4,128)S(1)} %add.184), channel_id=1, source_target_pairs={{0,16},{1,17},{2,18},{3,19},{4,20},{5,21},{6,22},{7,23},{8,24},{9,... | collective-permute-start | bytes 24584 | tf_op jit(solution)/shard_map/ppermute | solution.py:117
  159.2 3.1 %collective-permute-start.17 = (f32[3072]{0:T(1024)S(1)}, f32[3072]{0:T(1024)S(1)}, u32[]{:S(2)}, u32[]{:S(2)}) collective-permute-start(f32[3072]{0:T(1024)S(1)} %pad_maximum_fusion.4), channel_id=1, source_target_pairs={{0,32},{32,0},{64,96},{96,64},{128,160},{160,128},{192,224},{224,1... | collective-permute-start | bytes 36872 | tf_op jit(solution)/shard_map/ppermute | solution.py:124
  162.5 5.6 %collective-permute-start.18 = (f32[2560]{0:T(1024)S(1)}, f32[2560]{0:T(1024)S(1)}, u32[]{:S(2)}, u32[]{:S(2)}) collective-permute-start(f32[2560]{0:T(1024)S(1)} %pad_maximum_fusion.5), channel_id=1, source_target_pairs={{0,64},{32,96},{64,0},{96,32},{128,192},{160,224},{192,128},{224,1... | collective-permute-start | bytes 30728 | tf_op jit(solution)/shard_map/ppermute | solution.py:124
  168.4 7.1 %collective-permute-start.19 = (f32[2304]{0:T(1024)S(1)}, f32[2304]{0:T(1024)S(1)}, u32[]{:S(2)}, u32[]{:S(2)}) collective-permute-start(f32[2304]{0:T(1024)S(1)} %pad_maximum_fusion.6), channel_id=1, source_target_pairs={{0,128},{32,160},{64,192},{96,224},{128,0},{160,32},{192,64},{224,... | collective-permute-start | bytes 27656 | tf_op jit(solution)/shard_map/ppermute | solution.py:124
  175.7 14.4 %collective-permute-start.20 = (f32[2176]{0:T(1024)S(1)}, f32[2176]{0:T(1024)S(1)}, u32[]{:S(2)}, u32[]{:S(2)}) collective-permute-start(f32[2176]{0:T(1024)S(1)} %pad_maximum_fusion.7), channel_id=1, source_target_pairs={{0,256},{32,288},{64,320},{96,352},{128,384},{160,416},{192,448},{... | collective-permute-start | bytes 26120 | tf_op jit(solution)/shard_map/ppermute | solution.py:124
  (4 other events, 6.1 us)

commit v12 on v11

--- a/solution.py
+++ b/solution.py
@@ -127,6 +127,16 @@
     return x, rider
 
 
+def proof_terms(col_corpus, corpus_sq, block_rows, block_sq, block_vec, scales):
+    cdist = distances(col_corpus, corpus_sq, block_rows, block_sq)
+    weights = block_vec[:, 0]
+    proofs = []
+    for kernel_id in range(NB):
+        kern = jnp.exp(-cdist * scales[kernel_id]).astype(jnp.bfloat16)
+        proofs.append(jnp.dot(kern, weights, preferred_element_type=jnp.float32))
+    return jnp.stack(proofs)
+
+
 def body(samples, set_labels, sign_words, corpus, scale_grid, scale_pick):
     scales = band_scales(scale_grid, scale_pick)
     n_grp = lax.axis_size("grp")
@@ -168,13 +178,8 @@
         forms.append(jnp.sum(block_wide * product, axis=0))
     forms_part = jnp.stack(forms)
 
-    cdist = distances(col_corpus, corpus_sq, block_rows, block_sq)
-    weights = block_vec[:, 0]
-    proofs = []
-    for kernel_id in range(NB):
-        kern = jnp.exp(-cdist * scales[kernel_id]).astype(jnp.bfloat16)
-        proofs.append(jnp.dot(kern, weights, preferred_element_type=jnp.float32))
-    proof_part = jnp.stack(proofs).reshape(NB, n_grp, rows_here)
+    proof_part = proof_terms(col_corpus, corpus_sq, block_rows, block_sq, block_vec, scales)
+    proof_part = proof_part.reshape(NB, n_grp, rows_here)
     inverse = np.argsort(np.array(col_order))
     proof_part = jnp.take(proof_part, jnp.asarray(inverse, jnp.int32), axis=1)
     quad_forms, proof = xor_sum(forms_part, proof_part, n_grp, n_dev)

time: 193 us -> 193 us (level)
  no operation moved by 1% of the time
where the time goes in v12:
time: 193 us; the launch traced here: 192 us
  starting transfers between devices  79.8 us (41%)
  waiting for transfers between devices  66.2 us (34%)
  matrix products  18.3 us (9%)
  other arithmetic  17 us (9%)
  local copies, waits for them, and re-layouts  9.25 us (5%)
    ppermute x12, starting transfers between devices, xor_gather(): other = lax.ppermute(buf, axis, [(i, i ^ k) for i in range(n)])  49.8 us
    ppermute x12, waiting for transfers between devices, xor_gather(): other = lax.ppermute(buf, axis, [(i, i ^ k) for i in range(n)])  35.3 us
    ppermute x4, waiting for transfers between devices, xor_sum(): got = lax.ppermute(jnp.concatenate([x.ravel(), send.ravel()]), a, pairs)  17.9 us
    ppermute x5, starting transfers between devices, xor_sum(): x = x + lax.ppermute(x, a, pairs)  17.8 us
    ppermute x5, waiting for transfers between devices, xor_sum(): x = x + lax.ppermute(x, a, pairs)  13 us
    ppermute x4, starting transfers between devices, xor_sum(): got = lax.ppermute(jnp.concatenate([x.ravel(), send.ravel()]), a, pairs)  12.2 us
    dot_general x2, matrix products, distances(): lax.dot_general(left, right, (((1,), (1,)), ((), ())), preferred_element_...  8.7 us
    dot_general x4, matrix products, body(): product = jnp.dot(kern, col_vec, preferred_element_type=jnp.float32)  6.49 us
  transfers between devices with their start and end apart: 21, of which 18 were waited for; matrix products, arithmetic and copies ran while one was open for 7% of the time, Pallas kernels for 0%

profile of v12, /device:TPU:6, one launch (start us, length us, event | category | flops | bytes accessed | tf_op | source)
XLA Modules:
  0.0 191.8 jit_solution(3105546278893902215)
XLA Ops:
  5.7 15.7 %collective-permute-start.8 = (bf16[1,32,2176]{2,1,0:T(8,128)(2,1)S(1)}, bf16[1,32,2176]{2,1,0:T(8,128)(2,1)S(1)}, u32[]{:S(2)}, u32[]{:S(2)}) collective-permute-start(bf16[1,32,2176]{2,1,0:T(8,128)(2,1)S(1)} %maximum_bitcast_fusion), channel_id=1, source_target_pairs={{0,256},{32,288},{64,320},{96,352},{128,384},{160,416},{192,448},{... | collective-permute-start | bytes 417800 | tf_op jit(solution)/shard_map/ppermute | solution.py:86
  22.3 4.3 %collective-permute-start = (bf16[1,32,1152]{2,1,0:T(8,128)(2,1)S(1)}, bf16[1,32,1152]{2,1,0:T(8,128)(2,1)S(1)}, u32[]{:S(2)}, u32[]{:S(2)}) collective-permute-start(bf16[1,32,1152]{2,1,0:T(8,128)(2,1)S(1)} %maximum_bitcast_fusion.1), channel_id=1, source_target_pairs={{0,4},{1,5},{2,6},{3,7},{4,0},{5,1},{6,2},{7,3},{8,12},{9,13},{10,... | collective-permute-start | bytes 221192 | tf_op jit(solution)/shard_map/ppermute | solution.py:86
  27.4 13.4 %collective-permute-done = bf16[1,32,1152]{2,1,0:T(8,128)(2,1)S(1)} collective-permute-done((bf16[1,32,1152]{2,1,0:T(8,128)(2,1)S(1)}, bf16[1,32,1152]{2,1,0:T(8,128)(2,1)S(1)}, u32[]{:S(2)}, u32[]{:S(2)}) %collective-permute-start) | collective-permute-done | bytes 73760 | tf_op jit(solution)/shard_map/ppermute | solution.py:86
  40.9 5.1 %collective-permute-start.1 = (bf16[2,32,1152]{2,1,0:T(8,128)(2,1)S(1)}, bf16[2,32,1152]{2,1,0:T(8,128)(2,1)S(1)}, u32[]{:S(2)}, u32[]{:S(2)}) collective-permute-start(bf16[2,32,1152]{2,1,0:T(8,128)(2,1)S(1)} %maximum_select_fusion.11), channel_id=1, source_target_pairs={{0,16},{1,17},{2,18},{3,19},{4,20},{5,21},{6,22},{7,23},{8,24},{9,... | collective-permute-start | bytes 442376 | tf_op jit(solution)/shard_map/ppermute | solution.py:86
  46.7 3.4 %collective-permute-done.1 = bf16[2,32,1152]{2,1,0:T(8,128)(2,1)S(1)} collective-permute-done((bf16[2,32,1152]{2,1,0:T(8,128)(2,1)S(1)}, bf16[2,32,1152]{2,1,0:T(8,128)(2,1)S(1)}, u32[]{:S(2)}, u32[]{:S(2)}) %collective-permute-start.1) | collective-permute-done | bytes 147488 | tf_op jit(solution)/shard_map/ppermute | solution.py:86
  54.9 3.5 %collective-permute-start.5 = (bf16[4,16,1152]{2,1,0:T(8,128)(2,1)S(1)}, bf16[4,16,1152]{2,1,0:T(8,128)(2,1)S(1)}, u32[]{:S(2)}, u32[]{:S(2)}) collective-permute-start(bf16[4,16,1152]{2,1,0:T(8,128)(2,1)S(1)} %get-tuple-element.14), channel_id=1, source_target_pairs={{0,8},{1,9},{2,10},{3,11},{4,12},{5,13},{6,14},{7,15},{8,0},{9,1},... | collective-permute-start | bytes 442376 | tf_op jit(solution)/shard_map/ppermute | solution.py:86
  62.0 4.8 %collective-permute-start.6 = (bf16[8,16,1152]{2,1,0:T(8,128)(2,1)S(1)}, bf16[8,16,1152]{2,1,0:T(8,128)(2,1)S(1)}, u32[]{:S(2)}, u32[]{:S(2)}) collective-permute-start(bf16[8,16,1152]{2,1,0:T(8,128)(2,1)S(1)} %maximum_select_fusion.9), channel_id=1, source_target_pairs={{0,2},{1,3},{2,0},{3,1},{4,6},{5,7},{6,4},{7,5},{8,10},{9,11},{10,... | collective-permute-start | bytes 884744 | tf_op jit(solution)/shard_map/ppermute | solution.py:86
  66.9 3.0 %collective-permute-start.10 = (bf16[4,32,2176]{2,1,0:T(8,128)(2,1)S(1)}, bf16[4,32,2176]{2,1,0:T(8,128)(2,1)S(1)}, u32[]{:S(2)}, u32[]{:S(2)}) collective-permute-start(bf16[4,32,2176]{2,1,0:T(8,128)(2,1)S(1)} %maximum_select_fusion.6), channel_id=1, source_target_pairs={{0,128},{32,160},{64,192},{96,224},{128,0},{160,32},{192,64},{224,... | collective-permute-start | bytes 1671176 | tf_op jit(solution)/shard_map/ppermute | solution.py:86
  70.1 3.3 %collective-permute-done.3 = bf16[8,16,1152]{2,1,0:T(8,128)(2,1)S(1)} collective-permute-done((bf16[8,16,1152]{2,1,0:T(8,128)(2,1)S(1)}, bf16[8,16,1152]{2,1,0:T(8,128)(2,1)S(1)}, u32[]{:S(2)}, u32[]{:S(2)}) %collective-permute-start.3) | collective-permute-done | bytes 294944 | tf_op jit(solution)/shard_map/ppermute | solution.py:86
  73.5 2.8 %collective-permute-start.4 = (bf16[16,16,1152]{2,1,0:T(8,128)(2,1)S(1)}, bf16[16,16,1152]{2,1,0:T(8,128)(2,1)S(1)}, u32[]{:S(2)}, u32[]{:S(2)}) collective-permute-start(bf16[16,16,1152]{2,1,0:T(8,128)(2,1)S(1)} %maximum_select_fusion.4), channel_id=1, source_target_pairs={{0,8},{1,9},{2,10},{3,11},{4,12},{5,13},{6,14},{7,15},{8,0},{9,1},... | collective-permute-start | bytes 1769480 | tf_op jit(solution)/shard_map/ppermute | solution.py:86
  76.3 3.1 %collective-permute-done.6 = bf16[8,16,1152]{2,1,0:T(8,128)(2,1)S(1)} collective-permute-done((bf16[8,16,1152]{2,1,0:T(8,128)(2,1)S(1)}, bf16[8,16,1152]{2,1,0:T(8,128)(2,1)S(1)}, u32[]{:S(2)}, u32[]{:S(2)}) %collective-permute-start.6) | collective-permute-done | bytes 294944 | tf_op jit(solution)/shard_map/ppermute | solution.py:86
  85.6 4.0 %collective-permute-done.4 = bf16[16,16,1152]{2,1,0:T(8,128)(2,1)S(1)} collective-permute-done((bf16[16,16,1152]{2,1,0:T(8,128)(2,1)S(1)}, bf16[16,16,1152]{2,1,0:T(8,128)(2,1)S(1)}, u32[]{:S(2)}, u32[]{:S(2)}) %collective-permute-start.4) | collective-permute-done | bytes 589856 | tf_op jit(solution)/shard_map/ppermute | solution.py:86
  89.8 5.6 %collective-permute-done.7 = bf16[16,16,1152]{2,1,0:T(8,128)(2,1)S(1)} collective-permute-done((bf16[16,16,1152]{2,1,0:T(8,128)(2,1)S(1)}, bf16[16,16,1152]{2,1,0:T(8,128)(2,1)S(1)}, u32[]{:S(2)}, u32[]{:S(2)}) %collective-permute-start.7) | collective-permute-done | bytes 589856 | tf_op jit(solution)/shard_map/ppermute | solution.py:86
  118.2 6.1 %exponential_convert_fusion.3 = (bf16[512,1024]{1,0:T(8,128)(2,1)S(1)}, bf16[512,1024]{1,0:T(8,128)(2,1)S(1)}, bf16[512,1024]{1,0:T(8,128)(2,1)S(1)}, bf16[512,1024]{1,0:T(8,128)(2,1)S(1)}) fusion(f32[]{:T(128)} %bitcast.8, f32[]{:T(128)} %bitcast.15, f32[]{:T(128)} %bitcast.13, f32[]{:T(128)} %bitcast.11, bf16[1024,1152]{1,0:T(8,128)(2,1)S(1)} %bitcast.78, ...), kind=kOutput, calls=%fused_computation.21 | convolution fusion | flops 1080033280 | bytes 7348224 | tf_op jit(solution)/shard_map/dot_general | solution.py:41
  133.4 3.7 %collective-permute-done.13 = f32[4,512]{1,0:T(4,128)S(1)} collective-permute-done((f32[4,512]{1,0:T(4,128)S(1)}, f32[4,512]{1,0:T(4,128)S(1)}, u32[]{:S(2)}, u32[]{:S(2)}) %collective-permute-start.13) | collective-permute-done | bytes 8224 | tf_op jit(solution)/shard_map/ppermute | solution.py:117
  137.1 5.1 %collective-permute-start.14 = (f32[4,512]{1,0:T(4,128)S(1)}, f32[4,512]{1,0:T(4,128)S(1)}, u32[]{:S(2)}, u32[]{:S(2)}) collective-permute-start(f32[4,512]{1,0:T(4,128)S(1)} %fusion.66), channel_id=1, source_target_pairs={{0,4},{1,5},{2,6},{3,7},{4,0},{5,1},{6,2},{7,3},{8,12},{9,13},{10,... | collective-permute-start | bytes 24584 | tf_op jit(solution)/shard_map/ppermute | solution.py:117
  143.0 3.5 %collective-permute-done.14 = f32[4,512]{1,0:T(4,128)S(1)} collective-permute-done((f32[4,512]{1,0:T(4,128)S(1)}, f32[4,512]{1,0:T(4,128)S(1)}, u32[]{:S(2)}, u32[]{:S(2)}) %collective-permute-start.14) | collective-permute-done | bytes 8224 | tf_op jit(solution)/shard_map/ppermute | solution.py:117
  146.6 3.5 %collective-permute-start.15 = (f32[4,512]{1,0:T(4,128)S(1)}, f32[4,512]{1,0:T(4,128)S(1)}, u32[]{:S(2)}, u32[]{:S(2)}) collective-permute-start(f32[4,512]{1,0:T(4,128)S(1)} %add.183), channel_id=1, source_target_pairs={{0,8},{1,9},{2,10},{3,11},{4,12},{5,13},{6,14},{7,15},{8,0},{9,1},... | collective-permute-start | bytes 24584 | tf_op jit(solution)/shard_map/ppermute | solution.py:117
  152.1 5.1 %collective-permute-start.16 = (f32[4,512]{1,0:T(4,128)S(1)}, f32[4,512]{1,0:T(4,128)S(1)}, u32[]{:S(2)}, u32[]{:S(2)}) collective-permute-start(f32[4,512]{1,0:T(4,128)S(1)} %add.184), channel_id=1, source_target_pairs={{0,16},{1,17},{2,18},{3,19},{4,20},{5,21},{6,22},{7,23},{8,24},{9,... | collective-permute-start | bytes 24584 | tf_op jit(solution)/shard_map/ppermute | solution.py:117
  165.1 3.0 %collective-permute-done.18 = f32[2560]{0:T(1024)S(1)} collective-permute-done((f32[2560]{0:T(1024)S(1)}, f32[2560]{0:T(1024)S(1)}, u32[]{:S(2)}, u32[]{:S(2)}) %collective-permute-start.18) | collective-permute-done | bytes 10272 | tf_op jit(solution)/shard_map/ppermute | solution.py:124
  168.4 3.5 %collective-permute-start.19 = (f32[2304]{0:T(1024)S(1)}, f32[2304]{0:T(1024)S(1)}, u32[]{:S(2)}, u32[]{:S(2)}) collective-permute-start(f32[2304]{0:T(1024)S(1)} %pad_maximum_fusion.6), channel_id=1, source_target_pairs={{0,128},{32,160},{64,192},{96,224},{128,0},{160,32},{192,64},{224,... | collective-permute-start | bytes 27656 | tf_op jit(solution)/shard_map/ppermute | solution.py:124
  171.9 3.6 %collective-permute-done.19 = f32[2304]{0:T(1024)S(1)} collective-permute-done((f32[2304]{0:T(1024)S(1)}, f32[2304]{0:T(1024)S(1)}, u32[]{:S(2)}, u32[]{:S(2)}) %collective-permute-start.19) | collective-permute-done | bytes 9248 | tf_op jit(solution)/shard_map/ppermute | solution.py:124
  175.7 4.2 %collective-permute-start.20 = (f32[2176]{0:T(1024)S(1)}, f32[2176]{0:T(1024)S(1)}, u32[]{:S(2)}, u32[]{:S(2)}) collective-permute-start(f32[2176]{0:T(1024)S(1)} %pad_maximum_fusion.7), channel_id=1, source_target_pairs={{0,256},{32,288},{64,320},{96,352},{128,384},{160,416},{192,448},{... | collective-permute-start | bytes 26120 | tf_op jit(solution)/shard_map/ppermute | solution.py:124
  180.0 10.1 %collective-permute-done.20 = f32[2176]{0:T(1024)S(1)} collective-permute-done((f32[2176]{0:T(1024)S(1)}, f32[2176]{0:T(1024)S(1)}, u32[]{:S(2)}, u32[]{:S(2)}) %collective-permute-start.20) | collective-permute-done | bytes 8736 | tf_op jit(solution)/shard_map/ppermute | solution.py:124
  (154 shorter events, 67.0 us)
Async XLA Ops:
  5.7 46.4 %collective-permute-start.8 = (bf16[1,32,2176]{2,1,0:T(8,128)(2,1)S(1)}, bf16[1,32,2176]{2,1,0:T(8,128)(2,1)S(1)}, u32[]{:S(2)}, u32[]{:S(2)}) collective-permute-start(bf16[1,32,2176]{2,1,0:T(8,128)(2,1)S(1)} %maximum_bitcast_fusion), channel_id=1, source_target_pairs={{0,256},{32,288},{64,320},{96,352},{128,384},{160,416},{192,448},{... | collective-permute-start | bytes 417800 | tf_op jit(solution)/shard_map/ppermute | solution.py:86
  22.3 18.6 %collective-permute-start = (bf16[1,32,1152]{2,1,0:T(8,128)(2,1)S(1)}, bf16[1,32,1152]{2,1,0:T(8,128)(2,1)S(1)}, u32[]{:S(2)}, u32[]{:S(2)}) collective-permute-start(bf16[1,32,1152]{2,1,0:T(8,128)(2,1)S(1)} %maximum_bitcast_fusion.1), channel_id=1, source_target_pairs={{0,4},{1,5},{2,6},{3,7},{4,0},{5,1},{6,2},{7,3},{8,12},{9,13},{10,... | collective-permute-start | bytes 221192 | tf_op jit(solution)/shard_map/ppermute | solution.py:86
  40.9 29.1 %copy-start.6 = (s32[16]{0:T(128)S(1)}, s32[16]{0:T(128)}, u32[]{:S(2)}) copy-start(s32[16]{0:T(128)} %constant.128) | copy-start | bytes 196
  40.9 9.2 %collective-permute-start.1 = (bf16[2,32,1152]{2,1,0:T(8,128)(2,1)S(1)}, bf16[2,32,1152]{2,1,0:T(8,128)(2,1)S(1)}, u32[]{:S(2)}, u32[]{:S(2)}) collective-permute-start(bf16[2,32,1152]{2,1,0:T(8,128)(2,1)S(1)} %maximum_select_fusion.11), channel_id=1, source_target_pairs={{0,16},{1,17},{2,18},{3,19},{4,20},{5,21},{6,22},{7,23},{8,24},{9,... | collective-permute-start | bytes 442376 | tf_op jit(solution)/shard_map/ppermute | solution.py:86
  50.2 9.3 %collective-permute-start.2 = (bf16[4,16,1152]{2,1,0:T(8,128)(2,1)S(1)}, bf16[4,16,1152]{2,1,0:T(8,128)(2,1)S(1)}, u32[]{:S(2)}, u32[]{:S(2)}) collective-permute-start(bf16[4,16,1152]{2,1,0:T(8,128)(2,1)S(1)} %get-tuple-element.13), channel_id=1, source_target_pairs={{0,2},{1,3},{2,0},{3,1},{4,6},{5,7},{6,4},{7,5},{8,10},{9,11},{10,... | collective-permute-start | bytes 442376 | tf_op jit(solution)/shard_map/ppermute | solution.py:86
  52.1 14.7 %collective-permute-start.9 = (bf16[2,32,2176]{2,1,0:T(8,128)(2,1)S(1)}, bf16[2,32,2176]{2,1,0:T(8,128)(2,1)S(1)}, u32[]{:S(2)}, u32[]{:S(2)}) collective-permute-start(bf16[2,32,2176]{2,1,0:T(8,128)(2,1)S(1)} %maximum_select_fusion.10), channel_id=1, source_target_pairs={{0,64},{32,96},{64,0},{96,32},{128,192},{160,224},{192,128},{224,1... | collective-permute-start | bytes 835592 | tf_op jit(solution)/shard_map/ppermute | solution.py:86
  54.9 7.0 %collective-permute-start.5 = (bf16[4,16,1152]{2,1,0:T(8,128)(2,1)S(1)}, bf16[4,16,1152]{2,1,0:T(8,128)(2,1)S(1)}, u32[]{:S(2)}, u32[]{:S(2)}) collective-permute-start(bf16[4,16,1152]{2,1,0:T(8,128)(2,1)S(1)} %get-tuple-element.14), channel_id=1, source_target_pairs={{0,8},{1,9},{2,10},{3,11},{4,12},{5,13},{6,14},{7,15},{8,0},{9,1},... | collective-permute-start | bytes 442376 | tf_op jit(solution)/shard_map/ppermute | solution.py:86
  59.5 13.9 %collective-permute-start.3 = (bf16[8,16,1152]{2,1,0:T(8,128)(2,1)S(1)}, bf16[8,16,1152]{2,1,0:T(8,128)(2,1)S(1)}, u32[]{:S(2)}, u32[]{:S(2)}) collective-permute-start(bf16[8,16,1152]{2,1,0:T(8,128)(2,1)S(1)} %maximum_select_fusion.8), channel_id=1, source_target_pairs={{0,1},{1,0},{2,3},{3,2},{4,5},{5,4},{6,7},{7,6},{8,9},{9,8},{10,11... | collective-permute-start | bytes 884744 | tf_op jit(solution)/shard_map/ppermute | solution.py:86
  62.0 17.4 %collective-permute-start.6 = (bf16[8,16,1152]{2,1,0:T(8,128)(2,1)S(1)}, bf16[8,16,1152]{2,1,0:T(8,128)(2,1)S(1)}, u32[]{:S(2)}, u32[]{:S(2)}) collective-permute-start(bf16[8,16,1152]{2,1,0:T(8,128)(2,1)S(1)} %maximum_select_fusion.9), channel_id=1, source_target_pairs={{0,2},{1,3},{2,0},{3,1},{4,6},{5,7},{6,4},{7,5},{8,10},{9,11},{10,... | collective-permute-start | bytes 884744 | tf_op jit(solution)/shard_map/ppermute | solution.py:86
  66.9 15.4 %collective-permute-start.10 = (bf16[4,32,2176]{2,1,0:T(8,128)(2,1)S(1)}, bf16[4,32,2176]{2,1,0:T(8,128)(2,1)S(1)}, u32[]{:S(2)}, u32[]{:S(2)}) collective-permute-start(bf16[4,32,2176]{2,1,0:T(8,128)(2,1)S(1)} %maximum_select_fusion.6), channel_id=1, source_target_pairs={{0,128},{32,160},{64,192},{96,224},{128,0},{160,32},{192,64},{224,... | collective-permute-start | bytes 1671176 | tf_op jit(solution)/shard_map/ppermute | solution.py:86
  73.5 16.1 %collective-permute-start.4 = (bf16[16,16,1152]{2,1,0:T(8,128)(2,1)S(1)}, bf16[16,16,1152]{2,1,0:T(8,128)(2,1)S(1)}, u32[]{:S(2)}, u32[]{:S(2)}) collective-permute-start(bf16[16,16,1152]{2,1,0:T(8,128)(2,1)S(1)} %maximum_select_fusion.4), channel_id=1, source_target_pairs={{0,8},{1,9},{2,10},{3,11},{4,12},{5,13},{6,14},{7,15},{8,0},{9,1},... | collective-permute-start | bytes 1769480 | tf_op jit(solution)/shard_map/ppermute | solution.py:86
  79.5 15.9 %collective-permute-start.7 = (bf16[16,16,1152]{2,1,0:T(8,128)(2,1)S(1)}, bf16[16,16,1152]{2,1,0:T(8,128)(2,1)S(1)}, u32[]{:S(2)}, u32[]{:S(2)}) collective-permute-start(bf16[16,16,1152]{2,1,0:T(8,128)(2,1)S(1)} %maximum_select_fusion.5), channel_id=1, source_target_pairs={{0,1},{1,0},{2,3},{3,2},{4,5},{5,4},{6,7},{7,6},{8,9},{9,8},{10,11... | collective-permute-start | bytes 1769480 | tf_op jit(solution)/shard_map/ppermute | solution.py:86
  83.5 19.3 %collective-permute-start.11 = (bf16[8,32,2176]{2,1,0:T(8,128)(2,1)}, bf16[8,32,2176]{2,1,0:T(8,128)(2,1)}, u32[]{:S(2)}, u32[]{:S(2)}) collective-permute-start(bf16[8,32,2176]{2,1,0:T(8,128)(2,1)} %maximum_select_fusion.3), channel_id=1, source_target_pairs={{0,32},{32,0},{64,96},{96,64},{128,160},{160,128},{192,224},{224,1... | collective-permute-start | bytes 3342344 | tf_op jit(solution)/shard_map/ppermute | solution.py:86
  99.5 1.8 copy-start
  109.1 2.6 %copy-start.4 = (bf16[1024,511]{0,1:T(8,128)(2,1)S(1)}, bf16[1024,511]{0,1:T(8,128)(2,1)}, u32[]{:S(2)}) copy-start(bf16[1024,511]{0,1:T(8,128)(2,1)} %fusion.9) | copy-start | bytes 3139588
  125.1 5.5 %collective-permute-start.12 = (f32[4,512]{1,0:T(4,128)S(1)}, f32[4,512]{1,0:T(4,128)S(1)}, u32[]{:S(2)}, u32[]{:S(2)}) collective-permute-start(f32[4,512]{1,0:T(4,128)S(1)} %pad_maximum_fusion.8), channel_id=1, source_target_pairs={{0,1},{1,0},{2,3},{3,2},{4,5},{5,4},{6,7},{7,6},{8,9},{9,8},{10,11... | collective-permute-start | bytes 24584 | tf_op jit(solution)/shard_map/ppermute | solution.py:117
  130.6 6.4 %collective-permute-start.13 = (f32[4,512]{1,0:T(4,128)S(1)}, f32[4,512]{1,0:T(4,128)S(1)}, u32[]{:S(2)}, u32[]{:S(2)}) collective-permute-start(f32[4,512]{1,0:T(4,128)S(1)} %fusion.55), channel_id=1, source_target_pairs={{0,2},{1,3},{2,0},{3,1},{4,6},{5,7},{6,4},{7,5},{8,10},{9,11},{10,... | collective-permute-start | bytes 24584 | tf_op jit(solution)/shard_map/ppermute | solution.py:117
  137.1 9.5 %collective-permute-start.14 = (f32[4,512]{1,0:T(4,128)S(1)}, f32[4,512]{1,0:T(4,128)S(1)}, u32[]{:S(2)}, u32[]{:S(2)}) collective-permute-start(f32[4,512]{1,0:T(4,128)S(1)} %fusion.66), channel_id=1, source_target_pairs={{0,4},{1,5},{2,6},{3,7},{4,0},{5,1},{6,2},{7,3},{8,12},{9,13},{10,... | collective-permute-start | bytes 24584 | tf_op jit(solution)/shard_map/ppermute | solution.py:117
  146.6 5.5 %collective-permute-start.15 = (f32[4,512]{1,0:T(4,128)S(1)}, f32[4,512]{1,0:T(4,128)S(1)}, u32[]{:S(2)}, u32[]{:S(2)}) collective-permute-start(f32[4,512]{1,0:T(4,128)S(1)} %add.183), channel_id=1, source_target_pairs={{0,8},{1,9},{2,10},{3,11},{4,12},{5,13},{6,14},{7,15},{8,0},{9,1},... | collective-permute-start | bytes 24584 | tf_op jit(solution)/shard_map/ppermute | solution.py:117
  152.1 7.0 %collective-permute-start.16 = (f32[4,512]{1,0:T(4,128)S(1)}, f32[4,512]{1,0:T(4,128)S(1)}, u32[]{:S(2)}, u32[]{:S(2)}) collective-permute-start(f32[4,512]{1,0:T(4,128)S(1)} %add.184), channel_id=1, source_target_pairs={{0,16},{1,17},{2,18},{3,19},{4,20},{5,21},{6,22},{7,23},{8,24},{9,... | collective-permute-start | bytes 24584 | tf_op jit(solution)/shard_map/ppermute | solution.py:117
  159.2 3.1 %collective-permute-start.17 = (f32[3072]{0:T(1024)S(1)}, f32[3072]{0:T(1024)S(1)}, u32[]{:S(2)}, u32[]{:S(2)}) collective-permute-start(f32[3072]{0:T(1024)S(1)} %pad_maximum_fusion.4), channel_id=1, source_target_pairs={{0,32},{32,0},{64,96},{96,64},{128,160},{160,128},{192,224},{224,1... | collective-permute-start | bytes 36872 | tf_op jit(solution)/shard_map/ppermute | solution.py:124
  162.5 5.6 %collective-permute-start.18 = (f32[2560]{0:T(1024)S(1)}, f32[2560]{0:T(1024)S(1)}, u32[]{:S(2)}, u32[]{:S(2)}) collective-permute-start(f32[2560]{0:T(1024)S(1)} %pad_maximum_fusion.5), channel_id=1, source_target_pairs={{0,64},{32,96},{64,0},{96,32},{128,192},{160,224},{192,128},{224,1... | collective-permute-start | bytes 30728 | tf_op jit(solution)/shard_map/ppermute | solution.py:124
  168.4 7.1 %collective-permute-start.19 = (f32[2304]{0:T(1024)S(1)}, f32[2304]{0:T(1024)S(1)}, u32[]{:S(2)}, u32[]{:S(2)}) collective-permute-start(f32[2304]{0:T(1024)S(1)} %pad_maximum_fusion.6), channel_id=1, source_target_pairs={{0,128},{32,160},{64,192},{96,224},{128,0},{160,32},{192,64},{224,... | collective-permute-start | bytes 27656 | tf_op jit(solution)/shard_map/ppermute | solution.py:124
  175.7 14.4 %collective-permute-start.20 = (f32[2176]{0:T(1024)S(1)}, f32[2176]{0:T(1024)S(1)}, u32[]{:S(2)}, u32[]{:S(2)}) collective-permute-start(f32[2176]{0:T(1024)S(1)} %pad_maximum_fusion.7), channel_id=1, source_target_pairs={{0,256},{32,288},{64,320},{96,352},{128,384},{160,416},{192,448},{... | collective-permute-start | bytes 26120 | tf_op jit(solution)/shard_map/ppermute | solution.py:124
  (4 other events, 6.1 us)

commit v13 on v11

--- a/solution.py
+++ b/solution.py
@@ -78,12 +78,15 @@
     return rows, make_vectors(labels, sign_words), join3(buf[:, at:at + 3]), join3(buf[:, at + 3:at + 6])
 
 
-def xor_gather(x, axis, n, bits, buf=None):
+def xor_gather(x, axis, n, bits, buf=None, ordered=True):
     idx = lax.axis_index(axis)
     buf = x[None] if buf is None else buf
     for b in bits:
         k = 1 << b
         other = lax.ppermute(buf, axis, [(i, i ^ k) for i in range(n)])
+        if not ordered:
+            buf = jnp.concatenate([buf, other])
+            continue
         lo = (idx & k) == 0
         buf = jnp.where(lo, jnp.concatenate([buf, other]), jnp.concatenate([other, buf]))
     order = [sum(((t >> j) & 1) << b for j, b in enumerate(bits)) for t in range(n)]
@@ -143,13 +146,13 @@
     dev_nbits = n_dev.bit_length() - 1
     joint = [b for b in DEV_JOINT if b < dev_nbits]
     col_buf, col_order = xor_gather(own_wide, "grp", n_grp, grp_bits)
-    blk_buf, _ = xor_gather(own, "dev", n_dev, joint)
+    blk_buf, _ = xor_gather(own, "dev", n_dev, joint, ordered=False)
     half = rows_here // 2
     parts = []
     for h, o in zip((blk_buf[:, :half], blk_buf[:, half:]), DEV_ORDERS):
         rest = axis_order(n_dev, [b for b in o if b not in joint])
         rest = [b for b in rest if b not in joint]
-        parts.append(xor_gather(None, "dev", n_dev, rest, buf=h)[0])
+        parts.append(xor_gather(None, "dev", n_dev, rest, buf=h, ordered=False)[0])
     blk_buf = jnp.concatenate(parts, axis=1)
 
     col_buf = col_buf.reshape(n_grp * rows_here, -1)

time: 193 us -> 195 us (1.010)
    concatenate x1, other arithmetic: 0.2 us -> 2.39 us  [body(): blk_buf = jnp.concatenate(parts, axis=1)]
    select_n x12 -> x4, other arithmetic: 4.8 us -> 4.05 us  [xor_gather(): jnp.where(lo, jnp.concatenate([buf, other]), jnp.concatenate([other, buf]))]
  transfers between devices with their start and end apart: 21 -> 21, of which waited for: 18 -> 18; matrix products, arithmetic and copies ran while one was open for 7% -> 8% of each run, Pallas kernels for 0% -> 0%
where the time goes in v13:
time: 195 us; the launch traced here: 194 us
  starting transfers between devices  79.8 us (41%)
  waiting for transfers between devices  66.3 us (34%)
  other arithmetic  18.7 us (10%)
  matrix products  18.3 us (9%)
  local copies, waits for them, and re-layouts  9.25 us (5%)
    ppermute x12, starting transfers between devices, xor_gather(): other = lax.ppermute(buf, axis, [(i, i ^ k) for i in range(n)])  49.8 us
    ppermute x12, waiting for transfers between devices, xor_gather(): other = lax.ppermute(buf, axis, [(i, i ^ k) for i in range(n)])  35.5 us
    ppermute x5, starting transfers between devices, xor_sum(): x = x + lax.ppermute(x, a, pairs)  18 us
    ppermute x4, waiting for transfers between devices, xor_sum(): got = lax.ppermute(jnp.concatenate([x.ravel(), send.ravel()]), a, pairs)  18 us
    ppermute x5, waiting for transfers between devices, xor_sum(): x = x + lax.ppermute(x, a, pairs)  12.9 us
    ppermute x4, starting transfers between devices, xor_sum(): got = lax.ppermute(jnp.concatenate([x.ravel(), send.ravel()]), a, pairs)  12.1 us
    dot_general x2, matrix products, distances(): lax.dot_general(left, right, (((1,), (1,)), ((), ())), preferred_element_...  8.69 us
    dot_general x4, matrix products, body(): product = jnp.dot(kern, col_vec, preferred_element_type=jnp.float32)  6.5 us
  transfers between devices with their start and end apart: 21, of which 18 were waited for; matrix products, arithmetic and copies ran while one was open for 8% of the time, Pallas kernels for 0%

profile of v13, /device:TPU:6, one launch (start us, length us, event | category | flops | bytes accessed | tf_op | source)
XLA Modules:
  0.0 193.7 jit_solution(15538668047617587940)
XLA Ops:
  5.7 15.7 %collective-permute-start.8 = (bf16[1,32,2176]{2,1,0:T(8,128)(2,1)S(1)}, bf16[1,32,2176]{2,1,0:T(8,128)(2,1)S(1)}, u32[]{:S(2)}, u32[]{:S(2)}) collective-permute-start(bf16[1,32,2176]{2,1,0:T(8,128)(2,1)S(1)} %maximum_bitcast_fusion), channel_id=1, source_target_pairs={{0,256},{32,288},{64,320},{96,352},{128,384},{160,416},{192,448},{... | collective-permute-start | bytes 417800 | tf_op jit(solution)/shard_map/ppermute | solution.py:86
  22.3 4.3 %collective-permute-start = (bf16[1,32,1152]{2,1,0:T(8,128)(2,1)S(1)}, bf16[1,32,1152]{2,1,0:T(8,128)(2,1)S(1)}, u32[]{:S(2)}, u32[]{:S(2)}) collective-permute-start(bf16[1,32,1152]{2,1,0:T(8,128)(2,1)S(1)} %maximum_bitcast_fusion.1), channel_id=1, source_target_pairs={{0,4},{1,5},{2,6},{3,7},{4,0},{5,1},{6,2},{7,3},{8,12},{9,13},{10,... | collective-permute-start | bytes 221192 | tf_op jit(solution)/shard_map/ppermute | solution.py:86
  27.6 13.3 %collective-permute-done = bf16[1,32,1152]{2,1,0:T(8,128)(2,1)S(1)} collective-permute-done((bf16[1,32,1152]{2,1,0:T(8,128)(2,1)S(1)}, bf16[1,32,1152]{2,1,0:T(8,128)(2,1)S(1)}, u32[]{:S(2)}, u32[]{:S(2)}) %collective-permute-start) | collective-permute-done | bytes 73760 | tf_op jit(solution)/shard_map/ppermute | solution.py:86
  40.9 5.1 %collective-permute-start.1 = (bf16[2,32,1152]{2,1,0:T(8,128)(2,1)S(1)}, bf16[2,32,1152]{2,1,0:T(8,128)(2,1)S(1)}, u32[]{:S(2)}, u32[]{:S(2)}) collective-permute-start(bf16[2,32,1152]{2,1,0:T(8,128)(2,1)S(1)} %pad_maximum_fusion.7), channel_id=1, source_target_pairs={{0,16},{1,17},{2,18},{3,19},{4,20},{5,21},{6,22},{7,23},{8,24},{9,... | collective-permute-start | bytes 442376 | tf_op jit(solution)/shard_map/ppermute | solution.py:86
  46.0 4.0 %collective-permute-done.1 = bf16[2,32,1152]{2,1,0:T(8,128)(2,1)S(1)} collective-permute-done((bf16[2,32,1152]{2,1,0:T(8,128)(2,1)S(1)}, bf16[2,32,1152]{2,1,0:T(8,128)(2,1)S(1)}, u32[]{:S(2)}, u32[]{:S(2)}) %collective-permute-start.1) | collective-permute-done | bytes 147488 | tf_op jit(solution)/shard_map/ppermute | solution.py:86
  54.9 3.5 %collective-permute-start.5 = (bf16[4,16,1152]{2,1,0:T(8,128)(2,1)S(1)}, bf16[4,16,1152]{2,1,0:T(8,128)(2,1)S(1)}, u32[]{:S(2)}, u32[]{:S(2)}) collective-permute-start(bf16[4,16,1152]{2,1,0:T(8,128)(2,1)S(1)} %get-tuple-element.14), channel_id=1, source_target_pairs={{0,8},{1,9},{2,10},{3,11},{4,12},{5,13},{6,14},{7,15},{8,0},{9,1},... | collective-permute-start | bytes 442376 | tf_op jit(solution)/shard_map/ppermute | solution.py:86
  61.9 4.8 %collective-permute-start.6 = (bf16[8,16,1152]{2,1,0:T(8,128)(2,1)S(1)}, bf16[8,16,1152]{2,1,0:T(8,128)(2,1)S(1)}, u32[]{:S(2)}, u32[]{:S(2)}) collective-permute-start(bf16[8,16,1152]{2,1,0:T(8,128)(2,1)S(1)} %pad_maximum_fusion.6), channel_id=1, source_target_pairs={{0,2},{1,3},{2,0},{3,1},{4,6},{5,7},{6,4},{7,5},{8,10},{9,11},{10,... | collective-permute-start | bytes 884744 | tf_op jit(solution)/shard_map/ppermute | solution.py:86
  66.9 3.0 %collective-permute-start.10 = (bf16[4,32,2176]{2,1,0:T(8,128)(2,1)S(1)}, bf16[4,32,2176]{2,1,0:T(8,128)(2,1)S(1)}, u32[]{:S(2)}, u32[]{:S(2)}) collective-permute-start(bf16[4,32,2176]{2,1,0:T(8,128)(2,1)S(1)} %maximum_select_fusion.2), channel_id=1, source_target_pairs={{0,128},{32,160},{64,192},{96,224},{128,0},{160,32},{192,64},{224,... | collective-permute-start | bytes 1671176 | tf_op jit(solution)/shard_map/ppermute | solution.py:86
  69.9 3.5 %collective-permute-done.3 = bf16[8,16,1152]{2,1,0:T(8,128)(2,1)S(1)} collective-permute-done((bf16[8,16,1152]{2,1,0:T(8,128)(2,1)S(1)}, bf16[8,16,1152]{2,1,0:T(8,128)(2,1)S(1)}, u32[]{:S(2)}, u32[]{:S(2)}) %collective-permute-start.3) | collective-permute-done | bytes 294944 | tf_op jit(solution)/shard_map/ppermute | solution.py:86
  73.5 2.8 %collective-permute-start.4 = (bf16[16,16,1152]{2,1,0:T(8,128)(2,1)S(1)}, bf16[16,16,1152]{2,1,0:T(8,128)(2,1)S(1)}, u32[]{:S(2)}, u32[]{:S(2)}) collective-permute-start(bf16[16,16,1152]{2,1,0:T(8,128)(2,1)S(1)} %pad_maximum_fusion.1), channel_id=1, source_target_pairs={{0,8},{1,9},{2,10},{3,11},{4,12},{5,13},{6,14},{7,15},{8,0},{9,1},... | collective-permute-start | bytes 1769480 | tf_op jit(solution)/shard_map/ppermute | solution.py:86
  76.3 3.1 %collective-permute-done.6 = bf16[8,16,1152]{2,1,0:T(8,128)(2,1)S(1)} collective-permute-done((bf16[8,16,1152]{2,1,0:T(8,128)(2,1)S(1)}, bf16[8,16,1152]{2,1,0:T(8,128)(2,1)S(1)}, u32[]{:S(2)}, u32[]{:S(2)}) %collective-permute-start.6) | collective-permute-done | bytes 294944 | tf_op jit(solution)/shard_map/ppermute | solution.py:86
  85.6 4.0 %collective-permute-done.4 = bf16[16,16,1152]{2,1,0:T(8,128)(2,1)S(1)} collective-permute-done((bf16[16,16,1152]{2,1,0:T(8,128)(2,1)S(1)}, bf16[16,16,1152]{2,1,0:T(8,128)(2,1)S(1)}, u32[]{:S(2)}, u32[]{:S(2)}) %collective-permute-start.4) | collective-permute-done | bytes 589856 | tf_op jit(solution)/shard_map/ppermute | solution.py:86
  89.6 5.8 %collective-permute-done.7 = bf16[16,16,1152]{2,1,0:T(8,128)(2,1)S(1)} collective-permute-done((bf16[16,16,1152]{2,1,0:T(8,128)(2,1)S(1)}, bf16[16,16,1152]{2,1,0:T(8,128)(2,1)S(1)}, u32[]{:S(2)}, u32[]{:S(2)}) %collective-permute-start.7) | collective-permute-done | bytes 589856 | tf_op jit(solution)/shard_map/ppermute | solution.py:86
  120.1 6.1 %exponential_convert_fusion.3 = (bf16[512,1024]{1,0:T(8,128)(2,1)S(1)}, bf16[512,1024]{1,0:T(8,128)(2,1)S(1)}, bf16[512,1024]{1,0:T(8,128)(2,1)S(1)}, bf16[512,1024]{1,0:T(8,128)(2,1)S(1)}) fusion(f32[]{:T(128)} %bitcast.8, f32[]{:T(128)} %bitcast.15, f32[]{:T(128)} %bitcast.13, f32[]{:T(128)} %bitcast.11, bf16[1024,1152]{1,0:T(8,128)(2,1)S(1)} %bitcast.78, ...), kind=kOutput, calls=%fused_computation.21 | convolution fusion | flops 1080033280 | bytes 7348224 | tf_op jit(solution)/shard_map/dot_general | solution.py:41
  135.3 3.7 %collective-permute-done.13 = f32[4,512]{1,0:T(4,128)S(1)} collective-permute-done((f32[4,512]{1,0:T(4,128)S(1)}, f32[4,512]{1,0:T(4,128)S(1)}, u32[]{:S(2)}, u32[]{:S(2)}) %collective-permute-start.13) | collective-permute-done | bytes 8224 | tf_op jit(solution)/shard_map/ppermute | solution.py:120
  139.0 5.1 %collective-permute-start.14 = (f32[4,512]{1,0:T(4,128)S(1)}, f32[4,512]{1,0:T(4,128)S(1)}, u32[]{:S(2)}, u32[]{:S(2)}) collective-permute-start(f32[4,512]{1,0:T(4,128)S(1)} %fusion.66), channel_id=1, source_target_pairs={{0,4},{1,5},{2,6},{3,7},{4,0},{5,1},{6,2},{7,3},{8,12},{9,13},{10,... | collective-permute-start | bytes 24584 | tf_op jit(solution)/shard_map/ppermute | solution.py:120
  144.9 3.5 %collective-permute-done.14 = f32[4,512]{1,0:T(4,128)S(1)} collective-permute-done((f32[4,512]{1,0:T(4,128)S(1)}, f32[4,512]{1,0:T(4,128)S(1)}, u32[]{:S(2)}, u32[]{:S(2)}) %collective-permute-start.14) | collective-permute-done | bytes 8224 | tf_op jit(solution)/shard_map/ppermute | solution.py:120
  148.5 3.5 %collective-permute-start.15 = (f32[4,512]{1,0:T(4,128)S(1)}, f32[4,512]{1,0:T(4,128)S(1)}, u32[]{:S(2)}, u32[]{:S(2)}) collective-permute-start(f32[4,512]{1,0:T(4,128)S(1)} %add.183), channel_id=1, source_target_pairs={{0,8},{1,9},{2,10},{3,11},{4,12},{5,13},{6,14},{7,15},{8,0},{9,1},... | collective-permute-start | bytes 24584 | tf_op jit(solution)/shard_map/ppermute | solution.py:120
  154.1 5.1 %collective-permute-start.16 = (f32[4,512]{1,0:T(4,128)S(1)}, f32[4,512]{1,0:T(4,128)S(1)}, u32[]{:S(2)}, u32[]{:S(2)}) collective-permute-start(f32[4,512]{1,0:T(4,128)S(1)} %add.184), channel_id=1, source_target_pairs={{0,16},{1,17},{2,18},{3,19},{4,20},{5,21},{6,22},{7,23},{8,24},{9,... | collective-permute-start | bytes 24584 | tf_op jit(solution)/shard_map/ppermute | solution.py:120
  167.0 3.1 %collective-permute-done.18 = f32[2560]{0:T(1024)S(1)} collective-permute-done((f32[2560]{0:T(1024)S(1)}, f32[2560]{0:T(1024)S(1)}, u32[]{:S(2)}, u32[]{:S(2)}) %collective-permute-start.18) | collective-permute-done | bytes 10272 | tf_op jit(solution)/shard_map/ppermute | solution.py:127
  170.3 3.4 %collective-permute-start.19 = (f32[2304]{0:T(1024)S(1)}, f32[2304]{0:T(1024)S(1)}, u32[]{:S(2)}, u32[]{:S(2)}) collective-permute-start(f32[2304]{0:T(1024)S(1)} %pad_maximum_fusion.11), channel_id=1, source_target_pairs={{0,128},{32,160},{64,192},{96,224},{128,0},{160,32},{192,64},{224,... | collective-permute-start | bytes 27656 | tf_op jit(solution)/shard_map/ppermute | solution.py:127
  173.8 3.7 %collective-permute-done.19 = f32[2304]{0:T(1024)S(1)} collective-permute-done((f32[2304]{0:T(1024)S(1)}, f32[2304]{0:T(1024)S(1)}, u32[]{:S(2)}, u32[]{:S(2)}) %collective-permute-start.19) | collective-permute-done | bytes 9248 | tf_op jit(solution)/shard_map/ppermute | solution.py:127
  177.7 4.2 %collective-permute-start.20 = (f32[2176]{0:T(1024)S(1)}, f32[2176]{0:T(1024)S(1)}, u32[]{:S(2)}, u32[]{:S(2)}) collective-permute-start(f32[2176]{0:T(1024)S(1)} %pad_maximum_fusion.12), channel_id=1, source_target_pairs={{0,256},{32,288},{64,320},{96,352},{128,384},{160,416},{192,448},{... | collective-permute-start | bytes 26120 | tf_op jit(solution)/shard_map/ppermute | solution.py:127
  181.9 10.1 %collective-permute-done.20 = f32[2176]{0:T(1024)S(1)} collective-permute-done((f32[2176]{0:T(1024)S(1)}, f32[2176]{0:T(1024)S(1)}, u32[]{:S(2)}, u32[]{:S(2)}) %collective-permute-start.20) | collective-permute-done | bytes 8736 | tf_op jit(solution)/shard_map/ppermute | solution.py:127
  (152 shorter events, 68.1 us)
Async XLA Ops:
  5.7 46.4 %collective-permute-start.8 = (bf16[1,32,2176]{2,1,0:T(8,128)(2,1)S(1)}, bf16[1,32,2176]{2,1,0:T(8,128)(2,1)S(1)}, u32[]{:S(2)}, u32[]{:S(2)}) collective-permute-start(bf16[1,32,2176]{2,1,0:T(8,128)(2,1)S(1)} %maximum_bitcast_fusion), channel_id=1, source_target_pairs={{0,256},{32,288},{64,320},{96,352},{128,384},{160,416},{192,448},{... | collective-permute-start | bytes 417800 | tf_op jit(solution)/shard_map/ppermute | solution.py:86
  22.3 18.6 %collective-permute-start = (bf16[1,32,1152]{2,1,0:T(8,128)(2,1)S(1)}, bf16[1,32,1152]{2,1,0:T(8,128)(2,1)S(1)}, u32[]{:S(2)}, u32[]{:S(2)}) collective-permute-start(bf16[1,32,1152]{2,1,0:T(8,128)(2,1)S(1)} %maximum_bitcast_fusion.1), channel_id=1, source_target_pairs={{0,4},{1,5},{2,6},{3,7},{4,0},{5,1},{6,2},{7,3},{8,12},{9,13},{10,... | collective-permute-start | bytes 221192 | tf_op jit(solution)/shard_map/ppermute | solution.py:86
  40.9 9.2 %collective-permute-start.1 = (bf16[2,32,1152]{2,1,0:T(8,128)(2,1)S(1)}, bf16[2,32,1152]{2,1,0:T(8,128)(2,1)S(1)}, u32[]{:S(2)}, u32[]{:S(2)}) collective-permute-start(bf16[2,32,1152]{2,1,0:T(8,128)(2,1)S(1)} %pad_maximum_fusion.7), channel_id=1, source_target_pairs={{0,16},{1,17},{2,18},{3,19},{4,20},{5,21},{6,22},{7,23},{8,24},{9,... | collective-permute-start | bytes 442376 | tf_op jit(solution)/shard_map/ppermute | solution.py:86
  50.1 9.3 %collective-permute-start.2 = (bf16[4,16,1152]{2,1,0:T(8,128)(2,1)S(1)}, bf16[4,16,1152]{2,1,0:T(8,128)(2,1)S(1)}, u32[]{:S(2)}, u32[]{:S(2)}) collective-permute-start(bf16[4,16,1152]{2,1,0:T(8,128)(2,1)S(1)} %get-tuple-element.13), channel_id=1, source_target_pairs={{0,2},{1,3},{2,0},{3,1},{4,6},{5,7},{6,4},{7,5},{8,10},{9,11},{10,... | collective-permute-start | bytes 442376 | tf_op jit(solution)/shard_map/ppermute | solution.py:86
  52.1 14.7 %collective-permute-start.9 = (bf16[2,32,2176]{2,1,0:T(8,128)(2,1)S(1)}, bf16[2,32,2176]{2,1,0:T(8,128)(2,1)S(1)}, u32[]{:S(2)}, u32[]{:S(2)}) collective-permute-start(bf16[2,32,2176]{2,1,0:T(8,128)(2,1)S(1)} %maximum_select_fusion.3), channel_id=1, source_target_pairs={{0,64},{32,96},{64,0},{96,32},{128,192},{160,224},{192,128},{224,1... | collective-permute-start | bytes 835592 | tf_op jit(solution)/shard_map/ppermute | solution.py:86
  54.9 7.0 %collective-permute-start.5 = (bf16[4,16,1152]{2,1,0:T(8,128)(2,1)S(1)}, bf16[4,16,1152]{2,1,0:T(8,128)(2,1)S(1)}, u32[]{:S(2)}, u32[]{:S(2)}) collective-permute-start(bf16[4,16,1152]{2,1,0:T(8,128)(2,1)S(1)} %get-tuple-element.14), channel_id=1, source_target_pairs={{0,8},{1,9},{2,10},{3,11},{4,12},{5,13},{6,14},{7,15},{8,0},{9,1},... | collective-permute-start | bytes 442376 | tf_op jit(solution)/shard_map/ppermute | solution.py:86
  59.5 21.9 %copy-start.6 = (s32[16]{0:T(128)S(1)}, s32[16]{0:T(128)}, u32[]{:S(2)}) copy-start(s32[16]{0:T(128)} %constant.124) | copy-start | bytes 196
  59.5 13.9 %collective-permute-start.3 = (bf16[8,16,1152]{2,1,0:T(8,128)(2,1)S(1)}, bf16[8,16,1152]{2,1,0:T(8,128)(2,1)S(1)}, u32[]{:S(2)}, u32[]{:S(2)}) collective-permute-start(bf16[8,16,1152]{2,1,0:T(8,128)(2,1)S(1)} %pad_maximum_fusion.5), channel_id=1, source_target_pairs={{0,1},{1,0},{2,3},{3,2},{4,5},{5,4},{6,7},{7,6},{8,9},{9,8},{10,11... | collective-permute-start | bytes 884744 | tf_op jit(solution)/shard_map/ppermute | solution.py:86
  61.9 17.4 %collective-permute-start.6 = (bf16[8,16,1152]{2,1,0:T(8,128)(2,1)S(1)}, bf16[8,16,1152]{2,1,0:T(8,128)(2,1)S(1)}, u32[]{:S(2)}, u32[]{:S(2)}) collective-permute-start(bf16[8,16,1152]{2,1,0:T(8,128)(2,1)S(1)} %pad_maximum_fusion.6), channel_id=1, source_target_pairs={{0,2},{1,3},{2,0},{3,1},{4,6},{5,7},{6,4},{7,5},{8,10},{9,11},{10,... | collective-permute-start | bytes 884744 | tf_op jit(solution)/shard_map/ppermute | solution.py:86
  66.9 15.4 %collective-permute-start.10 = (bf16[4,32,2176]{2,1,0:T(8,128)(2,1)S(1)}, bf16[4,32,2176]{2,1,0:T(8,128)(2,1)S(1)}, u32[]{:S(2)}, u32[]{:S(2)}) collective-permute-start(bf16[4,32,2176]{2,1,0:T(8,128)(2,1)S(1)} %maximum_select_fusion.2), channel_id=1, source_target_pairs={{0,128},{32,160},{64,192},{96,224},{128,0},{160,32},{192,64},{224,... | collective-permute-start | bytes 1671176 | tf_op jit(solution)/shard_map/ppermute | solution.py:86
  73.5 16.1 %collective-permute-start.4 = (bf16[16,16,1152]{2,1,0:T(8,128)(2,1)S(1)}, bf16[16,16,1152]{2,1,0:T(8,128)(2,1)S(1)}, u32[]{:S(2)}, u32[]{:S(2)}) collective-permute-start(bf16[16,16,1152]{2,1,0:T(8,128)(2,1)S(1)} %pad_maximum_fusion.1), channel_id=1, source_target_pairs={{0,8},{1,9},{2,10},{3,11},{4,12},{5,13},{6,14},{7,15},{8,0},{9,1},... | collective-permute-start | bytes 1769480 | tf_op jit(solution)/shard_map/ppermute | solution.py:86
  79.5 15.9 %collective-permute-start.7 = (bf16[16,16,1152]{2,1,0:T(8,128)(2,1)S(1)}, bf16[16,16,1152]{2,1,0:T(8,128)(2,1)S(1)}, u32[]{:S(2)}, u32[]{:S(2)}) collective-permute-start(bf16[16,16,1152]{2,1,0:T(8,128)(2,1)S(1)} %pad_maximum_fusion.2), channel_id=1, source_target_pairs={{0,1},{1,0},{2,3},{3,2},{4,5},{5,4},{6,7},{7,6},{8,9},{9,8},{10,11... | collective-permute-start | bytes 1769480 | tf_op jit(solution)/shard_map/ppermute | solution.py:86
  83.5 21.3 %collective-permute-start.11 = (bf16[8,32,2176]{2,1,0:T(8,128)(2,1)}, bf16[8,32,2176]{2,1,0:T(8,128)(2,1)}, u32[]{:S(2)}, u32[]{:S(2)}) collective-permute-start(bf16[8,32,2176]{2,1,0:T(8,128)(2,1)} %maximum_select_fusion.1), channel_id=1, source_target_pairs={{0,32},{32,0},{64,96},{96,64},{128,160},{160,128},{192,224},{224,1... | collective-permute-start | bytes 3342344 | tf_op jit(solution)/shard_map/ppermute | solution.py:86
  101.4 1.8 copy-start
  111.0 2.6 %copy-start.4 = (bf16[1024,511]{0,1:T(8,128)(2,1)S(1)}, bf16[1024,511]{0,1:T(8,128)(2,1)}, u32[]{:S(2)}) copy-start(bf16[1024,511]{0,1:T(8,128)(2,1)} %fusion.9) | copy-start | bytes 3139588
  127.0 5.5 %collective-permute-start.12 = (f32[4,512]{1,0:T(4,128)S(1)}, f32[4,512]{1,0:T(4,128)S(1)}, u32[]{:S(2)}, u32[]{:S(2)}) collective-permute-start(f32[4,512]{1,0:T(4,128)S(1)} %pad_maximum_fusion.13), channel_id=1, source_target_pairs={{0,1},{1,0},{2,3},{3,2},{4,5},{5,4},{6,7},{7,6},{8,9},{9,8},{10,11... | collective-permute-start | bytes 24584 | tf_op jit(solution)/shard_map/ppermute | solution.py:120
  132.6 6.4 %collective-permute-start.13 = (f32[4,512]{1,0:T(4,128)S(1)}, f32[4,512]{1,0:T(4,128)S(1)}, u32[]{:S(2)}, u32[]{:S(2)}) collective-permute-start(f32[4,512]{1,0:T(4,128)S(1)} %fusion.55), channel_id=1, source_target_pairs={{0,2},{1,3},{2,0},{3,1},{4,6},{5,7},{6,4},{7,5},{8,10},{9,11},{10,... | collective-permute-start | bytes 24584 | tf_op jit(solution)/shard_map/ppermute | solution.py:120
  139.0 9.5 %collective-permute-start.14 = (f32[4,512]{1,0:T(4,128)S(1)}, f32[4,512]{1,0:T(4,128)S(1)}, u32[]{:S(2)}, u32[]{:S(2)}) collective-permute-start(f32[4,512]{1,0:T(4,128)S(1)} %fusion.66), channel_id=1, source_target_pairs={{0,4},{1,5},{2,6},{3,7},{4,0},{5,1},{6,2},{7,3},{8,12},{9,13},{10,... | collective-permute-start | bytes 24584 | tf_op jit(solution)/shard_map/ppermute | solution.py:120
  148.5 5.6 %collective-permute-start.15 = (f32[4,512]{1,0:T(4,128)S(1)}, f32[4,512]{1,0:T(4,128)S(1)}, u32[]{:S(2)}, u32[]{:S(2)}) collective-permute-start(f32[4,512]{1,0:T(4,128)S(1)} %add.183), channel_id=1, source_target_pairs={{0,8},{1,9},{2,10},{3,11},{4,12},{5,13},{6,14},{7,15},{8,0},{9,1},... | collective-permute-start | bytes 24584 | tf_op jit(solution)/shard_map/ppermute | solution.py:120
  154.1 7.0 %collective-permute-start.16 = (f32[4,512]{1,0:T(4,128)S(1)}, f32[4,512]{1,0:T(4,128)S(1)}, u32[]{:S(2)}, u32[]{:S(2)}) collective-permute-start(f32[4,512]{1,0:T(4,128)S(1)} %add.184), channel_id=1, source_target_pairs={{0,16},{1,17},{2,18},{3,19},{4,20},{5,21},{6,22},{7,23},{8,24},{9,... | collective-permute-start | bytes 24584 | tf_op jit(solution)/shard_map/ppermute | solution.py:120
  161.1 3.1 %collective-permute-start.17 = (f32[3072]{0:T(1024)S(1)}, f32[3072]{0:T(1024)S(1)}, u32[]{:S(2)}, u32[]{:S(2)}) collective-permute-start(f32[3072]{0:T(1024)S(1)} %pad_maximum_fusion.9), channel_id=1, source_target_pairs={{0,32},{32,0},{64,96},{96,64},{128,160},{160,128},{192,224},{224,1... | collective-permute-start | bytes 36872 | tf_op jit(solution)/shard_map/ppermute | solution.py:127
  164.5 5.6 %collective-permute-start.18 = (f32[2560]{0:T(1024)S(1)}, f32[2560]{0:T(1024)S(1)}, u32[]{:S(2)}, u32[]{:S(2)}) collective-permute-start(f32[2560]{0:T(1024)S(1)} %pad_maximum_fusion.10), channel_id=1, source_target_pairs={{0,64},{32,96},{64,0},{96,32},{128,192},{160,224},{192,128},{224,1... | collective-permute-start | bytes 30728 | tf_op jit(solution)/shard_map/ppermute | solution.py:127
  170.3 7.1 %collective-permute-start.19 = (f32[2304]{0:T(1024)S(1)}, f32[2304]{0:T(1024)S(1)}, u32[]{:S(2)}, u32[]{:S(2)}) collective-permute-start(f32[2304]{0:T(1024)S(1)} %pad_maximum_fusion.11), channel_id=1, source_target_pairs={{0,128},{32,160},{64,192},{96,224},{128,0},{160,32},{192,64},{224,... | collective-permute-start | bytes 27656 | tf_op jit(solution)/shard_map/ppermute | solution.py:127
  177.7 14.3 %collective-permute-start.20 = (f32[2176]{0:T(1024)S(1)}, f32[2176]{0:T(1024)S(1)}, u32[]{:S(2)}, u32[]{:S(2)}) collective-permute-start(f32[2176]{0:T(1024)S(1)} %pad_maximum_fusion.12), channel_id=1, source_target_pairs={{0,256},{32,288},{64,320},{96,352},{128,384},{160,416},{192,448},{... | collective-permute-start | bytes 26120 | tf_op jit(solution)/shard_map/ppermute | solution.py:127
  (4 other events, 6.1 us)
